TPU v7x, 256 devices: a whole 4x4x8 slice. The times are simulated.
256 devices in a mesh: chan: 64 (over y, z_lo, x), win: 4 (over z_hi, core).
Axes of the slice: x: 4, y: 4, z: 8 (z_hi: 2, z_lo: 4; z = z_hi * 4 + z_lo), core: 2. Of those that a mesh axis runs over, the one named last changes fastest.
Arguments:
- records: bfloat16 [4, 1024, 7680], P('win', 'chan'), may hold values from -6 to 6
- source_rows: int32 [1, 256], replicated, may hold values from 0 to 15
Outputs:
- correlation: float32 [256, 1024, 2048], P(None, ('chan', 'win'))
Inputs may be any that keep to these rules, and one draw needn't show every extreme that they name: Entry j of row b of source_rows names a channel of channel shard j // 4, counted within that shard; entries may repeat.
All inputs are finite; a program needn't handle non-finite values.
Results may differ from a plain program's by a relative error of at most 0.0063.
Values may be sent and summed in bfloat16 or wider, within the bound.
No kernel may reach another device: no remote copies, remote signals or barrier semaphores. Data moves between devices by JAX's collectives and lax.ppermute only.
A program may use at most 64 MiB of HBM per device.

v0:
```python
import math

import jax
import jax.numpy as jnp
from jax import lax
from jax.sharding import PartitionSpec as P

S = 7680
NBINS = 512
HALF = 32
FIRST_BIN = 64
MAXLAG = 1024


full_turn = 2.0 * math.pi


def band_table():
    bin_ids = FIRST_BIN - HALF + jnp.arange(NBINS + 2 * HALF, dtype=jnp.int32)
    sample_ids = jnp.arange(S, dtype=jnp.int32)
    angles = (sample_ids[:, None] * bin_ids[None, :] % S).astype(jnp.float32) * (full_turn / S)
    return jnp.concatenate([jnp.cos(angles), -jnp.sin(angles)], axis=1).astype(jnp.bfloat16)


def lag_weights():
    bin_ids = FIRST_BIN + jnp.arange(NBINS, dtype=jnp.int32)
    lag_ids = jnp.arange(2 * MAXLAG, dtype=jnp.int32) - MAXLAG
    angles = (bin_ids[:, None] * lag_ids[None, :] % S).astype(jnp.float32) * (full_turn / S)
    return jnp.concatenate([jnp.cos(angles), -jnp.sin(angles)], axis=0).astype(jnp.bfloat16)


def normalize(spectrum):
    extent = NBINS + 2 * HALF
    real_part = spectrum[:, :extent]
    imag_part = spectrum[:, extent:]
    magnitude = jnp.sqrt(real_part * real_part + imag_part * imag_part)
    smooth = magnitude[:, 0:NBINS]
    for offset in range(1, 2 * HALF + 1):
        smooth = smooth + magnitude[:, offset : offset + NBINS]
    smooth = smooth / (2 * HALF + 1) + 1e-06
    centre_re = real_part[:, HALF : HALF + NBINS] / smooth
    centre_im = imag_part[:, HALF : HALF + NBINS] / smooth
    return jnp.stack([centre_re, centre_im], axis=1).astype(jnp.bfloat16)


def whiten(row_data):
    return normalize(jnp.dot(row_data, band_table(), preferred_element_type=jnp.float32))


def cross_terms(source_part, receiver_part):
    real_sum = jnp.einsum(
        "wbi,wri->bri",
        source_part[:, :, 0],
        receiver_part[:, :, 0],
        preferred_element_type=jnp.float32,
    ) + jnp.einsum(
        "wbi,wri->bri",
        source_part[:, :, 1],
        receiver_part[:, :, 1],
        preferred_element_type=jnp.float32,
    )
    imag_sum = jnp.einsum(
        "wbi,wri->bri",
        source_part[:, :, 1],
        receiver_part[:, :, 0],
        preferred_element_type=jnp.float32,
    ) - jnp.einsum(
        "wbi,wri->bri",
        source_part[:, :, 0],
        receiver_part[:, :, 1],
        preferred_element_type=jnp.float32,
    )
    return jnp.stack([real_sum, imag_sum], axis=2)


def transform(spectra, weights, lag_scale):
    count_src, count_rec = (spectra.shape[0], spectra.shape[1])
    rounded = spectra.astype(jnp.bfloat16).reshape(count_src * count_rec, 2 * NBINS)
    result = jnp.dot(rounded, weights, preferred_element_type=jnp.float32) * lag_scale
    return result.reshape(count_src, count_rec, 2 * MAXLAG)


def collect(portion):
    portion = lax.all_gather(portion, "win", axis=0, tiled=True)
    return lax.all_gather(portion, "chan", axis=1, tiled=True)


def per_device(records, source_rows):
    windows_here, rows_here, samples = records.shape
    whitened = whiten(records.reshape(windows_here * rows_here, samples)).reshape(
        windows_here, rows_here, 2, NBINS
    )
    shards = lax.axis_size("chan")
    block_len = source_rows.shape[1]
    per_shard = block_len // shards
    weights = lag_weights()
    lag_scale = math.sqrt(2.0 / (lax.axis_size("win") * windows_here * NBINS))
    receivers = lax.all_to_all(whitened, "win", split_axis=1, concat_axis=0, tiled=True)
    everything = collect(whitened)
    base_rows = jnp.arange(block_len, dtype=jnp.int32) // per_shard * rows_here
    chosen_rows = source_rows[0]
    source_block = jnp.take(everything, base_rows + chosen_rows, axis=1)
    spectra = cross_terms(source_block, receivers)
    results = transform(spectra, weights, lag_scale)
    return results


def solution(mesh):
    in_specs = (P("win", "chan", None), P())
    out_specs = P(None, ("chan", "win"), None)
    return jax.shard_map(
        per_device, mesh=mesh, in_specs=in_specs, out_specs=out_specs, check_vma=False
    )
```

profile of v0, /device:TPU:2, one launch (start us, length us, event | category | flops | bytes accessed | tf_op | source)
XLA Modules:
  0.0 507.7 jit_solution(3730280382849712514)
XLA Ops:
  6.5 0.0 copy-start
  6.5 0.0 all-gather.2.cloned.1.call-start
  6.5 74.1 %cosine_convert_fusion = (bf16[7680,576]{0,1:T(8,128)(2,1)S(1)}, bf16[7680,576]{0,1:T(8,128)(2,1)S(1)}) fusion(s32[576]{0:T(1024)S(1)} %iota_add_fusion.1), kind=kLoop, calls=%fused_computation.9 | loop fusion | flops 53084160 | bytes 17697024 | tf_op jit(solution)/shard_map/convert.12
  80.6 0.0 copy-done
  80.6 0.0 copy-start.4
  80.6 4.6 fusion.17
  85.3 0.1 fusion.30
  85.4 0.6 fusion.35
  86.0 0.1 fusion.36
  86.1 10.8 %all_gather.6 = bf16[4,16,2,512]{3,1,2,0:T(8,128)(2,1)S(1)} all-gather(bf16[1,16,2,512]{3,1,2,0:T(8,128)(2,1)S(1)} %pad_maximum_fusion.1), channel_id=1, replica_groups=mesh['chan'=64,'win'=4] {'win'}, dimensions={0}, use_global_device_ids=true | all-gather | bytes 163840 | tf_op jit(solution)/shard_map/all_gather | solution.py:84
  96.9 0.8 copy.32
  97.7 0.0 all-gather.2.cloned.1.call-update
  97.7 0.6 copy.30
  98.4 7.1 %all-to-all-start = ((bf16[1,16,2,512]{3,2,0,1:T(2,128)(2,1)}), bf16[1,16,2,512]{3,2,0,1:T(2,128)(2,1)S(1)}, u32[]{:S(2)}, u32[]{:S(2)}) async-start(bf16[1,16,2,512]{3,2,0,1:T(2,128)(2,1)} %copy.30), calls=%async_computation | async-start | bytes 65536 | tf_op jit(solution)/shard_map/all_to_all | solution.py:98
  105.4 0.0 copy-done.4
  105.5 19.4 %cosine_convert_fusion.1 = (bf16[512,2048]{1,0:T(8,128)(2,1)}, bf16[512,2048]{1,0:T(8,128)(2,1)}) fusion(s32[2048]{0:T(1024)S(1)} %iota_add_fusion, s32[512]{0:T(512)S(1)} %iota_add_fusion.2), kind=kLoop, calls=%fused_computation.22 | loop fusion | flops 12582912 | bytes 4204544 | tf_op jit(solution)/shard_map/convert
  124.9 0.0 all-to-all-done
  124.9 0.1 fusion.44
  125.0 0.4 copy.36
  125.3 0.4 copy.37
  125.7 334.5 %all-gather.2.cloned.1.call-done = bf16[4,1024,2,512]{3,0,2,1:T(4,128)(2,1)} async-done(((bf16[4,16,2,512]{3,0,2,1:T(4,128)(2,1)}), bf16[4,1024,2,512]{3,0,2,1:T(4,128)(2,1)}) %all-gather.2.cloned.1.call-update) | async-done | bytes 8388624 | tf_op jit(solution)/shard_map/all_gather | solution.py:85
  460.2 5.8 %gather_fusion = bf16[256,4,2,512]{3,1,2,0:T(4,128)(2,1)S(1)} fusion(bf16[4,1024,2,512]{3,0,2,1:T(4,128)(2,1)} %all-gather.2.cloned.1.call-done, s32[1024]{0:T(1024)S(1)} %pad_clamp_fusion), kind=kCustom, calls=%fused_computation | custom fusion | bytes 4195328 | tf_op jit(solution)/shard_map/jit(_take)/gather | solution.py:102
  466.0 4.3 copy.33
  470.3 2.5 select_bitcast_fusion
  472.8 0.7 fusion.22
  473.5 0.7 fusion.23
  474.2 0.8 fusion.20
  475.0 0.8 fusion.21
  475.8 1.5 pad_maximum_fusion
  477.3 4.3 copy.35
  481.6 0.0 copy-start.2
  481.6 0.0 copy-start.3
  481.6 2.3 copy.38
  483.9 0.0 copy-done.2
  483.9 0.5 copy-done.3
  484.4 6.7 %convolution_multiply_fusion = f32[1024,2048]{1,0:T(8,128)} fusion(bf16[1024,1024]{1,0:T(8,128)(2,1)S(1)} %bitcast.47, bf16[512,2048]{1,0:T(8,128)(2,1)S(1)} %copy-done.3, bf16[512,2048]{1,0:T(8,128)(2,1)S(1)} %copy-done.2), kind=kOutput, calls=%fused_computation.15 | convolution fusion | flops 4305453056 | bytes 14680064 | tf_op jit(solution)/shard_map/dot_general | solution.py:79
  491.1 0.0 copy-start.1
  491.1 9.8 %reshape.122 = f32[256,4,2048]{2,1,0:T(4,128)} reshape(f32[1024,2048]{1,0:T(8,128)} %convolution_multiply_fusion) | data formatting | bytes 16777216 | tf_op jit(solution)/shard_map/reshape | solution.py:80
  500.9 0.0 copy-done.1
  (7 shorter events, 0.0 us)
Async XLA Ops:
  6.5 74.1 %copy-start = (bf16[1,16,7680]{2,1,0:T(8,128)(2,1)S(1)}, bf16[1,16,7680]{2,1,0:T(8,128)(2,1)}, u32[]{:S(2)}) copy-start(bf16[1,16,7680]{2,1,0:T(8,128)(2,1)} %param.2) | copy-start | bytes 737284
  6.5 453.6 %all-gather.2.cloned.1.call-start = ((), (), s32[]{:S(2)}) async-start(), calls=%async_computation.1 | async-start | bytes 8519680 | tf_op jit(solution)/shard_map/all_gather | solution.py:85
  80.6 24.8 %copy-start.4 = (s32[1,256]{1,0:T(1,128)S(1)}, s32[1,256]{1,0:T(1,128)}, u32[]{:S(2)}) copy-start(s32[1,256]{1,0:T(1,128)} %param.3) | copy-start | bytes 3076
  98.4 26.5 %all-to-all-start = ((bf16[1,16,2,512]{3,2,0,1:T(2,128)(2,1)}), bf16[1,16,2,512]{3,2,0,1:T(2,128)(2,1)S(1)}, u32[]{:S(2)}, u32[]{:S(2)}) async-start(bf16[1,16,2,512]{3,2,0,1:T(2,128)(2,1)} %copy.30), calls=%async_computation | async-start | bytes 65536 | tf_op jit(solution)/shard_map/all_to_all | solution.py:98
  481.6 2.3 copy-start.2
  481.6 2.9 copy-start.3
  491.1 9.8 %copy-start.1 = (bf16[1,16,7680]{2,1,0:T(8,128)(2,1)S(1)}, bf16[1,16,7680]{2,1,0:T(8,128)(2,1)}, u32[]{:S(2)}) copy-start(bf16[1,16,7680]{2,1,0:T(8,128)(2,1)} %param.2) | copy-start | bytes 737284
Sparse Core Ops, SparseCore 0:
  97.9 362.2 all-gather.1
where the time goes:
time: 508 us
  waiting for transfers between devices  334 us (66%)
  other arithmetic  98.3 us (19%)
  local copies, waits for them, and re-layouts  29.2 us (6%)
  matrix products  14.3 us (3%)
  between operations  13.5 us (3%)
  blocking collectives  10.8 us (2%)
  starting transfers between devices  7.07 us (1%)
    all_gather x1, waiting for transfers between devices, collect(): return lax.all_gather(portion, 'chan', axis=1, tiled=True)  334 us
    another operation x2, other arithmetic  93.5 us
    all_gather x1, blocking collectives, collect(): portion = lax.all_gather(portion, 'win', axis=0, tiled=True)  10.8 us
  transfers between devices with their start and end apart: 2, of which 1 were waited for; matrix products, arithmetic and copies ran while one was open for 4% of the time, Pallas kernels for 0%

commit v1 on v0

--- a/solution.py
+++ b/solution.py
@@ -96,10 +96,10 @@
     weights = lag_weights()
     lag_scale = math.sqrt(2.0 / (lax.axis_size("win") * windows_here * NBINS))
     receivers = lax.all_to_all(whitened, "win", split_axis=1, concat_axis=0, tiled=True)
-    everything = collect(whitened)
-    base_rows = jnp.arange(block_len, dtype=jnp.int32) // per_shard * rows_here
-    chosen_rows = source_rows[0]
-    source_block = jnp.take(everything, base_rows + chosen_rows, axis=1)
+    shard = lax.axis_index("chan")
+    own_rows = lax.dynamic_slice_in_dim(source_rows[0], shard * per_shard, per_shard)
+    own_sources = jnp.take(whitened, own_rows, axis=1)
+    source_block = collect(own_sources)
     spectra = cross_terms(source_block, receivers)
     results = transform(spectra, weights, lag_scale)
     return results

time: 508 us -> 493 us (0.970)
  waiting for transfers between devices: 334 us -> 323 us
    all_gather x1, waiting for transfers between devices: 334 us -> 322 us  [collect(): return lax.all_gather(portion, 'chan', axis=1, tiled=True)]
    gather x2 -> x1, local copies, waits for them, and re-layouts: 10.1 us -> 0.58 us  [per_device(): own_sources = jnp.take(whitened, own_rows, axis=1)]
where the time goes in v1:
time: 493 us; the launch traced here: 492 us
  waiting for transfers between devices  323 us (66%)
  other arithmetic  97.4 us (20%)
  local copies, waits for them, and re-layouts  26.7 us (5%)
  matrix products  14.4 us (3%)
  between operations  13.5 us (3%)
  blocking collectives  10.4 us (2%)
  starting transfers between devices  7.14 us (1%)
    all_gather x1, waiting for transfers between devices, collect(): return lax.all_gather(portion, 'chan', axis=1, tiled=True)  322 us
    another operation x2, other arithmetic  93.5 us
    all_gather x1, blocking collectives, collect(): portion = lax.all_gather(portion, 'win', axis=0, tiled=True)  10.4 us
  transfers between devices with their start and end apart: 2, of which 1 were waited for; matrix products, arithmetic and copies ran while one was open for 4% of the time, Pallas kernels for 0%

profile of v1, /device:TPU:2, one launch (start us, length us, event | category | flops | bytes accessed | tf_op | source)
XLA Modules:
  0.0 492.1 jit_solution(3120284951984374579)
XLA Ops:
  6.5 0.0 copy-start
  6.5 0.0 all-gather.2.cloned.1.call-start
  6.5 0.8 fusion.41
  7.3 0.7 compare_and_fusion
  8.0 74.1 %cosine_convert_fusion = (bf16[7680,576]{0,1:T(8,128)(2,1)S(1)}, bf16[7680,576]{0,1:T(8,128)(2,1)S(1)}) fusion(s32[576]{0:T(1024)S(1)} %iota_add_fusion.1), kind=kLoop, calls=%fused_computation.9 | loop fusion | flops 53084160 | bytes 17697024 | tf_op jit(solution)/shard_map/convert.12
  82.1 0.0 copy-done
  82.1 4.6 fusion.17
  86.8 0.1 fusion.34
  86.9 0.6 fusion.39
  87.5 0.1 fusion.40
  87.7 0.6 gather_fusion
  88.2 0.1 broadcast_select_fusion
  88.3 10.4 %all_gather.6 = bf16[4,4,2,512]{3,1,2,0:T(4,128)(2,1)S(1)} all-gather(bf16[1,4,2,512]{3,1,2,0:T(4,128)(2,1)S(1)} %copy.38), channel_id=1, replica_groups=mesh['chan'=64,'win'=4] {'win'}, dimensions={0}, use_global_device_ids=true | all-gather | bytes 40960 | tf_op jit(solution)/shard_map/all_gather | solution.py:84
  98.8 0.6 copy.39
  99.4 0.0 all-gather.2.cloned.1.call-update
  99.4 0.6 copy.35
  100.1 7.1 %all-to-all-start = ((bf16[1,16,2,512]{3,2,0,1:T(2,128)(2,1)}), bf16[1,16,2,512]{3,2,0,1:T(2,128)(2,1)S(1)}, u32[]{:S(2)}, u32[]{:S(2)}) async-start(bf16[1,16,2,512]{3,2,0,1:T(2,128)(2,1)} %copy.35), calls=%async_computation | async-start | bytes 65536 | tf_op jit(solution)/shard_map/all_to_all | solution.py:98
  107.2 19.4 %cosine_convert_fusion.1 = (bf16[512,2048]{1,0:T(8,128)(2,1)}, bf16[512,2048]{1,0:T(8,128)(2,1)}) fusion(s32[2048]{0:T(1024)S(1)} %iota_add_fusion, s32[512]{0:T(512)S(1)} %iota_add_fusion.2), kind=kLoop, calls=%fused_computation.22 | loop fusion | flops 12582912 | bytes 4204544 | tf_op jit(solution)/shard_map/convert
  126.6 0.0 all-to-all-done
  126.6 0.1 fusion.47
  126.7 0.4 copy.44
  127.0 0.4 copy.46
  127.4 322.5 %all-gather.2.cloned.1.call-done = bf16[4,256,2,512]{3,0,2,1:T(4,128)(2,1)} async-done(((bf16[4,4,2,512]{3,0,2,1:T(4,128)(2,1)}), bf16[4,256,2,512]{3,0,2,1:T(4,128)(2,1)}) %all-gather.2.cloned.1.call-update) | async-done | bytes 2097168 | tf_op jit(solution)/shard_map/all_gather | solution.py:85
  449.9 3.2 fusion.46
  453.1 1.2 copy.45
  454.4 2.7 copy.47
  457.1 0.7 fusion.26
  457.8 0.7 fusion.22
  458.5 0.9 fusion.20
  459.4 0.9 fusion.21
  460.2 1.5 pad_maximum_fusion
  461.7 4.3 copy.43
  466.0 0.0 copy-start.1
  466.0 0.0 copy-start.2
  466.0 2.3 copy.48
  468.3 0.0 copy-done.1
  468.3 0.5 copy-done.2
  468.8 6.7 %convolution_multiply_fusion = f32[1024,2048]{1,0:T(8,128)} fusion(bf16[1024,1024]{1,0:T(8,128)(2,1)S(1)} %bitcast.53, bf16[512,2048]{1,0:T(8,128)(2,1)S(1)} %copy-done.2, bf16[512,2048]{1,0:T(8,128)(2,1)S(1)} %copy-done.1), kind=kOutput, calls=%fused_computation.15 | convolution fusion | flops 4305453056 | bytes 14680064 | tf_op jit(solution)/shard_map/dot_general | solution.py:79
  475.5 9.7 %reshape.102 = f32[256,4,2048]{2,1,0:T(4,128)} reshape(f32[1024,2048]{1,0:T(8,128)} %convolution_multiply_fusion) | data formatting | bytes 16777216 | tf_op jit(solution)/shard_map/reshape | solution.py:80
  (7 shorter events, 0.1 us)
Async XLA Ops:
  6.5 75.6 %copy-start = (bf16[1,16,7680]{2,1,0:T(8,128)(2,1)S(1)}, bf16[1,16,7680]{2,1,0:T(8,128)(2,1)}, u32[]{:S(2)}) copy-start(bf16[1,16,7680]{2,1,0:T(8,128)(2,1)} %param.2) | copy-start | bytes 737284
  6.5 443.4 %all-gather.2.cloned.1.call-start = ((), (), s32[]{:S(2)}) async-start(), calls=%async_computation.1 | async-start | bytes 2129920 | tf_op jit(solution)/shard_map/all_gather | solution.py:85
  100.1 26.6 %all-to-all-start = ((bf16[1,16,2,512]{3,2,0,1:T(2,128)(2,1)}), bf16[1,16,2,512]{3,2,0,1:T(2,128)(2,1)S(1)}, u32[]{:S(2)}, u32[]{:S(2)}) async-start(bf16[1,16,2,512]{3,2,0,1:T(2,128)(2,1)} %copy.35), calls=%async_computation | async-start | bytes 65536 | tf_op jit(solution)/shard_map/all_to_all | solution.py:98
  466.0 2.3 copy-start.1
  466.0 2.9 copy-start.2
Sparse Core Ops, SparseCore 0:
  99.5 350.3 all-gather.1

commit v2 on v1

--- a/solution.py
+++ b/solution.py
@@ -1,9 +1,11 @@
 import math
+
+import numpy as np
 
 import jax
 import jax.numpy as jnp
 from jax import lax
-from jax.sharding import PartitionSpec as P
+from jax.sharding import Mesh, PartitionSpec as P
 
 S = 7680
 NBINS = 512
@@ -11,22 +13,41 @@
 FIRST_BIN = 64
 MAXLAG = 1024
 
+CHAN_AXES = ("y", "zl", "x")
+WIN_AXES = ("zh", "core")
 
-full_turn = 2.0 * math.pi
+
+def angle_table(rows, cols):
+    turns = np.mod(np.outer(rows.astype(np.int64), cols.astype(np.int64)), S).astype(np.float64)
+    angles = turns * (2.0 * np.pi / S)
+    return np.cos(angles).astype(np.float32), np.sin(angles).astype(np.float32)
 
 
 def band_table():
-    bin_ids = FIRST_BIN - HALF + jnp.arange(NBINS + 2 * HALF, dtype=jnp.int32)
-    sample_ids = jnp.arange(S, dtype=jnp.int32)
-    angles = (sample_ids[:, None] * bin_ids[None, :] % S).astype(jnp.float32) * (full_turn / S)
-    return jnp.concatenate([jnp.cos(angles), -jnp.sin(angles)], axis=1).astype(jnp.bfloat16)
+    extent = NBINS + 2 * HALF
+    bin_ids = np.arange(FIRST_BIN - HALF, FIRST_BIN - HALF + extent)
+    inner = 128
+    outer = S // inner
+    cq, sq = angle_table(np.arange(outer) * inner, bin_ids)
+    cr, sr = angle_table(np.arange(inner), bin_ids)
+    cq, sq, cr, sr = (jnp.asarray(a) for a in (cq, sq, cr, sr))
+    cos = cq[:, None, :] * cr[None, :, :] - sq[:, None, :] * sr[None, :, :]
+    sin = sq[:, None, :] * cr[None, :, :] + cq[:, None, :] * sr[None, :, :]
+    table = jnp.concatenate([cos, -sin], axis=2).astype(jnp.bfloat16)
+    return table.reshape(S, 2 * extent)
 
 
 def lag_weights():
-    bin_ids = FIRST_BIN + jnp.arange(NBINS, dtype=jnp.int32)
-    lag_ids = jnp.arange(2 * MAXLAG, dtype=jnp.int32) - MAXLAG
-    angles = (bin_ids[:, None] * lag_ids[None, :] % S).astype(jnp.float32) * (full_turn / S)
-    return jnp.concatenate([jnp.cos(angles), -jnp.sin(angles)], axis=0).astype(jnp.bfloat16)
+    bin_ids = FIRST_BIN + np.arange(NBINS)
+    inner = 64
+    outer = 2 * MAXLAG // inner
+    ca, sa = angle_table(bin_ids, (np.arange(outer) - MAXLAG // inner) * inner)
+    cb, sb = angle_table(bin_ids, np.arange(inner))
+    ca, sa, cb, sb = (jnp.asarray(a) for a in (ca, sa, cb, sb))
+    cos = ca[:, :, None] * cb[:, None, :] - sa[:, :, None] * sb[:, None, :]
+    sin = sa[:, :, None] * cb[:, None, :] + ca[:, :, None] * sb[:, None, :]
+    table = jnp.concatenate([cos, -sin], axis=0).astype(jnp.bfloat16)
+    return table.reshape(2 * NBINS, 2 * MAXLAG)
 
 
 def normalize(spectrum):
@@ -80,9 +101,28 @@
     return result.reshape(count_src, count_rec, 2 * MAXLAG)
 
 
-def collect(portion):
-    portion = lax.all_gather(portion, "win", axis=0, tiled=True)
-    return lax.all_gather(portion, "chan", axis=1, tiled=True)
+def ring_gather(value, axis_name, axis):
+    size = lax.axis_size(axis_name)
+    here = lax.axis_index(axis_name)
+    parts = [value] + [
+        lax.ppermute(value, axis_name, [(i, (i + shift) % size) for i in range(size)])
+        for shift in range(1, size)
+    ]
+    stacked = jnp.stack(parts, 0)
+    stacked = jnp.take(stacked, (here - jnp.arange(size)) % size, axis=0)
+    stacked = jnp.moveaxis(stacked, 0, axis)
+    shape = list(value.shape)
+    shape[axis] *= size
+    return stacked.reshape(shape)
+
+
+def collect(own):
+    part = ring_gather(own[None], "zh", 0)
+    for name in reversed(CHAN_AXES):
+        part = ring_gather(part, name, 2)
+    part = ring_gather(part[None], "core", 0)
+    part = jnp.swapaxes(part, 0, 1)
+    return part.reshape(-1, part.shape[3], 2, NBINS)
 
 
 def per_device(records, source_rows):
@@ -90,13 +130,13 @@
     whitened = whiten(records.reshape(windows_here * rows_here, samples)).reshape(
         windows_here, rows_here, 2, NBINS
     )
-    shards = lax.axis_size("chan")
+    shards = lax.axis_size(CHAN_AXES)
     block_len = source_rows.shape[1]
     per_shard = block_len // shards
     weights = lag_weights()
-    lag_scale = math.sqrt(2.0 / (lax.axis_size("win") * windows_here * NBINS))
-    receivers = lax.all_to_all(whitened, "win", split_axis=1, concat_axis=0, tiled=True)
-    shard = lax.axis_index("chan")
+    lag_scale = math.sqrt(2.0 / (lax.axis_size(WIN_AXES) * windows_here * NBINS))
+    receivers = lax.all_to_all(whitened, WIN_AXES, split_axis=1, concat_axis=0, tiled=True)
+    shard = lax.axis_index(CHAN_AXES)
     own_rows = lax.dynamic_slice_in_dim(source_rows[0], shard * per_shard, per_shard)
     own_sources = jnp.take(whitened, own_rows, axis=1)
     source_block = collect(own_sources)
@@ -105,9 +145,17 @@
     return results
 
 
+def split_mesh(mesh):
+    chan, win = mesh.shape["chan"], mesh.shape["win"]
+    side = round(chan ** (1 / 3))
+    devices = np.asarray(mesh.devices).reshape(side, side, chan // (side * side), win // 2, 2)
+    return Mesh(devices, CHAN_AXES + WIN_AXES)
+
+
 def solution(mesh):
-    in_specs = (P("win", "chan", None), P())
-    out_specs = P(None, ("chan", "win"), None)
+    fine = split_mesh(mesh)
+    in_specs = (P(WIN_AXES, CHAN_AXES, None), P())
+    out_specs = P(None, CHAN_AXES + WIN_AXES, None)
     return jax.shard_map(
-        per_device, mesh=mesh, in_specs=in_specs, out_specs=out_specs, check_vma=False
+        per_device, mesh=fine, in_specs=in_specs, out_specs=out_specs, check_vma=False
     )

time: 493 us -> 135 us (0.27)
  the two profiles are of different devices: /device:TPU:2 before, /device:TPU:1 now
where the time goes in v2:
time: 135 us; the launch traced here: 134 us
  local copies, waits for them, and re-layouts  38.3 us (28%)
  starting transfers between devices  31.1 us (23%)
  other arithmetic  25.6 us (19%)
  waiting for transfers between devices  21.1 us (16%)
  matrix products  17.5 us (13%)
    ppermute x11, starting transfers between devices, ring_gather(): lax.ppermute(value, axis_name, [(i, (i + shift) % size) for i in range(si...  24.9 us
    ppermute x11, waiting for transfers between devices, ring_gather(): lax.ppermute(value, axis_name, [(i, (i + shift) % size) for i in range(si...  17.4 us
    unnamed x1, other arithmetic  13.1 us
    reshape x1, local copies, waits for them, and re-layouts, transform(): return result.reshape(count_src, count_rec, 2 * MAXLAG)  9.79 us
    dot_general x1, matrix products, whiten(): jnp.dot(row_data, band_table(), preferred_element_type=jnp.float32)  7.52 us
    dot_general x1, matrix products, transform(): jnp.dot(rounded, weights, preferred_element_type=jnp.float32) * lag_scale  6.85 us
    all_to_all x1, starting transfers between devices, per_device(): lax.all_to_all(whitened, WIN_AXES, split_axis=1, concat_axis=0, tiled=True)  6.26 us
    gather x5, local copies, waits for them, and re-layouts, ring_gather(): stacked = jnp.take(stacked, (here - jnp.arange(size)) % size, axis=0)  4.96 us
  transfers between devices with their start and end apart: 12, of which 10 were waited for; matrix products, arithmetic and copies ran while one was open for 4% of the time, Pallas kernels for 0%

profile of v2, /device:TPU:1, one launch (start us, length us, event | category | flops | bytes accessed | tf_op | source)
XLA Modules:
  0.0 134.0 jit_solution(16759808137193148158)
XLA Ops:
  0.0 0.8 compare_and_fusion
  0.8 0.7 fusion.43
  1.5 13.1 %fusion.4 = (bf16[60,72,8,128]{3,2,1,0:T(8,128)(2,1)S(1)}, bf16[60,72,8,128]{3,2,1,0:T(8,128)(2,1)S(1)}) fusion(f32[128,576]{0,1:T(8,128)} %constant.179.clone, f32[60,576]{1,0:T(8,128)} %constant.177.clone, f32[128,576]{0,1:T(8,128)} %constant.178.clone, f32[60,576]{1,0:T(8,128)} %constant.176.clone), kind=kLoop, calls=%fused_computation.12 | loop fusion | flops 39813120 | bytes 18561024
  14.6 4.4 %copy_bitcast_fusion = (bf16[7680,576]{0,1:T(8,128)(2,1)S(1)}, bf16[7680,576]{0,1:T(8,128)(2,1)}) fusion(bf16[60,72,8,128]{3,2,1,0:T(8,128)(2,1)S(1)} %get-tuple-element.8, bf16[60,72,8,128]{3,2,1,0:T(8,128)(2,1)S(1)} %get-tuple-element.7), kind=kLoop, calls=%fused_computation.14 | loop fusion | bytes 35389440 | tf_op jit(solution)/shard_map/neg | solution.py:36
  19.0 7.5 %fusion.9 = f32[16,1152]{1,0:T(8,128)S(1)} fusion(bf16[7680,576]{0,1:T(8,128)(2,1)S(1)} %get-tuple-element.15, bf16[7680,576]{0,1:T(8,128)(2,1)} %get-tuple-element.16, bf16[1,16,7680]{2,1,0:T(8,128)(2,1)S(1)} %copy-done), kind=kOutput, calls=%fused_computation.22 | convolution fusion | flops 318504960 | bytes 18014208 | tf_op jit(solution)/shard_map/dot_general | solution.py:68
  26.5 0.1 fusion.26
  26.7 0.6 fusion.31
  27.4 0.6 gather_fusion
  28.0 0.1 broadcast_select_fusion.4
  28.1 7.8 %collective-permute-start = (bf16[1,1,4,2,512]{4,3,2,1,0:T(2,128)(2,1)S(1)}, bf16[1,1,4,2,512]{4,3,2,1,0:T(2,128)(2,1)S(1)}, u32[]{:S(2)}, u32[]{:S(2)}) collective-permute-start(bf16[1,1,4,2,512]{4,3,2,1,0:T(2,128)(2,1)S(1)} %broadcast_select_fusion.4), channel_id=1, source_target_pairs={{0,2},{2,0},{1,3},{3,1},{4,6},{6,4},{5,7},{7,5},{8,10},{10,8},{9,1... | collective-permute-start | bytes 24584 | tf_op jit(solution)/shard_map/ppermute | solution.py:108
  35.9 0.1 broadcast_select_fusion.5
  36.2 0.8 collective-permute-done
  37.0 0.6 gather_fusion.1
  37.6 0.1 broadcast_select_fusion.2
  37.7 2.6 %collective-permute-start.3 = (bf16[2,1,4,2,512]{4,3,2,0,1:T(2,128)(2,1)S(1)}, bf16[2,1,4,2,512]{4,3,2,0,1:T(2,128)(2,1)S(1)}, u32[]{:S(2)}, u32[]{:S(2)}) collective-permute-start(bf16[2,1,4,2,512]{4,3,2,0,1:T(2,128)(2,1)S(1)} %broadcast_select_fusion.2), channel_id=1, source_target_pairs={{0,12},{4,0},{8,4},{12,8},{1,13},{5,1},{9,5},{13,9},{2,14},{6,2},{... | collective-permute-start | bytes 49160 | tf_op jit(solution)/shard_map/ppermute | solution.py:108
  40.2 0.5 collective-permute-start.2
  40.8 0.6 collective-permute-start.1
  41.4 0.1 broadcast_select_fusion.3
  41.5 2.9 %collective-permute-done.2 = bf16[2,1,4,2,512]{4,3,2,0,1:T(2,128)(2,1)S(1)} collective-permute-done((bf16[2,1,4,2,512]{4,3,2,0,1:T(2,128)(2,1)S(1)}, bf16[2,1,4,2,512]{4,3,2,0,1:T(2,128)(2,1)S(1)}, u32[]{:S(2)}, u32[]{:S(2)}) %collective-permute-start.2) | collective-permute-done | bytes 16416 | tf_op jit(solution)/shard_map/ppermute | solution.py:108
  44.3 0.2 collective-permute-done.1
  44.6 0.1 maximum_bitcast_fusion.3
  44.7 0.7 gather_fusion.2
  45.4 0.1 fusion.24
  45.6 2.9 %collective-permute-start.6 = (bf16[2,1,16,2,512]{4,3,2,0,1:T(2,128)(2,1)S(1)}, bf16[2,1,16,2,512]{4,3,2,0,1:T(2,128)(2,1)S(1)}, u32[]{:S(2)}, u32[]{:S(2)}) collective-permute-start(bf16[2,1,16,2,512]{4,3,2,0,1:T(2,128)(2,1)S(1)} %bitcast.143), channel_id=1, source_target_pairs={{0,48},{16,0},{32,16},{48,32},{1,49},{17,1},{33,17},{49,33},{2,50}... | collective-permute-start | bytes 196616 | tf_op jit(solution)/shard_map/ppermute | solution.py:108
  48.4 0.4 collective-permute-start.4
  48.8 0.9 collective-permute-done.6
  49.8 3.6 %collective-permute-done.5 = bf16[2,1,16,2,512]{4,3,2,0,1:T(2,128)(2,1)S(1)} collective-permute-done((bf16[2,1,16,2,512]{4,3,2,0,1:T(2,128)(2,1)S(1)}, bf16[2,1,16,2,512]{4,3,2,0,1:T(2,128)(2,1)S(1)}, u32[]{:S(2)}, u32[]{:S(2)}) %collective-permute-start.5) | collective-permute-done | bytes 65568 | tf_op jit(solution)/shard_map/ppermute | solution.py:108
  53.4 0.2 collective-permute-done.4
  53.6 0.5 maximum_bitcast_fusion.2
  54.0 1.1 gather_fusion.3
  55.1 0.3 fusion.22
  55.5 2.8 %collective-permute-start.9 = (bf16[2,1,64,2,512]{4,2,3,0,1:T(8,128)(2,1)S(1)}, bf16[2,1,64,2,512]{4,2,3,0,1:T(8,128)(2,1)S(1)}, u32[]{:S(2)}, u32[]{:S(2)}) collective-permute-start(bf16[2,1,64,2,512]{4,2,3,0,1:T(8,128)(2,1)S(1)} %bitcast.138), channel_id=1, source_target_pairs={{0,192},{64,0},{128,64},{192,128},{1,193},{65,1},{129,65},{193,129... | collective-permute-start | bytes 786440 | tf_op jit(solution)/shard_map/ppermute | solution.py:108
  58.3 0.3 collective-permute-start.8
  58.6 0.7 collective-permute-start.7
  59.4 5.4 %collective-permute-done.9 = bf16[2,1,64,2,512]{4,2,3,0,1:T(8,128)(2,1)S(1)} collective-permute-done((bf16[2,1,64,2,512]{4,2,3,0,1:T(8,128)(2,1)S(1)}, bf16[2,1,64,2,512]{4,2,3,0,1:T(8,128)(2,1)S(1)}, u32[]{:S(2)}, u32[]{:S(2)}) %collective-permute-start.9) | collective-permute-done | bytes 262176 | tf_op jit(solution)/shard_map/ppermute | solution.py:108
  64.7 0.4 collective-permute-done.8
  65.1 3.1 %collective-permute-done.7 = bf16[2,1,64,2,512]{4,2,3,0,1:T(8,128)(2,1)S(1)} collective-permute-done((bf16[2,1,64,2,512]{4,2,3,0,1:T(8,128)(2,1)S(1)}, bf16[2,1,64,2,512]{4,2,3,0,1:T(8,128)(2,1)S(1)}, u32[]{:S(2)}, u32[]{:S(2)}) %collective-permute-start.7) | collective-permute-done | bytes 262176 | tf_op jit(solution)/shard_map/ppermute | solution.py:108
  68.2 0.1 maximum_bitcast_fusion.1
  68.3 0.6 gather_fusion.4
  68.9 0.2 fusion.15
  69.1 0.1 copy.75
  69.2 6.3 %collective-permute-start.10 = (bf16[1,2,1,256,2,512]{5,3,4,1,2,0:T(8,128)(2,1)S(1)}, bf16[1,2,1,256,2,512]{5,3,4,1,2,0:T(8,128)(2,1)S(1)}, u32[]{:S(2)}, u32[]{:S(2)}) collective-permute-start(bf16[1,2,1,256,2,512]{5,3,4,1,2,0:T(8,128)(2,1)S(1)} %bitcast.132), channel_id=1, source_target_pairs={{0,1},{1,0},{2,3},{3,2},{4,5},{5,4},{6,7},{7,6},{8,9},{9,8},{10,11... | collective-permute-start | bytes 3145736 | tf_op jit(solution)/shard_map/ppermute | solution.py:108
  75.5 0.6 copy.68
  76.1 6.3 %all-to-all-start = ((bf16[1,16,2,512]{3,2,0,1:T(2,128)(2,1)}), bf16[1,16,2,512]{3,2,0,1:T(2,128)(2,1)S(1)}, u32[]{:S(2)}, u32[]{:S(2)}) async-start(bf16[1,16,2,512]{3,2,0,1:T(2,128)(2,1)} %copy.68), calls=%async_computation | async-start | bytes 65536 | tf_op jit(solution)/shard_map/all_to_all | solution.py:138
  82.4 3.3 %subtract_convert_fusion.1 = (bf16[512,32,64]{0,2,1:T(8,128)(2,1)}, bf16[512,32,64]{0,2,1:T(8,128)(2,1)}) fusion(f32[512,64]{0,1:T(8,128)S(1)} %copy-done.6, f32[512,32]{0,1:T(8,128)S(1)} %copy-done.8, f32[512,64]{0,1:T(8,128)S(1)} %copy-done.7, f32[512,32]{0,1:T(8,128)S(1)} %copy-done.9), kind=kLoop, calls=%fused_computation.21 | loop fusion | flops 9437184 | bytes 4587520 | tf_op jit(solution)/shard_map/convert.3
  85.8 3.7 %all-to-all-done = bf16[1,16,2,512]{3,2,0,1:T(2,128)(2,1)S(1)} async-done(((bf16[1,16,2,512]{3,2,0,1:T(2,128)(2,1)}), bf16[1,16,2,512]{3,2,0,1:T(2,128)(2,1)S(1)}, u32[]{:S(2)}, u32[]{:S(2)}) %all-to-all-start) | async-done | bytes 32800 | tf_op jit(solution)/shard_map/all_to_all | solution.py:138
  89.5 0.4 copy.81
  89.9 0.4 copy.82
  90.3 1.0 copy-done.5
  91.2 1.7 %maximum_bitcast_fusion = bf16[2,2,256,2,512]{4,2,3,1,0:T(8,128)(2,1)S(1)} fusion(bf16[1,1,2,1,256,2,512]{6,4,5,2,0,3,1:T(8,128)(2,1)} %bitcast.137, bf16[1,1,2,1,256,2,512]{6,4,5,2,0,3,1:T(8,128)(2,1)} %bitcast.133), kind=kLoop, calls=%fused_computation.23 | loop fusion | flops 1048576 | bytes 4194304 | tf_op jit(solution)/shard_map/stack | solution.py:111
  92.9 2.0 %gather_fusion.5 = bf16[2,2,256,2,512]{4,2,3,1,0:T(8,128)(2,1)} fusion(bf16[2,2,256,2,512]{4,2,3,1,0:T(8,128)(2,1)S(1)} %maximum_bitcast_fusion, s32[1024]{0:T(1024)S(1)} %pad_clamp_fusion), kind=kCustom, calls=%fused_computation.5 | custom fusion | bytes 4194312 | tf_op jit(solution)/shard_map/jit(_take)/gather | solution.py:112
  94.9 1.9 %fusion.12 = bf16[2,2,1,256,2,512]{5,3,4,0,1,2:T(8,128)(2,1)S(1)} fusion(bf16[2,2,256,2,512]{4,2,3,1,0:T(8,128)(2,1)} %gather_fusion.5, pred[2]{0:T(512)(128)(4,1)S(1)} %compare_and_fusion.5), kind=kLoop, calls=%fused_computation.26 | loop fusion | flops 1048576 | bytes 4194306 | tf_op jit(solution)/shard_map/transpose | solution.py:124
  96.8 3.9 %copy.78 = bf16[2,2,1,256,2,512]{3,1,0,5,4,2:T(2,128)(2,1)} copy(bf16[2,2,1,256,2,512]{5,3,4,0,1,2:T(8,128)(2,1)S(1)} %fusion.12) | data formatting | bytes 4194304 | tf_op jit(solution)/shard_map/transpose | solution.py:124
  100.7 4.9 %reshape.493 = bf16[4,256,2,512]{1,0,3,2:T(4,128)(2,1)S(1)} reshape(bf16[2,2,1,256,2,512]{3,1,0,5,4,2:T(2,128)(2,1)} %copy.78) | data formatting | bytes 4194304 | tf_op jit(solution)/shard_map/reshape | solution.py:125
  105.7 0.7 fusion.17
  106.4 0.7 fusion.16
  107.1 0.9 fusion.14
  107.9 0.9 fusion.13
  108.8 1.5 %pad_maximum_fusion = bf16[256,4,2,512]{0,1,3,2:T(4,128)(2,1)S(1)} fusion(bf16[256,4,1,512]{0,1,3,2:T(4,128)(2,1)S(1)} %fusion.14, bf16[256,4,1,512]{0,1,3,2:T(4,128)(2,1)S(1)} %fusion.13), kind=kLoop, calls=%fused_computation.24 | loop fusion | flops 1048576 | bytes 4194304 | tf_op jit(solution)/shard_map/stack | solution.py:94
  110.3 4.3 %copy.80 = bf16[256,4,2,512]{3,2,1,0:T(2,128)(2,1)} copy(bf16[256,4,2,512]{0,1,3,2:T(4,128)(2,1)S(1)} %pad_maximum_fusion) | data formatting | bytes 4194304 | tf_op jit(solution)/shard_map/stack | solution.py:94
  114.5 2.3 %copy.85 = bf16[128,8,2,512]{3,1,2,0:T(8,128)(2,1)S(1)} copy(bf16[128,8,2,512]{3,2,1,0:T(2,128)(2,1)} %bitcast.131) | data formatting | bytes 4194304
  116.9 0.5 copy-done.4
  117.4 6.8 %convolution_multiply_fusion = f32[1024,2048]{1,0:T(8,128)} fusion(bf16[1024,1024]{1,0:T(8,128)(2,1)S(1)} %bitcast.136, bf16[512,2048]{0,1:T(8,128)(2,1)S(1)} %bitcast.135, bf16[512,2048]{0,1:T(8,128)(2,1)S(1)} %bitcast.134), kind=kOutput, calls=%fused_computation.16 | convolution fusion | flops 4305453056 | bytes 14680064 | tf_op jit(solution)/shard_map/dot_general | solution.py:100
  124.2 9.8 %reshape.494 = f32[256,4,2048]{2,1,0:T(4,128)} reshape(f32[1024,2048]{1,0:T(8,128)} %convolution_multiply_fusion) | data formatting | bytes 16777216 | tf_op jit(solution)/shard_map/reshape | solution.py:101
  (44 shorter events, 0.5 us)
Async XLA Ops:
  0.0 19.0 %copy-start = (bf16[1,16,7680]{2,1,0:T(8,128)(2,1)S(1)}, bf16[1,16,7680]{2,1,0:T(8,128)(2,1)}, u32[]{:S(2)}) copy-start(bf16[1,16,7680]{2,1,0:T(8,128)(2,1)} %param.10) | copy-start | bytes 737284
  28.1 8.9 %collective-permute-start = (bf16[1,1,4,2,512]{4,3,2,1,0:T(2,128)(2,1)S(1)}, bf16[1,1,4,2,512]{4,3,2,1,0:T(2,128)(2,1)S(1)}, u32[]{:S(2)}, u32[]{:S(2)}) collective-permute-start(bf16[1,1,4,2,512]{4,3,2,1,0:T(2,128)(2,1)S(1)} %broadcast_select_fusion.4), channel_id=1, source_target_pairs={{0,2},{2,0},{1,3},{3,1},{4,6},{6,4},{5,7},{7,5},{8,10},{10,8},{9,1... | collective-permute-start | bytes 24584 | tf_op jit(solution)/shard_map/ppermute | solution.py:108
  37.7 3.8 %collective-permute-start.3 = (bf16[2,1,4,2,512]{4,3,2,0,1:T(2,128)(2,1)S(1)}, bf16[2,1,4,2,512]{4,3,2,0,1:T(2,128)(2,1)S(1)}, u32[]{:S(2)}, u32[]{:S(2)}) collective-permute-start(bf16[2,1,4,2,512]{4,3,2,0,1:T(2,128)(2,1)S(1)} %broadcast_select_fusion.2), channel_id=1, source_target_pairs={{0,12},{4,0},{8,4},{12,8},{1,13},{5,1},{9,5},{13,9},{2,14},{6,2},{... | collective-permute-start | bytes 49160 | tf_op jit(solution)/shard_map/ppermute | solution.py:108
  40.2 4.1 %collective-permute-start.2 = (bf16[2,1,4,2,512]{4,3,2,0,1:T(2,128)(2,1)S(1)}, bf16[2,1,4,2,512]{4,3,2,0,1:T(2,128)(2,1)S(1)}, u32[]{:S(2)}, u32[]{:S(2)}) collective-permute-start(bf16[2,1,4,2,512]{4,3,2,0,1:T(2,128)(2,1)S(1)} %broadcast_select_fusion.2), channel_id=1, source_target_pairs={{0,8},{4,12},{8,0},{12,4},{1,9},{5,13},{9,1},{13,5},{2,10},{6,14},... | collective-permute-start | bytes 49160 | tf_op jit(solution)/shard_map/ppermute | solution.py:108
  40.8 3.8 %collective-permute-start.1 = (bf16[2,1,4,2,512]{4,3,2,0,1:T(2,128)(2,1)S(1)}, bf16[2,1,4,2,512]{4,3,2,0,1:T(2,128)(2,1)S(1)}, u32[]{:S(2)}, u32[]{:S(2)}) collective-permute-start(bf16[2,1,4,2,512]{4,3,2,0,1:T(2,128)(2,1)S(1)} %broadcast_select_fusion.2), channel_id=1, source_target_pairs={{0,4},{4,8},{8,12},{12,0},{1,5},{5,9},{9,13},{13,1},{2,6},{6,10},{... | collective-permute-start | bytes 49160 | tf_op jit(solution)/shard_map/ppermute | solution.py:108
  45.6 4.2 %collective-permute-start.6 = (bf16[2,1,16,2,512]{4,3,2,0,1:T(2,128)(2,1)S(1)}, bf16[2,1,16,2,512]{4,3,2,0,1:T(2,128)(2,1)S(1)}, u32[]{:S(2)}, u32[]{:S(2)}) collective-permute-start(bf16[2,1,16,2,512]{4,3,2,0,1:T(2,128)(2,1)S(1)} %bitcast.143), channel_id=1, source_target_pairs={{0,48},{16,0},{32,16},{48,32},{1,49},{17,1},{33,17},{49,33},{2,50}... | collective-permute-start | bytes 196616 | tf_op jit(solution)/shard_map/ppermute | solution.py:108
  48.4 5.0 %collective-permute-start.5 = (bf16[2,1,16,2,512]{4,3,2,0,1:T(2,128)(2,1)S(1)}, bf16[2,1,16,2,512]{4,3,2,0,1:T(2,128)(2,1)S(1)}, u32[]{:S(2)}, u32[]{:S(2)}) collective-permute-start(bf16[2,1,16,2,512]{4,3,2,0,1:T(2,128)(2,1)S(1)} %bitcast.144), channel_id=1, source_target_pairs={{0,32},{16,48},{32,0},{48,16},{1,33},{17,49},{33,1},{49,17},{2,34}... | collective-permute-start | bytes 196616 | tf_op jit(solution)/shard_map/ppermute | solution.py:108
  48.4 5.1 %collective-permute-start.4 = (bf16[2,1,16,2,512]{4,3,2,0,1:T(2,128)(2,1)S(1)}, bf16[2,1,16,2,512]{4,3,2,0,1:T(2,128)(2,1)S(1)}, u32[]{:S(2)}, u32[]{:S(2)}) collective-permute-start(bf16[2,1,16,2,512]{4,3,2,0,1:T(2,128)(2,1)S(1)} %bitcast.145), channel_id=1, source_target_pairs={{0,16},{16,32},{32,48},{48,0},{1,17},{17,33},{33,49},{49,1},{2,18}... | collective-permute-start | bytes 196616 | tf_op jit(solution)/shard_map/ppermute | solution.py:108
  55.5 9.3 %collective-permute-start.9 = (bf16[2,1,64,2,512]{4,2,3,0,1:T(8,128)(2,1)S(1)}, bf16[2,1,64,2,512]{4,2,3,0,1:T(8,128)(2,1)S(1)}, u32[]{:S(2)}, u32[]{:S(2)}) collective-permute-start(bf16[2,1,64,2,512]{4,2,3,0,1:T(8,128)(2,1)S(1)} %bitcast.138), channel_id=1, source_target_pairs={{0,192},{64,0},{128,64},{192,128},{1,193},{65,1},{129,65},{193,129... | collective-permute-start | bytes 786440 | tf_op jit(solution)/shard_map/ppermute | solution.py:108
  58.3 6.8 %collective-permute-start.8 = (bf16[2,1,64,2,512]{4,2,3,0,1:T(8,128)(2,1)S(1)}, bf16[2,1,64,2,512]{4,2,3,0,1:T(8,128)(2,1)S(1)}, u32[]{:S(2)}, u32[]{:S(2)}) collective-permute-start(bf16[2,1,64,2,512]{4,2,3,0,1:T(8,128)(2,1)S(1)} %bitcast.139), channel_id=1, source_target_pairs={{0,128},{64,192},{128,0},{192,64},{1,129},{65,193},{129,1},{193,65... | collective-permute-start | bytes 786440 | tf_op jit(solution)/shard_map/ppermute | solution.py:108
  58.6 9.5 %collective-permute-start.7 = (bf16[2,1,64,2,512]{4,2,3,0,1:T(8,128)(2,1)S(1)}, bf16[2,1,64,2,512]{4,2,3,0,1:T(8,128)(2,1)S(1)}, u32[]{:S(2)}, u32[]{:S(2)}) collective-permute-start(bf16[2,1,64,2,512]{4,2,3,0,1:T(8,128)(2,1)S(1)} %bitcast.140), channel_id=1, source_target_pairs={{0,64},{64,128},{128,192},{192,0},{1,65},{65,129},{129,193},{193,1... | collective-permute-start | bytes 786440 | tf_op jit(solution)/shard_map/ppermute | solution.py:108
  68.2 14.3 %copy-start.6 = (f32[512,64]{0,1:T(8,128)S(1)}, f32[512,64]{0,1:T(8,128)}, u32[]{:S(2)}) copy-start(f32[512,64]{0,1:T(8,128)} %constant.183.clone) | copy-start | bytes 393220
  68.2 14.3 %copy-start.7 = (f32[512,64]{0,1:T(8,128)S(1)}, f32[512,64]{0,1:T(8,128)}, u32[]{:S(2)}) copy-start(f32[512,64]{0,1:T(8,128)} %constant.182.clone) | copy-start | bytes 393220
  68.2 14.3 %copy-start.8 = (f32[512,32]{0,1:T(8,128)S(1)}, f32[512,32]{0,1:T(8,128)}, u32[]{:S(2)}) copy-start(f32[512,32]{0,1:T(8,128)} %constant.181.clone) | copy-start | bytes 196612
  68.2 14.3 %copy-start.9 = (f32[512,32]{0,1:T(8,128)S(1)}, f32[512,32]{0,1:T(8,128)}, u32[]{:S(2)}) copy-start(f32[512,32]{0,1:T(8,128)} %constant.180.clone) | copy-start | bytes 196612
  69.2 21.1 %copy-start.2 = (bf16[2,1,4,64,2,512]{5,3,2,4,0,1:T(8,128)(2,1)}, bf16[2,1,4,64,2,512]{5,3,2,4,0,1:T(8,128)(2,1)S(1)}, u32[]{:S(2)}) copy-start(bf16[2,1,4,64,2,512]{5,3,2,4,0,1:T(8,128)(2,1)S(1)} %copy.75) | copy-start | bytes 3145732
  69.2 21.0 %collective-permute-start.10 = (bf16[1,2,1,256,2,512]{5,3,4,1,2,0:T(8,128)(2,1)S(1)}, bf16[1,2,1,256,2,512]{5,3,4,1,2,0:T(8,128)(2,1)S(1)}, u32[]{:S(2)}, u32[]{:S(2)}) collective-permute-start(bf16[1,2,1,256,2,512]{5,3,4,1,2,0:T(8,128)(2,1)S(1)} %bitcast.132), channel_id=1, source_target_pairs={{0,1},{1,0},{2,3},{3,2},{4,5},{5,4},{6,7},{7,6},{8,9},{9,8},{10,11... | collective-permute-start | bytes 3145736 | tf_op jit(solution)/shard_map/ppermute | solution.py:108
  76.1 13.3 %all-to-all-start = ((bf16[1,16,2,512]{3,2,0,1:T(2,128)(2,1)}), bf16[1,16,2,512]{3,2,0,1:T(2,128)(2,1)S(1)}, u32[]{:S(2)}, u32[]{:S(2)}) async-start(bf16[1,16,2,512]{3,2,0,1:T(2,128)(2,1)} %copy.68), calls=%async_computation | async-start | bytes 65536 | tf_op jit(solution)/shard_map/all_to_all | solution.py:138
  90.2 1.0 copy-start.5
  114.5 2.3 %copy-start.3 = (bf16[512,32,64]{0,2,1:T(8,128)(2,1)S(1)}, bf16[512,32,64]{0,2,1:T(8,128)(2,1)}, u32[]{:S(2)}) copy-start(bf16[512,32,64]{0,2,1:T(8,128)(2,1)} %get-tuple-element.9) | copy-start | bytes 6291460
  114.5 2.9 %copy-start.4 = (bf16[512,32,64]{0,2,1:T(8,128)(2,1)S(1)}, bf16[512,32,64]{0,2,1:T(8,128)(2,1)}, u32[]{:S(2)}) copy-start(bf16[512,32,64]{0,2,1:T(8,128)(2,1)} %get-tuple-element.10) | copy-start | bytes 6291460
  124.2 9.8 %copy-start.1 = (bf16[1,16,7680]{2,1,0:T(8,128)(2,1)S(1)}, bf16[1,16,7680]{2,1,0:T(8,128)(2,1)}, u32[]{:S(2)}) copy-start(bf16[1,16,7680]{2,1,0:T(8,128)(2,1)} %param.10) | copy-start | bytes 737284

commit v3 on v2

--- a/solution.py
+++ b/solution.py
@@ -5,6 +5,7 @@
 import jax
 import jax.numpy as jnp
 from jax import lax
+from jax.experimental import pallas as pl
 from jax.sharding import Mesh, PartitionSpec as P
 
 S = 7680
@@ -23,18 +24,55 @@
     return np.cos(angles).astype(np.float32), np.sin(angles).astype(np.float32)
 
 
-def band_table():
+TILE = 128
+BIN_BLOCK = 128
+
+
+def band_factors():
     extent = NBINS + 2 * HALF
     bin_ids = np.arange(FIRST_BIN - HALF, FIRST_BIN - HALF + extent)
-    inner = 128
-    outer = S // inner
-    cq, sq = angle_table(np.arange(outer) * inner, bin_ids)
-    cr, sr = angle_table(np.arange(inner), bin_ids)
-    cq, sq, cr, sr = (jnp.asarray(a) for a in (cq, sq, cr, sr))
-    cos = cq[:, None, :] * cr[None, :, :] - sq[:, None, :] * sr[None, :, :]
-    sin = sq[:, None, :] * cr[None, :, :] + cq[:, None, :] * sr[None, :, :]
-    table = jnp.concatenate([cos, -sin], axis=2).astype(jnp.bfloat16)
-    return table.reshape(S, 2 * extent)
+    cq, sq = angle_table(bin_ids, np.arange(S // TILE) * TILE)
+    cr, sr = angle_table(bin_ids, np.arange(TILE))
+    a = np.concatenate([cq, -sq], axis=0)
+    b = np.concatenate([-sq, -cq], axis=0)
+    c = np.concatenate([cr, cr], axis=0)
+    d = np.concatenate([sr, sr], axis=0)
+    return tuple(jnp.asarray(v) for v in (a, b, c, d))
+
+
+def dft_kernel(x_ref, a_ref, b_ref, c_ref, d_ref, o_ref):
+    c = c_ref[...]
+    d = d_ref[...]
+    acc = jnp.zeros(o_ref.shape, jnp.float32)
+    for q in range(S // TILE):
+        twiddle = (a_ref[:, q : q + 1] * c + b_ref[:, q : q + 1] * d).astype(jnp.bfloat16)
+        acc = acc + lax.dot_general(
+            twiddle,
+            x_ref[:, q * TILE : (q + 1) * TILE],
+            (((1,), (1,)), ((), ())),
+            preferred_element_type=jnp.float32,
+        )
+    o_ref[...] = acc
+
+
+def band_spectrum(row_data):
+    a, b, c, d = band_factors()
+    bins = a.shape[0]
+    rows = row_data.shape[0]
+    out = pl.pallas_call(
+        dft_kernel,
+        out_shape=jax.ShapeDtypeStruct((bins, rows), jnp.float32),
+        grid=(bins // BIN_BLOCK,),
+        in_specs=[
+            pl.BlockSpec((rows, S), lambda i: (0, 0)),
+            pl.BlockSpec((BIN_BLOCK, a.shape[1]), lambda i: (i, 0)),
+            pl.BlockSpec((BIN_BLOCK, b.shape[1]), lambda i: (i, 0)),
+            pl.BlockSpec((BIN_BLOCK, TILE), lambda i: (i, 0)),
+            pl.BlockSpec((BIN_BLOCK, TILE), lambda i: (i, 0)),
+        ],
+        out_specs=pl.BlockSpec((BIN_BLOCK, rows), lambda i: (i, 0)),
+    )(row_data, a, b, c, d)
+    return out.T
 
 
 def lag_weights():
@@ -65,7 +103,7 @@
 
 
 def whiten(row_data):
-    return normalize(jnp.dot(row_data, band_table(), preferred_element_type=jnp.float32))
+    return normalize(band_spectrum(row_data))
 
 
 def cross_terms(source_part, receiver_part):

time: 135 us -> 138 us (1.022)
  Pallas kernels: 0 us -> 24.7 us
  other arithmetic: 25.6 us -> 15.9 us
  matrix products: 17.5 us -> 9.92 us
  local copies, waits for them, and re-layouts: 38.3 us -> 34 us
    pallas_call x0 -> x1, Pallas kernels: none -> 24.7 us  [band_spectrum(): pl.pallas_call(dft_kernel, out_shape=jax.ShapeDtypeStruct((bins, rows), j...]
    unnamed x1 -> x0, other arithmetic: 13.1 us -> none
    dot_general x1 -> x0, matrix products: 7.52 us -> none  [whiten(): jnp.dot(row_data, band_table(), preferred_element_type=jnp.float32)]
    neg x1 -> x0, local copies, waits for them, and re-layouts: 4.44 us -> none  [band_table(): table = jnp.concatenate([cos, -sin], axis=2).astype(jnp.bfloat16)]
    another operation x3, other arithmetic: 0.71 us -> 3.01 us  [normalize(): return jnp.stack([centre_re, centre_im], axis=1).astype(jnp.bfloat16)]
    unnamed x23 -> x19, local copies, waits for them, and re-layouts: 4.53 us -> 4.54 us
where the time goes in v3:
time: 138 us; the launch traced here: 137 us
  local copies, waits for them, and re-layouts  34 us (25%)
  starting transfers between devices  31 us (22%)
  Pallas kernels  24.7 us (18%)
  waiting for transfers between devices  21.1 us (15%)
  other arithmetic  15.9 us (12%)
  matrix products  9.92 us (7%)
    ppermute x11, starting transfers between devices, ring_gather(): lax.ppermute(value, axis_name, [(i, (i + shift) % size) for i in range(si...  24.7 us
    pallas_call x1, Pallas kernels, band_spectrum(): pl.pallas_call(dft_kernel, out_shape=jax.ShapeDtypeStruct((bins, rows), j...  24.7 us
    ppermute x11, waiting for transfers between devices, ring_gather(): lax.ppermute(value, axis_name, [(i, (i + shift) % size) for i in range(si...  17.5 us
    reshape x1, local copies, waits for them, and re-layouts, transform(): return result.reshape(count_src, count_rec, 2 * MAXLAG)  9.75 us
    dot_general x1, matrix products, transform(): jnp.dot(rounded, weights, preferred_element_type=jnp.float32) * lag_scale  6.84 us
    all_to_all x1, starting transfers between devices, per_device(): lax.all_to_all(whitened, WIN_AXES, split_axis=1, concat_axis=0, tiled=True)  6.29 us
    gather x5, local copies, waits for them, and re-layouts, ring_gather(): stacked = jnp.take(stacked, (here - jnp.arange(size)) % size, axis=0)  4.96 us
    reshape x1, local copies, waits for them, and re-layouts, collect(): return part.reshape(-1, part.shape[3], 2, NBINS)  4.93 us
  transfers between devices with their start and end apart: 12, of which 10 were waited for; matrix products, arithmetic and copies ran while one was open for 4% of the time, Pallas kernels for 0%

profile of v3, /device:TPU:1, one launch (start us, length us, event | category | flops | bytes accessed | tf_op | source)
XLA Modules:
  0.0 137.0 jit_solution(18032584837581393190)
XLA Ops:
  0.0 0.7 compare_and_fusion
  0.7 0.7 fusion.33
  1.5 24.7 %shard_map.100 = f32[1152,16]{1,0:T(8,128)} custom-call(bf16[16,7680]{1,0:T(8,128)(2,1)} %bitcast.142, f32[1152,60]{1,0:T(8,128)} %constant.176.clone.a_ref, f32[1152,60]{1,0:T(8,128)} %constant.177.clone.b_ref, f32[1152,128]{1,0:T(8,128)} %constant.178.clone.c_ref, f32[1152,128]{1,0:T(8,128)} %constant.179.clone.d_ref), custom_call_target="tpu_custom_call" | custom-call | tf_op jit(solution)/shard_map/pallas_call | solution.py:62
  26.2 1.2 fusion.14
  27.3 1.9 %fusion.20 = (bf16[1,16,1,512]{1,3,2,0:T(8,128)(2,1)S(1)}, f32[16,512]{0,1:T(8,128)S(1)}) fusion(f32[16,1152]{0,1:T(8,128)} %bitcast.122, f32[16,576]{0,1:T(8,128)S(1)} %fusion.14), kind=kLoop, calls=%fused_computation.109 | loop fusion | flops 557056 | bytes 2211840 | tf_op jit(solution)/shard_map/stack | solution.py:102
  29.2 1.0 fusion.21
  30.3 0.1 copy.47
  30.5 0.6 gather_fusion
  31.1 0.1 broadcast_select_fusion.4
  31.1 7.8 %collective-permute-start = (bf16[1,1,4,2,512]{4,3,2,1,0:T(2,128)(2,1)S(1)}, bf16[1,1,4,2,512]{4,3,2,1,0:T(2,128)(2,1)S(1)}, u32[]{:S(2)}, u32[]{:S(2)}) collective-permute-start(bf16[1,1,4,2,512]{4,3,2,1,0:T(2,128)(2,1)S(1)} %broadcast_select_fusion.4), channel_id=1, source_target_pairs={{0,2},{2,0},{1,3},{3,1},{4,6},{6,4},{5,7},{7,5},{8,10},{10,8},{9,1... | collective-permute-start | bytes 24584 | tf_op jit(solution)/shard_map/ppermute | solution.py:146
  39.0 0.1 broadcast_select_fusion.5
  39.2 0.8 collective-permute-done
  40.0 0.6 gather_fusion.1
  40.6 0.1 broadcast_select_fusion.2
  40.7 2.6 %collective-permute-start.3 = (bf16[2,1,4,2,512]{4,3,2,0,1:T(2,128)(2,1)S(1)}, bf16[2,1,4,2,512]{4,3,2,0,1:T(2,128)(2,1)S(1)}, u32[]{:S(2)}, u32[]{:S(2)}) collective-permute-start(bf16[2,1,4,2,512]{4,3,2,0,1:T(2,128)(2,1)S(1)} %broadcast_select_fusion.2), channel_id=1, source_target_pairs={{0,12},{4,0},{8,4},{12,8},{1,13},{5,1},{9,5},{13,9},{2,14},{6,2},{... | collective-permute-start | bytes 49160 | tf_op jit(solution)/shard_map/ppermute | solution.py:146
  43.3 0.5 collective-permute-start.2
  43.8 0.6 collective-permute-start.1
  44.4 0.1 broadcast_select_fusion.3
  44.5 2.9 %collective-permute-done.2 = bf16[2,1,4,2,512]{4,3,2,0,1:T(2,128)(2,1)S(1)} collective-permute-done((bf16[2,1,4,2,512]{4,3,2,0,1:T(2,128)(2,1)S(1)}, bf16[2,1,4,2,512]{4,3,2,0,1:T(2,128)(2,1)S(1)}, u32[]{:S(2)}, u32[]{:S(2)}) %collective-permute-start.2) | collective-permute-done | bytes 16416 | tf_op jit(solution)/shard_map/ppermute | solution.py:146
  47.4 0.2 collective-permute-done.1
  47.6 0.1 maximum_bitcast_fusion.3
  47.7 0.7 gather_fusion.2
  48.4 0.1 fusion.22
  48.6 2.9 %collective-permute-start.6 = (bf16[2,1,16,2,512]{4,3,2,0,1:T(2,128)(2,1)S(1)}, bf16[2,1,16,2,512]{4,3,2,0,1:T(2,128)(2,1)S(1)}, u32[]{:S(2)}, u32[]{:S(2)}) collective-permute-start(bf16[2,1,16,2,512]{4,3,2,0,1:T(2,128)(2,1)S(1)} %bitcast.135), channel_id=1, source_target_pairs={{0,48},{16,0},{32,16},{48,32},{1,49},{17,1},{33,17},{49,33},{2,50}... | collective-permute-start | bytes 196616 | tf_op jit(solution)/shard_map/ppermute | solution.py:146
  51.5 0.4 collective-permute-start.4
  51.9 0.9 collective-permute-done.6
  52.8 3.6 %collective-permute-done.5 = bf16[2,1,16,2,512]{4,3,2,0,1:T(2,128)(2,1)S(1)} collective-permute-done((bf16[2,1,16,2,512]{4,3,2,0,1:T(2,128)(2,1)S(1)}, bf16[2,1,16,2,512]{4,3,2,0,1:T(2,128)(2,1)S(1)}, u32[]{:S(2)}, u32[]{:S(2)}) %collective-permute-start.5) | collective-permute-done | bytes 65568 | tf_op jit(solution)/shard_map/ppermute | solution.py:146
  56.4 0.2 collective-permute-done.4
  56.6 0.5 maximum_bitcast_fusion.2
  57.1 1.1 gather_fusion.3
  58.1 0.3 fusion.19
  58.5 2.8 %collective-permute-start.9 = (bf16[2,1,64,2,512]{4,2,3,0,1:T(8,128)(2,1)S(1)}, bf16[2,1,64,2,512]{4,2,3,0,1:T(8,128)(2,1)S(1)}, u32[]{:S(2)}, u32[]{:S(2)}) collective-permute-start(bf16[2,1,64,2,512]{4,2,3,0,1:T(8,128)(2,1)S(1)} %bitcast.130), channel_id=1, source_target_pairs={{0,192},{64,0},{128,64},{192,128},{1,193},{65,1},{129,65},{193,129... | collective-permute-start | bytes 786440 | tf_op jit(solution)/shard_map/ppermute | solution.py:146
  61.3 0.3 collective-permute-start.8
  61.7 0.7 collective-permute-start.7
  62.4 5.4 %collective-permute-done.9 = bf16[2,1,64,2,512]{4,2,3,0,1:T(8,128)(2,1)S(1)} collective-permute-done((bf16[2,1,64,2,512]{4,2,3,0,1:T(8,128)(2,1)S(1)}, bf16[2,1,64,2,512]{4,2,3,0,1:T(8,128)(2,1)S(1)}, u32[]{:S(2)}, u32[]{:S(2)}) %collective-permute-start.9) | collective-permute-done | bytes 262176 | tf_op jit(solution)/shard_map/ppermute | solution.py:146
  67.8 0.4 collective-permute-done.8
  68.1 3.1 %collective-permute-done.7 = bf16[2,1,64,2,512]{4,2,3,0,1:T(8,128)(2,1)S(1)} collective-permute-done((bf16[2,1,64,2,512]{4,2,3,0,1:T(8,128)(2,1)S(1)}, bf16[2,1,64,2,512]{4,2,3,0,1:T(8,128)(2,1)S(1)}, u32[]{:S(2)}, u32[]{:S(2)}) %collective-permute-start.7) | collective-permute-done | bytes 262176 | tf_op jit(solution)/shard_map/ppermute | solution.py:146
  71.2 0.1 maximum_bitcast_fusion.1
  71.3 0.6 gather_fusion.4
  72.0 0.2 fusion.6
  72.2 0.1 copy.52
  72.3 6.1 %collective-permute-start.10 = (bf16[1,2,1,256,2,512]{5,3,4,1,2,0:T(8,128)(2,1)S(1)}, bf16[1,2,1,256,2,512]{5,3,4,1,2,0:T(8,128)(2,1)S(1)}, u32[]{:S(2)}, u32[]{:S(2)}) collective-permute-start(bf16[1,2,1,256,2,512]{5,3,4,1,2,0:T(8,128)(2,1)S(1)} %bitcast.124), channel_id=1, source_target_pairs={{0,1},{1,0},{2,3},{3,2},{4,5},{5,4},{6,7},{7,6},{8,9},{9,8},{10,11... | collective-permute-start | bytes 3145736 | tf_op jit(solution)/shard_map/ppermute | solution.py:146
  78.4 0.7 copy.45
  79.1 6.3 %all-to-all-start = ((bf16[1,16,2,512]{3,2,0,1:T(2,128)(2,1)}), bf16[1,16,2,512]{3,2,0,1:T(2,128)(2,1)S(1)}, u32[]{:S(2)}, u32[]{:S(2)}) async-start(bf16[1,16,2,512]{3,2,0,1:T(2,128)(2,1)} %copy.45), calls=%async_computation | async-start | bytes 65536 | tf_op jit(solution)/shard_map/all_to_all | solution.py:176
  85.5 3.3 %subtract_convert_fusion = (bf16[512,32,64]{0,2,1:T(8,128)(2,1)}, bf16[512,32,64]{0,2,1:T(8,128)(2,1)}) fusion(f32[512,64]{0,1:T(8,128)S(1)} %copy-done.4, f32[512,32]{0,1:T(8,128)S(1)} %copy-done.6, f32[512,64]{0,1:T(8,128)S(1)} %copy-done.5, f32[512,32]{0,1:T(8,128)S(1)} %copy-done.7), kind=kLoop, calls=%fused_computation.11 | loop fusion | flops 9437184 | bytes 4587520 | tf_op jit(solution)/shard_map/convert.3
  88.8 3.7 %all-to-all-done = bf16[1,16,2,512]{3,2,0,1:T(2,128)(2,1)S(1)} async-done(((bf16[1,16,2,512]{3,2,0,1:T(2,128)(2,1)}), bf16[1,16,2,512]{3,2,0,1:T(2,128)(2,1)S(1)}, u32[]{:S(2)}, u32[]{:S(2)}) %all-to-all-start) | async-done | bytes 32800 | tf_op jit(solution)/shard_map/all_to_all | solution.py:176
  92.5 0.4 copy.59
  92.9 0.4 copy.58
  93.3 1.0 copy-done.3
  94.2 1.7 %maximum_bitcast_fusion = bf16[2,2,256,2,512]{4,2,3,1,0:T(8,128)(2,1)S(1)} fusion(bf16[1,1,2,1,256,2,512]{6,4,5,2,0,3,1:T(8,128)(2,1)} %bitcast.129, bf16[1,1,2,1,256,2,512]{6,4,5,2,0,3,1:T(8,128)(2,1)} %bitcast.125), kind=kLoop, calls=%fused_computation.12 | loop fusion | flops 1048576 | bytes 4194304 | tf_op jit(solution)/shard_map/stack | solution.py:149
  96.0 2.0 %gather_fusion.5 = bf16[2,2,256,2,512]{4,2,3,1,0:T(8,128)(2,1)} fusion(bf16[2,2,256,2,512]{4,2,3,1,0:T(8,128)(2,1)S(1)} %maximum_bitcast_fusion, s32[1024]{0:T(1024)S(1)} %pad_clamp_fusion), kind=kCustom, calls=%fused_computation.5 | custom fusion | bytes 4194312 | tf_op jit(solution)/shard_map/jit(_take)/gather | solution.py:150
  98.0 1.9 %fusion.3 = bf16[2,2,1,256,2,512]{5,3,4,0,1,2:T(8,128)(2,1)S(1)} fusion(bf16[2,2,256,2,512]{4,2,3,1,0:T(8,128)(2,1)} %gather_fusion.5, pred[2]{0:T(512)(128)(4,1)S(1)} %compare_and_fusion.5), kind=kLoop, calls=%fused_computation.15 | loop fusion | flops 1048576 | bytes 4194306 | tf_op jit(solution)/shard_map/transpose | solution.py:162
  99.8 3.9 %copy.55 = bf16[2,2,1,256,2,512]{3,1,0,5,4,2:T(2,128)(2,1)} copy(bf16[2,2,1,256,2,512]{5,3,4,0,1,2:T(8,128)(2,1)S(1)} %fusion.3) | data formatting | bytes 4194304 | tf_op jit(solution)/shard_map/transpose | solution.py:162
  103.8 4.9 %reshape.469 = bf16[4,256,2,512]{1,0,3,2:T(4,128)(2,1)S(1)} reshape(bf16[2,2,1,256,2,512]{3,1,0,5,4,2:T(2,128)(2,1)} %copy.55) | data formatting | bytes 4194304 | tf_op jit(solution)/shard_map/reshape | solution.py:163
  108.7 0.7 fusion.8
  109.4 0.7 fusion.7
  110.1 0.9 fusion.5
  110.9 0.9 fusion.4
  111.8 1.5 %pad_maximum_fusion = bf16[256,4,2,512]{0,1,3,2:T(4,128)(2,1)S(1)} fusion(bf16[256,4,1,512]{0,1,3,2:T(4,128)(2,1)S(1)} %fusion.5, bf16[256,4,1,512]{0,1,3,2:T(4,128)(2,1)S(1)} %fusion.4), kind=kLoop, calls=%fused_computation.13 | loop fusion | flops 1048576 | bytes 4194304 | tf_op jit(solution)/shard_map/stack | solution.py:132
  113.3 4.3 %copy.57 = bf16[256,4,2,512]{3,2,1,0:T(2,128)(2,1)} copy(bf16[256,4,2,512]{0,1,3,2:T(4,128)(2,1)S(1)} %pad_maximum_fusion) | data formatting | bytes 4194304 | tf_op jit(solution)/shard_map/stack | solution.py:132
  117.6 2.3 %copy.60 = bf16[128,8,2,512]{3,1,2,0:T(8,128)(2,1)S(1)} copy(bf16[128,8,2,512]{3,2,1,0:T(2,128)(2,1)} %bitcast.120) | data formatting | bytes 4194304
  119.9 0.5 copy-done.2
  120.4 6.8 %convolution_multiply_fusion = f32[1024,2048]{1,0:T(8,128)} fusion(bf16[1024,1024]{1,0:T(8,128)(2,1)S(1)} %bitcast.128, bf16[512,2048]{0,1:T(8,128)(2,1)S(1)} %bitcast.127, bf16[512,2048]{0,1:T(8,128)(2,1)S(1)} %bitcast.126), kind=kOutput, calls=%fused_computation.6 | convolution fusion | flops 4305453056 | bytes 14680064 | tf_op jit(solution)/shard_map/dot_general | solution.py:138
  127.2 9.7 %reshape.470 = f32[256,4,2048]{2,1,0:T(4,128)} reshape(f32[1024,2048]{1,0:T(8,128)} %convolution_multiply_fusion) | data formatting | bytes 16777216 | tf_op jit(solution)/shard_map/reshape | solution.py:139
  (38 shorter events, 0.4 us)
Async XLA Ops:
  31.1 8.9 %collective-permute-start = (bf16[1,1,4,2,512]{4,3,2,1,0:T(2,128)(2,1)S(1)}, bf16[1,1,4,2,512]{4,3,2,1,0:T(2,128)(2,1)S(1)}, u32[]{:S(2)}, u32[]{:S(2)}) collective-permute-start(bf16[1,1,4,2,512]{4,3,2,1,0:T(2,128)(2,1)S(1)} %broadcast_select_fusion.4), channel_id=1, source_target_pairs={{0,2},{2,0},{1,3},{3,1},{4,6},{6,4},{5,7},{7,5},{8,10},{10,8},{9,1... | collective-permute-start | bytes 24584 | tf_op jit(solution)/shard_map/ppermute | solution.py:146
  40.7 3.8 %collective-permute-start.3 = (bf16[2,1,4,2,512]{4,3,2,0,1:T(2,128)(2,1)S(1)}, bf16[2,1,4,2,512]{4,3,2,0,1:T(2,128)(2,1)S(1)}, u32[]{:S(2)}, u32[]{:S(2)}) collective-permute-start(bf16[2,1,4,2,512]{4,3,2,0,1:T(2,128)(2,1)S(1)} %broadcast_select_fusion.2), channel_id=1, source_target_pairs={{0,12},{4,0},{8,4},{12,8},{1,13},{5,1},{9,5},{13,9},{2,14},{6,2},{... | collective-permute-start | bytes 49160 | tf_op jit(solution)/shard_map/ppermute | solution.py:146
  43.3 4.1 %collective-permute-start.2 = (bf16[2,1,4,2,512]{4,3,2,0,1:T(2,128)(2,1)S(1)}, bf16[2,1,4,2,512]{4,3,2,0,1:T(2,128)(2,1)S(1)}, u32[]{:S(2)}, u32[]{:S(2)}) collective-permute-start(bf16[2,1,4,2,512]{4,3,2,0,1:T(2,128)(2,1)S(1)} %broadcast_select_fusion.2), channel_id=1, source_target_pairs={{0,8},{4,12},{8,0},{12,4},{1,9},{5,13},{9,1},{13,5},{2,10},{6,14},... | collective-permute-start | bytes 49160 | tf_op jit(solution)/shard_map/ppermute | solution.py:146
  43.8 3.8 %collective-permute-start.1 = (bf16[2,1,4,2,512]{4,3,2,0,1:T(2,128)(2,1)S(1)}, bf16[2,1,4,2,512]{4,3,2,0,1:T(2,128)(2,1)S(1)}, u32[]{:S(2)}, u32[]{:S(2)}) collective-permute-start(bf16[2,1,4,2,512]{4,3,2,0,1:T(2,128)(2,1)S(1)} %broadcast_select_fusion.2), channel_id=1, source_target_pairs={{0,4},{4,8},{8,12},{12,0},{1,5},{5,9},{9,13},{13,1},{2,6},{6,10},{... | collective-permute-start | bytes 49160 | tf_op jit(solution)/shard_map/ppermute | solution.py:146
  48.6 4.2 %collective-permute-start.6 = (bf16[2,1,16,2,512]{4,3,2,0,1:T(2,128)(2,1)S(1)}, bf16[2,1,16,2,512]{4,3,2,0,1:T(2,128)(2,1)S(1)}, u32[]{:S(2)}, u32[]{:S(2)}) collective-permute-start(bf16[2,1,16,2,512]{4,3,2,0,1:T(2,128)(2,1)S(1)} %bitcast.135), channel_id=1, source_target_pairs={{0,48},{16,0},{32,16},{48,32},{1,49},{17,1},{33,17},{49,33},{2,50}... | collective-permute-start | bytes 196616 | tf_op jit(solution)/shard_map/ppermute | solution.py:146
  51.5 5.0 %collective-permute-start.5 = (bf16[2,1,16,2,512]{4,3,2,0,1:T(2,128)(2,1)S(1)}, bf16[2,1,16,2,512]{4,3,2,0,1:T(2,128)(2,1)S(1)}, u32[]{:S(2)}, u32[]{:S(2)}) collective-permute-start(bf16[2,1,16,2,512]{4,3,2,0,1:T(2,128)(2,1)S(1)} %bitcast.136), channel_id=1, source_target_pairs={{0,32},{16,48},{32,0},{48,16},{1,33},{17,49},{33,1},{49,17},{2,34}... | collective-permute-start | bytes 196616 | tf_op jit(solution)/shard_map/ppermute | solution.py:146
  51.5 5.1 %collective-permute-start.4 = (bf16[2,1,16,2,512]{4,3,2,0,1:T(2,128)(2,1)S(1)}, bf16[2,1,16,2,512]{4,3,2,0,1:T(2,128)(2,1)S(1)}, u32[]{:S(2)}, u32[]{:S(2)}) collective-permute-start(bf16[2,1,16,2,512]{4,3,2,0,1:T(2,128)(2,1)S(1)} %bitcast.137), channel_id=1, source_target_pairs={{0,16},{16,32},{32,48},{48,0},{1,17},{17,33},{33,49},{49,1},{2,18}... | collective-permute-start | bytes 196616 | tf_op jit(solution)/shard_map/ppermute | solution.py:146
  58.5 9.3 %collective-permute-start.9 = (bf16[2,1,64,2,512]{4,2,3,0,1:T(8,128)(2,1)S(1)}, bf16[2,1,64,2,512]{4,2,3,0,1:T(8,128)(2,1)S(1)}, u32[]{:S(2)}, u32[]{:S(2)}) collective-permute-start(bf16[2,1,64,2,512]{4,2,3,0,1:T(8,128)(2,1)S(1)} %bitcast.130), channel_id=1, source_target_pairs={{0,192},{64,0},{128,64},{192,128},{1,193},{65,1},{129,65},{193,129... | collective-permute-start | bytes 786440 | tf_op jit(solution)/shard_map/ppermute | solution.py:146
  61.3 6.8 %collective-permute-start.8 = (bf16[2,1,64,2,512]{4,2,3,0,1:T(8,128)(2,1)S(1)}, bf16[2,1,64,2,512]{4,2,3,0,1:T(8,128)(2,1)S(1)}, u32[]{:S(2)}, u32[]{:S(2)}) collective-permute-start(bf16[2,1,64,2,512]{4,2,3,0,1:T(8,128)(2,1)S(1)} %bitcast.131), channel_id=1, source_target_pairs={{0,128},{64,192},{128,0},{192,64},{1,129},{65,193},{129,1},{193,65... | collective-permute-start | bytes 786440 | tf_op jit(solution)/shard_map/ppermute | solution.py:146
  61.7 9.5 %collective-permute-start.7 = (bf16[2,1,64,2,512]{4,2,3,0,1:T(8,128)(2,1)S(1)}, bf16[2,1,64,2,512]{4,2,3,0,1:T(8,128)(2,1)S(1)}, u32[]{:S(2)}, u32[]{:S(2)}) collective-permute-start(bf16[2,1,64,2,512]{4,2,3,0,1:T(8,128)(2,1)S(1)} %bitcast.132), channel_id=1, source_target_pairs={{0,64},{64,128},{128,192},{192,0},{1,65},{65,129},{129,193},{193,1... | collective-permute-start | bytes 786440 | tf_op jit(solution)/shard_map/ppermute | solution.py:146
  72.0 13.5 %copy-start.4 = (f32[512,64]{0,1:T(8,128)S(1)}, f32[512,64]{0,1:T(8,128)}, u32[]{:S(2)}) copy-start(f32[512,64]{0,1:T(8,128)} %constant.183.clone) | copy-start | bytes 393220
  72.0 13.5 %copy-start.5 = (f32[512,64]{0,1:T(8,128)S(1)}, f32[512,64]{0,1:T(8,128)}, u32[]{:S(2)}) copy-start(f32[512,64]{0,1:T(8,128)} %constant.182.clone) | copy-start | bytes 393220
  72.0 13.5 %copy-start.6 = (f32[512,32]{0,1:T(8,128)S(1)}, f32[512,32]{0,1:T(8,128)}, u32[]{:S(2)}) copy-start(f32[512,32]{0,1:T(8,128)} %constant.181.clone) | copy-start | bytes 196612
  72.0 13.5 %copy-start.7 = (f32[512,32]{0,1:T(8,128)S(1)}, f32[512,32]{0,1:T(8,128)}, u32[]{:S(2)}) copy-start(f32[512,32]{0,1:T(8,128)} %constant.180.clone) | copy-start | bytes 196612
  72.3 16.5 %copy-start = (bf16[2,1,4,64,2,512]{5,3,2,4,0,1:T(8,128)(2,1)}, bf16[2,1,4,64,2,512]{5,3,2,4,0,1:T(8,128)(2,1)S(1)}, u32[]{:S(2)}) copy-start(bf16[2,1,4,64,2,512]{5,3,2,4,0,1:T(8,128)(2,1)S(1)} %copy.52) | copy-start | bytes 3145732
  72.3 21.0 %collective-permute-start.10 = (bf16[1,2,1,256,2,512]{5,3,4,1,2,0:T(8,128)(2,1)S(1)}, bf16[1,2,1,256,2,512]{5,3,4,1,2,0:T(8,128)(2,1)S(1)}, u32[]{:S(2)}, u32[]{:S(2)}) collective-permute-start(bf16[1,2,1,256,2,512]{5,3,4,1,2,0:T(8,128)(2,1)S(1)} %bitcast.124), channel_id=1, source_target_pairs={{0,1},{1,0},{2,3},{3,2},{4,5},{5,4},{6,7},{7,6},{8,9},{9,8},{10,11... | collective-permute-start | bytes 3145736 | tf_op jit(solution)/shard_map/ppermute | solution.py:146
  79.1 13.4 %all-to-all-start = ((bf16[1,16,2,512]{3,2,0,1:T(2,128)(2,1)}), bf16[1,16,2,512]{3,2,0,1:T(2,128)(2,1)S(1)}, u32[]{:S(2)}, u32[]{:S(2)}) async-start(bf16[1,16,2,512]{3,2,0,1:T(2,128)(2,1)} %copy.45), calls=%async_computation | async-start | bytes 65536 | tf_op jit(solution)/shard_map/all_to_all | solution.py:176
  93.3 1.0 copy-start.3
  117.5 2.3 %copy-start.1 = (bf16[512,32,64]{0,2,1:T(8,128)(2,1)S(1)}, bf16[512,32,64]{0,2,1:T(8,128)(2,1)}, u32[]{:S(2)}) copy-start(bf16[512,32,64]{0,2,1:T(8,128)(2,1)} %get-tuple-element.7) | copy-start | bytes 6291460
  117.5 2.9 %copy-start.2 = (bf16[512,32,64]{0,2,1:T(8,128)(2,1)S(1)}, bf16[512,32,64]{0,2,1:T(8,128)(2,1)}, u32[]{:S(2)}) copy-start(bf16[512,32,64]{0,2,1:T(8,128)(2,1)} %get-tuple-element.8) | copy-start | bytes 6291460

commit v4 on v2

--- a/solution.py
+++ b/solution.py
@@ -1,5 +1,6 @@
 import math
 
+import ml_dtypes
 import numpy as np
 
 import jax
@@ -26,15 +27,9 @@
 def band_table():
     extent = NBINS + 2 * HALF
     bin_ids = np.arange(FIRST_BIN - HALF, FIRST_BIN - HALF + extent)
-    inner = 128
-    outer = S // inner
-    cq, sq = angle_table(np.arange(outer) * inner, bin_ids)
-    cr, sr = angle_table(np.arange(inner), bin_ids)
-    cq, sq, cr, sr = (jnp.asarray(a) for a in (cq, sq, cr, sr))
-    cos = cq[:, None, :] * cr[None, :, :] - sq[:, None, :] * sr[None, :, :]
-    sin = sq[:, None, :] * cr[None, :, :] + cq[:, None, :] * sr[None, :, :]
-    table = jnp.concatenate([cos, -sin], axis=2).astype(jnp.bfloat16)
-    return table.reshape(S, 2 * extent)
+    cos, sin = angle_table(np.arange(S), bin_ids)
+    table = np.concatenate([cos, -sin], axis=1).astype(ml_dtypes.bfloat16)
+    return jnp.asarray(table)
 
 
 def lag_weights():

time: 135 us -> 117 us (0.87)
  other arithmetic: 25.6 us -> 12.5 us
  local copies, waits for them, and re-layouts: 38.3 us -> 33.9 us
    unnamed x1 -> x0, other arithmetic: 13.1 us -> none
    neg x1 -> x0, local copies, waits for them, and re-layouts: 4.44 us -> none  [band_table(): table = jnp.concatenate([cos, -sin], axis=2).astype(jnp.bfloat16)]
where the time goes in v4:
time: 117 us; the launch traced here: 116 us
  local copies, waits for them, and re-layouts  33.9 us (29%)
  starting transfers between devices  31 us (26%)
  waiting for transfers between devices  21.1 us (18%)
  matrix products  17.3 us (15%)
  other arithmetic  12.5 us (11%)
    ppermute x11, starting transfers between devices, ring_gather(): lax.ppermute(value, axis_name, [(i, (i + shift) % size) for i in range(si...  24.7 us
    ppermute x11, waiting for transfers between devices, ring_gather(): lax.ppermute(value, axis_name, [(i, (i + shift) % size) for i in range(si...  17.5 us
    reshape x1, local copies, waits for them, and re-layouts, transform(): return result.reshape(count_src, count_rec, 2 * MAXLAG)  9.79 us
    dot_general x1, matrix products, whiten(): jnp.dot(row_data, band_table(), preferred_element_type=jnp.float32)  7.3 us
    dot_general x1, matrix products, transform(): jnp.dot(rounded, weights, preferred_element_type=jnp.float32) * lag_scale  6.87 us
    all_to_all x1, starting transfers between devices, per_device(): lax.all_to_all(whitened, WIN_AXES, split_axis=1, concat_axis=0, tiled=True)  6.32 us
    gather x5, local copies, waits for them, and re-layouts, ring_gather(): stacked = jnp.take(stacked, (here - jnp.arange(size)) % size, axis=0)  4.96 us
    reshape x1, local copies, waits for them, and re-layouts, collect(): return part.reshape(-1, part.shape[3], 2, NBINS)  4.93 us
  transfers between devices with their start and end apart: 12, of which 10 were waited for; matrix products, arithmetic and copies ran while one was open for 4% of the time, Pallas kernels for 0%

profile of v4, /device:TPU:1, one launch (start us, length us, event | category | flops | bytes accessed | tf_op | source)
XLA Modules:
  0.0 116.2 jit_solution(1959357677052363641)
XLA Ops:
  0.0 0.8 compare_and_fusion
  0.8 0.7 fusion.34
  1.5 7.3 %convolution_bitcast_fusion = f32[16,1152]{1,0:T(8,128)S(1)} fusion(bf16[7680,1152]{1,0:T(8,128)(2,1)} %constant.170.clone, bf16[1,16,7680]{2,1,0:T(8,128)(2,1)S(1)} %copy-done), kind=kOutput, calls=%fused_computation.12 | convolution fusion | flops 283115520 | bytes 18014208 | tf_op jit(solution)/shard_map/dot_general | solution.py:63
  8.8 0.1 fusion.17
  8.9 0.6 fusion.22
  9.6 0.1 fusion.23
  9.7 0.6 gather_fusion
  10.3 0.1 broadcast_select_fusion.4
  10.4 7.8 %collective-permute-start = (bf16[1,1,4,2,512]{4,3,2,1,0:T(2,128)(2,1)S(1)}, bf16[1,1,4,2,512]{4,3,2,1,0:T(2,128)(2,1)S(1)}, u32[]{:S(2)}, u32[]{:S(2)}) collective-permute-start(bf16[1,1,4,2,512]{4,3,2,1,0:T(2,128)(2,1)S(1)} %broadcast_select_fusion.4), channel_id=1, source_target_pairs={{0,2},{2,0},{1,3},{3,1},{4,6},{6,4},{5,7},{7,5},{8,10},{10,8},{9,1... | collective-permute-start | bytes 24584 | tf_op jit(solution)/shard_map/ppermute | solution.py:103
  18.2 0.1 broadcast_select_fusion.5
  18.4 0.8 collective-permute-done
  19.3 0.6 gather_fusion.1
  19.8 0.1 broadcast_select_fusion.2
  19.9 2.6 %collective-permute-start.3 = (bf16[2,1,4,2,512]{4,3,2,0,1:T(2,128)(2,1)S(1)}, bf16[2,1,4,2,512]{4,3,2,0,1:T(2,128)(2,1)S(1)}, u32[]{:S(2)}, u32[]{:S(2)}) collective-permute-start(bf16[2,1,4,2,512]{4,3,2,0,1:T(2,128)(2,1)S(1)} %broadcast_select_fusion.2), channel_id=1, source_target_pairs={{0,12},{4,0},{8,4},{12,8},{1,13},{5,1},{9,5},{13,9},{2,14},{6,2},{... | collective-permute-start | bytes 49160 | tf_op jit(solution)/shard_map/ppermute | solution.py:103
  22.5 0.5 collective-permute-start.2
  23.0 0.6 collective-permute-start.1
  23.6 0.1 broadcast_select_fusion.3
  23.7 2.9 %collective-permute-done.2 = bf16[2,1,4,2,512]{4,3,2,0,1:T(2,128)(2,1)S(1)} collective-permute-done((bf16[2,1,4,2,512]{4,3,2,0,1:T(2,128)(2,1)S(1)}, bf16[2,1,4,2,512]{4,3,2,0,1:T(2,128)(2,1)S(1)}, u32[]{:S(2)}, u32[]{:S(2)}) %collective-permute-start.2) | collective-permute-done | bytes 16416 | tf_op jit(solution)/shard_map/ppermute | solution.py:103
  26.6 0.2 collective-permute-done.1
  26.8 0.1 maximum_bitcast_fusion.3
  26.9 0.7 gather_fusion.2
  27.6 0.1 fusion.15
  27.8 2.9 %collective-permute-start.6 = (bf16[2,1,16,2,512]{4,3,2,0,1:T(2,128)(2,1)S(1)}, bf16[2,1,16,2,512]{4,3,2,0,1:T(2,128)(2,1)S(1)}, u32[]{:S(2)}, u32[]{:S(2)}) collective-permute-start(bf16[2,1,16,2,512]{4,3,2,0,1:T(2,128)(2,1)S(1)} %bitcast.136), channel_id=1, source_target_pairs={{0,48},{16,0},{32,16},{48,32},{1,49},{17,1},{33,17},{49,33},{2,50}... | collective-permute-start | bytes 196616 | tf_op jit(solution)/shard_map/ppermute | solution.py:103
  30.7 0.4 collective-permute-start.4
  31.1 0.9 collective-permute-done.6
  32.0 3.6 %collective-permute-done.5 = bf16[2,1,16,2,512]{4,3,2,0,1:T(2,128)(2,1)S(1)} collective-permute-done((bf16[2,1,16,2,512]{4,3,2,0,1:T(2,128)(2,1)S(1)}, bf16[2,1,16,2,512]{4,3,2,0,1:T(2,128)(2,1)S(1)}, u32[]{:S(2)}, u32[]{:S(2)}) %collective-permute-start.5) | collective-permute-done | bytes 65568 | tf_op jit(solution)/shard_map/ppermute | solution.py:103
  35.6 0.2 collective-permute-done.4
  35.8 0.5 maximum_bitcast_fusion.2
  36.3 1.1 gather_fusion.3
  37.4 0.3 fusion.13
  37.7 2.8 %collective-permute-start.9 = (bf16[2,1,64,2,512]{4,2,3,0,1:T(8,128)(2,1)S(1)}, bf16[2,1,64,2,512]{4,2,3,0,1:T(8,128)(2,1)S(1)}, u32[]{:S(2)}, u32[]{:S(2)}) collective-permute-start(bf16[2,1,64,2,512]{4,2,3,0,1:T(8,128)(2,1)S(1)} %bitcast.131), channel_id=1, source_target_pairs={{0,192},{64,0},{128,64},{192,128},{1,193},{65,1},{129,65},{193,129... | collective-permute-start | bytes 786440 | tf_op jit(solution)/shard_map/ppermute | solution.py:103
  40.5 0.3 collective-permute-start.8
  40.9 0.7 collective-permute-start.7
  41.6 5.4 %collective-permute-done.9 = bf16[2,1,64,2,512]{4,2,3,0,1:T(8,128)(2,1)S(1)} collective-permute-done((bf16[2,1,64,2,512]{4,2,3,0,1:T(8,128)(2,1)S(1)}, bf16[2,1,64,2,512]{4,2,3,0,1:T(8,128)(2,1)S(1)}, u32[]{:S(2)}, u32[]{:S(2)}) %collective-permute-start.9) | collective-permute-done | bytes 262176 | tf_op jit(solution)/shard_map/ppermute | solution.py:103
  47.0 0.4 collective-permute-done.8
  47.3 3.1 %collective-permute-done.7 = bf16[2,1,64,2,512]{4,2,3,0,1:T(8,128)(2,1)S(1)} collective-permute-done((bf16[2,1,64,2,512]{4,2,3,0,1:T(8,128)(2,1)S(1)}, bf16[2,1,64,2,512]{4,2,3,0,1:T(8,128)(2,1)S(1)}, u32[]{:S(2)}, u32[]{:S(2)}) %collective-permute-start.7) | collective-permute-done | bytes 262176 | tf_op jit(solution)/shard_map/ppermute | solution.py:103
  50.4 0.1 maximum_bitcast_fusion.1
  50.5 0.6 gather_fusion.4
  51.2 0.0 copy-start.6
  51.2 0.2 fusion.6
  51.4 0.1 copy.44
  51.5 6.1 %collective-permute-start.10 = (bf16[1,2,1,256,2,512]{5,3,4,1,2,0:T(8,128)(2,1)S(1)}, bf16[1,2,1,256,2,512]{5,3,4,1,2,0:T(8,128)(2,1)S(1)}, u32[]{:S(2)}, u32[]{:S(2)}) collective-permute-start(bf16[1,2,1,256,2,512]{5,3,4,1,2,0:T(8,128)(2,1)S(1)} %bitcast.125), channel_id=1, source_target_pairs={{0,1},{1,0},{2,3},{3,2},{4,5},{5,4},{6,7},{7,6},{8,9},{9,8},{10,11... | collective-permute-start | bytes 3145736 | tf_op jit(solution)/shard_map/ppermute | solution.py:103
  57.6 0.6 copy.37
  58.2 6.3 %all-to-all-start = ((bf16[1,16,2,512]{3,2,0,1:T(2,128)(2,1)}), bf16[1,16,2,512]{3,2,0,1:T(2,128)(2,1)S(1)}, u32[]{:S(2)}, u32[]{:S(2)}) async-start(bf16[1,16,2,512]{3,2,0,1:T(2,128)(2,1)} %copy.37), calls=%async_computation | async-start | bytes 65536 | tf_op jit(solution)/shard_map/all_to_all | solution.py:133
  64.6 3.3 %subtract_convert_fusion = (bf16[512,32,64]{0,2,1:T(8,128)(2,1)}, bf16[512,32,64]{0,2,1:T(8,128)(2,1)}) fusion(f32[512,64]{0,1:T(8,128)S(1)} %copy-done.6, f32[512,32]{0,1:T(8,128)S(1)} %copy-done.8, f32[512,64]{0,1:T(8,128)S(1)} %copy-done.7, f32[512,32]{0,1:T(8,128)S(1)} %copy-done.9), kind=kLoop, calls=%fused_computation.11 | loop fusion | flops 9437184 | bytes 4587520 | tf_op jit(solution)/shard_map/convert.3
  67.9 3.7 %all-to-all-done = bf16[1,16,2,512]{3,2,0,1:T(2,128)(2,1)S(1)} async-done(((bf16[1,16,2,512]{3,2,0,1:T(2,128)(2,1)}), bf16[1,16,2,512]{3,2,0,1:T(2,128)(2,1)S(1)}, u32[]{:S(2)}, u32[]{:S(2)}) %all-to-all-start) | async-done | bytes 32800 | tf_op jit(solution)/shard_map/all_to_all | solution.py:133
  71.7 0.4 copy.51
  72.0 0.4 copy.50
  72.4 1.0 copy-done.5
  73.4 1.7 %maximum_bitcast_fusion = bf16[2,2,256,2,512]{4,2,3,1,0:T(8,128)(2,1)S(1)} fusion(bf16[1,1,2,1,256,2,512]{6,4,5,2,0,3,1:T(8,128)(2,1)} %bitcast.130, bf16[1,1,2,1,256,2,512]{6,4,5,2,0,3,1:T(8,128)(2,1)} %bitcast.126), kind=kLoop, calls=%fused_computation.13 | loop fusion | flops 1048576 | bytes 4194304 | tf_op jit(solution)/shard_map/stack | solution.py:106
  75.1 2.0 %gather_fusion.5 = bf16[2,2,256,2,512]{4,2,3,1,0:T(8,128)(2,1)} fusion(bf16[2,2,256,2,512]{4,2,3,1,0:T(8,128)(2,1)S(1)} %maximum_bitcast_fusion, s32[1024]{0:T(1024)S(1)} %pad_clamp_fusion), kind=kCustom, calls=%fused_computation.5 | custom fusion | bytes 4194312 | tf_op jit(solution)/shard_map/jit(_take)/gather | solution.py:107
  77.1 1.9 %fusion.3 = bf16[2,2,1,256,2,512]{5,3,4,0,1,2:T(8,128)(2,1)S(1)} fusion(bf16[2,2,256,2,512]{4,2,3,1,0:T(8,128)(2,1)} %gather_fusion.5, pred[2]{0:T(512)(128)(4,1)S(1)} %compare_and_fusion.5), kind=kLoop, calls=%fused_computation.16 | loop fusion | flops 1048576 | bytes 4194306 | tf_op jit(solution)/shard_map/transpose | solution.py:119
  79.0 3.9 %copy.47 = bf16[2,2,1,256,2,512]{3,1,0,5,4,2:T(2,128)(2,1)} copy(bf16[2,2,1,256,2,512]{5,3,4,0,1,2:T(8,128)(2,1)S(1)} %fusion.3) | data formatting | bytes 4194304 | tf_op jit(solution)/shard_map/transpose | solution.py:119
  82.9 4.9 %reshape.469 = bf16[4,256,2,512]{1,0,3,2:T(4,128)(2,1)S(1)} reshape(bf16[2,2,1,256,2,512]{3,1,0,5,4,2:T(2,128)(2,1)} %copy.47) | data formatting | bytes 4194304 | tf_op jit(solution)/shard_map/reshape | solution.py:120
  87.8 0.7 fusion.8
  88.5 0.7 fusion.7
  89.2 0.9 fusion.5
  90.1 0.9 fusion.4
  91.0 1.5 %pad_maximum_fusion = bf16[256,4,2,512]{0,1,3,2:T(4,128)(2,1)S(1)} fusion(bf16[256,4,1,512]{0,1,3,2:T(4,128)(2,1)S(1)} %fusion.5, bf16[256,4,1,512]{0,1,3,2:T(4,128)(2,1)S(1)} %fusion.4), kind=kLoop, calls=%fused_computation.14 | loop fusion | flops 1048576 | bytes 4194304 | tf_op jit(solution)/shard_map/stack | solution.py:89
  92.4 4.3 %copy.49 = bf16[256,4,2,512]{3,2,1,0:T(2,128)(2,1)} copy(bf16[256,4,2,512]{0,1,3,2:T(4,128)(2,1)S(1)} %pad_maximum_fusion) | data formatting | bytes 4194304 | tf_op jit(solution)/shard_map/stack | solution.py:89
  96.7 2.3 %copy.52 = bf16[128,8,2,512]{3,1,2,0:T(8,128)(2,1)S(1)} copy(bf16[128,8,2,512]{3,2,1,0:T(2,128)(2,1)} %bitcast.124) | data formatting | bytes 4194304
  99.0 0.5 copy-done.4
  99.6 6.9 %convolution_multiply_fusion = f32[1024,2048]{1,0:T(8,128)} fusion(bf16[1024,1024]{1,0:T(8,128)(2,1)S(1)} %bitcast.129, bf16[512,2048]{0,1:T(8,128)(2,1)S(1)} %bitcast.128, bf16[512,2048]{0,1:T(8,128)(2,1)S(1)} %bitcast.127), kind=kOutput, calls=%fused_computation.6 | convolution fusion | flops 4305453056 | bytes 14680064 | tf_op jit(solution)/shard_map/dot_general | solution.py:95
  106.4 9.8 %reshape.470 = f32[256,4,2048]{2,1,0:T(4,128)} reshape(f32[1024,2048]{1,0:T(8,128)} %convolution_multiply_fusion) | data formatting | bytes 16777216 | tf_op jit(solution)/shard_map/reshape | solution.py:96
  (42 shorter events, 0.4 us)
Async XLA Ops:
  0.0 1.5 %copy-start = (bf16[1,16,7680]{2,1,0:T(8,128)(2,1)S(1)}, bf16[1,16,7680]{2,1,0:T(8,128)(2,1)}, u32[]{:S(2)}) copy-start(bf16[1,16,7680]{2,1,0:T(8,128)(2,1)} %param.7) | copy-start | bytes 737284
  10.4 8.9 %collective-permute-start = (bf16[1,1,4,2,512]{4,3,2,1,0:T(2,128)(2,1)S(1)}, bf16[1,1,4,2,512]{4,3,2,1,0:T(2,128)(2,1)S(1)}, u32[]{:S(2)}, u32[]{:S(2)}) collective-permute-start(bf16[1,1,4,2,512]{4,3,2,1,0:T(2,128)(2,1)S(1)} %broadcast_select_fusion.4), channel_id=1, source_target_pairs={{0,2},{2,0},{1,3},{3,1},{4,6},{6,4},{5,7},{7,5},{8,10},{10,8},{9,1... | collective-permute-start | bytes 24584 | tf_op jit(solution)/shard_map/ppermute | solution.py:103
  19.9 3.8 %collective-permute-start.3 = (bf16[2,1,4,2,512]{4,3,2,0,1:T(2,128)(2,1)S(1)}, bf16[2,1,4,2,512]{4,3,2,0,1:T(2,128)(2,1)S(1)}, u32[]{:S(2)}, u32[]{:S(2)}) collective-permute-start(bf16[2,1,4,2,512]{4,3,2,0,1:T(2,128)(2,1)S(1)} %broadcast_select_fusion.2), channel_id=1, source_target_pairs={{0,12},{4,0},{8,4},{12,8},{1,13},{5,1},{9,5},{13,9},{2,14},{6,2},{... | collective-permute-start | bytes 49160 | tf_op jit(solution)/shard_map/ppermute | solution.py:103
  22.5 4.1 %collective-permute-start.2 = (bf16[2,1,4,2,512]{4,3,2,0,1:T(2,128)(2,1)S(1)}, bf16[2,1,4,2,512]{4,3,2,0,1:T(2,128)(2,1)S(1)}, u32[]{:S(2)}, u32[]{:S(2)}) collective-permute-start(bf16[2,1,4,2,512]{4,3,2,0,1:T(2,128)(2,1)S(1)} %broadcast_select_fusion.2), channel_id=1, source_target_pairs={{0,8},{4,12},{8,0},{12,4},{1,9},{5,13},{9,1},{13,5},{2,10},{6,14},... | collective-permute-start | bytes 49160 | tf_op jit(solution)/shard_map/ppermute | solution.py:103
  23.0 3.8 %collective-permute-start.1 = (bf16[2,1,4,2,512]{4,3,2,0,1:T(2,128)(2,1)S(1)}, bf16[2,1,4,2,512]{4,3,2,0,1:T(2,128)(2,1)S(1)}, u32[]{:S(2)}, u32[]{:S(2)}) collective-permute-start(bf16[2,1,4,2,512]{4,3,2,0,1:T(2,128)(2,1)S(1)} %broadcast_select_fusion.2), channel_id=1, source_target_pairs={{0,4},{4,8},{8,12},{12,0},{1,5},{5,9},{9,13},{13,1},{2,6},{6,10},{... | collective-permute-start | bytes 49160 | tf_op jit(solution)/shard_map/ppermute | solution.py:103
  27.8 4.2 %collective-permute-start.6 = (bf16[2,1,16,2,512]{4,3,2,0,1:T(2,128)(2,1)S(1)}, bf16[2,1,16,2,512]{4,3,2,0,1:T(2,128)(2,1)S(1)}, u32[]{:S(2)}, u32[]{:S(2)}) collective-permute-start(bf16[2,1,16,2,512]{4,3,2,0,1:T(2,128)(2,1)S(1)} %bitcast.136), channel_id=1, source_target_pairs={{0,48},{16,0},{32,16},{48,32},{1,49},{17,1},{33,17},{49,33},{2,50}... | collective-permute-start | bytes 196616 | tf_op jit(solution)/shard_map/ppermute | solution.py:103
  30.7 5.0 %collective-permute-start.5 = (bf16[2,1,16,2,512]{4,3,2,0,1:T(2,128)(2,1)S(1)}, bf16[2,1,16,2,512]{4,3,2,0,1:T(2,128)(2,1)S(1)}, u32[]{:S(2)}, u32[]{:S(2)}) collective-permute-start(bf16[2,1,16,2,512]{4,3,2,0,1:T(2,128)(2,1)S(1)} %bitcast.137), channel_id=1, source_target_pairs={{0,32},{16,48},{32,0},{48,16},{1,33},{17,49},{33,1},{49,17},{2,34}... | collective-permute-start | bytes 196616 | tf_op jit(solution)/shard_map/ppermute | solution.py:103
  30.7 5.1 %collective-permute-start.4 = (bf16[2,1,16,2,512]{4,3,2,0,1:T(2,128)(2,1)S(1)}, bf16[2,1,16,2,512]{4,3,2,0,1:T(2,128)(2,1)S(1)}, u32[]{:S(2)}, u32[]{:S(2)}) collective-permute-start(bf16[2,1,16,2,512]{4,3,2,0,1:T(2,128)(2,1)S(1)} %bitcast.138), channel_id=1, source_target_pairs={{0,16},{16,32},{32,48},{48,0},{1,17},{17,33},{33,49},{49,1},{2,18}... | collective-permute-start | bytes 196616 | tf_op jit(solution)/shard_map/ppermute | solution.py:103
  37.7 9.3 %collective-permute-start.9 = (bf16[2,1,64,2,512]{4,2,3,0,1:T(8,128)(2,1)S(1)}, bf16[2,1,64,2,512]{4,2,3,0,1:T(8,128)(2,1)S(1)}, u32[]{:S(2)}, u32[]{:S(2)}) collective-permute-start(bf16[2,1,64,2,512]{4,2,3,0,1:T(8,128)(2,1)S(1)} %bitcast.131), channel_id=1, source_target_pairs={{0,192},{64,0},{128,64},{192,128},{1,193},{65,1},{129,65},{193,129... | collective-permute-start | bytes 786440 | tf_op jit(solution)/shard_map/ppermute | solution.py:103
  40.5 6.8 %collective-permute-start.8 = (bf16[2,1,64,2,512]{4,2,3,0,1:T(8,128)(2,1)S(1)}, bf16[2,1,64,2,512]{4,2,3,0,1:T(8,128)(2,1)S(1)}, u32[]{:S(2)}, u32[]{:S(2)}) collective-permute-start(bf16[2,1,64,2,512]{4,2,3,0,1:T(8,128)(2,1)S(1)} %bitcast.132), channel_id=1, source_target_pairs={{0,128},{64,192},{128,0},{192,64},{1,129},{65,193},{129,1},{193,65... | collective-permute-start | bytes 786440 | tf_op jit(solution)/shard_map/ppermute | solution.py:103
  40.9 9.5 %collective-permute-start.7 = (bf16[2,1,64,2,512]{4,2,3,0,1:T(8,128)(2,1)S(1)}, bf16[2,1,64,2,512]{4,2,3,0,1:T(8,128)(2,1)S(1)}, u32[]{:S(2)}, u32[]{:S(2)}) collective-permute-start(bf16[2,1,64,2,512]{4,2,3,0,1:T(8,128)(2,1)S(1)} %bitcast.133), channel_id=1, source_target_pairs={{0,64},{64,128},{128,192},{192,0},{1,65},{65,129},{129,193},{193,1... | collective-permute-start | bytes 786440 | tf_op jit(solution)/shard_map/ppermute | solution.py:103
  51.2 13.4 %copy-start.6 = (f32[512,64]{0,1:T(8,128)S(1)}, f32[512,64]{0,1:T(8,128)}, u32[]{:S(2)}) copy-start(f32[512,64]{0,1:T(8,128)} %constant.174.clone) | copy-start | bytes 393220
  51.2 13.4 %copy-start.7 = (f32[512,64]{0,1:T(8,128)S(1)}, f32[512,64]{0,1:T(8,128)}, u32[]{:S(2)}) copy-start(f32[512,64]{0,1:T(8,128)} %constant.173.clone) | copy-start | bytes 393220
  51.2 13.4 %copy-start.8 = (f32[512,32]{0,1:T(8,128)S(1)}, f32[512,32]{0,1:T(8,128)}, u32[]{:S(2)}) copy-start(f32[512,32]{0,1:T(8,128)} %constant.172.clone) | copy-start | bytes 196612
  51.2 13.4 %copy-start.9 = (f32[512,32]{0,1:T(8,128)S(1)}, f32[512,32]{0,1:T(8,128)}, u32[]{:S(2)}) copy-start(f32[512,32]{0,1:T(8,128)} %constant.171.clone) | copy-start | bytes 196612
  51.5 16.5 %copy-start.2 = (bf16[2,1,4,64,2,512]{5,3,2,4,0,1:T(8,128)(2,1)}, bf16[2,1,4,64,2,512]{5,3,2,4,0,1:T(8,128)(2,1)S(1)}, u32[]{:S(2)}) copy-start(bf16[2,1,4,64,2,512]{5,3,2,4,0,1:T(8,128)(2,1)S(1)} %copy.44) | copy-start | bytes 3145732
  51.5 20.9 %collective-permute-start.10 = (bf16[1,2,1,256,2,512]{5,3,4,1,2,0:T(8,128)(2,1)S(1)}, bf16[1,2,1,256,2,512]{5,3,4,1,2,0:T(8,128)(2,1)S(1)}, u32[]{:S(2)}, u32[]{:S(2)}) collective-permute-start(bf16[1,2,1,256,2,512]{5,3,4,1,2,0:T(8,128)(2,1)S(1)} %bitcast.125), channel_id=1, source_target_pairs={{0,1},{1,0},{2,3},{3,2},{4,5},{5,4},{6,7},{7,6},{8,9},{9,8},{10,11... | collective-permute-start | bytes 3145736 | tf_op jit(solution)/shard_map/ppermute | solution.py:103
  58.2 13.4 %all-to-all-start = ((bf16[1,16,2,512]{3,2,0,1:T(2,128)(2,1)}), bf16[1,16,2,512]{3,2,0,1:T(2,128)(2,1)S(1)}, u32[]{:S(2)}, u32[]{:S(2)}) async-start(bf16[1,16,2,512]{3,2,0,1:T(2,128)(2,1)} %copy.37), calls=%async_computation | async-start | bytes 65536 | tf_op jit(solution)/shard_map/all_to_all | solution.py:133
  72.4 1.0 copy-start.5
  96.7 2.3 %copy-start.3 = (bf16[512,32,64]{0,2,1:T(8,128)(2,1)S(1)}, bf16[512,32,64]{0,2,1:T(8,128)(2,1)}, u32[]{:S(2)}) copy-start(bf16[512,32,64]{0,2,1:T(8,128)(2,1)} %get-tuple-element.7) | copy-start | bytes 6291460
  96.7 2.9 %copy-start.4 = (bf16[512,32,64]{0,2,1:T(8,128)(2,1)S(1)}, bf16[512,32,64]{0,2,1:T(8,128)(2,1)}, u32[]{:S(2)}) copy-start(bf16[512,32,64]{0,2,1:T(8,128)(2,1)} %get-tuple-element.8) | copy-start | bytes 6291460
  106.4 9.8 %copy-start.1 = (bf16[1,16,7680]{2,1,0:T(8,128)(2,1)S(1)}, bf16[1,16,7680]{2,1,0:T(8,128)(2,1)}, u32[]{:S(2)}) copy-start(bf16[1,16,7680]{2,1,0:T(8,128)(2,1)} %param.7) | copy-start | bytes 737284

commit v5 on v4

--- a/solution.py
+++ b/solution.py
@@ -63,61 +63,42 @@
     return normalize(jnp.dot(row_data, band_table(), preferred_element_type=jnp.float32))
 
 
-def cross_terms(source_part, receiver_part):
-    real_sum = jnp.einsum(
-        "wbi,wri->bri",
-        source_part[:, :, 0],
-        receiver_part[:, :, 0],
-        preferred_element_type=jnp.float32,
-    ) + jnp.einsum(
-        "wbi,wri->bri",
-        source_part[:, :, 1],
-        receiver_part[:, :, 1],
-        preferred_element_type=jnp.float32,
-    )
-    imag_sum = jnp.einsum(
-        "wbi,wri->bri",
-        source_part[:, :, 1],
-        receiver_part[:, :, 0],
-        preferred_element_type=jnp.float32,
-    ) - jnp.einsum(
-        "wbi,wri->bri",
-        source_part[:, :, 0],
-        receiver_part[:, :, 1],
-        preferred_element_type=jnp.float32,
-    )
-    return jnp.stack([real_sum, imag_sum], axis=2)
+def cross_lhs(sources, receivers):
+    src = sources.astype(jnp.float32)[:, :, None]
+    rec = receivers.astype(jnp.float32)[:, None]
+    real_sum = jnp.sum(src[..., 0, :] * rec[..., 0, :] + src[..., 1, :] * rec[..., 1, :], axis=0)
+    imag_sum = jnp.sum(src[..., 1, :] * rec[..., 0, :] - src[..., 0, :] * rec[..., 1, :], axis=0)
+    lhs = jnp.concatenate([real_sum, imag_sum], axis=2).reshape(-1, 2 * NBINS)
+    return lhs.astype(jnp.bfloat16)
 
 
-def transform(spectra, weights, lag_scale):
-    count_src, count_rec = (spectra.shape[0], spectra.shape[1])
-    rounded = spectra.astype(jnp.bfloat16).reshape(count_src * count_rec, 2 * NBINS)
-    result = jnp.dot(rounded, weights, preferred_element_type=jnp.float32) * lag_scale
-    return result.reshape(count_src, count_rec, 2 * MAXLAG)
+def transform(lhs, weights, lag_scale, count_rec):
+    result = jnp.dot(lhs, weights, preferred_element_type=jnp.float32) * lag_scale
+    return result.reshape(-1, count_rec, 2 * MAXLAG)
 
 
 def ring_gather(value, axis_name, axis):
     size = lax.axis_size(axis_name)
     here = lax.axis_index(axis_name)
-    parts = [value] + [
-        lax.ppermute(value, axis_name, [(i, (i + shift) % size) for i in range(size)])
-        for shift in range(1, size)
-    ]
-    stacked = jnp.stack(parts, 0)
-    stacked = jnp.take(stacked, (here - jnp.arange(size)) % size, axis=0)
-    stacked = jnp.moveaxis(stacked, 0, axis)
     shape = list(value.shape)
+    block = shape[axis]
     shape[axis] *= size
-    return stacked.reshape(shape)
+    out = jnp.zeros(shape, value.dtype)
+    for shift in range(size):
+        part = value if shift == 0 else lax.ppermute(
+            value, axis_name, [(i, (i + shift) % size) for i in range(size)]
+        )
+        start = [0] * len(shape)
+        start[axis] = ((here - shift) % size) * block
+        out = lax.dynamic_update_slice(out, part, start)
+    return out
 
 
 def collect(own):
-    part = ring_gather(own[None], "zh", 0)
+    part = ring_gather(own, "zh", 0)
     for name in reversed(CHAN_AXES):
-        part = ring_gather(part, name, 2)
-    part = ring_gather(part[None], "core", 0)
-    part = jnp.swapaxes(part, 0, 1)
-    return part.reshape(-1, part.shape[3], 2, NBINS)
+        part = ring_gather(part, name, 1)
+    return ring_gather(part, "core", 0)
 
 
 def per_device(records, source_rows):
@@ -131,13 +112,15 @@
     weights = lag_weights()
     lag_scale = math.sqrt(2.0 / (lax.axis_size(WIN_AXES) * windows_here * NBINS))
     receivers = lax.all_to_all(whitened, WIN_AXES, split_axis=1, concat_axis=0, tiled=True)
+    receivers = jnp.swapaxes(
+        receivers.reshape((lax.axis_size("zh"), lax.axis_size("core")) + receivers.shape[1:]), 0, 1
+    ).reshape(receivers.shape)
     shard = lax.axis_index(CHAN_AXES)
     own_rows = lax.dynamic_slice_in_dim(source_rows[0], shard * per_shard, per_shard)
     own_sources = jnp.take(whitened, own_rows, axis=1)
-    source_block = collect(own_sources)
-    spectra = cross_terms(source_block, receivers)
-    results = transform(spectra, weights, lag_scale)
-    return results
+    sources = collect(own_sources)
+    lhs = cross_lhs(sources, receivers)
+    return transform(lhs, weights, lag_scale, receivers.shape[1])
 
 
 def split_mesh(mesh):

time: 117 us -> 92.4 us (0.79)
  local copies, waits for them, and re-layouts: 33.9 us -> 15.9 us
  waiting for transfers between devices: 21.1 us -> 15.4 us
  other arithmetic: 12.5 us -> 9.74 us
  starting transfers between devices: 31 us -> 32.5 us
    all_to_all x1, starting transfers between devices: 6.32 us -> 11.6 us  [per_device(): lax.all_to_all(whitened, WIN_AXES, split_axis=1, concat_axis=0, tiled=True)]
    reshape x2 -> x1, local copies, waits for them, and re-layouts: 14.7 us -> 9.75 us  [transform(): return result.reshape(-1, count_rec, 2 * MAXLAG)]
    gather x5 -> x0, local copies, waits for them, and re-layouts: 4.96 us -> none  [ring_gather(): stacked = jnp.take(stacked, (here - jnp.arange(size)) % size, axis=0)]
    unnamed x23 -> x11, local copies, waits for them, and re-layouts: 4.55 us -> 0.05 us
    another operation x1 -> x0, local copies, waits for them, and re-layouts: 4.26 us -> none  [cross_terms(): return jnp.stack([real_sum, imag_sum], axis=2)]
    transpose x4 -> x0, local copies, waits for them, and re-layouts: 4.11 us -> none  [the longest x1 3.94 us: collect(): part = jnp.swapaxes(part, 0, 1)]
    another operation x7 -> x1, other arithmetic: 7.28 us -> 3.37 us
    ppermute x11, starting transfers between devices: 24.7 us -> 20.9 us  [ring_gather(): lax.ppermute(value, axis_name, [(i, (i + shift) % size) for i in range(si...]
  transfers between devices with their start and end apart: 12 -> 12, of which waited for: 10 -> 4; matrix products, arithmetic and copies ran while one was open for 4% -> 5% of each run, Pallas kernels for 0% -> 0%
where the time goes in v5:
time: 92.4 us; the launch traced here: 92 us
  starting transfers between devices  32.5 us (35%)
  matrix products  17.9 us (19%)
  local copies, waits for them, and re-layouts  15.9 us (17%)
  waiting for transfers between devices  15.4 us (17%)
  other arithmetic  9.74 us (11%)
    ppermute x11, starting transfers between devices, ring_gather(): lax.ppermute(value, axis_name, [(i, (i + shift) % size) for i in range(si...  20.9 us
    ppermute x11, waiting for transfers between devices, ring_gather(): lax.ppermute(value, axis_name, [(i, (i + shift) % size) for i in range(si...  15.4 us
    all_to_all x1, starting transfers between devices, per_device(): lax.all_to_all(whitened, WIN_AXES, split_axis=1, concat_axis=0, tiled=True)  11.6 us
    dot_general x1, matrix products, transform(): jnp.dot(lhs, weights, preferred_element_type=jnp.float32) * lag_scale  10.6 us
    reshape x1, local copies, waits for them, and re-layouts, transform(): return result.reshape(-1, count_rec, 2 * MAXLAG)  9.75 us
    dot_general x1, matrix products, whiten(): jnp.dot(row_data, band_table(), preferred_element_type=jnp.float32)  7.3 us
    another operation x1, other arithmetic  3.37 us
    reduce_sum x1, other arithmetic, cross_lhs(): jnp.sum(src[..., 0, :] * rec[..., 0, :] + src[..., 1, :] * rec[..., 1, :]...  3.15 us
  transfers between devices with their start and end apart: 12, of which 4 were waited for; matrix products, arithmetic and copies ran while one was open for 5% of the time, Pallas kernels for 0%

profile of v5, /device:TPU:1, one launch (start us, length us, event | category | flops | bytes accessed | tf_op | source)
XLA Modules:
  0.0 92.0 jit_solution(5093793880934895509)
XLA Ops:
  0.0 0.0 copy-start
  0.0 0.8 fusion.12
  0.8 0.7 compare_and_fusion
  1.5 0.0 copy-done
  1.5 7.3 %convolution_bitcast_fusion = f32[16,1152]{1,0:T(8,128)S(1)} fusion(bf16[7680,1152]{1,0:T(8,128)(2,1)} %constant.163.clone, bf16[1,16,7680]{2,1,0:T(8,128)(2,1)S(1)} %copy-done), kind=kOutput, calls=%fused_computation.9 | convolution fusion | flops 283115520 | bytes 18014208 | tf_op jit(solution)/shard_map/dot_general | solution.py:63
  8.8 0.0 copy-start.1
  8.8 0.0 copy-start.2
  8.9 0.0 copy-start.3
  8.9 0.0 copy-start.4
  8.9 0.1 fusion.5
  9.0 0.6 fusion.10
  9.6 0.1 fusion.11
  9.7 0.6 gather_fusion
  10.3 0.1 broadcast_select_fusion
  10.4 7.8 %collective-permute-start = (bf16[1,4,2,512]{3,2,1,0:T(2,128)(2,1)S(1)}, bf16[1,4,2,512]{3,2,1,0:T(2,128)(2,1)S(1)}, u32[]{:S(2)}, u32[]{:S(2)}) collective-permute-start(bf16[1,4,2,512]{3,2,1,0:T(2,128)(2,1)S(1)} %broadcast_select_fusion), channel_id=1, source_target_pairs={{0,2},{2,0},{1,3},{3,1},{4,6},{6,4},{5,7},{7,5},{8,10},{10,8},{9,1... | collective-permute-start | bytes 24584 | tf_op jit(solution)/shard_map/ppermute | solution.py:88
  18.4 0.8 collective-permute-done
  19.3 2.5 %collective-permute-start.3 = (bf16[2,4,2,512]{3,1,0,2:T(4,128)(2,1)S(1)}, bf16[2,4,2,512]{3,1,0,2:T(4,128)(2,1)S(1)}, u32[]{:S(2)}, u32[]{:S(2)}) collective-permute-start(bf16[2,4,2,512]{3,1,0,2:T(4,128)(2,1)S(1)} %copy_dynamic-update-slice_fusion), channel_id=1, source_target_pairs={{0,12},{4,0},{8,4},{12,8},{1,13},{5,1},{9,5},{13,9},{2,14},{6,2},{... | collective-permute-start | bytes 49160 | tf_op jit(solution)/shard_map/ppermute | solution.py:88
  21.8 0.5 collective-permute-start.2
  22.4 0.6 collective-permute-start.1
  23.0 3.2 %collective-permute-done.1 = bf16[2,4,2,512]{3,1,0,2:T(4,128)(2,1)S(1)} collective-permute-done((bf16[2,4,2,512]{3,1,0,2:T(4,128)(2,1)S(1)}, bf16[2,4,2,512]{3,1,0,2:T(4,128)(2,1)S(1)}, u32[]{:S(2)}, u32[]{:S(2)}) %collective-permute-start.1) | collective-permute-done | bytes 16416 | tf_op jit(solution)/shard_map/ppermute | solution.py:88
  26.2 0.0 collective-permute-done.2
  26.2 0.0 collective-permute-done.3
  26.2 2.9 %collective-permute-start.6 = (bf16[2,16,2,512]{3,1,0,2:T(8,128)(2,1)S(1)}, bf16[2,16,2,512]{3,1,0,2:T(8,128)(2,1)S(1)}, u32[]{:S(2)}, u32[]{:S(2)}) collective-permute-start(bf16[2,16,2,512]{3,1,0,2:T(8,128)(2,1)S(1)} %constant_dynamic-update-slice_fusion.8), channel_id=1, source_target_pairs={{0,48},{16,0},{32,16},{48,32},{1,49},{17,1},{33,17},{49,33},{2,50}... | collective-permute-start | bytes 196616 | tf_op jit(solution)/shard_map/ppermute | solution.py:88
  29.1 0.0 collective-permute-start.5
  29.1 0.4 collective-permute-start.4
  29.6 4.7 %collective-permute-done.4 = bf16[2,16,2,512]{3,1,0,2:T(8,128)(2,1)S(1)} collective-permute-done((bf16[2,16,2,512]{3,1,0,2:T(8,128)(2,1)S(1)}, bf16[2,16,2,512]{3,1,0,2:T(8,128)(2,1)S(1)}, u32[]{:S(2)}, u32[]{:S(2)}) %collective-permute-start.4) | collective-permute-done | bytes 65568 | tf_op jit(solution)/shard_map/ppermute | solution.py:88
  34.3 0.0 collective-permute-done.5
  34.3 0.0 collective-permute-done.6
  34.3 1.4 %collective-permute-start.7 = (bf16[2,64,2,512]{3,1,0,2:T(8,128)(2,1)S(1)}, bf16[2,64,2,512]{3,1,0,2:T(8,128)(2,1)S(1)}, u32[]{:S(2)}, u32[]{:S(2)}) collective-permute-start(bf16[2,64,2,512]{3,1,0,2:T(8,128)(2,1)S(1)} %constant_dynamic-update-slice_fusion.4), channel_id=1, source_target_pairs={{0,64},{64,128},{128,192},{192,0},{1,65},{65,129},{129,193},{193,1... | collective-permute-start | bytes 786440 | tf_op jit(solution)/shard_map/ppermute | solution.py:88
  35.7 2.6 %collective-permute-start.8 = (bf16[2,64,2,512]{3,1,0,2:T(8,128)(2,1)S(1)}, bf16[2,64,2,512]{3,1,0,2:T(8,128)(2,1)S(1)}, u32[]{:S(2)}, u32[]{:S(2)}) collective-permute-start(bf16[2,64,2,512]{3,1,0,2:T(8,128)(2,1)S(1)} %constant_dynamic-update-slice_fusion.4), channel_id=1, source_target_pairs={{0,128},{64,192},{128,0},{192,64},{1,129},{65,193},{129,1},{193,65... | collective-permute-start | bytes 786440 | tf_op jit(solution)/shard_map/ppermute | solution.py:88
  38.3 0.6 copy.21
  39.0 11.6 %all-to-all-start = ((bf16[1,16,2,512]{3,2,0,1:T(2,128)(2,1)}), bf16[1,16,2,512]{3,2,0,1:T(2,128)(2,1)S(1)}, u32[]{:S(2)}, u32[]{:S(2)}) async-start(bf16[1,16,2,512]{3,2,0,1:T(2,128)(2,1)} %copy.21), calls=%async_computation | async-start | bytes 65536 | tf_op jit(solution)/shard_map/all_to_all | solution.py:114
  50.6 1.1 %collective-permute-start.9 = (bf16[2,64,2,512]{3,1,0,2:T(8,128)(2,1)S(1)}, bf16[2,64,2,512]{3,1,0,2:T(8,128)(2,1)S(1)}, u32[]{:S(2)}, u32[]{:S(2)}) collective-permute-start(bf16[2,64,2,512]{3,1,0,2:T(8,128)(2,1)S(1)} %constant_dynamic-update-slice_fusion.4), channel_id=1, source_target_pairs={{0,192},{64,0},{128,64},{192,128},{1,193},{65,1},{129,65},{193,129... | collective-permute-start | bytes 786440 | tf_op jit(solution)/shard_map/ppermute | solution.py:88
  51.7 0.1 broadcast_in_dim.43
  51.8 0.0 collective-permute-done.7
  51.8 0.0 collective-permute-done.8
  51.9 6.7 %collective-permute-done.9 = bf16[2,64,2,512]{3,1,0,2:T(8,128)(2,1)S(1)} collective-permute-done((bf16[2,64,2,512]{3,1,0,2:T(8,128)(2,1)S(1)}, bf16[2,64,2,512]{3,1,0,2:T(8,128)(2,1)S(1)}, u32[]{:S(2)}, u32[]{:S(2)}) %collective-permute-start.9) | collective-permute-done | bytes 262176 | tf_op jit(solution)/shard_map/ppermute | solution.py:88
  58.6 1.1 %collective-permute-start.10 = (bf16[2,256,2,512]{3,1,0,2:T(8,128)(2,1)S(1)}, bf16[2,256,2,512]{3,1,0,2:T(8,128)(2,1)S(1)}, u32[]{:S(2)}, u32[]{:S(2)}) collective-permute-start(bf16[2,256,2,512]{3,1,0,2:T(8,128)(2,1)S(1)} %constant_dynamic-update-slice_fusion), channel_id=1, source_target_pairs={{0,1},{1,0},{2,3},{3,2},{4,5},{5,4},{6,7},{7,6},{8,9},{9,8},{10,11... | collective-permute-start | bytes 3145736 | tf_op jit(solution)/shard_map/ppermute | solution.py:88
  59.6 0.0 copy-done.1
  59.6 0.0 copy-done.2
  59.6 0.0 copy-done.3
  59.6 0.0 copy-done.4
  59.6 3.4 %subtract_convert_fusion = (bf16[512,32,64]{0,2,1:T(8,128)(2,1)}, bf16[512,32,64]{0,2,1:T(8,128)(2,1)}) fusion(f32[512,64]{0,1:T(8,128)S(1)} %copy-done.1, f32[512,32]{0,1:T(8,128)S(1)} %copy-done.3, f32[512,64]{0,1:T(8,128)S(1)} %copy-done.2, f32[512,32]{0,1:T(8,128)S(1)} %copy-done.4), kind=kLoop, calls=%fused_computation.8 | loop fusion | flops 9437184 | bytes 4587520 | tf_op jit(solution)/shard_map/convert.7
  63.0 0.0 all-to-all-done
  63.0 0.1 fusion.16
  63.1 0.2 broadcast_in_dim.42
  63.3 0.1 bitcast_dynamic-update-slice_fusion.1
  63.4 0.0 collective-permute-done.10
  63.4 0.1 bitcast_dynamic-update-slice_fusion
  63.5 0.6 broadcast_in_dim.51
  64.1 0.4 slice_bitcast_fusion.1
  64.5 3.2 %add_reduce_fusion = (bf16[256,4,512]{2,0,1:T(8,128)(2,1)S(1)}, bf16[256,4,512]{2,0,1:T(8,128)(2,1)S(1)}) fusion(f32[4,4,512]{2,1,0:T(4,128)S(1)} %get-tuple-element.17, f32[4,256,512]{2,1,0:T(8,128)S(1)} %get-tuple-element.10, f32[4,4,512]{2,1,0:T(4,128)S(1)} %get-tuple-element.18, f32[4,256,512]{2,1,0:T(8,128)S(1)} %get-tuple-element.9), kind=kLoop, calls=%fused_computation.2 | loop fusion | flops 15728640 | bytes 6356992 | tf_op jit(solution)/shard_map/reduce_sum | solution.py:69
  67.7 0.3 pad_maximum_fusion
  68.0 1.6 %copy.23 = bf16[256,4,1024]{2,1,0:T(4,128)(2,1)S(1)} copy(bf16[256,4,1024]{2,0,1:T(8,128)(2,1)S(1)} %pad_maximum_fusion) | data formatting | bytes 4194304 | tf_op jit(solution)/shard_map/concatenate | solution.py:71
  69.6 2.0 %convert_element_type.38 = bf16[1024,1024]{1,0:T(8,128)(2,1)} reshape(bf16[256,4,1024]{2,1,0:T(4,128)(2,1)S(1)} %copy.23) | data formatting | bytes 4194304 | tf_op jit(solution)/shard_map/convert_element_type | solution.py:72
  71.6 10.6 %convolution_multiply_fusion = f32[1024,2048]{1,0:T(8,128)} fusion(bf16[1024,1024]{1,0:T(8,128)(2,1)} %convert_element_type.38, bf16[512,2048]{0,1:T(8,128)(2,1)} %bitcast.41, bf16[512,2048]{0,1:T(8,128)(2,1)} %bitcast.40), kind=kOutput, calls=%fused_computation.3 | convolution fusion | flops 4305453056 | bytes 14680064 | tf_op jit(solution)/shard_map/dot_general | solution.py:76
  82.2 9.7 %reshape.138 = f32[256,4,2048]{2,1,0:T(4,128)} reshape(f32[1024,2048]{1,0:T(8,128)} %convolution_multiply_fusion) | data formatting | bytes 16777216 | tf_op jit(solution)/shard_map/reshape | solution.py:77
  (22 shorter events, 0.4 us)
Async XLA Ops:
  0.0 1.5 %copy-start = (bf16[1,16,7680]{2,1,0:T(8,128)(2,1)S(1)}, bf16[1,16,7680]{2,1,0:T(8,128)(2,1)}, u32[]{:S(2)}) copy-start(bf16[1,16,7680]{2,1,0:T(8,128)(2,1)} %param.7) | copy-start | bytes 737284
  8.8 50.8 %copy-start.1 = (f32[512,64]{0,1:T(8,128)S(1)}, f32[512,64]{0,1:T(8,128)}, u32[]{:S(2)}) copy-start(f32[512,64]{0,1:T(8,128)} %constant.167.clone) | copy-start | bytes 393220
  8.8 50.8 %copy-start.2 = (f32[512,64]{0,1:T(8,128)S(1)}, f32[512,64]{0,1:T(8,128)}, u32[]{:S(2)}) copy-start(f32[512,64]{0,1:T(8,128)} %constant.166.clone) | copy-start | bytes 393220
  8.9 50.8 %copy-start.3 = (f32[512,32]{0,1:T(8,128)S(1)}, f32[512,32]{0,1:T(8,128)}, u32[]{:S(2)}) copy-start(f32[512,32]{0,1:T(8,128)} %constant.165.clone) | copy-start | bytes 196612
  8.9 50.8 %copy-start.4 = (f32[512,32]{0,1:T(8,128)S(1)}, f32[512,32]{0,1:T(8,128)}, u32[]{:S(2)}) copy-start(f32[512,32]{0,1:T(8,128)} %constant.164.clone) | copy-start | bytes 196612
  10.4 8.9 %collective-permute-start = (bf16[1,4,2,512]{3,2,1,0:T(2,128)(2,1)S(1)}, bf16[1,4,2,512]{3,2,1,0:T(2,128)(2,1)S(1)}, u32[]{:S(2)}, u32[]{:S(2)}) collective-permute-start(bf16[1,4,2,512]{3,2,1,0:T(2,128)(2,1)S(1)} %broadcast_select_fusion), channel_id=1, source_target_pairs={{0,2},{2,0},{1,3},{3,1},{4,6},{6,4},{5,7},{7,5},{8,10},{10,8},{9,1... | collective-permute-start | bytes 24584 | tf_op jit(solution)/shard_map/ppermute | solution.py:88
  19.3 6.9 %collective-permute-start.3 = (bf16[2,4,2,512]{3,1,0,2:T(4,128)(2,1)S(1)}, bf16[2,4,2,512]{3,1,0,2:T(4,128)(2,1)S(1)}, u32[]{:S(2)}, u32[]{:S(2)}) collective-permute-start(bf16[2,4,2,512]{3,1,0,2:T(4,128)(2,1)S(1)} %copy_dynamic-update-slice_fusion), channel_id=1, source_target_pairs={{0,12},{4,0},{8,4},{12,8},{1,13},{5,1},{9,5},{13,9},{2,14},{6,2},{... | collective-permute-start | bytes 49160 | tf_op jit(solution)/shard_map/ppermute | solution.py:88
  21.8 4.3 %collective-permute-start.2 = (bf16[2,4,2,512]{3,1,0,2:T(4,128)(2,1)S(1)}, bf16[2,4,2,512]{3,1,0,2:T(4,128)(2,1)S(1)}, u32[]{:S(2)}, u32[]{:S(2)}) collective-permute-start(bf16[2,4,2,512]{3,1,0,2:T(4,128)(2,1)S(1)} %copy_dynamic-update-slice_fusion), channel_id=1, source_target_pairs={{0,8},{4,12},{8,0},{12,4},{1,9},{5,13},{9,1},{13,5},{2,10},{6,14},... | collective-permute-start | bytes 49160 | tf_op jit(solution)/shard_map/ppermute | solution.py:88
  22.4 3.8 %collective-permute-start.1 = (bf16[2,4,2,512]{3,1,0,2:T(4,128)(2,1)S(1)}, bf16[2,4,2,512]{3,1,0,2:T(4,128)(2,1)S(1)}, u32[]{:S(2)}, u32[]{:S(2)}) collective-permute-start(bf16[2,4,2,512]{3,1,0,2:T(4,128)(2,1)S(1)} %copy_dynamic-update-slice_fusion), channel_id=1, source_target_pairs={{0,4},{4,8},{8,12},{12,0},{1,5},{5,9},{9,13},{13,1},{2,6},{6,10},{... | collective-permute-start | bytes 49160 | tf_op jit(solution)/shard_map/ppermute | solution.py:88
  26.2 8.1 %collective-permute-start.6 = (bf16[2,16,2,512]{3,1,0,2:T(8,128)(2,1)S(1)}, bf16[2,16,2,512]{3,1,0,2:T(8,128)(2,1)S(1)}, u32[]{:S(2)}, u32[]{:S(2)}) collective-permute-start(bf16[2,16,2,512]{3,1,0,2:T(8,128)(2,1)S(1)} %constant_dynamic-update-slice_fusion.8), channel_id=1, source_target_pairs={{0,48},{16,0},{32,16},{48,32},{1,49},{17,1},{33,17},{49,33},{2,50}... | collective-permute-start | bytes 196616 | tf_op jit(solution)/shard_map/ppermute | solution.py:88
  29.1 5.1 %collective-permute-start.5 = (bf16[2,16,2,512]{3,1,0,2:T(8,128)(2,1)S(1)}, bf16[2,16,2,512]{3,1,0,2:T(8,128)(2,1)S(1)}, u32[]{:S(2)}, u32[]{:S(2)}) collective-permute-start(bf16[2,16,2,512]{3,1,0,2:T(8,128)(2,1)S(1)} %constant_dynamic-update-slice_fusion.8), channel_id=1, source_target_pairs={{0,32},{16,48},{32,0},{48,16},{1,33},{17,49},{33,1},{49,17},{2,34}... | collective-permute-start | bytes 196616 | tf_op jit(solution)/shard_map/ppermute | solution.py:88
  29.1 5.1 %collective-permute-start.4 = (bf16[2,16,2,512]{3,1,0,2:T(8,128)(2,1)S(1)}, bf16[2,16,2,512]{3,1,0,2:T(8,128)(2,1)S(1)}, u32[]{:S(2)}, u32[]{:S(2)}) collective-permute-start(bf16[2,16,2,512]{3,1,0,2:T(8,128)(2,1)S(1)} %constant_dynamic-update-slice_fusion.8), channel_id=1, source_target_pairs={{0,16},{16,32},{32,48},{48,0},{1,17},{17,33},{33,49},{49,1},{2,18}... | collective-permute-start | bytes 196616 | tf_op jit(solution)/shard_map/ppermute | solution.py:88
  34.3 17.5 %collective-permute-start.7 = (bf16[2,64,2,512]{3,1,0,2:T(8,128)(2,1)S(1)}, bf16[2,64,2,512]{3,1,0,2:T(8,128)(2,1)S(1)}, u32[]{:S(2)}, u32[]{:S(2)}) collective-permute-start(bf16[2,64,2,512]{3,1,0,2:T(8,128)(2,1)S(1)} %constant_dynamic-update-slice_fusion.4), channel_id=1, source_target_pairs={{0,64},{64,128},{128,192},{192,0},{1,65},{65,129},{129,193},{193,1... | collective-permute-start | bytes 786440 | tf_op jit(solution)/shard_map/ppermute | solution.py:88
  35.7 16.1 %collective-permute-start.8 = (bf16[2,64,2,512]{3,1,0,2:T(8,128)(2,1)S(1)}, bf16[2,64,2,512]{3,1,0,2:T(8,128)(2,1)S(1)}, u32[]{:S(2)}, u32[]{:S(2)}) collective-permute-start(bf16[2,64,2,512]{3,1,0,2:T(8,128)(2,1)S(1)} %constant_dynamic-update-slice_fusion.4), channel_id=1, source_target_pairs={{0,128},{64,192},{128,0},{192,64},{1,129},{65,193},{129,1},{193,65... | collective-permute-start | bytes 786440 | tf_op jit(solution)/shard_map/ppermute | solution.py:88
  39.0 24.0 %all-to-all-start = ((bf16[1,16,2,512]{3,2,0,1:T(2,128)(2,1)}), bf16[1,16,2,512]{3,2,0,1:T(2,128)(2,1)S(1)}, u32[]{:S(2)}, u32[]{:S(2)}) async-start(bf16[1,16,2,512]{3,2,0,1:T(2,128)(2,1)} %copy.21), calls=%async_computation | async-start | bytes 65536 | tf_op jit(solution)/shard_map/all_to_all | solution.py:114
  50.6 7.9 %collective-permute-start.9 = (bf16[2,64,2,512]{3,1,0,2:T(8,128)(2,1)S(1)}, bf16[2,64,2,512]{3,1,0,2:T(8,128)(2,1)S(1)}, u32[]{:S(2)}, u32[]{:S(2)}) collective-permute-start(bf16[2,64,2,512]{3,1,0,2:T(8,128)(2,1)S(1)} %constant_dynamic-update-slice_fusion.4), channel_id=1, source_target_pairs={{0,192},{64,0},{128,64},{192,128},{1,193},{65,1},{129,65},{193,129... | collective-permute-start | bytes 786440 | tf_op jit(solution)/shard_map/ppermute | solution.py:88
  58.6 4.8 %collective-permute-start.10 = (bf16[2,256,2,512]{3,1,0,2:T(8,128)(2,1)S(1)}, bf16[2,256,2,512]{3,1,0,2:T(8,128)(2,1)S(1)}, u32[]{:S(2)}, u32[]{:S(2)}) collective-permute-start(bf16[2,256,2,512]{3,1,0,2:T(8,128)(2,1)S(1)} %constant_dynamic-update-slice_fusion), channel_id=1, source_target_pairs={{0,1},{1,0},{2,3},{3,2},{4,5},{5,4},{6,7},{7,6},{8,9},{9,8},{10,11... | collective-permute-start | bytes 3145736 | tf_op jit(solution)/shard_map/ppermute | solution.py:88

commit v6 on v5

--- a/solution.py
+++ b/solution.py
@@ -34,15 +34,9 @@
 
 def lag_weights():
     bin_ids = FIRST_BIN + np.arange(NBINS)
-    inner = 64
-    outer = 2 * MAXLAG // inner
-    ca, sa = angle_table(bin_ids, (np.arange(outer) - MAXLAG // inner) * inner)
-    cb, sb = angle_table(bin_ids, np.arange(inner))
-    ca, sa, cb, sb = (jnp.asarray(a) for a in (ca, sa, cb, sb))
-    cos = ca[:, :, None] * cb[:, None, :] - sa[:, :, None] * sb[:, None, :]
-    sin = sa[:, :, None] * cb[:, None, :] + ca[:, :, None] * sb[:, None, :]
-    table = jnp.concatenate([cos, -sin], axis=0).astype(jnp.bfloat16)
-    return table.reshape(2 * NBINS, 2 * MAXLAG)
+    cos, sin = angle_table(bin_ids, np.arange(2 * MAXLAG) - MAXLAG)
+    table = np.concatenate([cos, -sin], axis=0).astype(ml_dtypes.bfloat16)
+    return jnp.asarray(table)
 
 
 def normalize(spectrum):

time: 92.4 us -> 94.3 us (1.021)
  waiting for transfers between devices: 15.4 us -> 21.5 us
  other arithmetic: 9.74 us -> 6.37 us
    all_to_all x1, waiting for transfers between devices: 0.01 us -> 7.08 us  [per_device(): lax.all_to_all(whitened, WIN_AXES, split_axis=1, concat_axis=0, tiled=True)]
    all_to_all x1, starting transfers between devices: 11.6 us -> 6.02 us  [per_device(): lax.all_to_all(whitened, WIN_AXES, split_axis=1, concat_axis=0, tiled=True)]
    ppermute x11, starting transfers between devices: 20.9 us -> 25.9 us  [ring_gather(): lax.ppermute(value, axis_name, [(i, (i + shift) % size) for i in range(si...]
    another operation x1 -> x0, other arithmetic: 3.37 us -> none
    ppermute x11, waiting for transfers between devices: 15.4 us -> 14.4 us  [ring_gather(): lax.ppermute(value, axis_name, [(i, (i + shift) % size) for i in range(si...]
  transfers between devices with their start and end apart: 12 -> 12, of which waited for: 4 -> 6; matrix products, arithmetic and copies ran while one was open for 5% -> 1% of each run, Pallas kernels for 0% -> 0%
where the time goes in v6:
time: 94.3 us; the launch traced here: 94 us
  starting transfers between devices  31.9 us (34%)
  waiting for transfers between devices  21.5 us (23%)
  matrix products  17.8 us (19%)
  local copies, waits for them, and re-layouts  15.9 us (17%)
  other arithmetic  6.37 us (7%)
    ppermute x11, starting transfers between devices, ring_gather(): lax.ppermute(value, axis_name, [(i, (i + shift) % size) for i in range(si...  25.9 us
    ppermute x11, waiting for transfers between devices, ring_gather(): lax.ppermute(value, axis_name, [(i, (i + shift) % size) for i in range(si...  14.4 us
    dot_general x1, matrix products, transform(): jnp.dot(lhs, weights, preferred_element_type=jnp.float32) * lag_scale  10.5 us
    reshape x1, local copies, waits for them, and re-layouts, transform(): return result.reshape(-1, count_rec, 2 * MAXLAG)  9.75 us
    dot_general x1, matrix products, whiten(): jnp.dot(row_data, band_table(), preferred_element_type=jnp.float32)  7.3 us
    all_to_all x1, waiting for transfers between devices, per_device(): lax.all_to_all(whitened, WIN_AXES, split_axis=1, concat_axis=0, tiled=True)  7.08 us
    all_to_all x1, starting transfers between devices, per_device(): lax.all_to_all(whitened, WIN_AXES, split_axis=1, concat_axis=0, tiled=True)  6.02 us
    reduce_sum x1, other arithmetic, cross_lhs(): jnp.sum(src[..., 0, :] * rec[..., 0, :] + src[..., 1, :] * rec[..., 1, :]...  3.15 us
  transfers between devices with their start and end apart: 12, of which 6 were waited for; matrix products, arithmetic and copies ran while one was open for 1% of the time, Pallas kernels for 0%

profile of v6, /device:TPU:1, one launch (start us, length us, event | category | flops | bytes accessed | tf_op | source)
XLA Modules:
  0.0 94.0 jit_solution(1573505886884621687)
XLA Ops:
  0.0 0.0 copy-start
  0.0 0.8 fusion.9
  0.8 0.7 compare_and_fusion
  1.5 0.0 copy-done
  1.5 7.3 %convolution_bitcast_fusion = f32[16,1152]{1,0:T(8,128)S(1)} fusion(bf16[7680,1152]{1,0:T(8,128)(2,1)} %constant.157.clone, bf16[1,16,7680]{2,1,0:T(8,128)(2,1)S(1)} %copy-done), kind=kOutput, calls=%fused_computation.4 | convolution fusion | flops 283115520 | bytes 18014208 | tf_op jit(solution)/shard_map/dot_general | solution.py:57
  8.8 0.1 fusion.2
  8.9 0.6 fusion.7
  9.6 0.1 fusion.8
  9.7 0.6 gather_fusion
  10.3 0.1 broadcast_select_fusion
  10.4 7.8 %collective-permute-start = (bf16[1,4,2,512]{3,2,1,0:T(2,128)(2,1)S(1)}, bf16[1,4,2,512]{3,2,1,0:T(2,128)(2,1)S(1)}, u32[]{:S(2)}, u32[]{:S(2)}) collective-permute-start(bf16[1,4,2,512]{3,2,1,0:T(2,128)(2,1)S(1)} %broadcast_select_fusion), channel_id=1, source_target_pairs={{0,2},{2,0},{1,3},{3,1},{4,6},{6,4},{5,7},{7,5},{8,10},{10,8},{9,1... | collective-permute-start | bytes 24584 | tf_op jit(solution)/shard_map/ppermute | solution.py:82
  18.4 0.8 collective-permute-done
  19.2 2.5 %collective-permute-start.3 = (bf16[2,4,2,512]{3,1,0,2:T(4,128)(2,1)S(1)}, bf16[2,4,2,512]{3,1,0,2:T(4,128)(2,1)S(1)}, u32[]{:S(2)}, u32[]{:S(2)}) collective-permute-start(bf16[2,4,2,512]{3,1,0,2:T(4,128)(2,1)S(1)} %copy_dynamic-update-slice_fusion), channel_id=1, source_target_pairs={{0,12},{4,0},{8,4},{12,8},{1,13},{5,1},{9,5},{13,9},{2,14},{6,2},{... | collective-permute-start | bytes 49160 | tf_op jit(solution)/shard_map/ppermute | solution.py:82
  21.8 0.5 collective-permute-start.2
  22.3 0.6 collective-permute-start.1
  22.9 3.2 %collective-permute-done.1 = bf16[2,4,2,512]{3,1,0,2:T(4,128)(2,1)S(1)} collective-permute-done((bf16[2,4,2,512]{3,1,0,2:T(4,128)(2,1)S(1)}, bf16[2,4,2,512]{3,1,0,2:T(4,128)(2,1)S(1)}, u32[]{:S(2)}, u32[]{:S(2)}) %collective-permute-start.1) | collective-permute-done | bytes 16416 | tf_op jit(solution)/shard_map/ppermute | solution.py:82
  26.1 0.0 collective-permute-done.2
  26.2 0.0 collective-permute-done.3
  26.2 2.9 %collective-permute-start.6 = (bf16[2,16,2,512]{3,1,0,2:T(8,128)(2,1)S(1)}, bf16[2,16,2,512]{3,1,0,2:T(8,128)(2,1)S(1)}, u32[]{:S(2)}, u32[]{:S(2)}) collective-permute-start(bf16[2,16,2,512]{3,1,0,2:T(8,128)(2,1)S(1)} %constant_dynamic-update-slice_fusion.8), channel_id=1, source_target_pairs={{0,48},{16,0},{32,16},{48,32},{1,49},{17,1},{33,17},{49,33},{2,50}... | collective-permute-start | bytes 196616 | tf_op jit(solution)/shard_map/ppermute | solution.py:82
  29.1 0.0 collective-permute-start.5
  29.1 0.4 collective-permute-start.4
  29.5 4.7 %collective-permute-done.4 = bf16[2,16,2,512]{3,1,0,2:T(8,128)(2,1)S(1)} collective-permute-done((bf16[2,16,2,512]{3,1,0,2:T(8,128)(2,1)S(1)}, bf16[2,16,2,512]{3,1,0,2:T(8,128)(2,1)S(1)}, u32[]{:S(2)}, u32[]{:S(2)}) %collective-permute-start.4) | collective-permute-done | bytes 65568 | tf_op jit(solution)/shard_map/ppermute | solution.py:82
  34.2 0.0 collective-permute-done.5
  34.3 0.0 collective-permute-done.6
  34.3 1.4 %collective-permute-start.7 = (bf16[2,64,2,512]{3,1,0,2:T(8,128)(2,1)S(1)}, bf16[2,64,2,512]{3,1,0,2:T(8,128)(2,1)S(1)}, u32[]{:S(2)}, u32[]{:S(2)}) collective-permute-start(bf16[2,64,2,512]{3,1,0,2:T(8,128)(2,1)S(1)} %constant_dynamic-update-slice_fusion.4), channel_id=1, source_target_pairs={{0,64},{64,128},{128,192},{192,0},{1,65},{65,129},{129,193},{193,1... | collective-permute-start | bytes 786440 | tf_op jit(solution)/shard_map/ppermute | solution.py:82
  35.7 2.6 %collective-permute-start.8 = (bf16[2,64,2,512]{3,1,0,2:T(8,128)(2,1)S(1)}, bf16[2,64,2,512]{3,1,0,2:T(8,128)(2,1)S(1)}, u32[]{:S(2)}, u32[]{:S(2)}) collective-permute-start(bf16[2,64,2,512]{3,1,0,2:T(8,128)(2,1)S(1)} %constant_dynamic-update-slice_fusion.4), channel_id=1, source_target_pairs={{0,128},{64,192},{128,0},{192,64},{1,129},{65,193},{129,1},{193,65... | collective-permute-start | bytes 786440 | tf_op jit(solution)/shard_map/ppermute | solution.py:82
  38.3 1.1 %collective-permute-start.9 = (bf16[2,64,2,512]{3,1,0,2:T(8,128)(2,1)S(1)}, bf16[2,64,2,512]{3,1,0,2:T(8,128)(2,1)S(1)}, u32[]{:S(2)}, u32[]{:S(2)}) collective-permute-start(bf16[2,64,2,512]{3,1,0,2:T(8,128)(2,1)S(1)} %constant_dynamic-update-slice_fusion.4), channel_id=1, source_target_pairs={{0,192},{64,0},{128,64},{192,128},{1,193},{65,1},{129,65},{193,129... | collective-permute-start | bytes 786440 | tf_op jit(solution)/shard_map/ppermute | solution.py:82
  39.3 0.1 broadcast_in_dim.35
  39.5 1.4 %collective-permute-done.7 = bf16[2,64,2,512]{3,1,0,2:T(8,128)(2,1)S(1)} collective-permute-done((bf16[2,64,2,512]{3,1,0,2:T(8,128)(2,1)S(1)}, bf16[2,64,2,512]{3,1,0,2:T(8,128)(2,1)S(1)}, u32[]{:S(2)}, u32[]{:S(2)}) %collective-permute-start.7) | collective-permute-done | bytes 262176 | tf_op jit(solution)/shard_map/ppermute | solution.py:82
  40.9 4.3 %collective-permute-done.8 = bf16[2,64,2,512]{3,1,0,2:T(8,128)(2,1)S(1)} collective-permute-done((bf16[2,64,2,512]{3,1,0,2:T(8,128)(2,1)S(1)}, bf16[2,64,2,512]{3,1,0,2:T(8,128)(2,1)S(1)}, u32[]{:S(2)}, u32[]{:S(2)}) %collective-permute-start.8) | collective-permute-done | bytes 262176 | tf_op jit(solution)/shard_map/ppermute | solution.py:82
  45.2 0.0 collective-permute-done.9
  45.2 6.1 %collective-permute-start.10 = (bf16[2,256,2,512]{3,1,0,2:T(8,128)(2,1)S(1)}, bf16[2,256,2,512]{3,1,0,2:T(8,128)(2,1)S(1)}, u32[]{:S(2)}, u32[]{:S(2)}) collective-permute-start(bf16[2,256,2,512]{3,1,0,2:T(8,128)(2,1)S(1)} %constant_dynamic-update-slice_fusion), channel_id=1, source_target_pairs={{0,1},{1,0},{2,3},{3,2},{4,5},{5,4},{6,7},{7,6},{8,9},{9,8},{10,11... | collective-permute-start | bytes 3145736 | tf_op jit(solution)/shard_map/ppermute | solution.py:82
  51.3 0.6 copy.18
  52.0 6.0 %all-to-all-start = ((bf16[1,16,2,512]{3,2,0,1:T(2,128)(2,1)}), bf16[1,16,2,512]{3,2,0,1:T(2,128)(2,1)S(1)}, u32[]{:S(2)}, u32[]{:S(2)}) async-start(bf16[1,16,2,512]{3,2,0,1:T(2,128)(2,1)} %copy.18), calls=%async_computation | async-start | bytes 65536 | tf_op jit(solution)/shard_map/all_to_all | solution.py:108
  58.0 7.1 %all-to-all-done = bf16[1,16,2,512]{3,2,0,1:T(2,128)(2,1)S(1)} async-done(((bf16[1,16,2,512]{3,2,0,1:T(2,128)(2,1)}), bf16[1,16,2,512]{3,2,0,1:T(2,128)(2,1)S(1)}, u32[]{:S(2)}, u32[]{:S(2)}) %all-to-all-start) | async-done | bytes 32800 | tf_op jit(solution)/shard_map/all_to_all | solution.py:108
  65.1 0.1 fusion.12
  65.2 0.2 broadcast_in_dim.34
  65.3 0.1 bitcast_dynamic-update-slice_fusion.1
  65.5 0.0 collective-permute-done.10
  65.5 0.1 bitcast_dynamic-update-slice_fusion
  65.6 0.6 broadcast_in_dim.43
  66.2 0.4 slice_bitcast_fusion.1
  66.6 3.1 %add_reduce_fusion = (bf16[256,4,512]{2,0,1:T(8,128)(2,1)S(1)}, bf16[256,4,512]{2,0,1:T(8,128)(2,1)S(1)}) fusion(f32[4,4,512]{2,1,0:T(4,128)S(1)} %get-tuple-element.15, f32[4,256,512]{2,1,0:T(8,128)S(1)} %get-tuple-element.10, f32[4,4,512]{2,1,0:T(4,128)S(1)} %get-tuple-element.16, f32[4,256,512]{2,1,0:T(8,128)S(1)} %get-tuple-element.9), kind=kLoop, calls=%fused_computation.2 | loop fusion | flops 15728640 | bytes 6356992 | tf_op jit(solution)/shard_map/reduce_sum | solution.py:63
  69.8 0.3 pad_maximum_fusion
  70.0 1.6 %copy.20 = bf16[256,4,1024]{2,1,0:T(4,128)(2,1)S(1)} copy(bf16[256,4,1024]{2,0,1:T(8,128)(2,1)S(1)} %pad_maximum_fusion) | data formatting | bytes 4194304 | tf_op jit(solution)/shard_map/concatenate | solution.py:65
  71.6 2.0 %convert_element_type.36 = bf16[1024,1024]{1,0:T(8,128)(2,1)} reshape(bf16[256,4,1024]{2,1,0:T(4,128)(2,1)S(1)} %copy.20) | data formatting | bytes 4194304 | tf_op jit(solution)/shard_map/convert_element_type | solution.py:66
  73.7 10.5 %convolution_multiply_fusion = f32[1024,2048]{1,0:T(8,128)} fusion(bf16[1024,1024]{1,0:T(8,128)(2,1)} %convert_element_type.36, bf16[1024,2048]{1,0:T(8,128)(2,1)} %constant.158.clone), kind=kOutput, calls=%fused_computation.3 | convolution fusion | flops 4297064448 | bytes 14680064 | tf_op jit(solution)/shard_map/dot_general | solution.py:70
  84.2 9.7 %reshape.114 = f32[256,4,2048]{2,1,0:T(4,128)} reshape(f32[1024,2048]{1,0:T(8,128)} %convolution_multiply_fusion) | data formatting | bytes 16777216 | tf_op jit(solution)/shard_map/reshape | solution.py:71
  (22 shorter events, 0.4 us)
Async XLA Ops:
  0.0 1.5 %copy-start = (bf16[1,16,7680]{2,1,0:T(8,128)(2,1)S(1)}, bf16[1,16,7680]{2,1,0:T(8,128)(2,1)}, u32[]{:S(2)}) copy-start(bf16[1,16,7680]{2,1,0:T(8,128)(2,1)} %param.4) | copy-start | bytes 737284
  10.4 8.9 %collective-permute-start = (bf16[1,4,2,512]{3,2,1,0:T(2,128)(2,1)S(1)}, bf16[1,4,2,512]{3,2,1,0:T(2,128)(2,1)S(1)}, u32[]{:S(2)}, u32[]{:S(2)}) collective-permute-start(bf16[1,4,2,512]{3,2,1,0:T(2,128)(2,1)S(1)} %broadcast_select_fusion), channel_id=1, source_target_pairs={{0,2},{2,0},{1,3},{3,1},{4,6},{6,4},{5,7},{7,5},{8,10},{10,8},{9,1... | collective-permute-start | bytes 24584 | tf_op jit(solution)/shard_map/ppermute | solution.py:82
  19.2 6.9 %collective-permute-start.3 = (bf16[2,4,2,512]{3,1,0,2:T(4,128)(2,1)S(1)}, bf16[2,4,2,512]{3,1,0,2:T(4,128)(2,1)S(1)}, u32[]{:S(2)}, u32[]{:S(2)}) collective-permute-start(bf16[2,4,2,512]{3,1,0,2:T(4,128)(2,1)S(1)} %copy_dynamic-update-slice_fusion), channel_id=1, source_target_pairs={{0,12},{4,0},{8,4},{12,8},{1,13},{5,1},{9,5},{13,9},{2,14},{6,2},{... | collective-permute-start | bytes 49160 | tf_op jit(solution)/shard_map/ppermute | solution.py:82
  21.8 4.3 %collective-permute-start.2 = (bf16[2,4,2,512]{3,1,0,2:T(4,128)(2,1)S(1)}, bf16[2,4,2,512]{3,1,0,2:T(4,128)(2,1)S(1)}, u32[]{:S(2)}, u32[]{:S(2)}) collective-permute-start(bf16[2,4,2,512]{3,1,0,2:T(4,128)(2,1)S(1)} %copy_dynamic-update-slice_fusion), channel_id=1, source_target_pairs={{0,8},{4,12},{8,0},{12,4},{1,9},{5,13},{9,1},{13,5},{2,10},{6,14},... | collective-permute-start | bytes 49160 | tf_op jit(solution)/shard_map/ppermute | solution.py:82
  22.3 3.8 %collective-permute-start.1 = (bf16[2,4,2,512]{3,1,0,2:T(4,128)(2,1)S(1)}, bf16[2,4,2,512]{3,1,0,2:T(4,128)(2,1)S(1)}, u32[]{:S(2)}, u32[]{:S(2)}) collective-permute-start(bf16[2,4,2,512]{3,1,0,2:T(4,128)(2,1)S(1)} %copy_dynamic-update-slice_fusion), channel_id=1, source_target_pairs={{0,4},{4,8},{8,12},{12,0},{1,5},{5,9},{9,13},{13,1},{2,6},{6,10},{... | collective-permute-start | bytes 49160 | tf_op jit(solution)/shard_map/ppermute | solution.py:82
  26.2 8.1 %collective-permute-start.6 = (bf16[2,16,2,512]{3,1,0,2:T(8,128)(2,1)S(1)}, bf16[2,16,2,512]{3,1,0,2:T(8,128)(2,1)S(1)}, u32[]{:S(2)}, u32[]{:S(2)}) collective-permute-start(bf16[2,16,2,512]{3,1,0,2:T(8,128)(2,1)S(1)} %constant_dynamic-update-slice_fusion.8), channel_id=1, source_target_pairs={{0,48},{16,0},{32,16},{48,32},{1,49},{17,1},{33,17},{49,33},{2,50}... | collective-permute-start | bytes 196616 | tf_op jit(solution)/shard_map/ppermute | solution.py:82
  29.1 5.1 %collective-permute-start.5 = (bf16[2,16,2,512]{3,1,0,2:T(8,128)(2,1)S(1)}, bf16[2,16,2,512]{3,1,0,2:T(8,128)(2,1)S(1)}, u32[]{:S(2)}, u32[]{:S(2)}) collective-permute-start(bf16[2,16,2,512]{3,1,0,2:T(8,128)(2,1)S(1)} %constant_dynamic-update-slice_fusion.8), channel_id=1, source_target_pairs={{0,32},{16,48},{32,0},{48,16},{1,33},{17,49},{33,1},{49,17},{2,34}... | collective-permute-start | bytes 196616 | tf_op jit(solution)/shard_map/ppermute | solution.py:82
  29.1 5.1 %collective-permute-start.4 = (bf16[2,16,2,512]{3,1,0,2:T(8,128)(2,1)S(1)}, bf16[2,16,2,512]{3,1,0,2:T(8,128)(2,1)S(1)}, u32[]{:S(2)}, u32[]{:S(2)}) collective-permute-start(bf16[2,16,2,512]{3,1,0,2:T(8,128)(2,1)S(1)} %constant_dynamic-update-slice_fusion.8), channel_id=1, source_target_pairs={{0,16},{16,32},{32,48},{48,0},{1,17},{17,33},{33,49},{49,1},{2,18}... | collective-permute-start | bytes 196616 | tf_op jit(solution)/shard_map/ppermute | solution.py:82
  34.3 6.6 %collective-permute-start.7 = (bf16[2,64,2,512]{3,1,0,2:T(8,128)(2,1)S(1)}, bf16[2,64,2,512]{3,1,0,2:T(8,128)(2,1)S(1)}, u32[]{:S(2)}, u32[]{:S(2)}) collective-permute-start(bf16[2,64,2,512]{3,1,0,2:T(8,128)(2,1)S(1)} %constant_dynamic-update-slice_fusion.4), channel_id=1, source_target_pairs={{0,64},{64,128},{128,192},{192,0},{1,65},{65,129},{129,193},{193,1... | collective-permute-start | bytes 786440 | tf_op jit(solution)/shard_map/ppermute | solution.py:82
  35.7 9.5 %collective-permute-start.8 = (bf16[2,64,2,512]{3,1,0,2:T(8,128)(2,1)S(1)}, bf16[2,64,2,512]{3,1,0,2:T(8,128)(2,1)S(1)}, u32[]{:S(2)}, u32[]{:S(2)}) collective-permute-start(bf16[2,64,2,512]{3,1,0,2:T(8,128)(2,1)S(1)} %constant_dynamic-update-slice_fusion.4), channel_id=1, source_target_pairs={{0,128},{64,192},{128,0},{192,64},{1,129},{65,193},{129,1},{193,65... | collective-permute-start | bytes 786440 | tf_op jit(solution)/shard_map/ppermute | solution.py:82
  38.3 6.9 %collective-permute-start.9 = (bf16[2,64,2,512]{3,1,0,2:T(8,128)(2,1)S(1)}, bf16[2,64,2,512]{3,1,0,2:T(8,128)(2,1)S(1)}, u32[]{:S(2)}, u32[]{:S(2)}) collective-permute-start(bf16[2,64,2,512]{3,1,0,2:T(8,128)(2,1)S(1)} %constant_dynamic-update-slice_fusion.4), channel_id=1, source_target_pairs={{0,192},{64,0},{128,64},{192,128},{1,193},{65,1},{129,65},{193,129... | collective-permute-start | bytes 786440 | tf_op jit(solution)/shard_map/ppermute | solution.py:82
  45.2 20.2 %collective-permute-start.10 = (bf16[2,256,2,512]{3,1,0,2:T(8,128)(2,1)S(1)}, bf16[2,256,2,512]{3,1,0,2:T(8,128)(2,1)S(1)}, u32[]{:S(2)}, u32[]{:S(2)}) collective-permute-start(bf16[2,256,2,512]{3,1,0,2:T(8,128)(2,1)S(1)} %constant_dynamic-update-slice_fusion), channel_id=1, source_target_pairs={{0,1},{1,0},{2,3},{3,2},{4,5},{5,4},{6,7},{7,6},{8,9},{9,8},{10,11... | collective-permute-start | bytes 3145736 | tf_op jit(solution)/shard_map/ppermute | solution.py:82
  52.0 13.1 %all-to-all-start = ((bf16[1,16,2,512]{3,2,0,1:T(2,128)(2,1)}), bf16[1,16,2,512]{3,2,0,1:T(2,128)(2,1)S(1)}, u32[]{:S(2)}, u32[]{:S(2)}) async-start(bf16[1,16,2,512]{3,2,0,1:T(2,128)(2,1)} %copy.18), calls=%async_computation | async-start | bytes 65536 | tf_op jit(solution)/shard_map/all_to_all | solution.py:108

commit v7 on v5

--- a/solution.py
+++ b/solution.py
@@ -101,6 +101,22 @@
     return ring_gather(part, "core", 0)
 
 
+def exchange_receivers(rows):
+    here = lax.axis_index(WIN_AXES)
+    count = lax.axis_size(WIN_AXES)
+    cores = lax.axis_size("core")
+    quarter = rows.shape[0] // count
+    out = jnp.zeros((count, quarter) + rows.shape[1:], rows.dtype)
+    for shift in range(count):
+        block = lax.dynamic_slice_in_dim(rows, ((here + shift) % count) * quarter, quarter)
+        if shift:
+            block = lax.ppermute(block, WIN_AXES, [(i, (i + shift) % count) for i in range(count)])
+        origin = (here - shift) % count
+        place = (origin % cores) * (count // cores) + origin // cores
+        out = lax.dynamic_update_slice(out, block[None], (place, 0, 0, 0))
+    return out
+
+
 def per_device(records, source_rows):
     windows_here, rows_here, samples = records.shape
     whitened = whiten(records.reshape(windows_here * rows_here, samples)).reshape(
@@ -111,10 +127,7 @@
     per_shard = block_len // shards
     weights = lag_weights()
     lag_scale = math.sqrt(2.0 / (lax.axis_size(WIN_AXES) * windows_here * NBINS))
-    receivers = lax.all_to_all(whitened, WIN_AXES, split_axis=1, concat_axis=0, tiled=True)
-    receivers = jnp.swapaxes(
-        receivers.reshape((lax.axis_size("zh"), lax.axis_size("core")) + receivers.shape[1:]), 0, 1
-    ).reshape(receivers.shape)
+    receivers = exchange_receivers(whitened[0])
     shard = lax.axis_index(CHAN_AXES)
     own_rows = lax.dynamic_slice_in_dim(source_rows[0], shard * per_shard, per_shard)
     own_sources = jnp.take(whitened, own_rows, axis=1)

time: 92.4 us -> 91 us (0.985)
  waiting for transfers between devices: 15.4 us -> 11.7 us
  starting transfers between devices: 32.5 us -> 35.6 us
  other arithmetic: 9.74 us -> 8.43 us
    ppermute x0 -> x3, starting transfers between devices: none -> 14.1 us  [exchange_receivers(): lax.ppermute(block, WIN_AXES, [(i, (i + shift) % count) for i in range(co...]
    all_to_all x1 -> x0, starting transfers between devices: 11.6 us -> none  [per_device(): lax.all_to_all(whitened, WIN_AXES, split_axis=1, concat_axis=0, tiled=True)]
    ppermute x11, waiting for transfers between devices: 15.4 us -> 11.7 us  [ring_gather(): lax.ppermute(value, axis_name, [(i, (i + shift) % size) for i in range(si...]
    another operation x1 -> x3, other arithmetic: 3.37 us -> 4.06 us
  transfers between devices with their start and end apart: 12 -> 14, of which waited for: 4 -> 5; matrix products, arithmetic and copies ran while one was open for 5% -> 5% of each run, Pallas kernels for 0% -> 0%
where the time goes in v7:
time: 91 us; the launch traced here: 90.7 us
  starting transfers between devices  35.6 us (39%)
  matrix products  18 us (20%)
  local copies, waits for them, and re-layouts  16.2 us (18%)
  waiting for transfers between devices  11.7 us (13%)
  other arithmetic  8.43 us (9%)
    ppermute x11, starting transfers between devices, ring_gather(): lax.ppermute(value, axis_name, [(i, (i + shift) % size) for i in range(si...  21.5 us
    ppermute x3, starting transfers between devices, exchange_receivers(): lax.ppermute(block, WIN_AXES, [(i, (i + shift) % count) for i in range(co...  14.1 us
    ppermute x11, waiting for transfers between devices, ring_gather(): lax.ppermute(value, axis_name, [(i, (i + shift) % size) for i in range(si...  11.7 us
    dot_general x1, matrix products, transform(): jnp.dot(lhs, weights, preferred_element_type=jnp.float32) * lag_scale  10.6 us
    reshape x1, local copies, waits for them, and re-layouts, transform(): return result.reshape(-1, count_rec, 2 * MAXLAG)  9.75 us
    dot_general x1, matrix products, whiten(): jnp.dot(row_data, band_table(), preferred_element_type=jnp.float32)  7.35 us
    another operation x3, other arithmetic  4.06 us
    reduce_sum x1, other arithmetic, cross_lhs(): jnp.sum(src[..., 0, :] * rec[..., 0, :] + src[..., 1, :] * rec[..., 1, :]...  3.15 us
  transfers between devices with their start and end apart: 14, of which 5 were waited for; matrix products, arithmetic and copies ran while one was open for 5% of the time, Pallas kernels for 0%

profile of v7, /device:TPU:1, one launch (start us, length us, event | category | flops | bytes accessed | tf_op | source)
XLA Modules:
  0.0 90.7 jit_solution(10015924366130603834)
XLA Ops:
  0.0 0.0 copy-start
  0.0 0.9 %copy-done = bf16[1,16,7680]{2,1,0:T(8,128)(2,1)S(1)} copy-done((bf16[1,16,7680]{2,1,0:T(8,128)(2,1)S(1)}, bf16[1,16,7680]{2,1,0:T(8,128)(2,1)}, u32[]{:S(2)}) %copy-start) | copy-done | bytes 245784
  0.9 0.0 copy-start.5
  0.9 0.0 copy-start.1
  0.9 0.0 copy-start.2
  1.0 0.0 copy-start.3
  1.0 0.0 copy-start.4
  1.0 7.4 %convolution_bitcast_fusion = f32[16,1152]{1,0:T(8,128)S(1)} fusion(bf16[7680,1152]{1,0:T(8,128)(2,1)} %constant.248.clone, bf16[1,16,7680]{2,1,0:T(8,128)(2,1)S(1)} %copy-done), kind=kOutput, calls=%fused_computation.9 | convolution fusion | flops 283115520 | bytes 18014208 | tf_op jit(solution)/shard_map/dot_general | solution.py:63
  8.3 0.1 fusion.5
  8.4 0.6 fusion.6
  9.1 0.1 fusion.9
  9.2 3.3 %collective-permute-start.13 = (bf16[4,2,512]{2,0,1:T(4,128)(2,1)S(1)}, bf16[4,2,512]{2,0,1:T(4,128)(2,1)S(1)}, u32[]{:S(2)}, u32[]{:S(2)}) collective-permute-start(bf16[4,2,512]{2,0,1:T(4,128)(2,1)S(1)} %get-tuple-element.15), channel_id=1, source_target_pairs={{0,3},{1,0},{2,1},{3,2},{4,7},{5,4},{6,5},{7,6},{8,11},{9,8},{10,9... | collective-permute-start | bytes 24584 | tf_op jit(solution)/shard_map/ppermute | solution.py:113
  12.5 5.1 %collective-permute-start.11 = (bf16[4,2,512]{2,0,1:T(4,128)(2,1)S(1)}, bf16[4,2,512]{2,0,1:T(4,128)(2,1)S(1)}, u32[]{:S(2)}, u32[]{:S(2)}) collective-permute-start(bf16[4,2,512]{2,0,1:T(4,128)(2,1)S(1)} %get-tuple-element.16), channel_id=1, source_target_pairs={{0,1},{1,2},{2,3},{3,0},{4,5},{5,6},{6,7},{7,4},{8,9},{9,10},{10,1... | collective-permute-start | bytes 24584 | tf_op jit(solution)/shard_map/ppermute | solution.py:113
  17.6 0.0 copy-done.5
  17.6 0.1 fusion.16
  17.7 0.1 compare_and_fusion
  17.9 0.6 gather_fusion
  18.4 0.1 broadcast_select_fusion
  18.5 5.1 %collective-permute-start = (bf16[1,4,2,512]{3,2,1,0:T(2,128)(2,1)S(1)}, bf16[1,4,2,512]{3,2,1,0:T(2,128)(2,1)S(1)}, u32[]{:S(2)}, u32[]{:S(2)}) collective-permute-start(bf16[1,4,2,512]{3,2,1,0:T(2,128)(2,1)S(1)} %broadcast_select_fusion), channel_id=1, source_target_pairs={{0,2},{2,0},{1,3},{3,1},{4,6},{6,4},{5,7},{7,5},{8,10},{10,8},{9,1... | collective-permute-start | bytes 24584 | tf_op jit(solution)/shard_map/ppermute | solution.py:88
  23.8 1.2 %collective-permute-done = bf16[1,4,2,512]{3,2,1,0:T(2,128)(2,1)S(1)} collective-permute-done((bf16[1,4,2,512]{3,2,1,0:T(2,128)(2,1)S(1)}, bf16[1,4,2,512]{3,2,1,0:T(2,128)(2,1)S(1)}, u32[]{:S(2)}, u32[]{:S(2)}) %collective-permute-start) | collective-permute-done | bytes 8224 | tf_op jit(solution)/shard_map/ppermute | solution.py:88
  25.0 2.5 %collective-permute-start.3 = (bf16[2,4,2,512]{3,1,0,2:T(4,128)(2,1)S(1)}, bf16[2,4,2,512]{3,1,0,2:T(4,128)(2,1)S(1)}, u32[]{:S(2)}, u32[]{:S(2)}) collective-permute-start(bf16[2,4,2,512]{3,1,0,2:T(4,128)(2,1)S(1)} %copy_dynamic-update-slice_fusion), channel_id=1, source_target_pairs={{0,12},{4,0},{8,4},{12,8},{1,13},{5,1},{9,5},{13,9},{2,14},{6,2},{... | collective-permute-start | bytes 49160 | tf_op jit(solution)/shard_map/ppermute | solution.py:88
  27.6 0.5 collective-permute-start.2
  28.1 0.6 collective-permute-start.1
  28.7 3.2 %collective-permute-done.1 = bf16[2,4,2,512]{3,1,0,2:T(4,128)(2,1)S(1)} collective-permute-done((bf16[2,4,2,512]{3,1,0,2:T(4,128)(2,1)S(1)}, bf16[2,4,2,512]{3,1,0,2:T(4,128)(2,1)S(1)}, u32[]{:S(2)}, u32[]{:S(2)}) %collective-permute-start.1) | collective-permute-done | bytes 16416 | tf_op jit(solution)/shard_map/ppermute | solution.py:88
  31.9 0.0 collective-permute-done.2
  32.0 0.0 collective-permute-done.3
  32.0 2.5 %collective-permute-start.6 = (bf16[2,16,2,512]{3,1,0,2:T(8,128)(2,1)S(1)}, bf16[2,16,2,512]{3,1,0,2:T(8,128)(2,1)S(1)}, u32[]{:S(2)}, u32[]{:S(2)}) collective-permute-start(bf16[2,16,2,512]{3,1,0,2:T(8,128)(2,1)S(1)} %constant_dynamic-update-slice_fusion.8), channel_id=1, source_target_pairs={{0,48},{16,0},{32,16},{48,32},{1,49},{17,1},{33,17},{49,33},{2,50}... | collective-permute-start | bytes 196616 | tf_op jit(solution)/shard_map/ppermute | solution.py:88
  34.5 0.0 collective-permute-start.5
  34.5 0.4 collective-permute-start.4
  35.0 5.0 %collective-permute-done.4 = bf16[2,16,2,512]{3,1,0,2:T(8,128)(2,1)S(1)} collective-permute-done((bf16[2,16,2,512]{3,1,0,2:T(8,128)(2,1)S(1)}, bf16[2,16,2,512]{3,1,0,2:T(8,128)(2,1)S(1)}, u32[]{:S(2)}, u32[]{:S(2)}) %collective-permute-start.4) | collective-permute-done | bytes 65568 | tf_op jit(solution)/shard_map/ppermute | solution.py:88
  40.0 0.0 collective-permute-done.5
  40.0 0.0 collective-permute-done.6
  40.0 1.4 %collective-permute-start.7 = (bf16[2,64,2,512]{3,1,0,2:T(8,128)(2,1)S(1)}, bf16[2,64,2,512]{3,1,0,2:T(8,128)(2,1)S(1)}, u32[]{:S(2)}, u32[]{:S(2)}) collective-permute-start(bf16[2,64,2,512]{3,1,0,2:T(8,128)(2,1)S(1)} %constant_dynamic-update-slice_fusion.4), channel_id=1, source_target_pairs={{0,64},{64,128},{128,192},{192,0},{1,65},{65,129},{129,193},{193,1... | collective-permute-start | bytes 786440 | tf_op jit(solution)/shard_map/ppermute | solution.py:88
  41.4 0.0 copy-done.1
  41.4 0.0 copy-done.2
  41.4 0.0 copy-done.3
  41.4 0.0 copy-done.4
  41.4 3.4 %subtract_convert_fusion = (bf16[512,32,64]{0,2,1:T(8,128)(2,1)}, bf16[512,32,64]{0,2,1:T(8,128)(2,1)}) fusion(f32[512,64]{0,1:T(8,128)S(1)} %copy-done.1, f32[512,32]{0,1:T(8,128)S(1)} %copy-done.3, f32[512,64]{0,1:T(8,128)S(1)} %copy-done.2, f32[512,32]{0,1:T(8,128)S(1)} %copy-done.4), kind=kLoop, calls=%fused_computation.8 | loop fusion | flops 9437184 | bytes 4587520 | tf_op jit(solution)/shard_map/convert.5
  44.8 2.6 %collective-permute-start.8 = (bf16[2,64,2,512]{3,1,0,2:T(8,128)(2,1)S(1)}, bf16[2,64,2,512]{3,1,0,2:T(8,128)(2,1)S(1)}, u32[]{:S(2)}, u32[]{:S(2)}) collective-permute-start(bf16[2,64,2,512]{3,1,0,2:T(8,128)(2,1)S(1)} %constant_dynamic-update-slice_fusion.4), channel_id=1, source_target_pairs={{0,128},{64,192},{128,0},{192,64},{1,129},{65,193},{129,1},{193,65... | collective-permute-start | bytes 786440 | tf_op jit(solution)/shard_map/ppermute | solution.py:88
  47.7 1.3 %collective-permute-start.9 = (bf16[2,64,2,512]{3,1,0,2:T(8,128)(2,1)S(1)}, bf16[2,64,2,512]{3,1,0,2:T(8,128)(2,1)S(1)}, u32[]{:S(2)}, u32[]{:S(2)}) collective-permute-start(bf16[2,64,2,512]{3,1,0,2:T(8,128)(2,1)S(1)} %constant_dynamic-update-slice_fusion.4), channel_id=1, source_target_pairs={{0,192},{64,0},{128,64},{192,128},{1,193},{65,1},{129,65},{193,129... | collective-permute-start | bytes 786440 | tf_op jit(solution)/shard_map/ppermute | solution.py:88
  49.0 0.1 broadcast_in_dim.61
  49.1 0.0 collective-permute-done.7
  49.1 5.7 %collective-permute-start.12 = (bf16[4,2,512]{2,0,1:T(4,128)(2,1)S(1)}, bf16[4,2,512]{2,0,1:T(4,128)(2,1)S(1)}, u32[]{:S(2)}, u32[]{:S(2)}) collective-permute-start(bf16[4,2,512]{2,0,1:T(4,128)(2,1)S(1)} %get-tuple-element.17), channel_id=1, source_target_pairs={{0,2},{1,3},{2,0},{3,1},{4,6},{5,7},{6,4},{7,5},{8,10},{9,11},{10,... | collective-permute-start | bytes 24584 | tf_op jit(solution)/shard_map/ppermute | solution.py:113
  54.8 0.0 collective-permute-done.8
  54.9 0.4 collective-permute-done.9
  55.3 4.5 %collective-permute-start.10 = (bf16[2,256,2,512]{3,1,0,2:T(8,128)(2,1)S(1)}, bf16[2,256,2,512]{3,1,0,2:T(8,128)(2,1)S(1)}, u32[]{:S(2)}, u32[]{:S(2)}) collective-permute-start(bf16[2,256,2,512]{3,1,0,2:T(8,128)(2,1)S(1)} %constant_dynamic-update-slice_fusion), channel_id=1, source_target_pairs={{0,1},{1,0},{2,3},{3,2},{4,5},{5,4},{6,7},{7,6},{8,9},{9,8},{10,11... | collective-permute-start | bytes 3145736 | tf_op jit(solution)/shard_map/ppermute | solution.py:88
  59.9 0.0 collective-permute-done.11
  59.9 0.0 collective-permute-done.12
  59.9 0.0 collective-permute-done.13
  60.0 0.2 broadcast_in_dim.60
  60.1 0.1 bitcast_dynamic-update-slice_fusion.1
  60.2 1.9 %collective-permute-done.10 = bf16[2,256,2,512]{3,1,0,2:T(8,128)(2,1)S(1)} collective-permute-done((bf16[2,256,2,512]{3,1,0,2:T(8,128)(2,1)S(1)}, bf16[2,256,2,512]{3,1,0,2:T(8,128)(2,1)S(1)}, u32[]{:S(2)}, u32[]{:S(2)}) %collective-permute-start.10) | collective-permute-done | bytes 1048608 | tf_op jit(solution)/shard_map/ppermute | solution.py:88
  62.1 0.1 bitcast_dynamic-update-slice_fusion
  62.2 0.6 broadcast_in_dim.69
  62.8 0.4 slice_bitcast_fusion.1
  63.3 3.2 %add_reduce_fusion = (bf16[256,4,512]{2,0,1:T(8,128)(2,1)S(1)}, bf16[256,4,512]{2,0,1:T(8,128)(2,1)S(1)}) fusion(f32[4,4,512]{2,1,0:T(4,128)S(1)} %get-tuple-element.14, f32[4,256,512]{2,1,0:T(8,128)S(1)} %get-tuple-element.10, f32[4,4,512]{2,1,0:T(4,128)S(1)} %get-tuple-element.13, f32[4,256,512]{2,1,0:T(8,128)S(1)} %get-tuple-element.9), kind=kLoop, calls=%fused_computation.2 | loop fusion | flops 15728640 | bytes 6356992 | tf_op jit(solution)/shard_map/reduce_sum | solution.py:69
  66.4 0.3 pad_maximum_fusion
  66.7 1.6 %copy.15 = bf16[256,4,1024]{2,1,0:T(4,128)(2,1)S(1)} copy(bf16[256,4,1024]{2,0,1:T(8,128)(2,1)S(1)} %pad_maximum_fusion) | data formatting | bytes 4194304 | tf_op jit(solution)/shard_map/concatenate | solution.py:71
  68.3 2.0 %convert_element_type.16 = bf16[1024,1024]{1,0:T(8,128)(2,1)} reshape(bf16[256,4,1024]{2,1,0:T(4,128)(2,1)S(1)} %copy.15) | data formatting | bytes 4194304 | tf_op jit(solution)/shard_map/convert_element_type | solution.py:72
  70.3 10.6 %convolution_multiply_fusion = f32[1024,2048]{1,0:T(8,128)} fusion(bf16[1024,1024]{1,0:T(8,128)(2,1)} %convert_element_type.16, bf16[512,2048]{0,1:T(8,128)(2,1)} %bitcast.46, bf16[512,2048]{0,1:T(8,128)(2,1)} %bitcast.45), kind=kOutput, calls=%fused_computation.3 | convolution fusion | flops 4305453056 | bytes 14680064 | tf_op jit(solution)/shard_map/dot_general | solution.py:76
  81.0 9.7 %reshape.130 = f32[256,4,2048]{2,1,0:T(4,128)} reshape(f32[1024,2048]{1,0:T(8,128)} %convolution_multiply_fusion) | data formatting | bytes 16777216 | tf_op jit(solution)/shard_map/reshape | solution.py:77
  (28 shorter events, 0.4 us)
Async XLA Ops:
  0.0 0.9 %copy-start = (bf16[1,16,7680]{2,1,0:T(8,128)(2,1)S(1)}, bf16[1,16,7680]{2,1,0:T(8,128)(2,1)}, u32[]{:S(2)}) copy-start(bf16[1,16,7680]{2,1,0:T(8,128)(2,1)} %param.7) | copy-start | bytes 737284
  0.9 16.7 %copy-start.5 = (s32[1,256]{1,0:T(1,128)S(1)}, s32[1,256]{1,0:T(1,128)}, u32[]{:S(2)}) copy-start(s32[1,256]{1,0:T(1,128)} %param.8) | copy-start | bytes 3076
  0.9 40.4 %copy-start.1 = (f32[512,64]{0,1:T(8,128)S(1)}, f32[512,64]{0,1:T(8,128)}, u32[]{:S(2)}) copy-start(f32[512,64]{0,1:T(8,128)} %constant.252.clone) | copy-start | bytes 393220
  0.9 40.4 %copy-start.2 = (f32[512,64]{0,1:T(8,128)S(1)}, f32[512,64]{0,1:T(8,128)}, u32[]{:S(2)}) copy-start(f32[512,64]{0,1:T(8,128)} %constant.251.clone) | copy-start | bytes 393220
  1.0 40.4 %copy-start.3 = (f32[512,32]{0,1:T(8,128)S(1)}, f32[512,32]{0,1:T(8,128)}, u32[]{:S(2)}) copy-start(f32[512,32]{0,1:T(8,128)} %constant.250.clone) | copy-start | bytes 196612
  1.0 40.4 %copy-start.4 = (f32[512,32]{0,1:T(8,128)S(1)}, f32[512,32]{0,1:T(8,128)}, u32[]{:S(2)}) copy-start(f32[512,32]{0,1:T(8,128)} %constant.249.clone) | copy-start | bytes 196612
  9.2 50.7 %collective-permute-start.13 = (bf16[4,2,512]{2,0,1:T(4,128)(2,1)S(1)}, bf16[4,2,512]{2,0,1:T(4,128)(2,1)S(1)}, u32[]{:S(2)}, u32[]{:S(2)}) collective-permute-start(bf16[4,2,512]{2,0,1:T(4,128)(2,1)S(1)} %get-tuple-element.15), channel_id=1, source_target_pairs={{0,3},{1,0},{2,1},{3,2},{4,7},{5,4},{6,5},{7,6},{8,11},{9,8},{10,9... | collective-permute-start | bytes 24584 | tf_op jit(solution)/shard_map/ppermute | solution.py:113
  12.5 47.4 %collective-permute-start.11 = (bf16[4,2,512]{2,0,1:T(4,128)(2,1)S(1)}, bf16[4,2,512]{2,0,1:T(4,128)(2,1)S(1)}, u32[]{:S(2)}, u32[]{:S(2)}) collective-permute-start(bf16[4,2,512]{2,0,1:T(4,128)(2,1)S(1)} %get-tuple-element.16), channel_id=1, source_target_pairs={{0,1},{1,2},{2,3},{3,0},{4,5},{5,6},{6,7},{7,4},{8,9},{9,10},{10,1... | collective-permute-start | bytes 24584 | tf_op jit(solution)/shard_map/ppermute | solution.py:113
  18.5 6.5 %collective-permute-start = (bf16[1,4,2,512]{3,2,1,0:T(2,128)(2,1)S(1)}, bf16[1,4,2,512]{3,2,1,0:T(2,128)(2,1)S(1)}, u32[]{:S(2)}, u32[]{:S(2)}) collective-permute-start(bf16[1,4,2,512]{3,2,1,0:T(2,128)(2,1)S(1)} %broadcast_select_fusion), channel_id=1, source_target_pairs={{0,2},{2,0},{1,3},{3,1},{4,6},{6,4},{5,7},{7,5},{8,10},{10,8},{9,1... | collective-permute-start | bytes 24584 | tf_op jit(solution)/shard_map/ppermute | solution.py:88
  25.0 6.9 %collective-permute-start.3 = (bf16[2,4,2,512]{3,1,0,2:T(4,128)(2,1)S(1)}, bf16[2,4,2,512]{3,1,0,2:T(4,128)(2,1)S(1)}, u32[]{:S(2)}, u32[]{:S(2)}) collective-permute-start(bf16[2,4,2,512]{3,1,0,2:T(4,128)(2,1)S(1)} %copy_dynamic-update-slice_fusion), channel_id=1, source_target_pairs={{0,12},{4,0},{8,4},{12,8},{1,13},{5,1},{9,5},{13,9},{2,14},{6,2},{... | collective-permute-start | bytes 49160 | tf_op jit(solution)/shard_map/ppermute | solution.py:88
  27.6 4.3 %collective-permute-start.2 = (bf16[2,4,2,512]{3,1,0,2:T(4,128)(2,1)S(1)}, bf16[2,4,2,512]{3,1,0,2:T(4,128)(2,1)S(1)}, u32[]{:S(2)}, u32[]{:S(2)}) collective-permute-start(bf16[2,4,2,512]{3,1,0,2:T(4,128)(2,1)S(1)} %copy_dynamic-update-slice_fusion), channel_id=1, source_target_pairs={{0,8},{4,12},{8,0},{12,4},{1,9},{5,13},{9,1},{13,5},{2,10},{6,14},... | collective-permute-start | bytes 49160 | tf_op jit(solution)/shard_map/ppermute | solution.py:88
  28.1 3.8 %collective-permute-start.1 = (bf16[2,4,2,512]{3,1,0,2:T(4,128)(2,1)S(1)}, bf16[2,4,2,512]{3,1,0,2:T(4,128)(2,1)S(1)}, u32[]{:S(2)}, u32[]{:S(2)}) collective-permute-start(bf16[2,4,2,512]{3,1,0,2:T(4,128)(2,1)S(1)} %copy_dynamic-update-slice_fusion), channel_id=1, source_target_pairs={{0,4},{4,8},{8,12},{12,0},{1,5},{5,9},{9,13},{13,1},{2,6},{6,10},{... | collective-permute-start | bytes 49160 | tf_op jit(solution)/shard_map/ppermute | solution.py:88
  32.0 8.0 %collective-permute-start.6 = (bf16[2,16,2,512]{3,1,0,2:T(8,128)(2,1)S(1)}, bf16[2,16,2,512]{3,1,0,2:T(8,128)(2,1)S(1)}, u32[]{:S(2)}, u32[]{:S(2)}) collective-permute-start(bf16[2,16,2,512]{3,1,0,2:T(8,128)(2,1)S(1)} %constant_dynamic-update-slice_fusion.8), channel_id=1, source_target_pairs={{0,48},{16,0},{32,16},{48,32},{1,49},{17,1},{33,17},{49,33},{2,50}... | collective-permute-start | bytes 196616 | tf_op jit(solution)/shard_map/ppermute | solution.py:88
  34.5 5.4 %collective-permute-start.5 = (bf16[2,16,2,512]{3,1,0,2:T(8,128)(2,1)S(1)}, bf16[2,16,2,512]{3,1,0,2:T(8,128)(2,1)S(1)}, u32[]{:S(2)}, u32[]{:S(2)}) collective-permute-start(bf16[2,16,2,512]{3,1,0,2:T(8,128)(2,1)S(1)} %constant_dynamic-update-slice_fusion.8), channel_id=1, source_target_pairs={{0,32},{16,48},{32,0},{48,16},{1,33},{17,49},{33,1},{49,17},{2,34}... | collective-permute-start | bytes 196616 | tf_op jit(solution)/shard_map/ppermute | solution.py:88
  34.5 5.4 %collective-permute-start.4 = (bf16[2,16,2,512]{3,1,0,2:T(8,128)(2,1)S(1)}, bf16[2,16,2,512]{3,1,0,2:T(8,128)(2,1)S(1)}, u32[]{:S(2)}, u32[]{:S(2)}) collective-permute-start(bf16[2,16,2,512]{3,1,0,2:T(8,128)(2,1)S(1)} %constant_dynamic-update-slice_fusion.8), channel_id=1, source_target_pairs={{0,16},{16,32},{32,48},{48,0},{1,17},{17,33},{33,49},{49,1},{2,18}... | collective-permute-start | bytes 196616 | tf_op jit(solution)/shard_map/ppermute | solution.py:88
  40.0 9.1 %collective-permute-start.7 = (bf16[2,64,2,512]{3,1,0,2:T(8,128)(2,1)S(1)}, bf16[2,64,2,512]{3,1,0,2:T(8,128)(2,1)S(1)}, u32[]{:S(2)}, u32[]{:S(2)}) collective-permute-start(bf16[2,64,2,512]{3,1,0,2:T(8,128)(2,1)S(1)} %constant_dynamic-update-slice_fusion.4), channel_id=1, source_target_pairs={{0,64},{64,128},{128,192},{192,0},{1,65},{65,129},{129,193},{193,1... | collective-permute-start | bytes 786440 | tf_op jit(solution)/shard_map/ppermute | solution.py:88
  44.8 10.1 %collective-permute-start.8 = (bf16[2,64,2,512]{3,1,0,2:T(8,128)(2,1)S(1)}, bf16[2,64,2,512]{3,1,0,2:T(8,128)(2,1)S(1)}, u32[]{:S(2)}, u32[]{:S(2)}) collective-permute-start(bf16[2,64,2,512]{3,1,0,2:T(8,128)(2,1)S(1)} %constant_dynamic-update-slice_fusion.4), channel_id=1, source_target_pairs={{0,128},{64,192},{128,0},{192,64},{1,129},{65,193},{129,1},{193,65... | collective-permute-start | bytes 786440 | tf_op jit(solution)/shard_map/ppermute | solution.py:88
  47.7 7.6 %collective-permute-start.9 = (bf16[2,64,2,512]{3,1,0,2:T(8,128)(2,1)S(1)}, bf16[2,64,2,512]{3,1,0,2:T(8,128)(2,1)S(1)}, u32[]{:S(2)}, u32[]{:S(2)}) collective-permute-start(bf16[2,64,2,512]{3,1,0,2:T(8,128)(2,1)S(1)} %constant_dynamic-update-slice_fusion.4), channel_id=1, source_target_pairs={{0,192},{64,0},{128,64},{192,128},{1,193},{65,1},{129,65},{193,129... | collective-permute-start | bytes 786440 | tf_op jit(solution)/shard_map/ppermute | solution.py:88
  49.1 10.7 %collective-permute-start.12 = (bf16[4,2,512]{2,0,1:T(4,128)(2,1)S(1)}, bf16[4,2,512]{2,0,1:T(4,128)(2,1)S(1)}, u32[]{:S(2)}, u32[]{:S(2)}) collective-permute-start(bf16[4,2,512]{2,0,1:T(4,128)(2,1)S(1)} %get-tuple-element.17), channel_id=1, source_target_pairs={{0,2},{1,3},{2,0},{3,1},{4,6},{5,7},{6,4},{7,5},{8,10},{9,11},{10,... | collective-permute-start | bytes 24584 | tf_op jit(solution)/shard_map/ppermute | solution.py:113
  55.3 6.8 %collective-permute-start.10 = (bf16[2,256,2,512]{3,1,0,2:T(8,128)(2,1)S(1)}, bf16[2,256,2,512]{3,1,0,2:T(8,128)(2,1)S(1)}, u32[]{:S(2)}, u32[]{:S(2)}) collective-permute-start(bf16[2,256,2,512]{3,1,0,2:T(8,128)(2,1)S(1)} %constant_dynamic-update-slice_fusion), channel_id=1, source_target_pairs={{0,1},{1,0},{2,3},{3,2},{4,5},{5,4},{6,7},{7,6},{8,9},{9,8},{10,11... | collective-permute-start | bytes 3145736 | tf_op jit(solution)/shard_map/ppermute | solution.py:88

commit v8 on v7

--- a/solution.py
+++ b/solution.py
@@ -1,3 +1,4 @@
+import functools
 import math
 
 import ml_dtypes
@@ -6,6 +7,7 @@
 import jax
 import jax.numpy as jnp
 from jax import lax
+from jax.experimental import pallas as pl
 from jax.sharding import Mesh, PartitionSpec as P
 
 S = 7680
@@ -72,9 +74,27 @@
     return lhs.astype(jnp.bfloat16)
 
 
+SOURCE_BLOCK = 32
+
+
+def lag_kernel(lhs_ref, w_ref, o_ref, *, scale):
+    result = jnp.dot(lhs_ref[...], w_ref[...], preferred_element_type=jnp.float32) * scale
+    o_ref[...] = result.reshape(o_ref.shape)
+
+
 def transform(lhs, weights, lag_scale, count_rec):
-    result = jnp.dot(lhs, weights, preferred_element_type=jnp.float32) * lag_scale
-    return result.reshape(-1, count_rec, 2 * MAXLAG)
+    count_src = lhs.shape[0] // count_rec
+    rows = SOURCE_BLOCK * count_rec
+    return pl.pallas_call(
+        functools.partial(lag_kernel, scale=lag_scale),
+        out_shape=jax.ShapeDtypeStruct((count_src, count_rec, 2 * MAXLAG), jnp.float32),
+        grid=(count_src // SOURCE_BLOCK,),
+        in_specs=[
+            pl.BlockSpec((rows, lhs.shape[1]), lambda i: (i, 0)),
+            pl.BlockSpec(weights.shape, lambda i: (0, 0)),
+        ],
+        out_specs=pl.BlockSpec((SOURCE_BLOCK, count_rec, 2 * MAXLAG), lambda i: (i, 0, 0)),
+    )(lhs, weights)
 
 
 def ring_gather(value, axis_name, axis):

time: 91 us -> 90.4 us (level)
  Pallas kernels: 0 us -> 10.7 us
  matrix products: 18 us -> 7.35 us
  starting transfers between devices: 35.6 us -> 27.7 us
  waiting for transfers between devices: 11.7 us -> 18.3 us
  other arithmetic: 8.43 us -> 12.6 us
  local copies, waits for them, and re-layouts: 16.2 us -> 12.8 us
    pallas_call x0 -> x1, Pallas kernels: none -> 10.7 us  [transform(): pl.pallas_call(functools.partial(lag_kernel, scale=lag_scale), out_shape=...]
    dot_general x1 -> x0, matrix products: 10.6 us -> none  [transform(): jnp.dot(lhs, weights, preferred_element_type=jnp.float32) * lag_scale]
    reshape x1 -> x0, local copies, waits for them, and re-layouts: 9.75 us -> none  [transform(): return result.reshape(-1, count_rec, 2 * MAXLAG)]
    ppermute x11, waiting for transfers between devices: 11.7 us -> 18.3 us  [ring_gather(): lax.ppermute(value, axis_name, [(i, (i + shift) % size) for i in range(si...]
    concatenate x0 -> x1, other arithmetic: none -> 4.76 us  [lag_weights(): table = jnp.concatenate([cos, -sin], axis=0).astype(jnp.bfloat16)]
    ppermute x3, starting transfers between devices: 14.1 us -> 9.76 us  [exchange_receivers(): lax.ppermute(block, WIN_AXES, [(i, (i + shift) % count) for i in range(co...]
    sub x0 -> x1, local copies, waits for them, and re-layouts: none -> 3.99 us  [lag_weights(): cos = ca[:, :, None] * cb[:, None, :] - sa[:, :, None] * sb[:, None, :]]
    ppermute x11, starting transfers between devices: 21.5 us -> 17.9 us  [ring_gather(): lax.ppermute(value, axis_name, [(i, (i + shift) % size) for i in range(si...]
  transfers between devices with their start and end apart: 14 -> 14, of which waited for: 5 -> 6; matrix products, arithmetic and copies ran while one was open for 5% -> 17% of each run, Pallas kernels for 0% -> 0%
where the time goes in v8:
time: 90.4 us; the launch traced here: 90.1 us
  starting transfers between devices  27.7 us (31%)
  waiting for transfers between devices  18.3 us (20%)
  local copies, waits for them, and re-layouts  12.8 us (14%)
  other arithmetic  12.6 us (14%)
  Pallas kernels  10.7 us (12%)
  matrix products  7.35 us (8%)
    ppermute x11, waiting for transfers between devices, ring_gather(): lax.ppermute(value, axis_name, [(i, (i + shift) % size) for i in range(si...  18.3 us
    ppermute x11, starting transfers between devices, ring_gather(): lax.ppermute(value, axis_name, [(i, (i + shift) % size) for i in range(si...  17.9 us
    pallas_call x1, Pallas kernels, transform(): pl.pallas_call(functools.partial(lag_kernel, scale=lag_scale), out_shape=...  10.7 us
    ppermute x3, starting transfers between devices, exchange_receivers(): lax.ppermute(block, WIN_AXES, [(i, (i + shift) % count) for i in range(co...  9.76 us
    dot_general x1, matrix products, whiten(): jnp.dot(row_data, band_table(), preferred_element_type=jnp.float32)  7.35 us
    concatenate x1, other arithmetic, lag_weights(): table = jnp.concatenate([cos, -sin], axis=0).astype(jnp.bfloat16)  4.76 us
    sub x1, local copies, waits for them, and re-layouts, lag_weights(): cos = ca[:, :, None] * cb[:, None, :] - sa[:, :, None] * sb[:, None, :]  3.99 us
    another operation x3, other arithmetic  3.45 us
  transfers between devices with their start and end apart: 14, of which 6 were waited for; matrix products, arithmetic and copies ran while one was open for 17% of the time, Pallas kernels for 0%

profile of v8, /device:TPU:1, one launch (start us, length us, event | category | flops | bytes accessed | tf_op | source)
XLA Modules:
  0.0 90.1 jit_solution(14133500870232687838)
XLA Ops:
  0.0 0.0 copy-start
  0.0 0.9 %copy-done = bf16[1,16,7680]{2,1,0:T(8,128)(2,1)S(1)} copy-done((bf16[1,16,7680]{2,1,0:T(8,128)(2,1)S(1)}, bf16[1,16,7680]{2,1,0:T(8,128)(2,1)}, u32[]{:S(2)}) %copy-start) | copy-done | bytes 245784
  0.9 0.0 copy-start.5
  0.9 0.0 copy-start.1
  0.9 0.0 copy-start.2
  1.0 0.0 copy-start.3
  1.0 0.0 copy-start.4
  1.0 7.4 %convolution_bitcast_fusion = f32[16,1152]{1,0:T(8,128)S(1)} fusion(bf16[7680,1152]{1,0:T(8,128)(2,1)} %constant.246.clone, bf16[1,16,7680]{2,1,0:T(8,128)(2,1)S(1)} %copy-done), kind=kOutput, calls=%fused_computation.6 | convolution fusion | flops 283115520 | bytes 18014208 | tf_op jit(solution)/shard_map/dot_general | solution.py:65
  8.3 0.1 fusion.2
  8.4 0.6 fusion.3
  9.1 0.1 fusion.6
  9.2 3.3 %collective-permute-start.13 = (bf16[4,2,512]{2,0,1:T(4,128)(2,1)S(1)}, bf16[4,2,512]{2,0,1:T(4,128)(2,1)S(1)}, u32[]{:S(2)}, u32[]{:S(2)}) collective-permute-start(bf16[4,2,512]{2,0,1:T(4,128)(2,1)S(1)} %get-tuple-element.15), channel_id=1, source_target_pairs={{0,3},{1,0},{2,1},{3,2},{4,7},{5,4},{6,5},{7,6},{8,11},{9,8},{10,9... | collective-permute-start | bytes 24584 | tf_op jit(solution)/shard_map/ppermute | solution.py:133
  12.5 5.1 %collective-permute-start.11 = (bf16[4,2,512]{2,0,1:T(4,128)(2,1)S(1)}, bf16[4,2,512]{2,0,1:T(4,128)(2,1)S(1)}, u32[]{:S(2)}, u32[]{:S(2)}) collective-permute-start(bf16[4,2,512]{2,0,1:T(4,128)(2,1)S(1)} %get-tuple-element.16), channel_id=1, source_target_pairs={{0,1},{1,2},{2,3},{3,0},{4,5},{5,6},{6,7},{7,4},{8,9},{9,10},{10,1... | collective-permute-start | bytes 24584 | tf_op jit(solution)/shard_map/ppermute | solution.py:133
  17.6 0.0 copy-done.5
  17.6 0.1 fusion.13
  17.7 0.1 compare_and_fusion
  17.9 0.6 gather_fusion
  18.4 0.1 broadcast_select_fusion
  18.5 5.1 %collective-permute-start = (bf16[1,4,2,512]{3,2,1,0:T(2,128)(2,1)S(1)}, bf16[1,4,2,512]{3,2,1,0:T(2,128)(2,1)S(1)}, u32[]{:S(2)}, u32[]{:S(2)}) collective-permute-start(bf16[1,4,2,512]{3,2,1,0:T(2,128)(2,1)S(1)} %broadcast_select_fusion), channel_id=1, source_target_pairs={{0,2},{2,0},{1,3},{3,1},{4,6},{6,4},{5,7},{7,5},{8,10},{10,8},{9,1... | collective-permute-start | bytes 24584 | tf_op jit(solution)/shard_map/ppermute | solution.py:108
  23.6 0.0 copy-done.1
  23.6 0.0 copy-done.2
  23.6 0.0 copy-done.3
  23.6 0.0 copy-done.4
  23.6 2.7 %subtract_convert_fusion = (bf16[512,32,64]{0,2,1:T(8,128)(2,1)}, bf16[512,32,64]{0,2,1:T(8,128)(2,1)S(1)}) fusion(f32[512,64]{0,1:T(8,128)S(1)} %copy-done.1, f32[512,32]{0,1:T(8,128)S(1)} %copy-done.3, f32[512,64]{0,1:T(8,128)S(1)} %copy-done.2, f32[512,32]{0,1:T(8,128)S(1)} %copy-done.4), kind=kLoop, calls=%fused_computation.5 | loop fusion | flops 9437184 | bytes 4587520 | tf_op jit(solution)/shard_map/convert.5
  26.6 4.0 %copy.15 = bf16[512,2048]{1,0:T(8,128)(2,1)} copy(bf16[512,2048]{0,1:T(8,128)(2,1)} %bitcast.45) | data formatting | bytes 4194304 | tf_op jit(solution)/shard_map/sub | solution.py:44
  30.5 2.4 %copy.16 = bf16[512,2048]{1,0:T(8,128)(2,1)} copy(bf16[512,2048]{0,1:T(8,128)(2,1)S(1)} %bitcast.44) | data formatting | bytes 4194304 | tf_op jit(solution)/shard_map/neg | solution.py:46
  32.9 0.0 collective-permute-done
  32.9 2.6 %collective-permute-start.3 = (bf16[2,4,2,512]{3,1,0,2:T(4,128)(2,1)S(1)}, bf16[2,4,2,512]{3,1,0,2:T(4,128)(2,1)S(1)}, u32[]{:S(2)}, u32[]{:S(2)}) collective-permute-start(bf16[2,4,2,512]{3,1,0,2:T(4,128)(2,1)S(1)} %copy_dynamic-update-slice_fusion), channel_id=1, source_target_pairs={{0,12},{4,0},{8,4},{12,8},{1,13},{5,1},{9,5},{13,9},{2,14},{6,2},{... | collective-permute-start | bytes 49160 | tf_op jit(solution)/shard_map/ppermute | solution.py:108
  35.5 0.5 collective-permute-start.2
  36.0 0.6 collective-permute-start.1
  36.6 3.2 %collective-permute-done.1 = bf16[2,4,2,512]{3,1,0,2:T(4,128)(2,1)S(1)} collective-permute-done((bf16[2,4,2,512]{3,1,0,2:T(4,128)(2,1)S(1)}, bf16[2,4,2,512]{3,1,0,2:T(4,128)(2,1)S(1)}, u32[]{:S(2)}, u32[]{:S(2)}) %collective-permute-start.1) | collective-permute-done | bytes 16416 | tf_op jit(solution)/shard_map/ppermute | solution.py:108
  39.8 0.0 collective-permute-done.2
  39.9 0.0 collective-permute-done.3
  39.9 1.7 %collective-permute-start.6 = (bf16[2,16,2,512]{3,1,0,2:T(8,128)(2,1)S(1)}, bf16[2,16,2,512]{3,1,0,2:T(8,128)(2,1)S(1)}, u32[]{:S(2)}, u32[]{:S(2)}) collective-permute-start(bf16[2,16,2,512]{3,1,0,2:T(8,128)(2,1)S(1)} %constant_dynamic-update-slice_fusion.8), channel_id=1, source_target_pairs={{0,48},{16,0},{32,16},{48,32},{1,49},{17,1},{33,17},{49,33},{2,50}... | collective-permute-start | bytes 196616 | tf_op jit(solution)/shard_map/ppermute | solution.py:108
  41.6 0.3 collective-permute-start.5
  41.9 0.7 collective-permute-start.4
  42.7 4.1 %collective-permute-done.4 = bf16[2,16,2,512]{3,1,0,2:T(8,128)(2,1)S(1)} collective-permute-done((bf16[2,16,2,512]{3,1,0,2:T(8,128)(2,1)S(1)}, bf16[2,16,2,512]{3,1,0,2:T(8,128)(2,1)S(1)}, u32[]{:S(2)}, u32[]{:S(2)}) %collective-permute-start.4) | collective-permute-done | bytes 65568 | tf_op jit(solution)/shard_map/ppermute | solution.py:108
  46.8 0.8 collective-permute-done.5
  47.7 0.0 collective-permute-done.6
  47.7 1.4 %collective-permute-start.7 = (bf16[2,64,2,512]{3,1,0,2:T(8,128)(2,1)S(1)}, bf16[2,64,2,512]{3,1,0,2:T(8,128)(2,1)S(1)}, u32[]{:S(2)}, u32[]{:S(2)}) collective-permute-start(bf16[2,64,2,512]{3,1,0,2:T(8,128)(2,1)S(1)} %constant_dynamic-update-slice_fusion.4), channel_id=1, source_target_pairs={{0,64},{64,128},{128,192},{192,0},{1,65},{65,129},{129,193},{193,1... | collective-permute-start | bytes 786440 | tf_op jit(solution)/shard_map/ppermute | solution.py:108
  49.1 4.8 %pad_maximum_fusion.w_ref = bf16[1024,2048]{1,0:T(8,128)(2,1)} fusion(bf16[512,2048]{1,0:T(8,128)(2,1)} %copy.16, bf16[512,2048]{1,0:T(8,128)(2,1)} %copy.15), kind=kLoop, calls=%fused_computation.3 | loop fusion | flops 8388608 | bytes 8388608 | tf_op jit(solution)/shard_map/concatenate | solution.py:46
  53.8 2.6 %collective-permute-start.8 = (bf16[2,64,2,512]{3,1,0,2:T(8,128)(2,1)S(1)}, bf16[2,64,2,512]{3,1,0,2:T(8,128)(2,1)S(1)}, u32[]{:S(2)}, u32[]{:S(2)}) collective-permute-start(bf16[2,64,2,512]{3,1,0,2:T(8,128)(2,1)S(1)} %constant_dynamic-update-slice_fusion.4), channel_id=1, source_target_pairs={{0,128},{64,192},{128,0},{192,64},{1,129},{65,193},{129,1},{193,65... | collective-permute-start | bytes 786440 | tf_op jit(solution)/shard_map/ppermute | solution.py:108
  56.7 1.1 %collective-permute-start.9 = (bf16[2,64,2,512]{3,1,0,2:T(8,128)(2,1)S(1)}, bf16[2,64,2,512]{3,1,0,2:T(8,128)(2,1)S(1)}, u32[]{:S(2)}, u32[]{:S(2)}) collective-permute-start(bf16[2,64,2,512]{3,1,0,2:T(8,128)(2,1)S(1)} %constant_dynamic-update-slice_fusion.4), channel_id=1, source_target_pairs={{0,192},{64,0},{128,64},{192,128},{1,193},{65,1},{129,65},{193,129... | collective-permute-start | bytes 786440 | tf_op jit(solution)/shard_map/ppermute | solution.py:108
  57.9 0.1 broadcast_in_dim.61
  58.0 0.0 collective-permute-done.7
  58.0 1.3 %collective-permute-start.12 = (bf16[4,2,512]{2,0,1:T(4,128)(2,1)S(1)}, bf16[4,2,512]{2,0,1:T(4,128)(2,1)S(1)}, u32[]{:S(2)}, u32[]{:S(2)}) collective-permute-start(bf16[4,2,512]{2,0,1:T(4,128)(2,1)S(1)} %get-tuple-element.17), channel_id=1, source_target_pairs={{0,2},{1,3},{2,0},{3,1},{4,6},{5,7},{6,4},{7,5},{8,10},{9,11},{10,... | collective-permute-start | bytes 24584 | tf_op jit(solution)/shard_map/ppermute | solution.py:133
  59.3 4.4 %collective-permute-done.8 = bf16[2,64,2,512]{3,1,0,2:T(8,128)(2,1)S(1)} collective-permute-done((bf16[2,64,2,512]{3,1,0,2:T(8,128)(2,1)S(1)}, bf16[2,64,2,512]{3,1,0,2:T(8,128)(2,1)S(1)}, u32[]{:S(2)}, u32[]{:S(2)}) %collective-permute-start.8) | collective-permute-done | bytes 262176 | tf_op jit(solution)/shard_map/ppermute | solution.py:108
  63.7 3.8 %collective-permute-done.9 = bf16[2,64,2,512]{3,1,0,2:T(8,128)(2,1)S(1)} collective-permute-done((bf16[2,64,2,512]{3,1,0,2:T(8,128)(2,1)S(1)}, bf16[2,64,2,512]{3,1,0,2:T(8,128)(2,1)S(1)}, u32[]{:S(2)}, u32[]{:S(2)}) %collective-permute-start.9) | collective-permute-done | bytes 262176 | tf_op jit(solution)/shard_map/ppermute | solution.py:108
  67.6 1.3 %collective-permute-start.10 = (bf16[2,256,2,512]{3,1,0,2:T(8,128)(2,1)S(1)}, bf16[2,256,2,512]{3,1,0,2:T(8,128)(2,1)S(1)}, u32[]{:S(2)}, u32[]{:S(2)}) collective-permute-start(bf16[2,256,2,512]{3,1,0,2:T(8,128)(2,1)S(1)} %constant_dynamic-update-slice_fusion), channel_id=1, source_target_pairs={{0,1},{1,0},{2,3},{3,2},{4,5},{5,4},{6,7},{7,6},{8,9},{9,8},{10,11... | collective-permute-start | bytes 3145736 | tf_op jit(solution)/shard_map/ppermute | solution.py:108
  68.9 0.0 collective-permute-done.11
  68.9 0.0 collective-permute-done.12
  68.9 0.0 collective-permute-done.13
  69.0 0.2 broadcast_in_dim.60
  69.2 0.1 bitcast_dynamic-update-slice_fusion.1
  69.3 1.9 %collective-permute-done.10 = bf16[2,256,2,512]{3,1,0,2:T(8,128)(2,1)S(1)} collective-permute-done((bf16[2,256,2,512]{3,1,0,2:T(8,128)(2,1)S(1)}, bf16[2,256,2,512]{3,1,0,2:T(8,128)(2,1)S(1)}, u32[]{:S(2)}, u32[]{:S(2)}) %collective-permute-start.10) | collective-permute-done | bytes 1048608 | tf_op jit(solution)/shard_map/ppermute | solution.py:108
  71.2 0.1 bitcast_dynamic-update-slice_fusion
  71.3 0.6 broadcast_in_dim.69
  71.8 0.4 slice_bitcast_fusion.1
  72.3 3.2 %add_reduce_fusion = (bf16[256,4,512]{2,0,1:T(8,128)(2,1)S(1)}, bf16[256,4,512]{2,0,1:T(8,128)(2,1)S(1)}) fusion(f32[4,4,512]{2,1,0:T(4,128)S(1)} %get-tuple-element.14, f32[4,256,512]{2,1,0:T(8,128)S(1)} %get-tuple-element.10, f32[4,4,512]{2,1,0:T(4,128)S(1)} %get-tuple-element.13, f32[4,256,512]{2,1,0:T(8,128)S(1)} %get-tuple-element.9), kind=kLoop, calls=%fused_computation.2 | loop fusion | flops 15728640 | bytes 6356992 | tf_op jit(solution)/shard_map/reduce_sum | solution.py:71
  75.5 0.3 pad_maximum_fusion.1
  75.7 1.6 %copy.14 = bf16[256,4,1024]{2,1,0:T(4,128)(2,1)S(1)} copy(bf16[256,4,1024]{2,0,1:T(8,128)(2,1)S(1)} %pad_maximum_fusion.1) | data formatting | bytes 4194304 | tf_op jit(solution)/shard_map/concatenate | solution.py:73
  77.3 2.1 %convert_element_type.15.lhs_ref = bf16[1024,1024]{1,0:T(8,128)(2,1)} reshape(bf16[256,4,1024]{2,1,0:T(4,128)(2,1)S(1)} %copy.14) | data formatting | bytes 4194304 | tf_op jit(solution)/shard_map/convert_element_type | solution.py:74
  79.4 10.7 %shard_map.73 = f32[256,4,2048]{2,1,0:T(4,128)} custom-call(bf16[1024,1024]{1,0:T(8,128)(2,1)} %convert_element_type.15.lhs_ref, bf16[1024,2048]{1,0:T(8,128)(2,1)} %pad_maximum_fusion.w_ref), custom_call_target="tpu_custom_call" | custom-call | tf_op jit(solution)/shard_map/pallas_call | solution.py:88
  (28 shorter events, 0.4 us)
Async XLA Ops:
  0.0 0.9 %copy-start = (bf16[1,16,7680]{2,1,0:T(8,128)(2,1)S(1)}, bf16[1,16,7680]{2,1,0:T(8,128)(2,1)}, u32[]{:S(2)}) copy-start(bf16[1,16,7680]{2,1,0:T(8,128)(2,1)} %param.7) | copy-start | bytes 737284
  0.9 16.7 %copy-start.5 = (s32[1,256]{1,0:T(1,128)S(1)}, s32[1,256]{1,0:T(1,128)}, u32[]{:S(2)}) copy-start(s32[1,256]{1,0:T(1,128)} %param.8) | copy-start | bytes 3076
  0.9 22.7 %copy-start.1 = (f32[512,64]{0,1:T(8,128)S(1)}, f32[512,64]{0,1:T(8,128)}, u32[]{:S(2)}) copy-start(f32[512,64]{0,1:T(8,128)} %constant.250.clone) | copy-start | bytes 393220
  0.9 22.7 %copy-start.2 = (f32[512,64]{0,1:T(8,128)S(1)}, f32[512,64]{0,1:T(8,128)}, u32[]{:S(2)}) copy-start(f32[512,64]{0,1:T(8,128)} %constant.249.clone) | copy-start | bytes 393220
  1.0 22.7 %copy-start.3 = (f32[512,32]{0,1:T(8,128)S(1)}, f32[512,32]{0,1:T(8,128)}, u32[]{:S(2)}) copy-start(f32[512,32]{0,1:T(8,128)} %constant.248.clone) | copy-start | bytes 196612
  1.0 22.7 %copy-start.4 = (f32[512,32]{0,1:T(8,128)S(1)}, f32[512,32]{0,1:T(8,128)}, u32[]{:S(2)}) copy-start(f32[512,32]{0,1:T(8,128)} %constant.247.clone) | copy-start | bytes 196612
  9.2 59.8 %collective-permute-start.13 = (bf16[4,2,512]{2,0,1:T(4,128)(2,1)S(1)}, bf16[4,2,512]{2,0,1:T(4,128)(2,1)S(1)}, u32[]{:S(2)}, u32[]{:S(2)}) collective-permute-start(bf16[4,2,512]{2,0,1:T(4,128)(2,1)S(1)} %get-tuple-element.15), channel_id=1, source_target_pairs={{0,3},{1,0},{2,1},{3,2},{4,7},{5,4},{6,5},{7,6},{8,11},{9,8},{10,9... | collective-permute-start | bytes 24584 | tf_op jit(solution)/shard_map/ppermute | solution.py:133
  12.5 56.4 %collective-permute-start.11 = (bf16[4,2,512]{2,0,1:T(4,128)(2,1)S(1)}, bf16[4,2,512]{2,0,1:T(4,128)(2,1)S(1)}, u32[]{:S(2)}, u32[]{:S(2)}) collective-permute-start(bf16[4,2,512]{2,0,1:T(4,128)(2,1)S(1)} %get-tuple-element.16), channel_id=1, source_target_pairs={{0,1},{1,2},{2,3},{3,0},{4,5},{5,6},{6,7},{7,4},{8,9},{9,10},{10,1... | collective-permute-start | bytes 24584 | tf_op jit(solution)/shard_map/ppermute | solution.py:133
  18.5 14.4 %collective-permute-start = (bf16[1,4,2,512]{3,2,1,0:T(2,128)(2,1)S(1)}, bf16[1,4,2,512]{3,2,1,0:T(2,128)(2,1)S(1)}, u32[]{:S(2)}, u32[]{:S(2)}) collective-permute-start(bf16[1,4,2,512]{3,2,1,0:T(2,128)(2,1)S(1)} %broadcast_select_fusion), channel_id=1, source_target_pairs={{0,2},{2,0},{1,3},{3,1},{4,6},{6,4},{5,7},{7,5},{8,10},{10,8},{9,1... | collective-permute-start | bytes 24584 | tf_op jit(solution)/shard_map/ppermute | solution.py:108
  32.9 6.9 %collective-permute-start.3 = (bf16[2,4,2,512]{3,1,0,2:T(4,128)(2,1)S(1)}, bf16[2,4,2,512]{3,1,0,2:T(4,128)(2,1)S(1)}, u32[]{:S(2)}, u32[]{:S(2)}) collective-permute-start(bf16[2,4,2,512]{3,1,0,2:T(4,128)(2,1)S(1)} %copy_dynamic-update-slice_fusion), channel_id=1, source_target_pairs={{0,12},{4,0},{8,4},{12,8},{1,13},{5,1},{9,5},{13,9},{2,14},{6,2},{... | collective-permute-start | bytes 49160 | tf_op jit(solution)/shard_map/ppermute | solution.py:108
  35.5 4.3 %collective-permute-start.2 = (bf16[2,4,2,512]{3,1,0,2:T(4,128)(2,1)S(1)}, bf16[2,4,2,512]{3,1,0,2:T(4,128)(2,1)S(1)}, u32[]{:S(2)}, u32[]{:S(2)}) collective-permute-start(bf16[2,4,2,512]{3,1,0,2:T(4,128)(2,1)S(1)} %copy_dynamic-update-slice_fusion), channel_id=1, source_target_pairs={{0,8},{4,12},{8,0},{12,4},{1,9},{5,13},{9,1},{13,5},{2,10},{6,14},... | collective-permute-start | bytes 49160 | tf_op jit(solution)/shard_map/ppermute | solution.py:108
  36.0 3.8 %collective-permute-start.1 = (bf16[2,4,2,512]{3,1,0,2:T(4,128)(2,1)S(1)}, bf16[2,4,2,512]{3,1,0,2:T(4,128)(2,1)S(1)}, u32[]{:S(2)}, u32[]{:S(2)}) collective-permute-start(bf16[2,4,2,512]{3,1,0,2:T(4,128)(2,1)S(1)} %copy_dynamic-update-slice_fusion), channel_id=1, source_target_pairs={{0,4},{4,8},{8,12},{12,0},{1,5},{5,9},{9,13},{13,1},{2,6},{6,10},{... | collective-permute-start | bytes 49160 | tf_op jit(solution)/shard_map/ppermute | solution.py:108
  39.9 7.8 %collective-permute-start.6 = (bf16[2,16,2,512]{3,1,0,2:T(8,128)(2,1)S(1)}, bf16[2,16,2,512]{3,1,0,2:T(8,128)(2,1)S(1)}, u32[]{:S(2)}, u32[]{:S(2)}) collective-permute-start(bf16[2,16,2,512]{3,1,0,2:T(8,128)(2,1)S(1)} %constant_dynamic-update-slice_fusion.8), channel_id=1, source_target_pairs={{0,48},{16,0},{32,16},{48,32},{1,49},{17,1},{33,17},{49,33},{2,50}... | collective-permute-start | bytes 196616 | tf_op jit(solution)/shard_map/ppermute | solution.py:108
  41.6 6.0 %collective-permute-start.5 = (bf16[2,16,2,512]{3,1,0,2:T(8,128)(2,1)S(1)}, bf16[2,16,2,512]{3,1,0,2:T(8,128)(2,1)S(1)}, u32[]{:S(2)}, u32[]{:S(2)}) collective-permute-start(bf16[2,16,2,512]{3,1,0,2:T(8,128)(2,1)S(1)} %constant_dynamic-update-slice_fusion.8), channel_id=1, source_target_pairs={{0,32},{16,48},{32,0},{48,16},{1,33},{17,49},{33,1},{49,17},{2,34}... | collective-permute-start | bytes 196616 | tf_op jit(solution)/shard_map/ppermute | solution.py:108
  41.9 4.9 %collective-permute-start.4 = (bf16[2,16,2,512]{3,1,0,2:T(8,128)(2,1)S(1)}, bf16[2,16,2,512]{3,1,0,2:T(8,128)(2,1)S(1)}, u32[]{:S(2)}, u32[]{:S(2)}) collective-permute-start(bf16[2,16,2,512]{3,1,0,2:T(8,128)(2,1)S(1)} %constant_dynamic-update-slice_fusion.8), channel_id=1, source_target_pairs={{0,16},{16,32},{32,48},{48,0},{1,17},{17,33},{33,49},{49,1},{2,18}... | collective-permute-start | bytes 196616 | tf_op jit(solution)/shard_map/ppermute | solution.py:108
  47.7 10.3 %collective-permute-start.7 = (bf16[2,64,2,512]{3,1,0,2:T(8,128)(2,1)S(1)}, bf16[2,64,2,512]{3,1,0,2:T(8,128)(2,1)S(1)}, u32[]{:S(2)}, u32[]{:S(2)}) collective-permute-start(bf16[2,64,2,512]{3,1,0,2:T(8,128)(2,1)S(1)} %constant_dynamic-update-slice_fusion.4), channel_id=1, source_target_pairs={{0,64},{64,128},{128,192},{192,0},{1,65},{65,129},{129,193},{193,1... | collective-permute-start | bytes 786440 | tf_op jit(solution)/shard_map/ppermute | solution.py:108
  53.8 9.9 %collective-permute-start.8 = (bf16[2,64,2,512]{3,1,0,2:T(8,128)(2,1)S(1)}, bf16[2,64,2,512]{3,1,0,2:T(8,128)(2,1)S(1)}, u32[]{:S(2)}, u32[]{:S(2)}) collective-permute-start(bf16[2,64,2,512]{3,1,0,2:T(8,128)(2,1)S(1)} %constant_dynamic-update-slice_fusion.4), channel_id=1, source_target_pairs={{0,128},{64,192},{128,0},{192,64},{1,129},{65,193},{129,1},{193,65... | collective-permute-start | bytes 786440 | tf_op jit(solution)/shard_map/ppermute | solution.py:108
  56.7 10.8 %collective-permute-start.9 = (bf16[2,64,2,512]{3,1,0,2:T(8,128)(2,1)S(1)}, bf16[2,64,2,512]{3,1,0,2:T(8,128)(2,1)S(1)}, u32[]{:S(2)}, u32[]{:S(2)}) collective-permute-start(bf16[2,64,2,512]{3,1,0,2:T(8,128)(2,1)S(1)} %constant_dynamic-update-slice_fusion.4), channel_id=1, source_target_pairs={{0,192},{64,0},{128,64},{192,128},{1,193},{65,1},{129,65},{193,129... | collective-permute-start | bytes 786440 | tf_op jit(solution)/shard_map/ppermute | solution.py:108
  58.0 10.9 %collective-permute-start.12 = (bf16[4,2,512]{2,0,1:T(4,128)(2,1)S(1)}, bf16[4,2,512]{2,0,1:T(4,128)(2,1)S(1)}, u32[]{:S(2)}, u32[]{:S(2)}) collective-permute-start(bf16[4,2,512]{2,0,1:T(4,128)(2,1)S(1)} %get-tuple-element.17), channel_id=1, source_target_pairs={{0,2},{1,3},{2,0},{3,1},{4,6},{5,7},{6,4},{7,5},{8,10},{9,11},{10,... | collective-permute-start | bytes 24584 | tf_op jit(solution)/shard_map/ppermute | solution.py:133
  67.6 3.6 %collective-permute-start.10 = (bf16[2,256,2,512]{3,1,0,2:T(8,128)(2,1)S(1)}, bf16[2,256,2,512]{3,1,0,2:T(8,128)(2,1)S(1)}, u32[]{:S(2)}, u32[]{:S(2)}) collective-permute-start(bf16[2,256,2,512]{3,1,0,2:T(8,128)(2,1)S(1)} %constant_dynamic-update-slice_fusion), channel_id=1, source_target_pairs={{0,1},{1,0},{2,3},{3,2},{4,5},{5,4},{6,7},{7,6},{8,9},{9,8},{10,11... | collective-permute-start | bytes 3145736 | tf_op jit(solution)/shard_map/ppermute | solution.py:108

commit v9 on v8

--- a/solution.py
+++ b/solution.py
@@ -36,15 +36,9 @@
 
 def lag_weights():
     bin_ids = FIRST_BIN + np.arange(NBINS)
-    inner = 64
-    outer = 2 * MAXLAG // inner
-    ca, sa = angle_table(bin_ids, (np.arange(outer) - MAXLAG // inner) * inner)
-    cb, sb = angle_table(bin_ids, np.arange(inner))
-    ca, sa, cb, sb = (jnp.asarray(a) for a in (ca, sa, cb, sb))
-    cos = ca[:, :, None] * cb[:, None, :] - sa[:, :, None] * sb[:, None, :]
-    sin = sa[:, :, None] * cb[:, None, :] + ca[:, :, None] * sb[:, None, :]
-    table = jnp.concatenate([cos, -sin], axis=0).astype(jnp.bfloat16)
-    return table.reshape(2 * NBINS, 2 * MAXLAG)
+    cos, sin = angle_table(bin_ids, np.arange(2 * MAXLAG) - MAXLAG)
+    table = np.concatenate([cos, -sin], axis=0).astype(ml_dtypes.bfloat16)
+    return jnp.asarray(table)
 
 
 def normalize(spectrum):

time: 90.4 us -> 78 us (0.86)
  local copies, waits for them, and re-layouts: 12.8 us -> 5.5 us
  other arithmetic: 12.6 us -> 6.45 us
  starting transfers between devices: 27.7 us -> 30.7 us
  waiting for transfers between devices: 18.3 us -> 16.4 us
    concatenate x1 -> x0, other arithmetic: 4.76 us -> none  [lag_weights(): table = jnp.concatenate([cos, -sin], axis=0).astype(jnp.bfloat16)]
    sub x1 -> x0, local copies, waits for them, and re-layouts: 3.99 us -> none  [lag_weights(): cos = ca[:, :, None] * cb[:, None, :] - sa[:, :, None] * sb[:, None, :]]
    another operation x3 -> x2, other arithmetic: 3.45 us -> 0.7 us
    neg x1 -> x0, local copies, waits for them, and re-layouts: 2.36 us -> none  [lag_weights(): table = jnp.concatenate([cos, -sin], axis=0).astype(jnp.bfloat16)]
    ppermute x11, starting transfers between devices: 17.9 us -> 20.2 us  [ring_gather(): lax.ppermute(value, axis_name, [(i, (i + shift) % size) for i in range(si...]
    ppermute x11, waiting for transfers between devices: 18.3 us -> 16.3 us  [ring_gather(): lax.ppermute(value, axis_name, [(i, (i + shift) % size) for i in range(si...]
    unnamed x12 -> x2, local copies, waits for them, and re-layouts: 0.97 us -> 0.01 us
  transfers between devices with their start and end apart: 14 -> 14, of which waited for: 6 -> 6; matrix products, arithmetic and copies ran while one was open for 17% -> 1% of each run, Pallas kernels for 0% -> 0%
where the time goes in v9:
time: 78 us; the launch traced here: 77.8 us
  starting transfers between devices  30.7 us (39%)
  waiting for transfers between devices  16.4 us (21%)
  Pallas kernels  10.7 us (14%)
  matrix products  7.3 us (9%)
  other arithmetic  6.45 us (8%)
  local copies, waits for them, and re-layouts  5.5 us (7%)
  between operations  0.79 us (1%)
    ppermute x11, starting transfers between devices, ring_gather(): lax.ppermute(value, axis_name, [(i, (i + shift) % size) for i in range(si...  20.2 us
    ppermute x11, waiting for transfers between devices, ring_gather(): lax.ppermute(value, axis_name, [(i, (i + shift) % size) for i in range(si...  16.3 us
    pallas_call x1, Pallas kernels, transform(): pl.pallas_call(functools.partial(lag_kernel, scale=lag_scale), out_shape=...  10.7 us
    ppermute x3, starting transfers between devices, exchange_receivers(): lax.ppermute(block, WIN_AXES, [(i, (i + shift) % count) for i in range(co...  10.5 us
    dot_general x1, matrix products, whiten(): jnp.dot(row_data, band_table(), preferred_element_type=jnp.float32)  7.3 us
    reduce_sum x1, other arithmetic, cross_lhs(): jnp.sum(src[..., 0, :] * rec[..., 0, :] + src[..., 1, :] * rec[..., 1, :]...  3.15 us
    convert_element_type x1, local copies, waits for them, and re-layouts, cross_lhs(): return lhs.astype(jnp.bfloat16)  2.05 us
    concatenate x1, local copies, waits for them, and re-layouts, cross_lhs(): lhs = jnp.concatenate([real_sum, imag_sum], axis=2).reshape(-1, 2 * NBINS)  1.63 us
  transfers between devices with their start and end apart: 14, of which 6 were waited for; matrix products, arithmetic and copies ran while one was open for 1% of the time, Pallas kernels for 0%

profile of v9, /device:TPU:1, one launch (start us, length us, event | category | flops | bytes accessed | tf_op | source)
XLA Modules:
  0.0 77.8 jit_solution(14897792115894395472)
XLA Ops:
  0.0 0.0 copy-start
  0.0 0.8 fusion.13
  0.8 0.7 compare_and_fusion
  1.5 0.0 copy-done
  1.5 7.3 %convolution_bitcast_fusion = f32[16,1152]{1,0:T(8,128)S(1)} fusion(bf16[7680,1152]{1,0:T(8,128)(2,1)} %constant.240.clone, bf16[1,16,7680]{2,1,0:T(8,128)(2,1)S(1)} %copy-done), kind=kOutput, calls=%fused_computation.3 | convolution fusion | flops 283115520 | bytes 18014208 | tf_op jit(solution)/shard_map/dot_general | solution.py:59
  8.8 0.1 fusion.2
  8.9 0.6 fusion.3
  9.6 0.1 fusion.6
  9.7 0.6 gather_fusion
  10.3 0.1 broadcast_select_fusion
  10.4 7.8 %collective-permute-start = (bf16[1,4,2,512]{3,2,1,0:T(2,128)(2,1)S(1)}, bf16[1,4,2,512]{3,2,1,0:T(2,128)(2,1)S(1)}, u32[]{:S(2)}, u32[]{:S(2)}) collective-permute-start(bf16[1,4,2,512]{3,2,1,0:T(2,128)(2,1)S(1)} %broadcast_select_fusion), channel_id=1, source_target_pairs={{0,2},{2,0},{1,3},{3,1},{4,6},{6,4},{5,7},{7,5},{8,10},{10,8},{9,1... | collective-permute-start | bytes 24584 | tf_op jit(solution)/shard_map/ppermute | solution.py:102
  18.4 0.8 %collective-permute-done = bf16[1,4,2,512]{3,2,1,0:T(2,128)(2,1)S(1)} collective-permute-done((bf16[1,4,2,512]{3,2,1,0:T(2,128)(2,1)S(1)}, bf16[1,4,2,512]{3,2,1,0:T(2,128)(2,1)S(1)}, u32[]{:S(2)}, u32[]{:S(2)}) %collective-permute-start) | collective-permute-done | bytes 8224 | tf_op jit(solution)/shard_map/ppermute | solution.py:102
  19.2 2.5 %collective-permute-start.3 = (bf16[2,4,2,512]{3,1,0,2:T(4,128)(2,1)S(1)}, bf16[2,4,2,512]{3,1,0,2:T(4,128)(2,1)S(1)}, u32[]{:S(2)}, u32[]{:S(2)}) collective-permute-start(bf16[2,4,2,512]{3,1,0,2:T(4,128)(2,1)S(1)} %copy_dynamic-update-slice_fusion), channel_id=1, source_target_pairs={{0,12},{4,0},{8,4},{12,8},{1,13},{5,1},{9,5},{13,9},{2,14},{6,2},{... | collective-permute-start | bytes 49160 | tf_op jit(solution)/shard_map/ppermute | solution.py:102
  21.8 0.5 collective-permute-start.2
  22.3 0.6 collective-permute-start.1
  22.9 3.2 %collective-permute-done.1 = bf16[2,4,2,512]{3,1,0,2:T(4,128)(2,1)S(1)} collective-permute-done((bf16[2,4,2,512]{3,1,0,2:T(4,128)(2,1)S(1)}, bf16[2,4,2,512]{3,1,0,2:T(4,128)(2,1)S(1)}, u32[]{:S(2)}, u32[]{:S(2)}) %collective-permute-start.1) | collective-permute-done | bytes 16416 | tf_op jit(solution)/shard_map/ppermute | solution.py:102
  26.1 0.0 collective-permute-done.2
  26.2 0.0 collective-permute-done.3
  26.2 2.9 %collective-permute-start.6 = (bf16[2,16,2,512]{3,1,0,2:T(8,128)(2,1)S(1)}, bf16[2,16,2,512]{3,1,0,2:T(8,128)(2,1)S(1)}, u32[]{:S(2)}, u32[]{:S(2)}) collective-permute-start(bf16[2,16,2,512]{3,1,0,2:T(8,128)(2,1)S(1)} %constant_dynamic-update-slice_fusion.8), channel_id=1, source_target_pairs={{0,48},{16,0},{32,16},{48,32},{1,49},{17,1},{33,17},{49,33},{2,50}... | collective-permute-start | bytes 196616 | tf_op jit(solution)/shard_map/ppermute | solution.py:102
  29.1 0.0 collective-permute-start.5
  29.1 0.4 collective-permute-start.4
  29.5 4.7 %collective-permute-done.4 = bf16[2,16,2,512]{3,1,0,2:T(8,128)(2,1)S(1)} collective-permute-done((bf16[2,16,2,512]{3,1,0,2:T(8,128)(2,1)S(1)}, bf16[2,16,2,512]{3,1,0,2:T(8,128)(2,1)S(1)}, u32[]{:S(2)}, u32[]{:S(2)}) %collective-permute-start.4) | collective-permute-done | bytes 65568 | tf_op jit(solution)/shard_map/ppermute | solution.py:102
  34.2 0.0 collective-permute-done.5
  34.2 0.0 collective-permute-done.6
  34.3 1.4 %collective-permute-start.7 = (bf16[2,64,2,512]{3,1,0,2:T(8,128)(2,1)S(1)}, bf16[2,64,2,512]{3,1,0,2:T(8,128)(2,1)S(1)}, u32[]{:S(2)}, u32[]{:S(2)}) collective-permute-start(bf16[2,64,2,512]{3,1,0,2:T(8,128)(2,1)S(1)} %constant_dynamic-update-slice_fusion.4), channel_id=1, source_target_pairs={{0,64},{64,128},{128,192},{192,0},{1,65},{65,129},{129,193},{193,1... | collective-permute-start | bytes 786440 | tf_op jit(solution)/shard_map/ppermute | solution.py:102
  35.7 5.1 %collective-permute-start.13 = (bf16[4,2,512]{2,0,1:T(4,128)(2,1)S(1)}, bf16[4,2,512]{2,0,1:T(4,128)(2,1)S(1)}, u32[]{:S(2)}, u32[]{:S(2)}) collective-permute-start(bf16[4,2,512]{2,0,1:T(4,128)(2,1)S(1)} %get-tuple-element.13), channel_id=1, source_target_pairs={{0,3},{1,0},{2,1},{3,2},{4,7},{5,4},{6,5},{7,6},{8,11},{9,8},{10,9... | collective-permute-start | bytes 24584 | tf_op jit(solution)/shard_map/ppermute | solution.py:127
  40.8 4.7 %collective-permute-start.11 = (bf16[4,2,512]{2,0,1:T(4,128)(2,1)S(1)}, bf16[4,2,512]{2,0,1:T(4,128)(2,1)S(1)}, u32[]{:S(2)}, u32[]{:S(2)}) collective-permute-start(bf16[4,2,512]{2,0,1:T(4,128)(2,1)S(1)} %get-tuple-element.14), channel_id=1, source_target_pairs={{0,1},{1,2},{2,3},{3,0},{4,5},{5,6},{6,7},{7,4},{8,9},{9,10},{10,1... | collective-permute-start | bytes 24584 | tf_op jit(solution)/shard_map/ppermute | solution.py:127
  45.5 2.6 %collective-permute-start.8 = (bf16[2,64,2,512]{3,1,0,2:T(8,128)(2,1)S(1)}, bf16[2,64,2,512]{3,1,0,2:T(8,128)(2,1)S(1)}, u32[]{:S(2)}, u32[]{:S(2)}) collective-permute-start(bf16[2,64,2,512]{3,1,0,2:T(8,128)(2,1)S(1)} %constant_dynamic-update-slice_fusion.4), channel_id=1, source_target_pairs={{0,128},{64,192},{128,0},{192,64},{1,129},{65,193},{129,1},{193,65... | collective-permute-start | bytes 786440 | tf_op jit(solution)/shard_map/ppermute | solution.py:102
  48.4 1.1 %collective-permute-start.9 = (bf16[2,64,2,512]{3,1,0,2:T(8,128)(2,1)S(1)}, bf16[2,64,2,512]{3,1,0,2:T(8,128)(2,1)S(1)}, u32[]{:S(2)}, u32[]{:S(2)}) collective-permute-start(bf16[2,64,2,512]{3,1,0,2:T(8,128)(2,1)S(1)} %constant_dynamic-update-slice_fusion.4), channel_id=1, source_target_pairs={{0,192},{64,0},{128,64},{192,128},{1,193},{65,1},{129,65},{193,129... | collective-permute-start | bytes 786440 | tf_op jit(solution)/shard_map/ppermute | solution.py:102
  49.6 0.1 broadcast_in_dim.53
  49.7 0.0 collective-permute-done.7
  49.7 0.7 collective-permute-start.12
  50.4 2.7 %collective-permute-done.8 = bf16[2,64,2,512]{3,1,0,2:T(8,128)(2,1)S(1)} collective-permute-done((bf16[2,64,2,512]{3,1,0,2:T(8,128)(2,1)S(1)}, bf16[2,64,2,512]{3,1,0,2:T(8,128)(2,1)S(1)}, u32[]{:S(2)}, u32[]{:S(2)}) %collective-permute-start.8) | collective-permute-done | bytes 262176 | tf_op jit(solution)/shard_map/ppermute | solution.py:102
  53.2 2.7 %collective-permute-done.9 = bf16[2,64,2,512]{3,1,0,2:T(8,128)(2,1)S(1)} collective-permute-done((bf16[2,64,2,512]{3,1,0,2:T(8,128)(2,1)S(1)}, bf16[2,64,2,512]{3,1,0,2:T(8,128)(2,1)S(1)}, u32[]{:S(2)}, u32[]{:S(2)}) %collective-permute-start.9) | collective-permute-done | bytes 262176 | tf_op jit(solution)/shard_map/ppermute | solution.py:102
  55.9 0.3 collective-permute-start.10
  56.2 0.0 collective-permute-done.11
  56.2 0.0 collective-permute-done.12
  56.3 0.0 collective-permute-done.13
  56.3 0.2 broadcast_in_dim.52
  56.5 0.1 bitcast_dynamic-update-slice_fusion.1
  56.6 2.2 %collective-permute-done.10 = bf16[2,256,2,512]{3,1,0,2:T(8,128)(2,1)S(1)} collective-permute-done((bf16[2,256,2,512]{3,1,0,2:T(8,128)(2,1)S(1)}, bf16[2,256,2,512]{3,1,0,2:T(8,128)(2,1)S(1)}, u32[]{:S(2)}, u32[]{:S(2)}) %collective-permute-start.10) | collective-permute-done | bytes 1048608 | tf_op jit(solution)/shard_map/ppermute | solution.py:102
  58.8 0.1 bitcast_dynamic-update-slice_fusion
  58.9 0.6 broadcast_in_dim.61
  59.5 0.4 slice_bitcast_fusion.1
  60.0 3.2 %add_reduce_fusion = (bf16[256,4,512]{2,0,1:T(8,128)(2,1)S(1)}, bf16[256,4,512]{2,0,1:T(8,128)(2,1)S(1)}) fusion(f32[4,4,512]{2,1,0:T(4,128)S(1)} %get-tuple-element.12, f32[4,256,512]{2,1,0:T(8,128)S(1)} %get-tuple-element.10, f32[4,4,512]{2,1,0:T(4,128)S(1)} %get-tuple-element.11, f32[4,256,512]{2,1,0:T(8,128)S(1)} %get-tuple-element.9), kind=kLoop, calls=%fused_computation.2 | loop fusion | flops 15728640 | bytes 6356992 | tf_op jit(solution)/shard_map/reduce_sum | solution.py:65
  63.1 0.3 pad_maximum_fusion
  63.4 1.6 %copy.9 = bf16[256,4,1024]{2,1,0:T(4,128)(2,1)S(1)} copy(bf16[256,4,1024]{2,0,1:T(8,128)(2,1)S(1)} %pad_maximum_fusion) | data formatting | bytes 4194304 | tf_op jit(solution)/shard_map/concatenate | solution.py:67
  65.1 2.0 %convert_element_type.13.lhs_ref = bf16[1024,1024]{1,0:T(8,128)(2,1)} reshape(bf16[256,4,1024]{2,1,0:T(4,128)(2,1)S(1)} %copy.9) | data formatting | bytes 4194304 | tf_op jit(solution)/shard_map/convert_element_type | solution.py:68
  67.1 10.7 %shard_map.46 = f32[256,4,2048]{2,1,0:T(4,128)} custom-call(bf16[1024,1024]{1,0:T(8,128)(2,1)} %convert_element_type.13.lhs_ref, bf16[1024,2048]{1,0:T(8,128)(2,1)} %constant.241.clone.w_ref), custom_call_target="tpu_custom_call" | custom-call | tf_op jit(solution)/shard_map/pallas_call | solution.py:82
  (28 shorter events, 0.4 us)
Async XLA Ops:
  0.0 1.5 %copy-start = (bf16[1,16,7680]{2,1,0:T(8,128)(2,1)S(1)}, bf16[1,16,7680]{2,1,0:T(8,128)(2,1)}, u32[]{:S(2)}) copy-start(bf16[1,16,7680]{2,1,0:T(8,128)(2,1)} %param.4) | copy-start | bytes 737284
  10.4 8.9 %collective-permute-start = (bf16[1,4,2,512]{3,2,1,0:T(2,128)(2,1)S(1)}, bf16[1,4,2,512]{3,2,1,0:T(2,128)(2,1)S(1)}, u32[]{:S(2)}, u32[]{:S(2)}) collective-permute-start(bf16[1,4,2,512]{3,2,1,0:T(2,128)(2,1)S(1)} %broadcast_select_fusion), channel_id=1, source_target_pairs={{0,2},{2,0},{1,3},{3,1},{4,6},{6,4},{5,7},{7,5},{8,10},{10,8},{9,1... | collective-permute-start | bytes 24584 | tf_op jit(solution)/shard_map/ppermute | solution.py:102
  19.2 6.9 %collective-permute-start.3 = (bf16[2,4,2,512]{3,1,0,2:T(4,128)(2,1)S(1)}, bf16[2,4,2,512]{3,1,0,2:T(4,128)(2,1)S(1)}, u32[]{:S(2)}, u32[]{:S(2)}) collective-permute-start(bf16[2,4,2,512]{3,1,0,2:T(4,128)(2,1)S(1)} %copy_dynamic-update-slice_fusion), channel_id=1, source_target_pairs={{0,12},{4,0},{8,4},{12,8},{1,13},{5,1},{9,5},{13,9},{2,14},{6,2},{... | collective-permute-start | bytes 49160 | tf_op jit(solution)/shard_map/ppermute | solution.py:102
  21.8 4.3 %collective-permute-start.2 = (bf16[2,4,2,512]{3,1,0,2:T(4,128)(2,1)S(1)}, bf16[2,4,2,512]{3,1,0,2:T(4,128)(2,1)S(1)}, u32[]{:S(2)}, u32[]{:S(2)}) collective-permute-start(bf16[2,4,2,512]{3,1,0,2:T(4,128)(2,1)S(1)} %copy_dynamic-update-slice_fusion), channel_id=1, source_target_pairs={{0,8},{4,12},{8,0},{12,4},{1,9},{5,13},{9,1},{13,5},{2,10},{6,14},... | collective-permute-start | bytes 49160 | tf_op jit(solution)/shard_map/ppermute | solution.py:102
  22.3 3.8 %collective-permute-start.1 = (bf16[2,4,2,512]{3,1,0,2:T(4,128)(2,1)S(1)}, bf16[2,4,2,512]{3,1,0,2:T(4,128)(2,1)S(1)}, u32[]{:S(2)}, u32[]{:S(2)}) collective-permute-start(bf16[2,4,2,512]{3,1,0,2:T(4,128)(2,1)S(1)} %copy_dynamic-update-slice_fusion), channel_id=1, source_target_pairs={{0,4},{4,8},{8,12},{12,0},{1,5},{5,9},{9,13},{13,1},{2,6},{6,10},{... | collective-permute-start | bytes 49160 | tf_op jit(solution)/shard_map/ppermute | solution.py:102
  26.2 8.1 %collective-permute-start.6 = (bf16[2,16,2,512]{3,1,0,2:T(8,128)(2,1)S(1)}, bf16[2,16,2,512]{3,1,0,2:T(8,128)(2,1)S(1)}, u32[]{:S(2)}, u32[]{:S(2)}) collective-permute-start(bf16[2,16,2,512]{3,1,0,2:T(8,128)(2,1)S(1)} %constant_dynamic-update-slice_fusion.8), channel_id=1, source_target_pairs={{0,48},{16,0},{32,16},{48,32},{1,49},{17,1},{33,17},{49,33},{2,50}... | collective-permute-start | bytes 196616 | tf_op jit(solution)/shard_map/ppermute | solution.py:102
  29.1 5.1 %collective-permute-start.5 = (bf16[2,16,2,512]{3,1,0,2:T(8,128)(2,1)S(1)}, bf16[2,16,2,512]{3,1,0,2:T(8,128)(2,1)S(1)}, u32[]{:S(2)}, u32[]{:S(2)}) collective-permute-start(bf16[2,16,2,512]{3,1,0,2:T(8,128)(2,1)S(1)} %constant_dynamic-update-slice_fusion.8), channel_id=1, source_target_pairs={{0,32},{16,48},{32,0},{48,16},{1,33},{17,49},{33,1},{49,17},{2,34}... | collective-permute-start | bytes 196616 | tf_op jit(solution)/shard_map/ppermute | solution.py:102
  29.1 5.1 %collective-permute-start.4 = (bf16[2,16,2,512]{3,1,0,2:T(8,128)(2,1)S(1)}, bf16[2,16,2,512]{3,1,0,2:T(8,128)(2,1)S(1)}, u32[]{:S(2)}, u32[]{:S(2)}) collective-permute-start(bf16[2,16,2,512]{3,1,0,2:T(8,128)(2,1)S(1)} %constant_dynamic-update-slice_fusion.8), channel_id=1, source_target_pairs={{0,16},{16,32},{32,48},{48,0},{1,17},{17,33},{33,49},{49,1},{2,18}... | collective-permute-start | bytes 196616 | tf_op jit(solution)/shard_map/ppermute | solution.py:102
  34.3 15.4 %collective-permute-start.7 = (bf16[2,64,2,512]{3,1,0,2:T(8,128)(2,1)S(1)}, bf16[2,64,2,512]{3,1,0,2:T(8,128)(2,1)S(1)}, u32[]{:S(2)}, u32[]{:S(2)}) collective-permute-start(bf16[2,64,2,512]{3,1,0,2:T(8,128)(2,1)S(1)} %constant_dynamic-update-slice_fusion.4), channel_id=1, source_target_pairs={{0,64},{64,128},{128,192},{192,0},{1,65},{65,129},{129,193},{193,1... | collective-permute-start | bytes 786440 | tf_op jit(solution)/shard_map/ppermute | solution.py:102
  35.7 20.6 %collective-permute-start.13 = (bf16[4,2,512]{2,0,1:T(4,128)(2,1)S(1)}, bf16[4,2,512]{2,0,1:T(4,128)(2,1)S(1)}, u32[]{:S(2)}, u32[]{:S(2)}) collective-permute-start(bf16[4,2,512]{2,0,1:T(4,128)(2,1)S(1)} %get-tuple-element.13), channel_id=1, source_target_pairs={{0,3},{1,0},{2,1},{3,2},{4,7},{5,4},{6,5},{7,6},{8,11},{9,8},{10,9... | collective-permute-start | bytes 24584 | tf_op jit(solution)/shard_map/ppermute | solution.py:127
  40.8 15.4 %collective-permute-start.11 = (bf16[4,2,512]{2,0,1:T(4,128)(2,1)S(1)}, bf16[4,2,512]{2,0,1:T(4,128)(2,1)S(1)}, u32[]{:S(2)}, u32[]{:S(2)}) collective-permute-start(bf16[4,2,512]{2,0,1:T(4,128)(2,1)S(1)} %get-tuple-element.14), channel_id=1, source_target_pairs={{0,1},{1,2},{2,3},{3,0},{4,5},{5,6},{6,7},{7,4},{8,9},{9,10},{10,1... | collective-permute-start | bytes 24584 | tf_op jit(solution)/shard_map/ppermute | solution.py:127
  45.5 7.6 %collective-permute-start.8 = (bf16[2,64,2,512]{3,1,0,2:T(8,128)(2,1)S(1)}, bf16[2,64,2,512]{3,1,0,2:T(8,128)(2,1)S(1)}, u32[]{:S(2)}, u32[]{:S(2)}) collective-permute-start(bf16[2,64,2,512]{3,1,0,2:T(8,128)(2,1)S(1)} %constant_dynamic-update-slice_fusion.4), channel_id=1, source_target_pairs={{0,128},{64,192},{128,0},{192,64},{1,129},{65,193},{129,1},{193,65... | collective-permute-start | bytes 786440 | tf_op jit(solution)/shard_map/ppermute | solution.py:102
  48.4 7.5 %collective-permute-start.9 = (bf16[2,64,2,512]{3,1,0,2:T(8,128)(2,1)S(1)}, bf16[2,64,2,512]{3,1,0,2:T(8,128)(2,1)S(1)}, u32[]{:S(2)}, u32[]{:S(2)}) collective-permute-start(bf16[2,64,2,512]{3,1,0,2:T(8,128)(2,1)S(1)} %constant_dynamic-update-slice_fusion.4), channel_id=1, source_target_pairs={{0,192},{64,0},{128,64},{192,128},{1,193},{65,1},{129,65},{193,129... | collective-permute-start | bytes 786440 | tf_op jit(solution)/shard_map/ppermute | solution.py:102
  49.7 6.5 %collective-permute-start.12 = (bf16[4,2,512]{2,0,1:T(4,128)(2,1)S(1)}, bf16[4,2,512]{2,0,1:T(4,128)(2,1)S(1)}, u32[]{:S(2)}, u32[]{:S(2)}) collective-permute-start(bf16[4,2,512]{2,0,1:T(4,128)(2,1)S(1)} %get-tuple-element.15), channel_id=1, source_target_pairs={{0,2},{1,3},{2,0},{3,1},{4,6},{5,7},{6,4},{7,5},{8,10},{9,11},{10,... | collective-permute-start | bytes 24584 | tf_op jit(solution)/shard_map/ppermute | solution.py:127
  55.9 2.9 %collective-permute-start.10 = (bf16[2,256,2,512]{3,1,0,2:T(8,128)(2,1)S(1)}, bf16[2,256,2,512]{3,1,0,2:T(8,128)(2,1)S(1)}, u32[]{:S(2)}, u32[]{:S(2)}) collective-permute-start(bf16[2,256,2,512]{3,1,0,2:T(8,128)(2,1)S(1)} %constant_dynamic-update-slice_fusion), channel_id=1, source_target_pairs={{0,1},{1,0},{2,3},{3,2},{4,5},{5,4},{6,7},{7,6},{8,9},{9,8},{10,11... | collective-permute-start | bytes 3145736 | tf_op jit(solution)/shard_map/ppermute | solution.py:102

commit v10 on v9

--- a/solution.py
+++ b/solution.py
@@ -91,28 +91,32 @@
     )(lhs, weights)
 
 
-def ring_gather(value, axis_name, axis):
-    size = lax.axis_size(axis_name)
-    here = lax.axis_index(axis_name)
+def group_gather(value, names, axes):
+    sizes = [lax.axis_size(name) for name in names]
+    total = math.prod(sizes)
+    here = lax.axis_index(tuple(names))
     shape = list(value.shape)
-    block = shape[axis]
-    shape[axis] *= size
+    for name, axis in zip(names, axes):
+        shape[axis] *= lax.axis_size(name)
     out = jnp.zeros(shape, value.dtype)
-    for shift in range(size):
+    for shift in range(total):
         part = value if shift == 0 else lax.ppermute(
-            value, axis_name, [(i, (i + shift) % size) for i in range(size)]
+            value, tuple(names), [(i, (i + shift) % total) for i in range(total)]
         )
+        origin = (here - shift) % total
         start = [0] * len(shape)
-        start[axis] = ((here - shift) % size) * block
+        for k, (name, axis) in enumerate(zip(names, axes)):
+            coord = origin // math.prod(sizes[k + 1 :]) % sizes[k]
+            later = [s for s, a in zip(sizes[k + 1 :], axes[k + 1 :]) if a == axis]
+            start[axis] = start[axis] + coord * math.prod(later) * value.shape[axis]
         out = lax.dynamic_update_slice(out, part, start)
     return out
 
 
 def collect(own):
-    part = ring_gather(own, "zh", 0)
-    for name in reversed(CHAN_AXES):
-        part = ring_gather(part, name, 1)
-    return ring_gather(part, "core", 0)
+    part = group_gather(own, ("x", "zh"), (1, 0))
+    part = group_gather(part, ("y", "zl"), (1, 1))
+    return group_gather(part, ("core",), (0,))
 
 
 def exchange_receivers(rows):

time: 78 us -> 173 us (2.22)
  waiting for transfers between devices: 16.4 us -> 87.1 us
  starting transfers between devices: 30.7 us -> 55.1 us
    ppermute x11 -> x23, waiting for transfers between devices: 16.3 us -> 87.1 us  [group_gather(): lax.ppermute(value, tuple(names), [(i, (i + shift) % total) for i in rang...]
    ppermute x11 -> x23, starting transfers between devices: 20.2 us -> 44.7 us  [group_gather(): lax.ppermute(value, tuple(names), [(i, (i + shift) % total) for i in rang...]
  transfers between devices with their start and end apart: 14 -> 26, of which waited for: 6 -> 18; matrix products, arithmetic and copies ran while one was open for 1% -> 0% of each run, Pallas kernels for 0% -> 0%
where the time goes in v10:
time: 173 us
  waiting for transfers between devices  87.1 us (50%)
  starting transfers between devices  55.1 us (32%)
  Pallas kernels  10.7 us (6%)
  matrix products  7.3 us (4%)
  other arithmetic  6.46 us (4%)
  local copies, waits for them, and re-layouts  5.51 us (3%)
    ppermute x23, waiting for transfers between devices, group_gather(): lax.ppermute(value, tuple(names), [(i, (i + shift) % total) for i in rang...  87.1 us
    ppermute x23, starting transfers between devices, group_gather(): lax.ppermute(value, tuple(names), [(i, (i + shift) % total) for i in rang...  44.7 us
    pallas_call x1, Pallas kernels, transform(): pl.pallas_call(functools.partial(lag_kernel, scale=lag_scale), out_shape=...  10.7 us
    ppermute x3, starting transfers between devices, exchange_receivers(): lax.ppermute(block, WIN_AXES, [(i, (i + shift) % count) for i in range(co...  10.4 us
    dot_general x1, matrix products, whiten(): jnp.dot(row_data, band_table(), preferred_element_type=jnp.float32)  7.3 us
  transfers between devices with their start and end apart: 26, of which 18 were waited for; matrix products, arithmetic and copies ran while one was open for 0% of the time, Pallas kernels for 0%

profile of v10, /device:TPU:1, one launch (start us, length us, event | category | flops | bytes accessed | tf_op | source)
XLA Modules:
  0.0 172.8 jit_solution(18146206781021256787)
XLA Ops:
  0.0 0.8 fusion.12
  0.8 0.7 compare_and_fusion
  1.5 7.3 %convolution_bitcast_fusion = f32[16,1152]{1,0:T(8,128)S(1)} fusion(bf16[7680,1152]{1,0:T(8,128)(2,1)} %constant.888.clone, bf16[1,16,7680]{2,1,0:T(8,128)(2,1)S(1)} %copy-done), kind=kOutput, calls=%fused_computation.3 | convolution fusion | flops 283115520 | bytes 18014208 | tf_op jit(solution)/shard_map/dot_general | solution.py:59
  8.8 0.1 fusion.2
  8.9 0.6 fusion.3
  9.6 0.1 fusion.6
  9.7 0.6 gather_fusion
  10.3 0.1 broadcast_select_fusion
  10.4 10.0 %collective-permute-start.6 = (bf16[1,4,2,512]{3,2,1,0:T(2,128)(2,1)S(1)}, bf16[1,4,2,512]{3,2,1,0:T(2,128)(2,1)S(1)}, u32[]{:S(2)}, u32[]{:S(2)}) collective-permute-start(bf16[1,4,2,512]{3,2,1,0:T(2,128)(2,1)S(1)} %broadcast_select_fusion), channel_id=1, source_target_pairs={{0,14},{2,0},{4,2},{6,4},{8,6},{10,8},{12,10},{14,12},{1,15},{3,1}... | collective-permute-start | bytes 24584 | tf_op jit(solution)/shard_map/ppermute | solution.py:103
  20.4 0.5 collective-permute-start.5
  20.9 0.1 collective-permute-start.4
  21.0 2.5 %collective-permute-start.3 = (bf16[1,4,2,512]{3,2,1,0:T(2,128)(2,1)S(1)}, bf16[1,4,2,512]{3,2,1,0:T(2,128)(2,1)S(1)}, u32[]{:S(2)}, u32[]{:S(2)}) collective-permute-start(bf16[1,4,2,512]{3,2,1,0:T(2,128)(2,1)S(1)} %broadcast_select_fusion), channel_id=1, source_target_pairs={{0,8},{2,10},{4,12},{6,14},{8,0},{10,2},{12,4},{14,6},{1,9},{3,11}... | collective-permute-start | bytes 24584 | tf_op jit(solution)/shard_map/ppermute | solution.py:103
  23.4 5.3 %collective-permute-start = (bf16[1,4,2,512]{3,2,1,0:T(2,128)(2,1)S(1)}, bf16[1,4,2,512]{3,2,1,0:T(2,128)(2,1)S(1)}, u32[]{:S(2)}, u32[]{:S(2)}) collective-permute-start(bf16[1,4,2,512]{3,2,1,0:T(2,128)(2,1)S(1)} %broadcast_select_fusion), channel_id=1, source_target_pairs={{0,2},{2,4},{4,6},{6,8},{8,10},{10,12},{12,14},{14,0},{1,3},{3,5},... | collective-permute-start | bytes 24584 | tf_op jit(solution)/shard_map/ppermute | solution.py:103
  29.2 2.8 %collective-permute-done = bf16[1,4,2,512]{3,2,1,0:T(2,128)(2,1)S(1)} collective-permute-done((bf16[1,4,2,512]{3,2,1,0:T(2,128)(2,1)S(1)}, bf16[1,4,2,512]{3,2,1,0:T(2,128)(2,1)S(1)}, u32[]{:S(2)}, u32[]{:S(2)}) %collective-permute-start) | collective-permute-done | bytes 8224 | tf_op jit(solution)/shard_map/ppermute | solution.py:103
  31.9 0.0 collective-permute-start.1
  32.0 3.7 %collective-permute-done.1 = bf16[1,4,2,512]{3,2,1,0:T(2,128)(2,1)S(1)} collective-permute-done((bf16[1,4,2,512]{3,2,1,0:T(2,128)(2,1)S(1)}, bf16[1,4,2,512]{3,2,1,0:T(2,128)(2,1)S(1)}, u32[]{:S(2)}, u32[]{:S(2)}) %collective-permute-start.1) | collective-permute-done | bytes 8224 | tf_op jit(solution)/shard_map/ppermute | solution.py:103
  35.7 1.7 collective-permute-start.2
  37.4 7.1 %collective-permute-done.2 = bf16[1,4,2,512]{3,2,1,0:T(2,128)(2,1)S(1)} collective-permute-done((bf16[1,4,2,512]{3,2,1,0:T(2,128)(2,1)S(1)}, bf16[1,4,2,512]{3,2,1,0:T(2,128)(2,1)S(1)}, u32[]{:S(2)}, u32[]{:S(2)}) %collective-permute-start.2) | collective-permute-done | bytes 8224 | tf_op jit(solution)/shard_map/ppermute | solution.py:103
  44.5 5.0 %collective-permute-start.25 = (bf16[4,2,512]{2,0,1:T(4,128)(2,1)S(1)}, bf16[4,2,512]{2,0,1:T(4,128)(2,1)S(1)}, u32[]{:S(2)}, u32[]{:S(2)}) collective-permute-start(bf16[4,2,512]{2,0,1:T(4,128)(2,1)S(1)} %get-tuple-element.13), channel_id=1, source_target_pairs={{0,3},{1,0},{2,1},{3,2},{4,7},{5,4},{6,5},{7,6},{8,11},{9,8},{10,9... | collective-permute-start | bytes 24584 | tf_op jit(solution)/shard_map/ppermute | solution.py:131
  49.4 0.0 collective-permute-done.3
  49.5 3.1 %collective-permute-start.23 = (bf16[4,2,512]{2,0,1:T(4,128)(2,1)S(1)}, bf16[4,2,512]{2,0,1:T(4,128)(2,1)S(1)}, u32[]{:S(2)}, u32[]{:S(2)}) collective-permute-start(bf16[4,2,512]{2,0,1:T(4,128)(2,1)S(1)} %get-tuple-element.14), channel_id=1, source_target_pairs={{0,1},{1,2},{2,3},{3,0},{4,5},{5,6},{6,7},{7,4},{8,9},{9,10},{10,1... | collective-permute-start | bytes 24584 | tf_op jit(solution)/shard_map/ppermute | solution.py:131
  52.6 0.0 collective-permute-done.4
  52.6 2.3 %collective-permute-start.24 = (bf16[4,2,512]{2,0,1:T(4,128)(2,1)S(1)}, bf16[4,2,512]{2,0,1:T(4,128)(2,1)S(1)}, u32[]{:S(2)}, u32[]{:S(2)}) collective-permute-start(bf16[4,2,512]{2,0,1:T(4,128)(2,1)S(1)} %get-tuple-element.15), channel_id=1, source_target_pairs={{0,2},{1,3},{2,0},{3,1},{4,6},{5,7},{6,4},{7,5},{8,10},{9,11},{10,... | collective-permute-start | bytes 24584 | tf_op jit(solution)/shard_map/ppermute | solution.py:131
  54.9 0.0 collective-permute-done.5
  55.0 0.0 collective-permute-done.6
  55.0 5.5 %collective-permute-start.21 = (bf16[2,16,2,512]{3,1,0,2:T(8,128)(2,1)S(1)}, bf16[2,16,2,512]{3,1,0,2:T(8,128)(2,1)S(1)}, u32[]{:S(2)}, u32[]{:S(2)}) collective-permute-start(bf16[2,16,2,512]{3,1,0,2:T(8,128)(2,1)S(1)} %constant_dynamic-update-slice_fusion.20), channel_id=1, source_target_pairs={{0,240},{16,0},{32,16},{48,32},{64,48},{80,64},{96,80},{112,96},{1... | collective-permute-start | bytes 196616 | tf_op jit(solution)/shard_map/ppermute | solution.py:103
  60.5 0.0 collective-permute-start.7
  60.5 0.1 broadcast_in_dim.47
  60.6 6.9 %collective-permute-done.7 = bf16[2,16,2,512]{3,1,0,2:T(8,128)(2,1)S(1)} collective-permute-done((bf16[2,16,2,512]{3,1,0,2:T(8,128)(2,1)S(1)}, bf16[2,16,2,512]{3,1,0,2:T(8,128)(2,1)S(1)}, u32[]{:S(2)}, u32[]{:S(2)}) %collective-permute-start.7) | collective-permute-done | bytes 65568 | tf_op jit(solution)/shard_map/ppermute | solution.py:103
  67.5 0.0 collective-permute-start.8
  67.5 6.1 %collective-permute-done.8 = bf16[2,16,2,512]{3,1,0,2:T(8,128)(2,1)S(1)} collective-permute-done((bf16[2,16,2,512]{3,1,0,2:T(8,128)(2,1)S(1)}, bf16[2,16,2,512]{3,1,0,2:T(8,128)(2,1)S(1)}, u32[]{:S(2)}, u32[]{:S(2)}) %collective-permute-start.8) | collective-permute-done | bytes 65568 | tf_op jit(solution)/shard_map/ppermute | solution.py:103
  73.7 5.9 %collective-permute-done.9 = bf16[2,16,2,512]{3,1,0,2:T(8,128)(2,1)S(1)} collective-permute-done((bf16[2,16,2,512]{3,1,0,2:T(8,128)(2,1)S(1)}, bf16[2,16,2,512]{3,1,0,2:T(8,128)(2,1)S(1)}, u32[]{:S(2)}, u32[]{:S(2)}) %collective-permute-start.9) | collective-permute-done | bytes 65568 | tf_op jit(solution)/shard_map/ppermute | solution.py:103
  79.6 0.0 collective-permute-start.10
  79.6 4.3 %collective-permute-done.10 = bf16[2,16,2,512]{3,1,0,2:T(8,128)(2,1)S(1)} collective-permute-done((bf16[2,16,2,512]{3,1,0,2:T(8,128)(2,1)S(1)}, bf16[2,16,2,512]{3,1,0,2:T(8,128)(2,1)S(1)}, u32[]{:S(2)}, u32[]{:S(2)}) %collective-permute-start.10) | collective-permute-done | bytes 65568 | tf_op jit(solution)/shard_map/ppermute | solution.py:103
  83.9 7.3 %collective-permute-done.11 = bf16[2,16,2,512]{3,1,0,2:T(8,128)(2,1)S(1)} collective-permute-done((bf16[2,16,2,512]{3,1,0,2:T(8,128)(2,1)S(1)}, bf16[2,16,2,512]{3,1,0,2:T(8,128)(2,1)S(1)}, u32[]{:S(2)}, u32[]{:S(2)}) %collective-permute-start.11) | collective-permute-done | bytes 65568 | tf_op jit(solution)/shard_map/ppermute | solution.py:103
  91.2 0.0 collective-permute-start.12
  91.3 6.4 %collective-permute-done.12 = bf16[2,16,2,512]{3,1,0,2:T(8,128)(2,1)S(1)} collective-permute-done((bf16[2,16,2,512]{3,1,0,2:T(8,128)(2,1)S(1)}, bf16[2,16,2,512]{3,1,0,2:T(8,128)(2,1)S(1)}, u32[]{:S(2)}, u32[]{:S(2)}) %collective-permute-start.12) | collective-permute-done | bytes 65568 | tf_op jit(solution)/shard_map/ppermute | solution.py:103
  97.7 5.5 %collective-permute-done.13 = bf16[2,16,2,512]{3,1,0,2:T(8,128)(2,1)S(1)} collective-permute-done((bf16[2,16,2,512]{3,1,0,2:T(8,128)(2,1)S(1)}, bf16[2,16,2,512]{3,1,0,2:T(8,128)(2,1)S(1)}, u32[]{:S(2)}, u32[]{:S(2)}) %collective-permute-start.13) | collective-permute-done | bytes 65568 | tf_op jit(solution)/shard_map/ppermute | solution.py:103
  103.2 5.3 %collective-permute-done.14 = bf16[2,16,2,512]{3,1,0,2:T(8,128)(2,1)S(1)} collective-permute-done((bf16[2,16,2,512]{3,1,0,2:T(8,128)(2,1)S(1)}, bf16[2,16,2,512]{3,1,0,2:T(8,128)(2,1)S(1)}, u32[]{:S(2)}, u32[]{:S(2)}) %collective-permute-start.14) | collective-permute-done | bytes 65568 | tf_op jit(solution)/shard_map/ppermute | solution.py:103
  108.5 0.0 collective-permute-start.15
  108.5 5.8 %collective-permute-done.15 = bf16[2,16,2,512]{3,1,0,2:T(8,128)(2,1)S(1)} collective-permute-done((bf16[2,16,2,512]{3,1,0,2:T(8,128)(2,1)S(1)}, bf16[2,16,2,512]{3,1,0,2:T(8,128)(2,1)S(1)}, u32[]{:S(2)}, u32[]{:S(2)}) %collective-permute-start.15) | collective-permute-done | bytes 65568 | tf_op jit(solution)/shard_map/ppermute | solution.py:103
  114.3 4.9 %collective-permute-done.16 = bf16[2,16,2,512]{3,1,0,2:T(8,128)(2,1)S(1)} collective-permute-done((bf16[2,16,2,512]{3,1,0,2:T(8,128)(2,1)S(1)}, bf16[2,16,2,512]{3,1,0,2:T(8,128)(2,1)S(1)}, u32[]{:S(2)}, u32[]{:S(2)}) %collective-permute-start.16) | collective-permute-done | bytes 65568 | tf_op jit(solution)/shard_map/ppermute | solution.py:103
  119.2 0.6 collective-permute-start.17
  119.8 3.4 %collective-permute-done.17 = bf16[2,16,2,512]{3,1,0,2:T(8,128)(2,1)S(1)} collective-permute-done((bf16[2,16,2,512]{3,1,0,2:T(8,128)(2,1)S(1)}, bf16[2,16,2,512]{3,1,0,2:T(8,128)(2,1)S(1)}, u32[]{:S(2)}, u32[]{:S(2)}) %collective-permute-start.17) | collective-permute-done | bytes 65568 | tf_op jit(solution)/shard_map/ppermute | solution.py:103
  123.2 4.0 %collective-permute-start.18 = (bf16[2,16,2,512]{3,1,0,2:T(8,128)(2,1)S(1)}, bf16[2,16,2,512]{3,1,0,2:T(8,128)(2,1)S(1)}, u32[]{:S(2)}, u32[]{:S(2)}) collective-permute-start(bf16[2,16,2,512]{3,1,0,2:T(8,128)(2,1)S(1)} %constant_dynamic-update-slice_fusion.20), channel_id=1, source_target_pairs={{0,192},{16,208},{32,224},{48,240},{64,0},{80,16},{96,32},{112,48}... | collective-permute-start | bytes 196616 | tf_op jit(solution)/shard_map/ppermute | solution.py:103
  127.3 1.3 collective-permute-done.18
  128.6 0.0 collective-permute-start.19
  128.6 5.0 %collective-permute-done.19 = bf16[2,16,2,512]{3,1,0,2:T(8,128)(2,1)S(1)} collective-permute-done((bf16[2,16,2,512]{3,1,0,2:T(8,128)(2,1)S(1)}, bf16[2,16,2,512]{3,1,0,2:T(8,128)(2,1)S(1)}, u32[]{:S(2)}, u32[]{:S(2)}) %collective-permute-start.19) | collective-permute-done | bytes 65568 | tf_op jit(solution)/shard_map/ppermute | solution.py:103
  133.6 1.3 collective-permute-start.20
  134.9 3.4 %collective-permute-done.20 = bf16[2,16,2,512]{3,1,0,2:T(8,128)(2,1)S(1)} collective-permute-done((bf16[2,16,2,512]{3,1,0,2:T(8,128)(2,1)S(1)}, bf16[2,16,2,512]{3,1,0,2:T(8,128)(2,1)S(1)}, u32[]{:S(2)}, u32[]{:S(2)}) %collective-permute-start.20) | collective-permute-done | bytes 65568 | tf_op jit(solution)/shard_map/ppermute | solution.py:103
  138.3 0.0 collective-permute-done.21
  138.4 13.2 %collective-permute-start.22 = (bf16[2,256,2,512]{3,1,0,2:T(8,128)(2,1)S(1)}, bf16[2,256,2,512]{3,1,0,2:T(8,128)(2,1)S(1)}, u32[]{:S(2)}, u32[]{:S(2)}) collective-permute-start(bf16[2,256,2,512]{3,1,0,2:T(8,128)(2,1)S(1)} %constant_dynamic-update-slice_fusion.4), channel_id=1, source_target_pairs={{0,1},{1,0},{2,3},{3,2},{4,5},{5,4},{6,7},{7,6},{8,9},{9,8},{10,11... | collective-permute-start | bytes 3145736 | tf_op jit(solution)/shard_map/ppermute | solution.py:103
  151.6 0.0 collective-permute-done.23
  151.7 0.2 broadcast_in_dim.46
  151.9 0.1 bitcast_dynamic-update-slice_fusion.1
  152.0 1.9 %collective-permute-done.22 = bf16[2,256,2,512]{3,1,0,2:T(8,128)(2,1)S(1)} collective-permute-done((bf16[2,256,2,512]{3,1,0,2:T(8,128)(2,1)S(1)}, bf16[2,256,2,512]{3,1,0,2:T(8,128)(2,1)S(1)}, u32[]{:S(2)}, u32[]{:S(2)}) %collective-permute-start.22) | collective-permute-done | bytes 1048608 | tf_op jit(solution)/shard_map/ppermute | solution.py:103
  153.9 0.1 bitcast_dynamic-update-slice_fusion
  154.0 0.6 broadcast_in_dim.53
  154.5 0.4 slice_bitcast_fusion.1
  155.0 3.2 %add_reduce_fusion = (bf16[256,4,512]{2,0,1:T(8,128)(2,1)S(1)}, bf16[256,4,512]{2,0,1:T(8,128)(2,1)S(1)}) fusion(f32[4,4,512]{2,1,0:T(4,128)S(1)} %get-tuple-element.12, f32[4,256,512]{2,1,0:T(8,128)S(1)} %get-tuple-element.10, f32[4,4,512]{2,1,0:T(4,128)S(1)} %get-tuple-element.11, f32[4,256,512]{2,1,0:T(8,128)S(1)} %get-tuple-element.9), kind=kLoop, calls=%fused_computation.2 | loop fusion | flops 15728640 | bytes 6356992 | tf_op jit(solution)/shard_map/reduce_sum | solution.py:65
  158.2 0.3 pad_maximum_fusion
  158.5 1.6 copy.15
  160.1 2.1 %convert_element_type.13.lhs_ref = bf16[1024,1024]{1,0:T(8,128)(2,1)} reshape(bf16[256,4,1024]{2,1,0:T(4,128)(2,1)S(1)} %copy.15) | data formatting | bytes 4194304 | tf_op jit(solution)/shard_map/convert_element_type | solution.py:68
  162.2 10.7 %shard_map.46 = f32[256,4,2048]{2,1,0:T(4,128)} custom-call(bf16[1024,1024]{1,0:T(8,128)(2,1)} %convert_element_type.13.lhs_ref, bf16[1024,2048]{1,0:T(8,128)(2,1)} %constant.889.clone.w_ref), custom_call_target="tpu_custom_call" | custom-call | tf_op jit(solution)/shard_map/pallas_call | solution.py:82
  (45 shorter events, 0.5 us)
Async XLA Ops:
  0.0 1.5 copy-start
  10.4 44.6 %collective-permute-start.6 = (bf16[1,4,2,512]{3,2,1,0:T(2,128)(2,1)S(1)}, bf16[1,4,2,512]{3,2,1,0:T(2,128)(2,1)S(1)}, u32[]{:S(2)}, u32[]{:S(2)}) collective-permute-start(bf16[1,4,2,512]{3,2,1,0:T(2,128)(2,1)S(1)} %broadcast_select_fusion), channel_id=1, source_target_pairs={{0,14},{2,0},{4,2},{6,4},{8,6},{10,8},{12,10},{14,12},{1,15},{3,1}... | collective-permute-start | bytes 24584 | tf_op jit(solution)/shard_map/ppermute | solution.py:103
  20.4 34.6 %collective-permute-start.5 = (bf16[1,4,2,512]{3,2,1,0:T(2,128)(2,1)S(1)}, bf16[1,4,2,512]{3,2,1,0:T(2,128)(2,1)S(1)}, u32[]{:S(2)}, u32[]{:S(2)}) collective-permute-start(bf16[1,4,2,512]{3,2,1,0:T(2,128)(2,1)S(1)} %broadcast_select_fusion), channel_id=1, source_target_pairs={{0,12},{2,14},{4,0},{6,2},{8,4},{10,6},{12,8},{14,10},{1,13},{3,15... | collective-permute-start | bytes 24584 | tf_op jit(solution)/shard_map/ppermute | solution.py:103
  20.9 31.7 %collective-permute-start.4 = (bf16[1,4,2,512]{3,2,1,0:T(2,128)(2,1)S(1)}, bf16[1,4,2,512]{3,2,1,0:T(2,128)(2,1)S(1)}, u32[]{:S(2)}, u32[]{:S(2)}) collective-permute-start(bf16[1,4,2,512]{3,2,1,0:T(2,128)(2,1)S(1)} %broadcast_select_fusion), channel_id=1, source_target_pairs={{0,10},{2,12},{4,14},{6,0},{8,2},{10,4},{12,6},{14,8},{1,11},{3,13... | collective-permute-start | bytes 24584 | tf_op jit(solution)/shard_map/ppermute | solution.py:103
  21.0 28.5 %collective-permute-start.3 = (bf16[1,4,2,512]{3,2,1,0:T(2,128)(2,1)S(1)}, bf16[1,4,2,512]{3,2,1,0:T(2,128)(2,1)S(1)}, u32[]{:S(2)}, u32[]{:S(2)}) collective-permute-start(bf16[1,4,2,512]{3,2,1,0:T(2,128)(2,1)S(1)} %broadcast_select_fusion), channel_id=1, source_target_pairs={{0,8},{2,10},{4,12},{6,14},{8,0},{10,2},{12,4},{14,6},{1,9},{3,11}... | collective-permute-start | bytes 24584 | tf_op jit(solution)/shard_map/ppermute | solution.py:103
  23.4 8.5 %collective-permute-start = (bf16[1,4,2,512]{3,2,1,0:T(2,128)(2,1)S(1)}, bf16[1,4,2,512]{3,2,1,0:T(2,128)(2,1)S(1)}, u32[]{:S(2)}, u32[]{:S(2)}) collective-permute-start(bf16[1,4,2,512]{3,2,1,0:T(2,128)(2,1)S(1)} %broadcast_select_fusion), channel_id=1, source_target_pairs={{0,2},{2,4},{4,6},{6,8},{8,10},{10,12},{12,14},{14,0},{1,3},{3,5},... | collective-permute-start | bytes 24584 | tf_op jit(solution)/shard_map/ppermute | solution.py:103
  31.9 3.7 %collective-permute-start.1 = (bf16[1,4,2,512]{3,2,1,0:T(2,128)(2,1)S(1)}, bf16[1,4,2,512]{3,2,1,0:T(2,128)(2,1)S(1)}, u32[]{:S(2)}, u32[]{:S(2)}) collective-permute-start(bf16[1,4,2,512]{3,2,1,0:T(2,128)(2,1)S(1)} %broadcast_select_fusion), channel_id=1, source_target_pairs={{0,4},{2,6},{4,8},{6,10},{8,12},{10,14},{12,0},{14,2},{1,5},{3,7},... | collective-permute-start | bytes 24584 | tf_op jit(solution)/shard_map/ppermute | solution.py:103
  35.7 8.8 %collective-permute-start.2 = (bf16[1,4,2,512]{3,2,1,0:T(2,128)(2,1)S(1)}, bf16[1,4,2,512]{3,2,1,0:T(2,128)(2,1)S(1)}, u32[]{:S(2)}, u32[]{:S(2)}) collective-permute-start(bf16[1,4,2,512]{3,2,1,0:T(2,128)(2,1)S(1)} %broadcast_select_fusion), channel_id=1, source_target_pairs={{0,6},{2,8},{4,10},{6,12},{8,14},{10,0},{12,2},{14,4},{1,7},{3,9},... | collective-permute-start | bytes 24584 | tf_op jit(solution)/shard_map/ppermute | solution.py:103
  44.5 107.2 %collective-permute-start.25 = (bf16[4,2,512]{2,0,1:T(4,128)(2,1)S(1)}, bf16[4,2,512]{2,0,1:T(4,128)(2,1)S(1)}, u32[]{:S(2)}, u32[]{:S(2)}) collective-permute-start(bf16[4,2,512]{2,0,1:T(4,128)(2,1)S(1)} %get-tuple-element.13), channel_id=1, source_target_pairs={{0,3},{1,0},{2,1},{3,2},{4,7},{5,4},{6,5},{7,6},{8,11},{9,8},{10,9... | collective-permute-start | bytes 24584 | tf_op jit(solution)/shard_map/ppermute | solution.py:131
  49.5 102.1 %collective-permute-start.23 = (bf16[4,2,512]{2,0,1:T(4,128)(2,1)S(1)}, bf16[4,2,512]{2,0,1:T(4,128)(2,1)S(1)}, u32[]{:S(2)}, u32[]{:S(2)}) collective-permute-start(bf16[4,2,512]{2,0,1:T(4,128)(2,1)S(1)} %get-tuple-element.14), channel_id=1, source_target_pairs={{0,1},{1,2},{2,3},{3,0},{4,5},{5,6},{6,7},{7,4},{8,9},{9,10},{10,1... | collective-permute-start | bytes 24584 | tf_op jit(solution)/shard_map/ppermute | solution.py:131
  52.6 99.0 %collective-permute-start.24 = (bf16[4,2,512]{2,0,1:T(4,128)(2,1)S(1)}, bf16[4,2,512]{2,0,1:T(4,128)(2,1)S(1)}, u32[]{:S(2)}, u32[]{:S(2)}) collective-permute-start(bf16[4,2,512]{2,0,1:T(4,128)(2,1)S(1)} %get-tuple-element.15), channel_id=1, source_target_pairs={{0,2},{1,3},{2,0},{3,1},{4,6},{5,7},{6,4},{7,5},{8,10},{9,11},{10,... | collective-permute-start | bytes 24584 | tf_op jit(solution)/shard_map/ppermute | solution.py:131
  55.0 83.4 %collective-permute-start.21 = (bf16[2,16,2,512]{3,1,0,2:T(8,128)(2,1)S(1)}, bf16[2,16,2,512]{3,1,0,2:T(8,128)(2,1)S(1)}, u32[]{:S(2)}, u32[]{:S(2)}) collective-permute-start(bf16[2,16,2,512]{3,1,0,2:T(8,128)(2,1)S(1)} %constant_dynamic-update-slice_fusion.20), channel_id=1, source_target_pairs={{0,240},{16,0},{32,16},{48,32},{64,48},{80,64},{96,80},{112,96},{1... | collective-permute-start | bytes 196616 | tf_op jit(solution)/shard_map/ppermute | solution.py:103
  60.5 7.0 %collective-permute-start.7 = (bf16[2,16,2,512]{3,1,0,2:T(8,128)(2,1)S(1)}, bf16[2,16,2,512]{3,1,0,2:T(8,128)(2,1)S(1)}, u32[]{:S(2)}, u32[]{:S(2)}) collective-permute-start(bf16[2,16,2,512]{3,1,0,2:T(8,128)(2,1)S(1)} %constant_dynamic-update-slice_fusion.20), channel_id=1, source_target_pairs={{0,16},{16,32},{32,48},{48,64},{64,80},{80,96},{96,112},{112,128},... | collective-permute-start | bytes 196616 | tf_op jit(solution)/shard_map/ppermute | solution.py:103
  67.5 6.1 %collective-permute-start.8 = (bf16[2,16,2,512]{3,1,0,2:T(8,128)(2,1)S(1)}, bf16[2,16,2,512]{3,1,0,2:T(8,128)(2,1)S(1)}, u32[]{:S(2)}, u32[]{:S(2)}) collective-permute-start(bf16[2,16,2,512]{3,1,0,2:T(8,128)(2,1)S(1)} %constant_dynamic-update-slice_fusion.20), channel_id=1, source_target_pairs={{0,32},{16,48},{32,64},{48,80},{64,96},{80,112},{96,128},{112,144}... | collective-permute-start | bytes 196616 | tf_op jit(solution)/shard_map/ppermute | solution.py:103
  73.7 5.9 %collective-permute-start.9 = (bf16[2,16,2,512]{3,1,0,2:T(8,128)(2,1)S(1)}, bf16[2,16,2,512]{3,1,0,2:T(8,128)(2,1)S(1)}, u32[]{:S(2)}, u32[]{:S(2)}) collective-permute-start(bf16[2,16,2,512]{3,1,0,2:T(8,128)(2,1)S(1)} %constant_dynamic-update-slice_fusion.20), channel_id=1, source_target_pairs={{0,48},{16,64},{32,80},{48,96},{64,112},{80,128},{96,144},{112,160... | collective-permute-start | bytes 196616 | tf_op jit(solution)/shard_map/ppermute | solution.py:103
  79.6 4.3 %collective-permute-start.10 = (bf16[2,16,2,512]{3,1,0,2:T(8,128)(2,1)S(1)}, bf16[2,16,2,512]{3,1,0,2:T(8,128)(2,1)S(1)}, u32[]{:S(2)}, u32[]{:S(2)}) collective-permute-start(bf16[2,16,2,512]{3,1,0,2:T(8,128)(2,1)S(1)} %constant_dynamic-update-slice_fusion.20), channel_id=1, source_target_pairs={{0,64},{16,80},{32,96},{48,112},{64,128},{80,144},{96,160},{112,17... | collective-permute-start | bytes 196616 | tf_op jit(solution)/shard_map/ppermute | solution.py:103
  83.9 7.3 %collective-permute-start.11 = (bf16[2,16,2,512]{3,1,0,2:T(8,128)(2,1)S(1)}, bf16[2,16,2,512]{3,1,0,2:T(8,128)(2,1)S(1)}, u32[]{:S(2)}, u32[]{:S(2)}) collective-permute-start(bf16[2,16,2,512]{3,1,0,2:T(8,128)(2,1)S(1)} %constant_dynamic-update-slice_fusion.20), channel_id=1, source_target_pairs={{0,80},{16,96},{32,112},{48,128},{64,144},{80,160},{96,176},{112,1... | collective-permute-start | bytes 196616 | tf_op jit(solution)/shard_map/ppermute | solution.py:103
  91.2 6.4 %collective-permute-start.12 = (bf16[2,16,2,512]{3,1,0,2:T(8,128)(2,1)S(1)}, bf16[2,16,2,512]{3,1,0,2:T(8,128)(2,1)S(1)}, u32[]{:S(2)}, u32[]{:S(2)}) collective-permute-start(bf16[2,16,2,512]{3,1,0,2:T(8,128)(2,1)S(1)} %constant_dynamic-update-slice_fusion.20), channel_id=1, source_target_pairs={{0,96},{16,112},{32,128},{48,144},{64,160},{80,176},{96,192},{112,... | collective-permute-start | bytes 196616 | tf_op jit(solution)/shard_map/ppermute | solution.py:103
  97.7 5.5 %collective-permute-start.13 = (bf16[2,16,2,512]{3,1,0,2:T(8,128)(2,1)S(1)}, bf16[2,16,2,512]{3,1,0,2:T(8,128)(2,1)S(1)}, u32[]{:S(2)}, u32[]{:S(2)}) collective-permute-start(bf16[2,16,2,512]{3,1,0,2:T(8,128)(2,1)S(1)} %constant_dynamic-update-slice_fusion.20), channel_id=1, source_target_pairs={{0,112},{16,128},{32,144},{48,160},{64,176},{80,192},{96,208},{112... | collective-permute-start | bytes 196616 | tf_op jit(solution)/shard_map/ppermute | solution.py:103
  103.2 5.3 %collective-permute-start.14 = (bf16[2,16,2,512]{3,1,0,2:T(8,128)(2,1)S(1)}, bf16[2,16,2,512]{3,1,0,2:T(8,128)(2,1)S(1)}, u32[]{:S(2)}, u32[]{:S(2)}) collective-permute-start(bf16[2,16,2,512]{3,1,0,2:T(8,128)(2,1)S(1)} %constant_dynamic-update-slice_fusion.20), channel_id=1, source_target_pairs={{0,128},{16,144},{32,160},{48,176},{64,192},{80,208},{96,224},{112... | collective-permute-start | bytes 196616 | tf_op jit(solution)/shard_map/ppermute | solution.py:103
  108.5 5.8 %collective-permute-start.15 = (bf16[2,16,2,512]{3,1,0,2:T(8,128)(2,1)S(1)}, bf16[2,16,2,512]{3,1,0,2:T(8,128)(2,1)S(1)}, u32[]{:S(2)}, u32[]{:S(2)}) collective-permute-start(bf16[2,16,2,512]{3,1,0,2:T(8,128)(2,1)S(1)} %constant_dynamic-update-slice_fusion.20), channel_id=1, source_target_pairs={{0,144},{16,160},{32,176},{48,192},{64,208},{80,224},{96,240},{112... | collective-permute-start | bytes 196616 | tf_op jit(solution)/shard_map/ppermute | solution.py:103
  114.3 4.9 %collective-permute-start.16 = (bf16[2,16,2,512]{3,1,0,2:T(8,128)(2,1)S(1)}, bf16[2,16,2,512]{3,1,0,2:T(8,128)(2,1)S(1)}, u32[]{:S(2)}, u32[]{:S(2)}) collective-permute-start(bf16[2,16,2,512]{3,1,0,2:T(8,128)(2,1)S(1)} %constant_dynamic-update-slice_fusion.20), channel_id=1, source_target_pairs={{0,160},{16,176},{32,192},{48,208},{64,224},{80,240},{96,0},{112,1... | collective-permute-start | bytes 196616 | tf_op jit(solution)/shard_map/ppermute | solution.py:103
  119.2 4.0 %collective-permute-start.17 = (bf16[2,16,2,512]{3,1,0,2:T(8,128)(2,1)S(1)}, bf16[2,16,2,512]{3,1,0,2:T(8,128)(2,1)S(1)}, u32[]{:S(2)}, u32[]{:S(2)}) collective-permute-start(bf16[2,16,2,512]{3,1,0,2:T(8,128)(2,1)S(1)} %constant_dynamic-update-slice_fusion.20), channel_id=1, source_target_pairs={{0,176},{16,192},{32,208},{48,224},{64,240},{80,0},{96,16},{112,32... | collective-permute-start | bytes 196616 | tf_op jit(solution)/shard_map/ppermute | solution.py:103
  123.2 5.4 %collective-permute-start.18 = (bf16[2,16,2,512]{3,1,0,2:T(8,128)(2,1)S(1)}, bf16[2,16,2,512]{3,1,0,2:T(8,128)(2,1)S(1)}, u32[]{:S(2)}, u32[]{:S(2)}) collective-permute-start(bf16[2,16,2,512]{3,1,0,2:T(8,128)(2,1)S(1)} %constant_dynamic-update-slice_fusion.20), channel_id=1, source_target_pairs={{0,192},{16,208},{32,224},{48,240},{64,0},{80,16},{96,32},{112,48}... | collective-permute-start | bytes 196616 | tf_op jit(solution)/shard_map/ppermute | solution.py:103
  128.6 5.0 %collective-permute-start.19 = (bf16[2,16,2,512]{3,1,0,2:T(8,128)(2,1)S(1)}, bf16[2,16,2,512]{3,1,0,2:T(8,128)(2,1)S(1)}, u32[]{:S(2)}, u32[]{:S(2)}) collective-permute-start(bf16[2,16,2,512]{3,1,0,2:T(8,128)(2,1)S(1)} %constant_dynamic-update-slice_fusion.20), channel_id=1, source_target_pairs={{0,208},{16,224},{32,240},{48,0},{64,16},{80,32},{96,48},{112,64},... | collective-permute-start | bytes 196616 | tf_op jit(solution)/shard_map/ppermute | solution.py:103
  133.6 4.7 %collective-permute-start.20 = (bf16[2,16,2,512]{3,1,0,2:T(8,128)(2,1)S(1)}, bf16[2,16,2,512]{3,1,0,2:T(8,128)(2,1)S(1)}, u32[]{:S(2)}, u32[]{:S(2)}) collective-permute-start(bf16[2,16,2,512]{3,1,0,2:T(8,128)(2,1)S(1)} %constant_dynamic-update-slice_fusion.20), channel_id=1, source_target_pairs={{0,224},{16,240},{32,0},{48,16},{64,32},{80,48},{96,64},{112,80},{... | collective-permute-start | bytes 196616 | tf_op jit(solution)/shard_map/ppermute | solution.py:103
  138.4 15.5 %collective-permute-start.22 = (bf16[2,256,2,512]{3,1,0,2:T(8,128)(2,1)S(1)}, bf16[2,256,2,512]{3,1,0,2:T(8,128)(2,1)S(1)}, u32[]{:S(2)}, u32[]{:S(2)}) collective-permute-start(bf16[2,256,2,512]{3,1,0,2:T(8,128)(2,1)S(1)} %constant_dynamic-update-slice_fusion.4), channel_id=1, source_target_pairs={{0,1},{1,0},{2,3},{3,2},{4,5},{5,4},{6,7},{7,6},{8,9},{9,8},{10,11... | collective-permute-start | bytes 3145736 | tf_op jit(solution)/shard_map/ppermute | solution.py:103

commit v11 on v9

--- a/solution.py
+++ b/solution.py
@@ -59,36 +59,37 @@
     return normalize(jnp.dot(row_data, band_table(), preferred_element_type=jnp.float32))
 
 
-def cross_lhs(sources, receivers):
-    src = sources.astype(jnp.float32)[:, :, None]
-    rec = receivers.astype(jnp.float32)[:, None]
-    real_sum = jnp.sum(src[..., 0, :] * rec[..., 0, :] + src[..., 1, :] * rec[..., 1, :], axis=0)
-    imag_sum = jnp.sum(src[..., 1, :] * rec[..., 0, :] - src[..., 0, :] * rec[..., 1, :], axis=0)
-    lhs = jnp.concatenate([real_sum, imag_sum], axis=2).reshape(-1, 2 * NBINS)
-    return lhs.astype(jnp.bfloat16)
-
-
 SOURCE_BLOCK = 32
 
 
-def lag_kernel(lhs_ref, w_ref, o_ref, *, scale):
-    result = jnp.dot(lhs_ref[...], w_ref[...], preferred_element_type=jnp.float32) * scale
+def lag_kernel(src_ref, rec_ref, w_ref, o_ref, *, scale):
+    real_sum = 0.0
+    imag_sum = 0.0
+    for window in range(src_ref.shape[0]):
+        src = src_ref[window].astype(jnp.float32)[:, None]
+        rec = rec_ref[window].astype(jnp.float32)[None]
+        real_sum = real_sum + src[:, :, 0] * rec[:, :, 0] + src[:, :, 1] * rec[:, :, 1]
+        imag_sum = imag_sum + src[:, :, 1] * rec[:, :, 0] - src[:, :, 0] * rec[:, :, 1]
+    lhs = jnp.concatenate([real_sum, imag_sum], axis=2)
+    lhs = lhs.reshape(-1, lhs.shape[2]).astype(jnp.bfloat16)
+    result = jnp.dot(lhs, w_ref[...], preferred_element_type=jnp.float32) * scale
     o_ref[...] = result.reshape(o_ref.shape)
 
 
-def transform(lhs, weights, lag_scale, count_rec):
-    count_src = lhs.shape[0] // count_rec
-    rows = SOURCE_BLOCK * count_rec
+def cross_transform(sources, receivers, weights, lag_scale):
+    windows, count_src = sources.shape[0], sources.shape[1]
+    count_rec = receivers.shape[1]
     return pl.pallas_call(
         functools.partial(lag_kernel, scale=lag_scale),
         out_shape=jax.ShapeDtypeStruct((count_src, count_rec, 2 * MAXLAG), jnp.float32),
         grid=(count_src // SOURCE_BLOCK,),
         in_specs=[
-            pl.BlockSpec((rows, lhs.shape[1]), lambda i: (i, 0)),
+            pl.BlockSpec((windows, SOURCE_BLOCK, 2, NBINS), lambda i: (0, i, 0, 0)),
+            pl.BlockSpec(receivers.shape, lambda i: (0, 0, 0, 0)),
             pl.BlockSpec(weights.shape, lambda i: (0, 0)),
         ],
         out_specs=pl.BlockSpec((SOURCE_BLOCK, count_rec, 2 * MAXLAG), lambda i: (i, 0, 0)),
-    )(lhs, weights)
+    )(sources, receivers, weights)
 
 
 def ring_gather(value, axis_name, axis):
@@ -146,8 +147,7 @@
     own_rows = lax.dynamic_slice_in_dim(source_rows[0], shard * per_shard, per_shard)
     own_sources = jnp.take(whitened, own_rows, axis=1)
     sources = collect(own_sources)
-    lhs = cross_lhs(sources, receivers)
-    return transform(lhs, weights, lag_scale, receivers.shape[1])
+    return cross_transform(sources, receivers, weights, lag_scale)
 
 
 def split_mesh(mesh):

time: 78 us -> 85 us (1.090)
  starting transfers between devices: 30.7 us -> 36.2 us
  Pallas kernels: 10.7 us -> 15.2 us
  other arithmetic: 6.45 us -> 2.51 us
  local copies, waits for them, and re-layouts: 5.5 us -> 7.87 us
  waiting for transfers between devices: 16.4 us -> 15.4 us
    ppermute x11, starting transfers between devices: 20.2 us -> 25.9 us  [ring_gather(): lax.ppermute(value, axis_name, [(i, (i + shift) % size) for i in range(si...]
    pallas_call x1, Pallas kernels: 10.7 us -> 15.2 us  [cross_transform(): pl.pallas_call(functools.partial(lag_kernel, scale=lag_scale), out_shape=...]
    dynamic_update_slice x16 -> x15, local copies, waits for them, and re-layouts: 0.41 us -> 3.98 us  [ring_gather(): out = lax.dynamic_update_slice(out, part, start)]
    reduce_sum x1 -> x0, other arithmetic: 3.15 us -> none  [cross_lhs(): jnp.sum(src[..., 0, :] * rec[..., 0, :] + src[..., 1, :] * rec[..., 1, :]...]
    ppermute x11, waiting for transfers between devices: 16.3 us -> 13.6 us  [ring_gather(): lax.ppermute(value, axis_name, [(i, (i + shift) % size) for i in range(si...]
    convert_element_type x1 -> x0, local copies, waits for them, and re-layouts: 2.05 us -> none  [cross_lhs(): return lhs.astype(jnp.bfloat16)]
    ppermute x3, waiting for transfers between devices: 0.01 us -> 1.78 us  [exchange_receivers(): lax.ppermute(block, WIN_AXES, [(i, (i + shift) % count) for i in range(co...]
    broadcast_in_dim x4 -> x5, local copies, waits for them, and re-layouts: 0.11 us -> 1.81 us  [ring_gather(): out = jnp.zeros(shape, value.dtype)]
  transfers between devices with their start and end apart: 14 -> 14, of which waited for: 6 -> 6; matrix products, arithmetic and copies ran while one was open for 1% -> 4% of each run, Pallas kernels for 0% -> 0%
where the time goes in v11:
time: 85 us; the launch traced here: 84.9 us
  starting transfers between devices  36.2 us (43%)
  waiting for transfers between devices  15.4 us (18%)
  Pallas kernels  15.2 us (18%)
  local copies, waits for them, and re-layouts  7.87 us (9%)
  matrix products  7.3 us (9%)
  other arithmetic  2.51 us (3%)
    ppermute x11, starting transfers between devices, ring_gather(): lax.ppermute(value, axis_name, [(i, (i + shift) % size) for i in range(si...  25.9 us
    pallas_call x1, Pallas kernels, cross_transform(): pl.pallas_call(functools.partial(lag_kernel, scale=lag_scale), out_shape=...  15.2 us
    ppermute x11, waiting for transfers between devices, ring_gather(): lax.ppermute(value, axis_name, [(i, (i + shift) % size) for i in range(si...  13.6 us
    ppermute x3, starting transfers between devices, exchange_receivers(): lax.ppermute(block, WIN_AXES, [(i, (i + shift) % count) for i in range(co...  10.3 us
    dot_general x1, matrix products, whiten(): jnp.dot(row_data, band_table(), preferred_element_type=jnp.float32)  7.3 us
    dynamic_update_slice x15, local copies, waits for them, and re-layouts, ring_gather(): out = lax.dynamic_update_slice(out, part, start)  3.98 us
    broadcast_in_dim x5, local copies, waits for them, and re-layouts, ring_gather(): out = jnp.zeros(shape, value.dtype)  1.81 us
    ppermute x3, waiting for transfers between devices, exchange_receivers(): lax.ppermute(block, WIN_AXES, [(i, (i + shift) % count) for i in range(co...  1.78 us
  transfers between devices with their start and end apart: 14, of which 6 were waited for; matrix products, arithmetic and copies ran while one was open for 4% of the time, Pallas kernels for 0%

profile of v11, /device:TPU:1, one launch (start us, length us, event | category | flops | bytes accessed | tf_op | source)
XLA Modules:
  0.0 84.9 jit_solution(9316657121692759615)
XLA Ops:
  0.0 0.0 copy-start
  0.0 0.8 fusion.8
  0.8 0.7 compare_and_fusion
  1.5 0.0 copy-done
  1.5 7.3 %convolution_bitcast_fusion = f32[16,1152]{1,0:T(8,128)S(1)} fusion(bf16[7680,1152]{1,0:T(8,128)(2,1)} %constant.232.clone, bf16[1,16,7680]{2,1,0:T(8,128)(2,1)S(1)} %copy-done), kind=kOutput, calls=%fused_computation.1 | convolution fusion | flops 283115520 | bytes 18014208 | tf_op jit(solution)/shard_map/dot_general | solution.py:59
  8.8 0.1 fusion.2
  8.9 0.6 fusion.6
  9.6 0.1 fusion.3
  9.7 0.6 gather_fusion
  10.3 0.1 constant_dynamic-update-slice_fusion.15
  10.4 7.8 %collective-permute-start = (bf16[1,4,2,512]{3,2,1,0:T(2,128)(2,1)S(1)}, bf16[1,4,2,512]{3,2,1,0:T(2,128)(2,1)S(1)}, u32[]{:S(2)}, u32[]{:S(2)}) collective-permute-start(bf16[1,4,2,512]{3,2,1,0:T(2,128)(2,1)S(1)} %get-tuple-element.6), channel_id=1, source_target_pairs={{0,2},{2,0},{1,3},{3,1},{4,6},{6,4},{5,7},{7,5},{8,10},{10,8},{9,1... | collective-permute-start | bytes 24584 | tf_op jit(solution)/shard_map/ppermute | solution.py:103
  18.2 1.0 %collective-permute-done = bf16[1,4,2,512]{3,2,1,0:T(2,128)(2,1)S(1)} collective-permute-done((bf16[1,4,2,512]{3,2,1,0:T(2,128)(2,1)S(1)}, bf16[1,4,2,512]{3,2,1,0:T(2,128)(2,1)S(1)}, u32[]{:S(2)}, u32[]{:S(2)}) %collective-permute-start) | collective-permute-done | bytes 8224 | tf_op jit(solution)/shard_map/ppermute | solution.py:103
  19.3 2.6 %collective-permute-start.3 = (bf16[2,4,2,512]{3,2,1,0:T(2,128)(2,1)S(1)}, bf16[2,4,2,512]{3,2,1,0:T(2,128)(2,1)S(1)}, u32[]{:S(2)}, u32[]{:S(2)}) collective-permute-start(bf16[2,4,2,512]{3,2,1,0:T(2,128)(2,1)S(1)} %constant_dynamic-update-slice_fusion.14), channel_id=1, source_target_pairs={{0,12},{4,0},{8,4},{12,8},{1,13},{5,1},{9,5},{13,9},{2,14},{6,2},{... | collective-permute-start | bytes 49160 | tf_op jit(solution)/shard_map/ppermute | solution.py:103
  21.8 0.5 collective-permute-start.2
  22.3 0.6 collective-permute-start.1
  23.0 3.1 %collective-permute-done.1 = bf16[2,4,2,512]{3,2,1,0:T(2,128)(2,1)S(1)} collective-permute-done((bf16[2,4,2,512]{3,2,1,0:T(2,128)(2,1)S(1)}, bf16[2,4,2,512]{3,2,1,0:T(2,128)(2,1)S(1)}, u32[]{:S(2)}, u32[]{:S(2)}) %collective-permute-start.1) | collective-permute-done | bytes 16416 | tf_op jit(solution)/shard_map/ppermute | solution.py:103
  26.2 0.0 collective-permute-done.2
  26.2 0.0 collective-permute-done.3
  26.2 2.9 %collective-permute-start.6 = (bf16[2,16,2,512]{3,2,1,0:T(2,128)(2,1)S(1)}, bf16[2,16,2,512]{3,2,1,0:T(2,128)(2,1)S(1)}, u32[]{:S(2)}, u32[]{:S(2)}) collective-permute-start(bf16[2,16,2,512]{3,2,1,0:T(2,128)(2,1)S(1)} %constant_dynamic-update-slice_fusion.10), channel_id=1, source_target_pairs={{0,48},{16,0},{32,16},{48,32},{1,49},{17,1},{33,17},{49,33},{2,50}... | collective-permute-start | bytes 196616 | tf_op jit(solution)/shard_map/ppermute | solution.py:103
  29.1 0.0 collective-permute-start.5
  29.1 0.4 collective-permute-start.4
  29.5 0.1 broadcast_in_dim.42
  29.6 0.1 constant_dynamic-update-slice_fusion.9
  29.7 4.5 %collective-permute-done.4 = bf16[2,16,2,512]{3,2,1,0:T(2,128)(2,1)S(1)} collective-permute-done((bf16[2,16,2,512]{3,2,1,0:T(2,128)(2,1)S(1)}, bf16[2,16,2,512]{3,2,1,0:T(2,128)(2,1)S(1)}, u32[]{:S(2)}, u32[]{:S(2)}) %collective-permute-start.4) | collective-permute-done | bytes 65568 | tf_op jit(solution)/shard_map/ppermute | solution.py:103
  34.2 0.1 constant_dynamic-update-slice_fusion.8
  34.3 0.0 collective-permute-done.5
  34.3 0.1 constant_dynamic-update-slice_fusion.7
  34.4 0.0 collective-permute-done.6
  34.4 0.1 constant_dynamic-update-slice_fusion.6
  34.5 1.4 %collective-permute-start.7 = (bf16[2,64,2,512]{3,2,1,0:T(2,128)(2,1)S(1)}, bf16[2,64,2,512]{3,2,1,0:T(2,128)(2,1)S(1)}, u32[]{:S(2)}, u32[]{:S(2)}) collective-permute-start(bf16[2,64,2,512]{3,2,1,0:T(2,128)(2,1)S(1)} %constant_dynamic-update-slice_fusion.6), channel_id=1, source_target_pairs={{0,64},{64,128},{128,192},{192,0},{1,65},{65,129},{129,193},{193,1... | collective-permute-start | bytes 786440 | tf_op jit(solution)/shard_map/ppermute | solution.py:103
  35.8 2.6 %collective-permute-start.8 = (bf16[2,64,2,512]{3,2,1,0:T(2,128)(2,1)S(1)}, bf16[2,64,2,512]{3,2,1,0:T(2,128)(2,1)S(1)}, u32[]{:S(2)}, u32[]{:S(2)}) collective-permute-start(bf16[2,64,2,512]{3,2,1,0:T(2,128)(2,1)S(1)} %constant_dynamic-update-slice_fusion.6), channel_id=1, source_target_pairs={{0,128},{64,192},{128,0},{192,64},{1,129},{65,193},{129,1},{193,65... | collective-permute-start | bytes 786440 | tf_op jit(solution)/shard_map/ppermute | solution.py:103
  38.5 1.1 %collective-permute-start.9 = (bf16[2,64,2,512]{3,2,1,0:T(2,128)(2,1)S(1)}, bf16[2,64,2,512]{3,2,1,0:T(2,128)(2,1)S(1)}, u32[]{:S(2)}, u32[]{:S(2)}) collective-permute-start(bf16[2,64,2,512]{3,2,1,0:T(2,128)(2,1)S(1)} %constant_dynamic-update-slice_fusion.6), channel_id=1, source_target_pairs={{0,192},{64,0},{128,64},{192,128},{1,193},{65,1},{129,65},{193,129... | collective-permute-start | bytes 786440 | tf_op jit(solution)/shard_map/ppermute | solution.py:103
  39.5 0.5 broadcast_in_dim.41
  40.1 0.2 constant_dynamic-update-slice_fusion.5
  40.3 0.8 collective-permute-done.7
  41.0 0.2 constant_dynamic-update-slice_fusion.4
  41.2 4.1 %collective-permute-done.8 = bf16[2,64,2,512]{3,2,1,0:T(2,128)(2,1)S(1)} collective-permute-done((bf16[2,64,2,512]{3,2,1,0:T(2,128)(2,1)S(1)}, bf16[2,64,2,512]{3,2,1,0:T(2,128)(2,1)S(1)}, u32[]{:S(2)}, u32[]{:S(2)}) %collective-permute-start.8) | collective-permute-done | bytes 262176 | tf_op jit(solution)/shard_map/ppermute | solution.py:103
  45.4 0.2 constant_dynamic-update-slice_fusion.3
  45.6 0.0 collective-permute-done.9
  45.6 0.2 constant_dynamic-update-slice_fusion.2
  45.8 6.1 %collective-permute-start.10 = (bf16[2,256,2,512]{3,2,1,0:T(2,128)(2,1)S(1)}, bf16[2,256,2,512]{3,2,1,0:T(2,128)(2,1)}, u32[]{:S(2)}, u32[]{:S(2)}) collective-permute-start(bf16[2,256,2,512]{3,2,1,0:T(2,128)(2,1)S(1)} %constant_dynamic-update-slice_fusion.2), channel_id=1, source_target_pairs={{0,1},{1,0},{2,3},{3,2},{4,5},{5,4},{6,7},{7,6},{8,9},{9,8},{10,11... | collective-permute-start | bytes 3145736 | tf_op jit(solution)/shard_map/ppermute | solution.py:103
  51.9 0.1 dynamic-slice_maximum_fusion
  52.0 0.3 collective-permute-start.13
  52.3 5.6 %collective-permute-start.11 = (bf16[4,2,512]{2,1,0:T(2,128)(2,1)S(1)}, bf16[4,2,512]{2,1,0:T(2,128)(2,1)S(1)}, u32[]{:S(2)}, u32[]{:S(2)}) collective-permute-start(bf16[4,2,512]{2,1,0:T(2,128)(2,1)S(1)} %get-tuple-element.10), channel_id=1, source_target_pairs={{0,1},{1,2},{2,3},{3,0},{4,5},{5,6},{6,7},{7,4},{8,9},{9,10},{10,1... | collective-permute-start | bytes 24584 | tf_op jit(solution)/shard_map/ppermute | solution.py:128
  57.9 4.4 %collective-permute-start.12 = (bf16[4,2,512]{2,1,0:T(2,128)(2,1)S(1)}, bf16[4,2,512]{2,1,0:T(2,128)(2,1)S(1)}, u32[]{:S(2)}, u32[]{:S(2)}) collective-permute-start(bf16[4,2,512]{2,1,0:T(2,128)(2,1)S(1)} %get-tuple-element.11), channel_id=1, source_target_pairs={{0,2},{1,3},{2,0},{3,1},{4,6},{5,7},{6,4},{7,5},{8,10},{9,11},{10,... | collective-permute-start | bytes 24584 | tf_op jit(solution)/shard_map/ppermute | solution.py:128
  62.5 0.0 collective-permute-done.11
  62.5 1.8 %collective-permute-done.12 = bf16[4,2,512]{2,1,0:T(2,128)(2,1)S(1)} collective-permute-done((bf16[4,2,512]{2,1,0:T(2,128)(2,1)S(1)}, bf16[4,2,512]{2,1,0:T(2,128)(2,1)S(1)}, u32[]{:S(2)}, u32[]{:S(2)}) %collective-permute-start.12) | collective-permute-done | bytes 8224 | tf_op jit(solution)/shard_map/ppermute | solution.py:128
  64.3 0.0 collective-permute-done.13
  64.4 0.0 copy-start.2
  64.4 1.1 %broadcast_in_dim.40 = bf16[4,256,2,512]{3,2,1,0:T(2,128)(2,1)S(1)} broadcast(bf16[]{:T(256)} %constant.211.clone.1), dimensions={} | broadcast | bytes 2097154 | tf_op jit(solution)/shard_map/broadcast_in_dim | solution.py:101
  65.5 0.8 constant_dynamic-update-slice_fusion.1
  66.2 0.0 copy-done.2
  66.3 0.0 collective-permute-done.10
  66.3 2.0 %constant_dynamic-update-slice_fusion.src_ref = bf16[4,256,2,512]{3,2,1,0:T(2,128)(2,1)S(1)} fusion(bf16[4,256,2,512]{3,2,1,0:T(2,128)(2,1)S(1)} %constant_dynamic-update-slice_fusion.1, bf16[2,256,2,512]{3,2,1,0:T(2,128)(2,1)} %collective-permute-done.10, s32[]{:T(128)S(6)} %select_n.264), kind=kLoop, calls=%fused_computation.87 | loop fusion | bytes 2097156 | tf_op jit(solution)/shard_map/dynamic_update_slice | solution.py:108
  68.3 0.0 copy-start.1
  68.3 1.3 %copy-done.1 = bf16[4,256,2,512]{3,2,1,0:T(2,128)(2,1)} copy-done((bf16[4,256,2,512]{3,2,1,0:T(2,128)(2,1)}, bf16[4,256,2,512]{3,2,1,0:T(2,128)(2,1)S(1)}, u32[]{:S(2)}) %copy-start.1) | copy-done | bytes 2097176
  69.6 15.2 %shard_map.46 = f32[256,4,2048]{2,1,0:T(4,128)} custom-call(bf16[4,256,2,512]{3,2,1,0:T(2,128)(2,1)} %copy-done.1, bf16[4,4,2,512]{3,2,1,0:T(2,128)(2,1)} %copy-done.2, bf16[1024,2048]{1,0:T(8,128)(2,1)} %constant.233.clone.w_ref), custom_call_target="tpu_custom_call" | custom-call | tf_op jit(solution)/shard_map/pallas_call | solution.py:82
  (17 shorter events, 0.4 us)
Async XLA Ops:
  0.0 1.5 %copy-start = (bf16[1,16,7680]{2,1,0:T(8,128)(2,1)S(1)}, bf16[1,16,7680]{2,1,0:T(8,128)(2,1)}, u32[]{:S(2)}) copy-start(bf16[1,16,7680]{2,1,0:T(8,128)(2,1)} %param.4) | copy-start | bytes 737284
  10.4 8.9 %collective-permute-start = (bf16[1,4,2,512]{3,2,1,0:T(2,128)(2,1)S(1)}, bf16[1,4,2,512]{3,2,1,0:T(2,128)(2,1)S(1)}, u32[]{:S(2)}, u32[]{:S(2)}) collective-permute-start(bf16[1,4,2,512]{3,2,1,0:T(2,128)(2,1)S(1)} %get-tuple-element.6), channel_id=1, source_target_pairs={{0,2},{2,0},{1,3},{3,1},{4,6},{6,4},{5,7},{7,5},{8,10},{10,8},{9,1... | collective-permute-start | bytes 24584 | tf_op jit(solution)/shard_map/ppermute | solution.py:103
  19.3 6.9 %collective-permute-start.3 = (bf16[2,4,2,512]{3,2,1,0:T(2,128)(2,1)S(1)}, bf16[2,4,2,512]{3,2,1,0:T(2,128)(2,1)S(1)}, u32[]{:S(2)}, u32[]{:S(2)}) collective-permute-start(bf16[2,4,2,512]{3,2,1,0:T(2,128)(2,1)S(1)} %constant_dynamic-update-slice_fusion.14), channel_id=1, source_target_pairs={{0,12},{4,0},{8,4},{12,8},{1,13},{5,1},{9,5},{13,9},{2,14},{6,2},{... | collective-permute-start | bytes 49160 | tf_op jit(solution)/shard_map/ppermute | solution.py:103
  21.8 4.3 %collective-permute-start.2 = (bf16[2,4,2,512]{3,2,1,0:T(2,128)(2,1)S(1)}, bf16[2,4,2,512]{3,2,1,0:T(2,128)(2,1)S(1)}, u32[]{:S(2)}, u32[]{:S(2)}) collective-permute-start(bf16[2,4,2,512]{3,2,1,0:T(2,128)(2,1)S(1)} %constant_dynamic-update-slice_fusion.14), channel_id=1, source_target_pairs={{0,8},{4,12},{8,0},{12,4},{1,9},{5,13},{9,1},{13,5},{2,10},{6,14},... | collective-permute-start | bytes 49160 | tf_op jit(solution)/shard_map/ppermute | solution.py:103
  22.3 3.8 %collective-permute-start.1 = (bf16[2,4,2,512]{3,2,1,0:T(2,128)(2,1)S(1)}, bf16[2,4,2,512]{3,2,1,0:T(2,128)(2,1)S(1)}, u32[]{:S(2)}, u32[]{:S(2)}) collective-permute-start(bf16[2,4,2,512]{3,2,1,0:T(2,128)(2,1)S(1)} %constant_dynamic-update-slice_fusion.14), channel_id=1, source_target_pairs={{0,4},{4,8},{8,12},{12,0},{1,5},{5,9},{9,13},{13,1},{2,6},{6,10},{... | collective-permute-start | bytes 49160 | tf_op jit(solution)/shard_map/ppermute | solution.py:103
  26.2 8.1 %collective-permute-start.6 = (bf16[2,16,2,512]{3,2,1,0:T(2,128)(2,1)S(1)}, bf16[2,16,2,512]{3,2,1,0:T(2,128)(2,1)S(1)}, u32[]{:S(2)}, u32[]{:S(2)}) collective-permute-start(bf16[2,16,2,512]{3,2,1,0:T(2,128)(2,1)S(1)} %constant_dynamic-update-slice_fusion.10), channel_id=1, source_target_pairs={{0,48},{16,0},{32,16},{48,32},{1,49},{17,1},{33,17},{49,33},{2,50}... | collective-permute-start | bytes 196616 | tf_op jit(solution)/shard_map/ppermute | solution.py:103
  29.1 5.2 %collective-permute-start.5 = (bf16[2,16,2,512]{3,2,1,0:T(2,128)(2,1)S(1)}, bf16[2,16,2,512]{3,2,1,0:T(2,128)(2,1)S(1)}, u32[]{:S(2)}, u32[]{:S(2)}) collective-permute-start(bf16[2,16,2,512]{3,2,1,0:T(2,128)(2,1)S(1)} %constant_dynamic-update-slice_fusion.10), channel_id=1, source_target_pairs={{0,32},{16,48},{32,0},{48,16},{1,33},{17,49},{33,1},{49,17},{2,34}... | collective-permute-start | bytes 196616 | tf_op jit(solution)/shard_map/ppermute | solution.py:103
  29.1 5.1 %collective-permute-start.4 = (bf16[2,16,2,512]{3,2,1,0:T(2,128)(2,1)S(1)}, bf16[2,16,2,512]{3,2,1,0:T(2,128)(2,1)S(1)}, u32[]{:S(2)}, u32[]{:S(2)}) collective-permute-start(bf16[2,16,2,512]{3,2,1,0:T(2,128)(2,1)S(1)} %constant_dynamic-update-slice_fusion.10), channel_id=1, source_target_pairs={{0,16},{16,32},{32,48},{48,0},{1,17},{17,33},{33,49},{49,1},{2,18}... | collective-permute-start | bytes 196616 | tf_op jit(solution)/shard_map/ppermute | solution.py:103
  34.5 6.6 %collective-permute-start.7 = (bf16[2,64,2,512]{3,2,1,0:T(2,128)(2,1)S(1)}, bf16[2,64,2,512]{3,2,1,0:T(2,128)(2,1)S(1)}, u32[]{:S(2)}, u32[]{:S(2)}) collective-permute-start(bf16[2,64,2,512]{3,2,1,0:T(2,128)(2,1)S(1)} %constant_dynamic-update-slice_fusion.6), channel_id=1, source_target_pairs={{0,64},{64,128},{128,192},{192,0},{1,65},{65,129},{129,193},{193,1... | collective-permute-start | bytes 786440 | tf_op jit(solution)/shard_map/ppermute | solution.py:103
  35.8 9.5 %collective-permute-start.8 = (bf16[2,64,2,512]{3,2,1,0:T(2,128)(2,1)S(1)}, bf16[2,64,2,512]{3,2,1,0:T(2,128)(2,1)S(1)}, u32[]{:S(2)}, u32[]{:S(2)}) collective-permute-start(bf16[2,64,2,512]{3,2,1,0:T(2,128)(2,1)S(1)} %constant_dynamic-update-slice_fusion.6), channel_id=1, source_target_pairs={{0,128},{64,192},{128,0},{192,64},{1,129},{65,193},{129,1},{193,65... | collective-permute-start | bytes 786440 | tf_op jit(solution)/shard_map/ppermute | solution.py:103
  38.5 7.1 %collective-permute-start.9 = (bf16[2,64,2,512]{3,2,1,0:T(2,128)(2,1)S(1)}, bf16[2,64,2,512]{3,2,1,0:T(2,128)(2,1)S(1)}, u32[]{:S(2)}, u32[]{:S(2)}) collective-permute-start(bf16[2,64,2,512]{3,2,1,0:T(2,128)(2,1)S(1)} %constant_dynamic-update-slice_fusion.6), channel_id=1, source_target_pairs={{0,192},{64,0},{128,64},{192,128},{1,193},{65,1},{129,65},{193,129... | collective-permute-start | bytes 786440 | tf_op jit(solution)/shard_map/ppermute | solution.py:103
  45.8 20.5 %collective-permute-start.10 = (bf16[2,256,2,512]{3,2,1,0:T(2,128)(2,1)S(1)}, bf16[2,256,2,512]{3,2,1,0:T(2,128)(2,1)}, u32[]{:S(2)}, u32[]{:S(2)}) collective-permute-start(bf16[2,256,2,512]{3,2,1,0:T(2,128)(2,1)S(1)} %constant_dynamic-update-slice_fusion.2), channel_id=1, source_target_pairs={{0,1},{1,0},{2,3},{3,2},{4,5},{5,4},{6,7},{7,6},{8,9},{9,8},{10,11... | collective-permute-start | bytes 3145736 | tf_op jit(solution)/shard_map/ppermute | solution.py:103
  52.0 12.3 %collective-permute-start.13 = (bf16[4,2,512]{2,1,0:T(2,128)(2,1)S(1)}, bf16[4,2,512]{2,1,0:T(2,128)(2,1)S(1)}, u32[]{:S(2)}, u32[]{:S(2)}) collective-permute-start(bf16[4,2,512]{2,1,0:T(2,128)(2,1)S(1)} %get-tuple-element.9), channel_id=1, source_target_pairs={{0,3},{1,0},{2,1},{3,2},{4,7},{5,4},{6,5},{7,6},{8,11},{9,8},{10,9... | collective-permute-start | bytes 24584 | tf_op jit(solution)/shard_map/ppermute | solution.py:128
  52.3 10.2 %collective-permute-start.11 = (bf16[4,2,512]{2,1,0:T(2,128)(2,1)S(1)}, bf16[4,2,512]{2,1,0:T(2,128)(2,1)S(1)}, u32[]{:S(2)}, u32[]{:S(2)}) collective-permute-start(bf16[4,2,512]{2,1,0:T(2,128)(2,1)S(1)} %get-tuple-element.10), channel_id=1, source_target_pairs={{0,1},{1,2},{2,3},{3,0},{4,5},{5,6},{6,7},{7,4},{8,9},{9,10},{10,1... | collective-permute-start | bytes 24584 | tf_op jit(solution)/shard_map/ppermute | solution.py:128
  57.9 6.4 %collective-permute-start.12 = (bf16[4,2,512]{2,1,0:T(2,128)(2,1)S(1)}, bf16[4,2,512]{2,1,0:T(2,128)(2,1)S(1)}, u32[]{:S(2)}, u32[]{:S(2)}) collective-permute-start(bf16[4,2,512]{2,1,0:T(2,128)(2,1)S(1)} %get-tuple-element.11), channel_id=1, source_target_pairs={{0,2},{1,3},{2,0},{3,1},{4,6},{5,7},{6,4},{7,5},{8,10},{9,11},{10,... | collective-permute-start | bytes 24584 | tf_op jit(solution)/shard_map/ppermute | solution.py:128
  64.4 1.9 %copy-start.2 = (bf16[4,4,2,512]{3,2,1,0:T(2,128)(2,1)}, bf16[4,4,2,512]{3,2,1,0:T(2,128)(2,1)S(1)}, u32[]{:S(2)}) copy-start(bf16[4,4,2,512]{3,2,1,0:T(2,128)(2,1)S(1)} %bitcast_dynamic-update-slice_fusion.rec_ref) | copy-start | bytes 98308
  68.3 1.3 %copy-start.1 = (bf16[4,256,2,512]{3,2,1,0:T(2,128)(2,1)}, bf16[4,256,2,512]{3,2,1,0:T(2,128)(2,1)S(1)}, u32[]{:S(2)}) copy-start(bf16[4,256,2,512]{3,2,1,0:T(2,128)(2,1)S(1)} %constant_dynamic-update-slice_fusion.src_ref) | copy-start | bytes 6291460

commit v12 on v9

--- a/solution.py
+++ b/solution.py
@@ -108,27 +108,35 @@
     return out
 
 
-def collect(own):
+def swap(value, axis_name):
+    return lax.ppermute(value, axis_name, [(0, 1), (1, 0)])
+
+
+def collect(own, rows):
+    zh, core = lax.axis_index("zh"), lax.axis_index("core")
+    other_zh, other_core = 1 - zh, 1 - core
+    cores = lax.axis_size("core")
+    quarter = rows.shape[0] // lax.axis_size(WIN_AXES)
+
+    def rows_of(zh_of, core_of):
+        return lax.dynamic_slice_in_dim(rows, (zh_of * cores + core_of) * quarter, quarter)
+
+    from_zh = swap(jnp.stack([rows_of(other_zh, core), rows_of(other_zh, other_core)]), "zh")
     part = ring_gather(own, "zh", 0)
     for name in reversed(CHAN_AXES):
         part = ring_gather(part, name, 1)
-    return ring_gather(part, "core", 0)
-
-
-def exchange_receivers(rows):
-    here = lax.axis_index(WIN_AXES)
-    count = lax.axis_size(WIN_AXES)
-    cores = lax.axis_size("core")
-    quarter = rows.shape[0] // count
-    out = jnp.zeros((count, quarter) + rows.shape[1:], rows.dtype)
-    for shift in range(count):
-        block = lax.dynamic_slice_in_dim(rows, ((here + shift) % count) * quarter, quarter)
-        if shift:
-            block = lax.ppermute(block, WIN_AXES, [(i, (i + shift) % count) for i in range(count)])
-        origin = (here - shift) % count
-        place = (origin % cores) * (count // cores) + origin // cores
-        out = lax.dynamic_update_slice(out, block[None], (place, 0, 0, 0))
-    return out
+    from_core = swap(jnp.stack([rows_of(zh, other_core), from_zh[1]]), "core")
+    sources = ring_gather(part, "core", 0)
+    receivers = jnp.zeros((cores * lax.axis_size("zh"),) + from_zh.shape[1:], rows.dtype)
+    for block, (zh_of, core_of) in (
+        (rows_of(zh, core), (zh, core)),
+        (from_zh[0], (other_zh, core)),
+        (from_core[0], (zh, other_core)),
+        (from_core[1], (other_zh, other_core)),
+    ):
+        place = core_of * lax.axis_size("zh") + zh_of
+        receivers = lax.dynamic_update_slice(receivers, block[None], (place, 0, 0, 0))
+    return sources, receivers
 
 
 def per_device(records, source_rows):
@@ -141,11 +149,10 @@
     per_shard = block_len // shards
     weights = lag_weights()
     lag_scale = math.sqrt(2.0 / (lax.axis_size(WIN_AXES) * windows_here * NBINS))
-    receivers = exchange_receivers(whitened[0])
     shard = lax.axis_index(CHAN_AXES)
     own_rows = lax.dynamic_slice_in_dim(source_rows[0], shard * per_shard, per_shard)
     own_sources = jnp.take(whitened, own_rows, axis=1)
-    sources = collect(own_sources)
+    sources, receivers = collect(own_sources, whitened[0])
     lhs = cross_lhs(sources, receivers)
     return transform(lhs, weights, lag_scale, receivers.shape[1])
 

time: 78 us -> 80 us (1.026)
  waiting for transfers between devices: 16.4 us -> 22.5 us
  starting transfers between devices: 30.7 us -> 27 us
  other arithmetic: 6.45 us -> 5.14 us
  local copies, waits for them, and re-layouts: 5.5 us -> 6.45 us
    ppermute x11, starting transfers between devices: 20.2 us -> 13 us  [ring_gather(): lax.ppermute(value, axis_name, [(i, (i + shift) % size) for i in range(si...]
    ppermute x11, waiting for transfers between devices: 16.3 us -> 22.5 us  [ring_gather(): lax.ppermute(value, axis_name, [(i, (i + shift) % size) for i in range(si...]
    ppermute x3 -> x2, starting transfers between devices: 10.5 us -> 14 us  [swap(): return lax.ppermute(value, axis_name, [(0, 1), (1, 0)])]
    unnamed x2 -> x4, local copies, waits for them, and re-layouts: 0.01 us -> 0.95 us
  transfers between devices with their start and end apart: 14 -> 13, of which waited for: 6 -> 5; matrix products, arithmetic and copies ran while one was open for 1% -> 2% of each run, Pallas kernels for 0% -> 0%
where the time goes in v12:
time: 80 us; the launch traced here: 79.7 us
  starting transfers between devices  27 us (34%)
  waiting for transfers between devices  22.5 us (28%)
  Pallas kernels  10.7 us (13%)
  matrix products  7.3 us (9%)
  local copies, waits for them, and re-layouts  6.45 us (8%)
  other arithmetic  5.14 us (6%)
    ppermute x11, waiting for transfers between devices, ring_gather(): lax.ppermute(value, axis_name, [(i, (i + shift) % size) for i in range(si...  22.5 us
    ppermute x2, starting transfers between devices, swap(): return lax.ppermute(value, axis_name, [(0, 1), (1, 0)])  14 us
    ppermute x11, starting transfers between devices, ring_gather(): lax.ppermute(value, axis_name, [(i, (i + shift) % size) for i in range(si...  13 us
    pallas_call x1, Pallas kernels, transform(): pl.pallas_call(functools.partial(lag_kernel, scale=lag_scale), out_shape=...  10.7 us
    dot_general x1, matrix products, whiten(): jnp.dot(row_data, band_table(), preferred_element_type=jnp.float32)  7.3 us
    reduce_sum x1, other arithmetic, cross_lhs(): jnp.sum(src[..., 0, :] * rec[..., 0, :] + src[..., 1, :] * rec[..., 1, :]...  3.15 us
    convert_element_type x1, local copies, waits for them, and re-layouts, cross_lhs(): return lhs.astype(jnp.bfloat16)  2.05 us
    concatenate x1, local copies, waits for them, and re-layouts, cross_lhs(): lhs = jnp.concatenate([real_sum, imag_sum], axis=2).reshape(-1, 2 * NBINS)  1.63 us
  transfers between devices with their start and end apart: 13, of which 5 were waited for; matrix products, arithmetic and copies ran while one was open for 2% of the time, Pallas kernels for 0%

profile of v12, /device:TPU:1, one launch (start us, length us, event | category | flops | bytes accessed | tf_op | source)
XLA Modules:
  0.0 79.7 jit_solution(13620733201284276076)
XLA Ops:
  0.0 0.0 copy-start
  0.0 0.9 %copy-done = bf16[1,16,7680]{2,1,0:T(8,128)(2,1)S(1)} copy-done((bf16[1,16,7680]{2,1,0:T(8,128)(2,1)S(1)}, bf16[1,16,7680]{2,1,0:T(8,128)(2,1)}, u32[]{:S(2)}) %copy-start) | copy-done | bytes 245784
  0.9 0.0 copy-start.1
  0.9 7.3 %convolution_bitcast_fusion = f32[16,1152]{1,0:T(8,128)S(1)} fusion(bf16[7680,1152]{1,0:T(8,128)(2,1)} %constant.160.clone, bf16[1,16,7680]{2,1,0:T(8,128)(2,1)S(1)} %copy-done), kind=kOutput, calls=%fused_computation.3 | convolution fusion | flops 283115520 | bytes 18014208 | tf_op jit(solution)/shard_map/dot_general | solution.py:59
  8.3 0.1 fusion.2
  8.4 0.6 fusion.3
  9.0 0.1 fusion.6
  9.1 7.8 %collective-permute-start.11 = (bf16[2,4,2,512]{3,1,2,0:T(4,128)(2,1)S(1)}, bf16[2,4,2,512]{3,1,2,0:T(4,128)(2,1)S(1)}, u32[]{:S(2)}, u32[]{:S(2)}) collective-permute-start(bf16[2,4,2,512]{3,1,2,0:T(4,128)(2,1)S(1)} %pad_maximum_fusion.1), channel_id=1, source_target_pairs={{0,2},{2,0},{1,3},{3,1},{4,6},{6,4},{5,7},{7,5},{8,10},{10,8},{9,1... | collective-permute-start | bytes 49160 | tf_op jit(solution)/shard_map/ppermute | solution.py:112
  16.9 0.0 copy-done.1
  16.9 0.1 fusion.19
  17.0 0.1 compare_and_fusion
  17.2 0.6 gather_fusion
  17.7 0.1 broadcast_select_fusion
  17.8 0.1 collective-permute-start
  18.2 6.2 %collective-permute-done = bf16[1,4,2,512]{3,2,1,0:T(2,128)(2,1)S(1)} collective-permute-done((bf16[1,4,2,512]{3,2,1,0:T(2,128)(2,1)S(1)}, bf16[1,4,2,512]{3,2,1,0:T(2,128)(2,1)S(1)}, u32[]{:S(2)}, u32[]{:S(2)}) %collective-permute-start) | collective-permute-done | bytes 8224 | tf_op jit(solution)/shard_map/ppermute | solution.py:102
  24.3 2.5 %collective-permute-start.3 = (bf16[2,4,2,512]{3,1,0,2:T(4,128)(2,1)S(1)}, bf16[2,4,2,512]{3,1,0,2:T(4,128)(2,1)S(1)}, u32[]{:S(2)}, u32[]{:S(2)}) collective-permute-start(bf16[2,4,2,512]{3,1,0,2:T(4,128)(2,1)S(1)} %copy_dynamic-update-slice_fusion), channel_id=1, source_target_pairs={{0,12},{4,0},{8,4},{12,8},{1,13},{5,1},{9,5},{13,9},{2,14},{6,2},{... | collective-permute-start | bytes 49160 | tf_op jit(solution)/shard_map/ppermute | solution.py:102
  26.9 0.5 collective-permute-start.2
  27.4 0.6 collective-permute-start.1
  28.0 3.2 %collective-permute-done.1 = bf16[2,4,2,512]{3,1,0,2:T(4,128)(2,1)S(1)} collective-permute-done((bf16[2,4,2,512]{3,1,0,2:T(4,128)(2,1)S(1)}, bf16[2,4,2,512]{3,1,0,2:T(4,128)(2,1)S(1)}, u32[]{:S(2)}, u32[]{:S(2)}) %collective-permute-start.1) | collective-permute-done | bytes 16416 | tf_op jit(solution)/shard_map/ppermute | solution.py:102
  31.2 0.0 collective-permute-done.2
  31.3 0.0 collective-permute-done.3
  31.3 1.7 %collective-permute-start.6 = (bf16[2,16,2,512]{3,1,0,2:T(8,128)(2,1)S(1)}, bf16[2,16,2,512]{3,1,0,2:T(8,128)(2,1)S(1)}, u32[]{:S(2)}, u32[]{:S(2)}) collective-permute-start(bf16[2,16,2,512]{3,1,0,2:T(8,128)(2,1)S(1)} %constant_dynamic-update-slice_fusion.8), channel_id=1, source_target_pairs={{0,48},{16,0},{32,16},{48,32},{1,49},{17,1},{33,17},{49,33},{2,50}... | collective-permute-start | bytes 196616 | tf_op jit(solution)/shard_map/ppermute | solution.py:102
  33.0 0.3 collective-permute-start.5
  33.3 0.7 collective-permute-start.4
  34.1 4.1 %collective-permute-done.4 = bf16[2,16,2,512]{3,1,0,2:T(8,128)(2,1)S(1)} collective-permute-done((bf16[2,16,2,512]{3,1,0,2:T(8,128)(2,1)S(1)}, bf16[2,16,2,512]{3,1,0,2:T(8,128)(2,1)S(1)}, u32[]{:S(2)}, u32[]{:S(2)}) %collective-permute-start.4) | collective-permute-done | bytes 65568 | tf_op jit(solution)/shard_map/ppermute | solution.py:102
  38.2 0.0 collective-permute-done.5
  38.3 0.0 collective-permute-done.6
  38.3 1.4 %collective-permute-start.7 = (bf16[2,64,2,512]{3,1,0,2:T(8,128)(2,1)S(1)}, bf16[2,64,2,512]{3,1,0,2:T(8,128)(2,1)S(1)}, u32[]{:S(2)}, u32[]{:S(2)}) collective-permute-start(bf16[2,64,2,512]{3,1,0,2:T(8,128)(2,1)S(1)} %constant_dynamic-update-slice_fusion.4), channel_id=1, source_target_pairs={{0,64},{64,128},{128,192},{192,0},{1,65},{65,129},{129,193},{193,1... | collective-permute-start | bytes 786440 | tf_op jit(solution)/shard_map/ppermute | solution.py:102
  39.8 0.0 collective-permute-done.11
  39.9 2.7 %collective-permute-start.8 = (bf16[2,64,2,512]{3,1,0,2:T(8,128)(2,1)S(1)}, bf16[2,64,2,512]{3,1,0,2:T(8,128)(2,1)S(1)}, u32[]{:S(2)}, u32[]{:S(2)}) collective-permute-start(bf16[2,64,2,512]{3,1,0,2:T(8,128)(2,1)S(1)} %constant_dynamic-update-slice_fusion.4), channel_id=1, source_target_pairs={{0,128},{64,192},{128,0},{192,64},{1,129},{65,193},{129,1},{193,65... | collective-permute-start | bytes 786440 | tf_op jit(solution)/shard_map/ppermute | solution.py:102
  42.6 6.2 %collective-permute-start.12 = (bf16[2,4,2,512]{3,1,2,0:T(4,128)(2,1)S(1)}, bf16[2,4,2,512]{3,1,2,0:T(4,128)(2,1)S(1)}, u32[]{:S(2)}, u32[]{:S(2)}) collective-permute-start(bf16[2,4,2,512]{3,1,2,0:T(4,128)(2,1)S(1)} %pad_maximum_fusion.2), channel_id=1, source_target_pairs={{0,1},{1,0},{2,3},{3,2},{4,5},{5,4},{6,7},{7,6},{8,9},{9,8},{10,11... | collective-permute-start | bytes 49160 | tf_op jit(solution)/shard_map/ppermute | solution.py:112
  48.7 1.1 %collective-permute-start.9 = (bf16[2,64,2,512]{3,1,0,2:T(8,128)(2,1)S(1)}, bf16[2,64,2,512]{3,1,0,2:T(8,128)(2,1)S(1)}, u32[]{:S(2)}, u32[]{:S(2)}) collective-permute-start(bf16[2,64,2,512]{3,1,0,2:T(8,128)(2,1)S(1)} %constant_dynamic-update-slice_fusion.4), channel_id=1, source_target_pairs={{0,192},{64,0},{128,64},{192,128},{1,193},{65,1},{129,65},{193,129... | collective-permute-start | bytes 786440 | tf_op jit(solution)/shard_map/ppermute | solution.py:102
  49.8 0.1 broadcast_in_dim.50
  49.9 0.0 collective-permute-done.7
  50.0 0.0 collective-permute-done.8
  50.0 7.1 %collective-permute-done.9 = bf16[2,64,2,512]{3,1,0,2:T(8,128)(2,1)S(1)} collective-permute-done((bf16[2,64,2,512]{3,1,0,2:T(8,128)(2,1)S(1)}, bf16[2,64,2,512]{3,1,0,2:T(8,128)(2,1)S(1)}, u32[]{:S(2)}, u32[]{:S(2)}) %collective-permute-start.9) | collective-permute-done | bytes 262176 | tf_op jit(solution)/shard_map/ppermute | solution.py:102
  57.2 1.3 %collective-permute-start.10 = (bf16[2,256,2,512]{3,1,0,2:T(8,128)(2,1)S(1)}, bf16[2,256,2,512]{3,1,0,2:T(8,128)(2,1)S(1)}, u32[]{:S(2)}, u32[]{:S(2)}) collective-permute-start(bf16[2,256,2,512]{3,1,0,2:T(8,128)(2,1)S(1)} %constant_dynamic-update-slice_fusion), channel_id=1, source_target_pairs={{0,1},{1,0},{2,3},{3,2},{4,5},{5,4},{6,7},{7,6},{8,9},{9,8},{10,11... | collective-permute-start | bytes 3145736 | tf_op jit(solution)/shard_map/ppermute | solution.py:102
  58.5 0.0 collective-permute-done.12
  58.6 0.2 broadcast_in_dim.49
  58.8 0.1 bitcast_dynamic-update-slice_fusion.1
  58.9 1.9 %collective-permute-done.10 = bf16[2,256,2,512]{3,1,0,2:T(8,128)(2,1)S(1)} collective-permute-done((bf16[2,256,2,512]{3,1,0,2:T(8,128)(2,1)S(1)}, bf16[2,256,2,512]{3,1,0,2:T(8,128)(2,1)S(1)}, u32[]{:S(2)}, u32[]{:S(2)}) %collective-permute-start.10) | collective-permute-done | bytes 1048608 | tf_op jit(solution)/shard_map/ppermute | solution.py:102
  60.8 0.1 bitcast_dynamic-update-slice_fusion
  60.9 0.6 broadcast_in_dim.58
  61.5 0.4 slice_bitcast_fusion.1
  61.9 3.2 %add_reduce_fusion = (bf16[256,4,512]{2,0,1:T(8,128)(2,1)S(1)}, bf16[256,4,512]{2,0,1:T(8,128)(2,1)S(1)}) fusion(f32[4,4,512]{2,1,0:T(4,128)S(1)} %get-tuple-element.12, f32[4,256,512]{2,1,0:T(8,128)S(1)} %get-tuple-element.10, f32[4,4,512]{2,1,0:T(4,128)S(1)} %get-tuple-element.11, f32[4,256,512]{2,1,0:T(8,128)S(1)} %get-tuple-element.9), kind=kLoop, calls=%fused_computation.2 | loop fusion | flops 15728640 | bytes 6356992 | tf_op jit(solution)/shard_map/reduce_sum | solution.py:65
  65.1 0.3 pad_maximum_fusion
  65.4 1.6 %copy.10 = bf16[256,4,1024]{2,1,0:T(4,128)(2,1)S(1)} copy(bf16[256,4,1024]{2,0,1:T(8,128)(2,1)S(1)} %pad_maximum_fusion) | data formatting | bytes 4194304 | tf_op jit(solution)/shard_map/concatenate | solution.py:67
  67.0 2.0 %convert_element_type.13.lhs_ref = bf16[1024,1024]{1,0:T(8,128)(2,1)} reshape(bf16[256,4,1024]{2,1,0:T(4,128)(2,1)S(1)} %copy.10) | data formatting | bytes 4194304 | tf_op jit(solution)/shard_map/convert_element_type | solution.py:68
  69.1 10.7 %shard_map.46 = f32[256,4,2048]{2,1,0:T(4,128)} custom-call(bf16[1024,1024]{1,0:T(8,128)(2,1)} %convert_element_type.13.lhs_ref, bf16[1024,2048]{1,0:T(8,128)(2,1)} %constant.161.clone.w_ref), custom_call_target="tpu_custom_call" | custom-call | tf_op jit(solution)/shard_map/pallas_call | solution.py:82
  (31 shorter events, 0.5 us)
Async XLA Ops:
  0.0 0.9 %copy-start = (bf16[1,16,7680]{2,1,0:T(8,128)(2,1)S(1)}, bf16[1,16,7680]{2,1,0:T(8,128)(2,1)}, u32[]{:S(2)}) copy-start(bf16[1,16,7680]{2,1,0:T(8,128)(2,1)} %param.4) | copy-start | bytes 737284
  0.9 16.0 %copy-start.1 = (s32[1,256]{1,0:T(1,128)S(1)}, s32[1,256]{1,0:T(1,128)}, u32[]{:S(2)}) copy-start(s32[1,256]{1,0:T(1,128)} %param.5) | copy-start | bytes 3076
  9.1 30.7 %collective-permute-start.11 = (bf16[2,4,2,512]{3,1,2,0:T(4,128)(2,1)S(1)}, bf16[2,4,2,512]{3,1,2,0:T(4,128)(2,1)S(1)}, u32[]{:S(2)}, u32[]{:S(2)}) collective-permute-start(bf16[2,4,2,512]{3,1,2,0:T(4,128)(2,1)S(1)} %pad_maximum_fusion.1), channel_id=1, source_target_pairs={{0,2},{2,0},{1,3},{3,1},{4,6},{6,4},{5,7},{7,5},{8,10},{10,8},{9,1... | collective-permute-start | bytes 49160 | tf_op jit(solution)/shard_map/ppermute | solution.py:112
  17.8 6.5 %collective-permute-start = (bf16[1,4,2,512]{3,2,1,0:T(2,128)(2,1)S(1)}, bf16[1,4,2,512]{3,2,1,0:T(2,128)(2,1)S(1)}, u32[]{:S(2)}, u32[]{:S(2)}) collective-permute-start(bf16[1,4,2,512]{3,2,1,0:T(2,128)(2,1)S(1)} %broadcast_select_fusion), channel_id=1, source_target_pairs={{0,2},{2,0},{1,3},{3,1},{4,6},{6,4},{5,7},{7,5},{8,10},{10,8},{9,1... | collective-permute-start | bytes 24584 | tf_op jit(solution)/shard_map/ppermute | solution.py:102
  24.3 6.9 %collective-permute-start.3 = (bf16[2,4,2,512]{3,1,0,2:T(4,128)(2,1)S(1)}, bf16[2,4,2,512]{3,1,0,2:T(4,128)(2,1)S(1)}, u32[]{:S(2)}, u32[]{:S(2)}) collective-permute-start(bf16[2,4,2,512]{3,1,0,2:T(4,128)(2,1)S(1)} %copy_dynamic-update-slice_fusion), channel_id=1, source_target_pairs={{0,12},{4,0},{8,4},{12,8},{1,13},{5,1},{9,5},{13,9},{2,14},{6,2},{... | collective-permute-start | bytes 49160 | tf_op jit(solution)/shard_map/ppermute | solution.py:102
  26.9 4.3 %collective-permute-start.2 = (bf16[2,4,2,512]{3,1,0,2:T(4,128)(2,1)S(1)}, bf16[2,4,2,512]{3,1,0,2:T(4,128)(2,1)S(1)}, u32[]{:S(2)}, u32[]{:S(2)}) collective-permute-start(bf16[2,4,2,512]{3,1,0,2:T(4,128)(2,1)S(1)} %copy_dynamic-update-slice_fusion), channel_id=1, source_target_pairs={{0,8},{4,12},{8,0},{12,4},{1,9},{5,13},{9,1},{13,5},{2,10},{6,14},... | collective-permute-start | bytes 49160 | tf_op jit(solution)/shard_map/ppermute | solution.py:102
  27.4 3.8 %collective-permute-start.1 = (bf16[2,4,2,512]{3,1,0,2:T(4,128)(2,1)S(1)}, bf16[2,4,2,512]{3,1,0,2:T(4,128)(2,1)S(1)}, u32[]{:S(2)}, u32[]{:S(2)}) collective-permute-start(bf16[2,4,2,512]{3,1,0,2:T(4,128)(2,1)S(1)} %copy_dynamic-update-slice_fusion), channel_id=1, source_target_pairs={{0,4},{4,8},{8,12},{12,0},{1,5},{5,9},{9,13},{13,1},{2,6},{6,10},{... | collective-permute-start | bytes 49160 | tf_op jit(solution)/shard_map/ppermute | solution.py:102
  31.3 7.0 %collective-permute-start.6 = (bf16[2,16,2,512]{3,1,0,2:T(8,128)(2,1)S(1)}, bf16[2,16,2,512]{3,1,0,2:T(8,128)(2,1)S(1)}, u32[]{:S(2)}, u32[]{:S(2)}) collective-permute-start(bf16[2,16,2,512]{3,1,0,2:T(8,128)(2,1)S(1)} %constant_dynamic-update-slice_fusion.8), channel_id=1, source_target_pairs={{0,48},{16,0},{32,16},{48,32},{1,49},{17,1},{33,17},{49,33},{2,50}... | collective-permute-start | bytes 196616 | tf_op jit(solution)/shard_map/ppermute | solution.py:102
  33.0 5.2 %collective-permute-start.5 = (bf16[2,16,2,512]{3,1,0,2:T(8,128)(2,1)S(1)}, bf16[2,16,2,512]{3,1,0,2:T(8,128)(2,1)S(1)}, u32[]{:S(2)}, u32[]{:S(2)}) collective-permute-start(bf16[2,16,2,512]{3,1,0,2:T(8,128)(2,1)S(1)} %constant_dynamic-update-slice_fusion.8), channel_id=1, source_target_pairs={{0,32},{16,48},{32,0},{48,16},{1,33},{17,49},{33,1},{49,17},{2,34}... | collective-permute-start | bytes 196616 | tf_op jit(solution)/shard_map/ppermute | solution.py:102
  33.3 4.9 %collective-permute-start.4 = (bf16[2,16,2,512]{3,1,0,2:T(8,128)(2,1)S(1)}, bf16[2,16,2,512]{3,1,0,2:T(8,128)(2,1)S(1)}, u32[]{:S(2)}, u32[]{:S(2)}) collective-permute-start(bf16[2,16,2,512]{3,1,0,2:T(8,128)(2,1)S(1)} %constant_dynamic-update-slice_fusion.8), channel_id=1, source_target_pairs={{0,16},{16,32},{32,48},{48,0},{1,17},{17,33},{33,49},{49,1},{2,18}... | collective-permute-start | bytes 196616 | tf_op jit(solution)/shard_map/ppermute | solution.py:102
  38.3 11.7 %collective-permute-start.7 = (bf16[2,64,2,512]{3,1,0,2:T(8,128)(2,1)S(1)}, bf16[2,64,2,512]{3,1,0,2:T(8,128)(2,1)S(1)}, u32[]{:S(2)}, u32[]{:S(2)}) collective-permute-start(bf16[2,64,2,512]{3,1,0,2:T(8,128)(2,1)S(1)} %constant_dynamic-update-slice_fusion.4), channel_id=1, source_target_pairs={{0,64},{64,128},{128,192},{192,0},{1,65},{65,129},{129,193},{193,1... | collective-permute-start | bytes 786440 | tf_op jit(solution)/shard_map/ppermute | solution.py:102
  39.9 10.1 %collective-permute-start.8 = (bf16[2,64,2,512]{3,1,0,2:T(8,128)(2,1)S(1)}, bf16[2,64,2,512]{3,1,0,2:T(8,128)(2,1)S(1)}, u32[]{:S(2)}, u32[]{:S(2)}) collective-permute-start(bf16[2,64,2,512]{3,1,0,2:T(8,128)(2,1)S(1)} %constant_dynamic-update-slice_fusion.4), channel_id=1, source_target_pairs={{0,128},{64,192},{128,0},{192,64},{1,129},{65,193},{129,1},{193,65... | collective-permute-start | bytes 786440 | tf_op jit(solution)/shard_map/ppermute | solution.py:102
  42.6 15.9 %collective-permute-start.12 = (bf16[2,4,2,512]{3,1,2,0:T(4,128)(2,1)S(1)}, bf16[2,4,2,512]{3,1,2,0:T(4,128)(2,1)S(1)}, u32[]{:S(2)}, u32[]{:S(2)}) collective-permute-start(bf16[2,4,2,512]{3,1,2,0:T(4,128)(2,1)S(1)} %pad_maximum_fusion.2), channel_id=1, source_target_pairs={{0,1},{1,0},{2,3},{3,2},{4,5},{5,4},{6,7},{7,6},{8,9},{9,8},{10,11... | collective-permute-start | bytes 49160 | tf_op jit(solution)/shard_map/ppermute | solution.py:112
  48.7 8.4 %collective-permute-start.9 = (bf16[2,64,2,512]{3,1,0,2:T(8,128)(2,1)S(1)}, bf16[2,64,2,512]{3,1,0,2:T(8,128)(2,1)S(1)}, u32[]{:S(2)}, u32[]{:S(2)}) collective-permute-start(bf16[2,64,2,512]{3,1,0,2:T(8,128)(2,1)S(1)} %constant_dynamic-update-slice_fusion.4), channel_id=1, source_target_pairs={{0,192},{64,0},{128,64},{192,128},{1,193},{65,1},{129,65},{193,129... | collective-permute-start | bytes 786440 | tf_op jit(solution)/shard_map/ppermute | solution.py:102
  57.2 3.6 %collective-permute-start.10 = (bf16[2,256,2,512]{3,1,0,2:T(8,128)(2,1)S(1)}, bf16[2,256,2,512]{3,1,0,2:T(8,128)(2,1)S(1)}, u32[]{:S(2)}, u32[]{:S(2)}) collective-permute-start(bf16[2,256,2,512]{3,1,0,2:T(8,128)(2,1)S(1)} %constant_dynamic-update-slice_fusion), channel_id=1, source_target_pairs={{0,1},{1,0},{2,3},{3,2},{4,5},{5,4},{6,7},{7,6},{8,9},{9,8},{10,11... | collective-permute-start | bytes 3145736 | tf_op jit(solution)/shard_map/ppermute | solution.py:102

commit v13 on v9

--- a/solution.py
+++ b/solution.py
@@ -28,10 +28,29 @@
 
 def band_table():
     extent = NBINS + 2 * HALF
+    half = S // 2
+    rows = (half + 1 + 127) // 128 * 128
     bin_ids = np.arange(FIRST_BIN - HALF, FIRST_BIN - HALF + extent)
-    cos, sin = angle_table(np.arange(S), bin_ids)
-    table = np.concatenate([cos, -sin], axis=1).astype(ml_dtypes.bfloat16)
-    return jnp.asarray(table)
+    cos, sin = angle_table(np.arange(rows), bin_ids)
+    table = np.concatenate([cos, -sin], axis=1)
+    table[half + 1 :] = 0.0
+    return jnp.asarray(table.astype(ml_dtypes.bfloat16))
+
+
+def band_spectrum(row_data):
+    extent = NBINS + 2 * HALF
+    half = S // 2
+    table = band_table()
+    count = row_data.shape[0]
+    pad = table.shape[0] - (half + 1)
+    gap = jnp.zeros((count, 1), row_data.dtype)
+    head = row_data[:, : half + 1]
+    mirror = jnp.concatenate([gap, row_data[:, half + 1 :][:, ::-1], gap], axis=1)
+    lhs = jnp.pad(jnp.concatenate([head, mirror], axis=0), ((0, 0), (0, pad)))
+    both = jnp.dot(lhs, table, preferred_element_type=jnp.float32)
+    real_part = both[:count, :extent] + both[count:, :extent]
+    imag_part = both[:count, extent:] - both[count:, extent:]
+    return jnp.concatenate([real_part, imag_part], axis=1)
 
 
 def lag_weights():
@@ -56,7 +75,7 @@
 
 
 def whiten(row_data):
-    return normalize(jnp.dot(row_data, band_table(), preferred_element_type=jnp.float32))
+    return normalize(band_spectrum(row_data))
 
 
 def cross_lhs(sources, receivers):

time: 78 us -> 80.7 us (1.035)
  local copies, waits for them, and re-layouts: 5.5 us -> 10.1 us
  matrix products: 7.3 us -> 5.33 us
    unnamed x2, local copies, waits for them, and re-layouts: 0.01 us -> 2.51 us
    dot_general x1, matrix products: 7.3 us -> 5.33 us  [band_spectrum(): both = jnp.dot(lhs, table, preferred_element_type=jnp.float32)]
    slice x0 -> x2, local copies, waits for them, and re-layouts: none -> 1.91 us  [the longest x1 1 us: band_spectrum(): row_data[:, half + 1:][:, ::-1]]
where the time goes in v13:
time: 80.7 us; the launch traced here: 80.4 us
  starting transfers between devices  30.7 us (38%)
  waiting for transfers between devices  16.3 us (20%)
  Pallas kernels  10.7 us (13%)
  local copies, waits for them, and re-layouts  10.1 us (13%)
  other arithmetic  6.51 us (8%)
  matrix products  5.33 us (7%)
  between operations  0.82 us (1%)
    ppermute x11, starting transfers between devices, ring_gather(): lax.ppermute(value, axis_name, [(i, (i + shift) % size) for i in range(si...  20.2 us
    ppermute x11, waiting for transfers between devices, ring_gather(): lax.ppermute(value, axis_name, [(i, (i + shift) % size) for i in range(si...  16.3 us
    pallas_call x1, Pallas kernels, transform(): pl.pallas_call(functools.partial(lag_kernel, scale=lag_scale), out_shape=...  10.7 us
    ppermute x3, starting transfers between devices, exchange_receivers(): lax.ppermute(block, WIN_AXES, [(i, (i + shift) % count) for i in range(co...  10.5 us
    dot_general x1, matrix products, band_spectrum(): both = jnp.dot(lhs, table, preferred_element_type=jnp.float32)  5.33 us
    reduce_sum x1, other arithmetic, cross_lhs(): jnp.sum(src[..., 0, :] * rec[..., 0, :] + src[..., 1, :] * rec[..., 1, :]...  3.15 us
    unnamed x2, local copies, waits for them, and re-layouts  2.51 us
    convert_element_type x1, local copies, waits for them, and re-layouts, cross_lhs(): return lhs.astype(jnp.bfloat16)  2.05 us
  transfers between devices with their start and end apart: 14, of which 6 were waited for; matrix products, arithmetic and copies ran while one was open for 1% of the time, Pallas kernels for 0%

profile of v13, /device:TPU:1, one launch (start us, length us, event | category | flops | bytes accessed | tf_op | source)
XLA Modules:
  0.0 80.4 jit_solution(10489608294946171004)
XLA Ops:
  0.0 0.7 fusion.16
  0.7 0.7 compare_and_fusion
  1.5 1.0 %slice.315 = bf16[16,3839]{1,0:T(8,128)(2,1)S(1)} slice(bf16[16,7680]{1,0:T(8,128)(2,1)} %bitcast.45), slice={[0:16], [3841:7680]} | slice | bytes 245696 | tf_op jit(solution)/shard_map/slice | solution.py:48
  2.5 0.9 %slice.314 = bf16[16,3841]{1,0:T(8,128)(2,1)S(1)} slice(bf16[16,7680]{1,0:T(8,128)(2,1)} %bitcast.46), slice={[0:16], [0:3841]} | slice | bytes 245824 | tf_op jit(solution)/shard_map/slice | solution.py:47
  3.4 2.4 %reverse = bf16[16,3840]{1,0:T(8,128)(2,1)S(1)} reverse(bf16[16,3840]{1,0:T(8,128)(2,1)S(1)} %bitcast.41), dimensions={1} | reverse | bytes 245760
  5.8 0.1 slice.600
  5.9 0.2 concatenate.18
  6.1 5.3 %fusion.3 = f32[32,1152]{1,0:T(8,128)S(1)} fusion(bf16[3968,1152]{1,0:T(8,128)(2,1)} %constant.242.clone, bf16[16,3841]{1,0:T(8,128)(2,1)S(1)} %concatenate.18, bf16[16,3841]{1,0:T(8,128)(2,1)S(1)} %slice.314), kind=kOutput, calls=%fused_computation.12 | convolution fusion | flops 293441536 | bytes 9535552 | tf_op jit(solution)/shard_map/dot_general | solution.py:50
  11.4 0.1 add_sqrt_fusion
  11.5 0.6 fusion.6
  12.2 0.1 fusion.22
  12.3 0.6 gather_fusion
  12.9 0.1 broadcast_select_fusion
  13.0 7.8 %collective-permute-start = (bf16[1,4,2,512]{3,2,1,0:T(2,128)(2,1)S(1)}, bf16[1,4,2,512]{3,2,1,0:T(2,128)(2,1)S(1)}, u32[]{:S(2)}, u32[]{:S(2)}) collective-permute-start(bf16[1,4,2,512]{3,2,1,0:T(2,128)(2,1)S(1)} %broadcast_select_fusion), channel_id=1, source_target_pairs={{0,2},{2,0},{1,3},{3,1},{4,6},{6,4},{5,7},{7,5},{8,10},{10,8},{9,1... | collective-permute-start | bytes 24584 | tf_op jit(solution)/shard_map/ppermute | solution.py:121
  20.8 0.1 fusion.23
  21.1 0.7 collective-permute-done
  21.8 2.5 %collective-permute-start.3 = (bf16[2,4,2,512]{3,1,0,2:T(4,128)(2,1)S(1)}, bf16[2,4,2,512]{3,1,0,2:T(4,128)(2,1)S(1)}, u32[]{:S(2)}, u32[]{:S(2)}) collective-permute-start(bf16[2,4,2,512]{3,1,0,2:T(4,128)(2,1)S(1)} %copy_dynamic-update-slice_fusion), channel_id=1, source_target_pairs={{0,12},{4,0},{8,4},{12,8},{1,13},{5,1},{9,5},{13,9},{2,14},{6,2},{... | collective-permute-start | bytes 49160 | tf_op jit(solution)/shard_map/ppermute | solution.py:121
  24.4 0.5 collective-permute-start.2
  24.9 0.6 collective-permute-start.1
  25.5 3.2 %collective-permute-done.1 = bf16[2,4,2,512]{3,1,0,2:T(4,128)(2,1)S(1)} collective-permute-done((bf16[2,4,2,512]{3,1,0,2:T(4,128)(2,1)S(1)}, bf16[2,4,2,512]{3,1,0,2:T(4,128)(2,1)S(1)}, u32[]{:S(2)}, u32[]{:S(2)}) %collective-permute-start.1) | collective-permute-done | bytes 16416 | tf_op jit(solution)/shard_map/ppermute | solution.py:121
  28.7 0.0 collective-permute-done.2
  28.8 0.0 collective-permute-done.3
  28.8 2.9 %collective-permute-start.6 = (bf16[2,16,2,512]{3,1,0,2:T(8,128)(2,1)S(1)}, bf16[2,16,2,512]{3,1,0,2:T(8,128)(2,1)S(1)}, u32[]{:S(2)}, u32[]{:S(2)}) collective-permute-start(bf16[2,16,2,512]{3,1,0,2:T(8,128)(2,1)S(1)} %constant_dynamic-update-slice_fusion.8), channel_id=1, source_target_pairs={{0,48},{16,0},{32,16},{48,32},{1,49},{17,1},{33,17},{49,33},{2,50}... | collective-permute-start | bytes 196616 | tf_op jit(solution)/shard_map/ppermute | solution.py:121
  31.7 0.0 collective-permute-start.5
  31.7 0.4 collective-permute-start.4
  32.1 4.7 %collective-permute-done.4 = bf16[2,16,2,512]{3,1,0,2:T(8,128)(2,1)S(1)} collective-permute-done((bf16[2,16,2,512]{3,1,0,2:T(8,128)(2,1)S(1)}, bf16[2,16,2,512]{3,1,0,2:T(8,128)(2,1)S(1)}, u32[]{:S(2)}, u32[]{:S(2)}) %collective-permute-start.4) | collective-permute-done | bytes 65568 | tf_op jit(solution)/shard_map/ppermute | solution.py:121
  36.8 0.0 collective-permute-done.5
  36.8 0.0 collective-permute-done.6
  36.9 1.4 %collective-permute-start.7 = (bf16[2,64,2,512]{3,1,0,2:T(8,128)(2,1)S(1)}, bf16[2,64,2,512]{3,1,0,2:T(8,128)(2,1)S(1)}, u32[]{:S(2)}, u32[]{:S(2)}) collective-permute-start(bf16[2,64,2,512]{3,1,0,2:T(8,128)(2,1)S(1)} %constant_dynamic-update-slice_fusion.4), channel_id=1, source_target_pairs={{0,64},{64,128},{128,192},{192,0},{1,65},{65,129},{129,193},{193,1... | collective-permute-start | bytes 786440 | tf_op jit(solution)/shard_map/ppermute | solution.py:121
  38.3 5.1 %collective-permute-start.13 = (bf16[4,2,512]{2,0,1:T(4,128)(2,1)S(1)}, bf16[4,2,512]{2,0,1:T(4,128)(2,1)S(1)}, u32[]{:S(2)}, u32[]{:S(2)}) collective-permute-start(bf16[4,2,512]{2,0,1:T(4,128)(2,1)S(1)} %get-tuple-element.16), channel_id=1, source_target_pairs={{0,3},{1,0},{2,1},{3,2},{4,7},{5,4},{6,5},{7,6},{8,11},{9,8},{10,9... | collective-permute-start | bytes 24584 | tf_op jit(solution)/shard_map/ppermute | solution.py:146
  43.4 4.7 %collective-permute-start.11 = (bf16[4,2,512]{2,0,1:T(4,128)(2,1)S(1)}, bf16[4,2,512]{2,0,1:T(4,128)(2,1)S(1)}, u32[]{:S(2)}, u32[]{:S(2)}) collective-permute-start(bf16[4,2,512]{2,0,1:T(4,128)(2,1)S(1)} %get-tuple-element.17), channel_id=1, source_target_pairs={{0,1},{1,2},{2,3},{3,0},{4,5},{5,6},{6,7},{7,4},{8,9},{9,10},{10,1... | collective-permute-start | bytes 24584 | tf_op jit(solution)/shard_map/ppermute | solution.py:146
  48.1 2.6 %collective-permute-start.8 = (bf16[2,64,2,512]{3,1,0,2:T(8,128)(2,1)S(1)}, bf16[2,64,2,512]{3,1,0,2:T(8,128)(2,1)S(1)}, u32[]{:S(2)}, u32[]{:S(2)}) collective-permute-start(bf16[2,64,2,512]{3,1,0,2:T(8,128)(2,1)S(1)} %constant_dynamic-update-slice_fusion.4), channel_id=1, source_target_pairs={{0,128},{64,192},{128,0},{192,64},{1,129},{65,193},{129,1},{193,65... | collective-permute-start | bytes 786440 | tf_op jit(solution)/shard_map/ppermute | solution.py:121
  51.0 1.1 %collective-permute-start.9 = (bf16[2,64,2,512]{3,1,0,2:T(8,128)(2,1)S(1)}, bf16[2,64,2,512]{3,1,0,2:T(8,128)(2,1)S(1)}, u32[]{:S(2)}, u32[]{:S(2)}) collective-permute-start(bf16[2,64,2,512]{3,1,0,2:T(8,128)(2,1)S(1)} %constant_dynamic-update-slice_fusion.4), channel_id=1, source_target_pairs={{0,192},{64,0},{128,64},{192,128},{1,193},{65,1},{129,65},{193,129... | collective-permute-start | bytes 786440 | tf_op jit(solution)/shard_map/ppermute | solution.py:121
  52.2 0.1 broadcast_in_dim.53
  52.3 0.0 collective-permute-done.7
  52.3 0.7 collective-permute-start.12
  53.0 2.7 %collective-permute-done.8 = bf16[2,64,2,512]{3,1,0,2:T(8,128)(2,1)S(1)} collective-permute-done((bf16[2,64,2,512]{3,1,0,2:T(8,128)(2,1)S(1)}, bf16[2,64,2,512]{3,1,0,2:T(8,128)(2,1)S(1)}, u32[]{:S(2)}, u32[]{:S(2)}) %collective-permute-start.8) | collective-permute-done | bytes 262176 | tf_op jit(solution)/shard_map/ppermute | solution.py:121
  55.8 2.7 %collective-permute-done.9 = bf16[2,64,2,512]{3,1,0,2:T(8,128)(2,1)S(1)} collective-permute-done((bf16[2,64,2,512]{3,1,0,2:T(8,128)(2,1)S(1)}, bf16[2,64,2,512]{3,1,0,2:T(8,128)(2,1)S(1)}, u32[]{:S(2)}, u32[]{:S(2)}) %collective-permute-start.9) | collective-permute-done | bytes 262176 | tf_op jit(solution)/shard_map/ppermute | solution.py:121
  58.5 0.3 collective-permute-start.10
  58.8 0.0 collective-permute-done.11
  58.8 0.0 collective-permute-done.12
  58.9 0.0 collective-permute-done.13
  58.9 0.2 broadcast_in_dim.52
  59.1 0.1 bitcast_dynamic-update-slice_fusion.1
  59.2 2.2 %collective-permute-done.10 = bf16[2,256,2,512]{3,1,0,2:T(8,128)(2,1)S(1)} collective-permute-done((bf16[2,256,2,512]{3,1,0,2:T(8,128)(2,1)S(1)}, bf16[2,256,2,512]{3,1,0,2:T(8,128)(2,1)S(1)}, u32[]{:S(2)}, u32[]{:S(2)}) %collective-permute-start.10) | collective-permute-done | bytes 1048608 | tf_op jit(solution)/shard_map/ppermute | solution.py:121
  61.5 0.1 bitcast_dynamic-update-slice_fusion
  61.5 0.6 broadcast_in_dim.61
  62.1 0.4 slice_bitcast_fusion.1
  62.6 3.2 %add_reduce_fusion = (bf16[256,4,512]{2,0,1:T(8,128)(2,1)S(1)}, bf16[256,4,512]{2,0,1:T(8,128)(2,1)S(1)}) fusion(f32[4,4,512]{2,1,0:T(4,128)S(1)} %get-tuple-element.15, f32[4,256,512]{2,1,0:T(8,128)S(1)} %get-tuple-element.13, f32[4,4,512]{2,1,0:T(4,128)S(1)} %get-tuple-element.14, f32[4,256,512]{2,1,0:T(8,128)S(1)} %get-tuple-element.12), kind=kLoop, calls=%fused_computation.2 | loop fusion | flops 15728640 | bytes 6356992 | tf_op jit(solution)/shard_map/reduce_sum | solution.py:84
  65.7 0.3 pad_maximum_fusion
  66.0 1.6 %copy.9 = bf16[256,4,1024]{2,1,0:T(4,128)(2,1)S(1)} copy(bf16[256,4,1024]{2,0,1:T(8,128)(2,1)S(1)} %pad_maximum_fusion) | data formatting | bytes 4194304 | tf_op jit(solution)/shard_map/concatenate | solution.py:86
  67.7 2.0 %convert_element_type.15.lhs_ref = bf16[1024,1024]{1,0:T(8,128)(2,1)} reshape(bf16[256,4,1024]{2,1,0:T(4,128)(2,1)S(1)} %copy.9) | data formatting | bytes 4194304 | tf_op jit(solution)/shard_map/convert_element_type | solution.py:87
  69.7 10.7 %shard_map.46 = f32[256,4,2048]{2,1,0:T(4,128)} custom-call(bf16[1024,1024]{1,0:T(8,128)(2,1)} %convert_element_type.15.lhs_ref, bf16[1024,2048]{1,0:T(8,128)(2,1)} %constant.243.clone.w_ref), custom_call_target="tpu_custom_call" | custom-call | tf_op jit(solution)/shard_map/pallas_call | solution.py:101
  (29 shorter events, 0.4 us)
Async XLA Ops:
  13.0 8.9 %collective-permute-start = (bf16[1,4,2,512]{3,2,1,0:T(2,128)(2,1)S(1)}, bf16[1,4,2,512]{3,2,1,0:T(2,128)(2,1)S(1)}, u32[]{:S(2)}, u32[]{:S(2)}) collective-permute-start(bf16[1,4,2,512]{3,2,1,0:T(2,128)(2,1)S(1)} %broadcast_select_fusion), channel_id=1, source_target_pairs={{0,2},{2,0},{1,3},{3,1},{4,6},{6,4},{5,7},{7,5},{8,10},{10,8},{9,1... | collective-permute-start | bytes 24584 | tf_op jit(solution)/shard_map/ppermute | solution.py:121
  21.8 6.9 %collective-permute-start.3 = (bf16[2,4,2,512]{3,1,0,2:T(4,128)(2,1)S(1)}, bf16[2,4,2,512]{3,1,0,2:T(4,128)(2,1)S(1)}, u32[]{:S(2)}, u32[]{:S(2)}) collective-permute-start(bf16[2,4,2,512]{3,1,0,2:T(4,128)(2,1)S(1)} %copy_dynamic-update-slice_fusion), channel_id=1, source_target_pairs={{0,12},{4,0},{8,4},{12,8},{1,13},{5,1},{9,5},{13,9},{2,14},{6,2},{... | collective-permute-start | bytes 49160 | tf_op jit(solution)/shard_map/ppermute | solution.py:121
  24.4 4.3 %collective-permute-start.2 = (bf16[2,4,2,512]{3,1,0,2:T(4,128)(2,1)S(1)}, bf16[2,4,2,512]{3,1,0,2:T(4,128)(2,1)S(1)}, u32[]{:S(2)}, u32[]{:S(2)}) collective-permute-start(bf16[2,4,2,512]{3,1,0,2:T(4,128)(2,1)S(1)} %copy_dynamic-update-slice_fusion), channel_id=1, source_target_pairs={{0,8},{4,12},{8,0},{12,4},{1,9},{5,13},{9,1},{13,5},{2,10},{6,14},... | collective-permute-start | bytes 49160 | tf_op jit(solution)/shard_map/ppermute | solution.py:121
  24.9 3.8 %collective-permute-start.1 = (bf16[2,4,2,512]{3,1,0,2:T(4,128)(2,1)S(1)}, bf16[2,4,2,512]{3,1,0,2:T(4,128)(2,1)S(1)}, u32[]{:S(2)}, u32[]{:S(2)}) collective-permute-start(bf16[2,4,2,512]{3,1,0,2:T(4,128)(2,1)S(1)} %copy_dynamic-update-slice_fusion), channel_id=1, source_target_pairs={{0,4},{4,8},{8,12},{12,0},{1,5},{5,9},{9,13},{13,1},{2,6},{6,10},{... | collective-permute-start | bytes 49160 | tf_op jit(solution)/shard_map/ppermute | solution.py:121
  28.8 8.1 %collective-permute-start.6 = (bf16[2,16,2,512]{3,1,0,2:T(8,128)(2,1)S(1)}, bf16[2,16,2,512]{3,1,0,2:T(8,128)(2,1)S(1)}, u32[]{:S(2)}, u32[]{:S(2)}) collective-permute-start(bf16[2,16,2,512]{3,1,0,2:T(8,128)(2,1)S(1)} %constant_dynamic-update-slice_fusion.8), channel_id=1, source_target_pairs={{0,48},{16,0},{32,16},{48,32},{1,49},{17,1},{33,17},{49,33},{2,50}... | collective-permute-start | bytes 196616 | tf_op jit(solution)/shard_map/ppermute | solution.py:121
  31.7 5.1 %collective-permute-start.5 = (bf16[2,16,2,512]{3,1,0,2:T(8,128)(2,1)S(1)}, bf16[2,16,2,512]{3,1,0,2:T(8,128)(2,1)S(1)}, u32[]{:S(2)}, u32[]{:S(2)}) collective-permute-start(bf16[2,16,2,512]{3,1,0,2:T(8,128)(2,1)S(1)} %constant_dynamic-update-slice_fusion.8), channel_id=1, source_target_pairs={{0,32},{16,48},{32,0},{48,16},{1,33},{17,49},{33,1},{49,17},{2,34}... | collective-permute-start | bytes 196616 | tf_op jit(solution)/shard_map/ppermute | solution.py:121
  31.7 5.1 %collective-permute-start.4 = (bf16[2,16,2,512]{3,1,0,2:T(8,128)(2,1)S(1)}, bf16[2,16,2,512]{3,1,0,2:T(8,128)(2,1)S(1)}, u32[]{:S(2)}, u32[]{:S(2)}) collective-permute-start(bf16[2,16,2,512]{3,1,0,2:T(8,128)(2,1)S(1)} %constant_dynamic-update-slice_fusion.8), channel_id=1, source_target_pairs={{0,16},{16,32},{32,48},{48,0},{1,17},{17,33},{33,49},{49,1},{2,18}... | collective-permute-start | bytes 196616 | tf_op jit(solution)/shard_map/ppermute | solution.py:121
  36.9 15.4 %collective-permute-start.7 = (bf16[2,64,2,512]{3,1,0,2:T(8,128)(2,1)S(1)}, bf16[2,64,2,512]{3,1,0,2:T(8,128)(2,1)S(1)}, u32[]{:S(2)}, u32[]{:S(2)}) collective-permute-start(bf16[2,64,2,512]{3,1,0,2:T(8,128)(2,1)S(1)} %constant_dynamic-update-slice_fusion.4), channel_id=1, source_target_pairs={{0,64},{64,128},{128,192},{192,0},{1,65},{65,129},{129,193},{193,1... | collective-permute-start | bytes 786440 | tf_op jit(solution)/shard_map/ppermute | solution.py:121
  38.3 20.6 %collective-permute-start.13 = (bf16[4,2,512]{2,0,1:T(4,128)(2,1)S(1)}, bf16[4,2,512]{2,0,1:T(4,128)(2,1)S(1)}, u32[]{:S(2)}, u32[]{:S(2)}) collective-permute-start(bf16[4,2,512]{2,0,1:T(4,128)(2,1)S(1)} %get-tuple-element.16), channel_id=1, source_target_pairs={{0,3},{1,0},{2,1},{3,2},{4,7},{5,4},{6,5},{7,6},{8,11},{9,8},{10,9... | collective-permute-start | bytes 24584 | tf_op jit(solution)/shard_map/ppermute | solution.py:146
  43.4 15.4 %collective-permute-start.11 = (bf16[4,2,512]{2,0,1:T(4,128)(2,1)S(1)}, bf16[4,2,512]{2,0,1:T(4,128)(2,1)S(1)}, u32[]{:S(2)}, u32[]{:S(2)}) collective-permute-start(bf16[4,2,512]{2,0,1:T(4,128)(2,1)S(1)} %get-tuple-element.17), channel_id=1, source_target_pairs={{0,1},{1,2},{2,3},{3,0},{4,5},{5,6},{6,7},{7,4},{8,9},{9,10},{10,1... | collective-permute-start | bytes 24584 | tf_op jit(solution)/shard_map/ppermute | solution.py:146
  48.1 7.6 %collective-permute-start.8 = (bf16[2,64,2,512]{3,1,0,2:T(8,128)(2,1)S(1)}, bf16[2,64,2,512]{3,1,0,2:T(8,128)(2,1)S(1)}, u32[]{:S(2)}, u32[]{:S(2)}) collective-permute-start(bf16[2,64,2,512]{3,1,0,2:T(8,128)(2,1)S(1)} %constant_dynamic-update-slice_fusion.4), channel_id=1, source_target_pairs={{0,128},{64,192},{128,0},{192,64},{1,129},{65,193},{129,1},{193,65... | collective-permute-start | bytes 786440 | tf_op jit(solution)/shard_map/ppermute | solution.py:121
  51.0 7.5 %collective-permute-start.9 = (bf16[2,64,2,512]{3,1,0,2:T(8,128)(2,1)S(1)}, bf16[2,64,2,512]{3,1,0,2:T(8,128)(2,1)S(1)}, u32[]{:S(2)}, u32[]{:S(2)}) collective-permute-start(bf16[2,64,2,512]{3,1,0,2:T(8,128)(2,1)S(1)} %constant_dynamic-update-slice_fusion.4), channel_id=1, source_target_pairs={{0,192},{64,0},{128,64},{192,128},{1,193},{65,1},{129,65},{193,129... | collective-permute-start | bytes 786440 | tf_op jit(solution)/shard_map/ppermute | solution.py:121
  52.3 6.5 %collective-permute-start.12 = (bf16[4,2,512]{2,0,1:T(4,128)(2,1)S(1)}, bf16[4,2,512]{2,0,1:T(4,128)(2,1)S(1)}, u32[]{:S(2)}, u32[]{:S(2)}) collective-permute-start(bf16[4,2,512]{2,0,1:T(4,128)(2,1)S(1)} %get-tuple-element.18), channel_id=1, source_target_pairs={{0,2},{1,3},{2,0},{3,1},{4,6},{5,7},{6,4},{7,5},{8,10},{9,11},{10,... | collective-permute-start | bytes 24584 | tf_op jit(solution)/shard_map/ppermute | solution.py:146
  58.5 2.9 %collective-permute-start.10 = (bf16[2,256,2,512]{3,1,0,2:T(8,128)(2,1)S(1)}, bf16[2,256,2,512]{3,1,0,2:T(8,128)(2,1)S(1)}, u32[]{:S(2)}, u32[]{:S(2)}) collective-permute-start(bf16[2,256,2,512]{3,1,0,2:T(8,128)(2,1)S(1)} %constant_dynamic-update-slice_fusion), channel_id=1, source_target_pairs={{0,1},{1,0},{2,3},{3,2},{4,5},{5,4},{6,7},{7,6},{8,9},{9,8},{10,11... | collective-permute-start | bytes 3145736 | tf_op jit(solution)/shard_map/ppermute | solution.py:121

commit v14 on v9

--- a/solution.py
+++ b/solution.py
@@ -68,7 +68,7 @@
     return lhs.astype(jnp.bfloat16)
 
 
-SOURCE_BLOCK = 32
+SOURCE_BLOCK = 64
 
 
 def lag_kernel(lhs_ref, w_ref, o_ref, *, scale):

time: 78 us -> 76.2 us (0.977)
  Pallas kernels: 10.7 us -> 8.95 us
    pallas_call x1, Pallas kernels: 10.7 us -> 8.95 us  [transform(): pl.pallas_call(functools.partial(lag_kernel, scale=lag_scale), out_shape=...]
where the time goes in v14:
time: 76.2 us; the launch traced here: 76.1 us
  starting transfers between devices  30.7 us (40%)
  waiting for transfers between devices  16.4 us (22%)
  Pallas kernels  8.95 us (12%)
  matrix products  7.3 us (10%)
  other arithmetic  6.45 us (8%)
  local copies, waits for them, and re-layouts  5.5 us (7%)
  between operations  0.79 us (1%)
    ppermute x11, starting transfers between devices, ring_gather(): lax.ppermute(value, axis_name, [(i, (i + shift) % size) for i in range(si...  20.2 us
    ppermute x11, waiting for transfers between devices, ring_gather(): lax.ppermute(value, axis_name, [(i, (i + shift) % size) for i in range(si...  16.3 us
    ppermute x3, starting transfers between devices, exchange_receivers(): lax.ppermute(block, WIN_AXES, [(i, (i + shift) % count) for i in range(co...  10.5 us
    pallas_call x1, Pallas kernels, transform(): pl.pallas_call(functools.partial(lag_kernel, scale=lag_scale), out_shape=...  8.95 us
    dot_general x1, matrix products, whiten(): jnp.dot(row_data, band_table(), preferred_element_type=jnp.float32)  7.3 us
    reduce_sum x1, other arithmetic, cross_lhs(): jnp.sum(src[..., 0, :] * rec[..., 0, :] + src[..., 1, :] * rec[..., 1, :]...  3.15 us
    convert_element_type x1, local copies, waits for them, and re-layouts, cross_lhs(): return lhs.astype(jnp.bfloat16)  2.05 us
    concatenate x1, local copies, waits for them, and re-layouts, cross_lhs(): lhs = jnp.concatenate([real_sum, imag_sum], axis=2).reshape(-1, 2 * NBINS)  1.63 us
  transfers between devices with their start and end apart: 14, of which 6 were waited for; matrix products, arithmetic and copies ran while one was open for 1% of the time, Pallas kernels for 0%

profile of v14, /device:TPU:1, one launch (start us, length us, event | category | flops | bytes accessed | tf_op | source)
XLA Modules:
  0.0 76.1 jit_solution(12087008467492473483)
XLA Ops:
  0.0 0.0 copy-start
  0.0 0.8 %fusion.13 = s32[4]{0:T(128)S(1)} fusion(s32[1,256]{1,0:T(1,128)} %param.5, s32[]{:T(128)S(6)} %select_n.229), kind=kLoop, calls=%fused_computation.124 | loop fusion | flops 12 | bytes 36 | tf_op jit(solution)/shard_map/jit(_take)/jit(_where)/select_n | solution.py:147
  0.8 0.7 compare_and_fusion
  1.5 0.0 copy-done
  1.5 7.3 %convolution_bitcast_fusion = f32[16,1152]{1,0:T(8,128)S(1)} fusion(bf16[7680,1152]{1,0:T(8,128)(2,1)} %constant.240.clone, bf16[1,16,7680]{2,1,0:T(8,128)(2,1)S(1)} %copy-done), kind=kOutput, calls=%fused_computation.3 | convolution fusion | flops 283115520 | bytes 18014208 | tf_op jit(solution)/shard_map/dot_general | solution.py:59
  8.8 0.1 fusion.2
  8.9 0.6 fusion.3
  9.6 0.1 fusion.6
  9.7 0.6 gather_fusion
  10.3 0.1 broadcast_select_fusion
  10.4 7.8 %collective-permute-start = (bf16[1,4,2,512]{3,2,1,0:T(2,128)(2,1)S(1)}, bf16[1,4,2,512]{3,2,1,0:T(2,128)(2,1)S(1)}, u32[]{:S(2)}, u32[]{:S(2)}) collective-permute-start(bf16[1,4,2,512]{3,2,1,0:T(2,128)(2,1)S(1)} %broadcast_select_fusion), channel_id=1, source_target_pairs={{0,2},{2,0},{1,3},{3,1},{4,6},{6,4},{5,7},{7,5},{8,10},{10,8},{9,1... | collective-permute-start | bytes 24584 | tf_op jit(solution)/shard_map/ppermute | solution.py:102
  18.4 0.8 %collective-permute-done = bf16[1,4,2,512]{3,2,1,0:T(2,128)(2,1)S(1)} collective-permute-done((bf16[1,4,2,512]{3,2,1,0:T(2,128)(2,1)S(1)}, bf16[1,4,2,512]{3,2,1,0:T(2,128)(2,1)S(1)}, u32[]{:S(2)}, u32[]{:S(2)}) %collective-permute-start) | collective-permute-done | bytes 8224 | tf_op jit(solution)/shard_map/ppermute | solution.py:102
  19.2 2.5 %collective-permute-start.3 = (bf16[2,4,2,512]{3,1,0,2:T(4,128)(2,1)S(1)}, bf16[2,4,2,512]{3,1,0,2:T(4,128)(2,1)S(1)}, u32[]{:S(2)}, u32[]{:S(2)}) collective-permute-start(bf16[2,4,2,512]{3,1,0,2:T(4,128)(2,1)S(1)} %copy_dynamic-update-slice_fusion), channel_id=1, source_target_pairs={{0,12},{4,0},{8,4},{12,8},{1,13},{5,1},{9,5},{13,9},{2,14},{6,2},{... | collective-permute-start | bytes 49160 | tf_op jit(solution)/shard_map/ppermute | solution.py:102
  21.8 0.5 collective-permute-start.2
  22.3 0.6 collective-permute-start.1
  22.9 3.2 %collective-permute-done.1 = bf16[2,4,2,512]{3,1,0,2:T(4,128)(2,1)S(1)} collective-permute-done((bf16[2,4,2,512]{3,1,0,2:T(4,128)(2,1)S(1)}, bf16[2,4,2,512]{3,1,0,2:T(4,128)(2,1)S(1)}, u32[]{:S(2)}, u32[]{:S(2)}) %collective-permute-start.1) | collective-permute-done | bytes 16416 | tf_op jit(solution)/shard_map/ppermute | solution.py:102
  26.1 0.0 collective-permute-done.2
  26.2 0.0 collective-permute-done.3
  26.2 2.9 %collective-permute-start.6 = (bf16[2,16,2,512]{3,1,0,2:T(8,128)(2,1)S(1)}, bf16[2,16,2,512]{3,1,0,2:T(8,128)(2,1)S(1)}, u32[]{:S(2)}, u32[]{:S(2)}) collective-permute-start(bf16[2,16,2,512]{3,1,0,2:T(8,128)(2,1)S(1)} %constant_dynamic-update-slice_fusion.8), channel_id=1, source_target_pairs={{0,48},{16,0},{32,16},{48,32},{1,49},{17,1},{33,17},{49,33},{2,50}... | collective-permute-start | bytes 196616 | tf_op jit(solution)/shard_map/ppermute | solution.py:102
  29.1 0.0 collective-permute-start.5
  29.1 0.4 collective-permute-start.4
  29.5 4.7 %collective-permute-done.4 = bf16[2,16,2,512]{3,1,0,2:T(8,128)(2,1)S(1)} collective-permute-done((bf16[2,16,2,512]{3,1,0,2:T(8,128)(2,1)S(1)}, bf16[2,16,2,512]{3,1,0,2:T(8,128)(2,1)S(1)}, u32[]{:S(2)}, u32[]{:S(2)}) %collective-permute-start.4) | collective-permute-done | bytes 65568 | tf_op jit(solution)/shard_map/ppermute | solution.py:102
  34.2 0.0 collective-permute-done.5
  34.2 0.0 collective-permute-done.6
  34.3 1.4 %collective-permute-start.7 = (bf16[2,64,2,512]{3,1,0,2:T(8,128)(2,1)S(1)}, bf16[2,64,2,512]{3,1,0,2:T(8,128)(2,1)S(1)}, u32[]{:S(2)}, u32[]{:S(2)}) collective-permute-start(bf16[2,64,2,512]{3,1,0,2:T(8,128)(2,1)S(1)} %constant_dynamic-update-slice_fusion.4), channel_id=1, source_target_pairs={{0,64},{64,128},{128,192},{192,0},{1,65},{65,129},{129,193},{193,1... | collective-permute-start | bytes 786440 | tf_op jit(solution)/shard_map/ppermute | solution.py:102
  35.7 5.1 %collective-permute-start.13 = (bf16[4,2,512]{2,0,1:T(4,128)(2,1)S(1)}, bf16[4,2,512]{2,0,1:T(4,128)(2,1)S(1)}, u32[]{:S(2)}, u32[]{:S(2)}) collective-permute-start(bf16[4,2,512]{2,0,1:T(4,128)(2,1)S(1)} %get-tuple-element.13), channel_id=1, source_target_pairs={{0,3},{1,0},{2,1},{3,2},{4,7},{5,4},{6,5},{7,6},{8,11},{9,8},{10,9... | collective-permute-start | bytes 24584 | tf_op jit(solution)/shard_map/ppermute | solution.py:127
  40.8 4.7 %collective-permute-start.11 = (bf16[4,2,512]{2,0,1:T(4,128)(2,1)S(1)}, bf16[4,2,512]{2,0,1:T(4,128)(2,1)S(1)}, u32[]{:S(2)}, u32[]{:S(2)}) collective-permute-start(bf16[4,2,512]{2,0,1:T(4,128)(2,1)S(1)} %get-tuple-element.14), channel_id=1, source_target_pairs={{0,1},{1,2},{2,3},{3,0},{4,5},{5,6},{6,7},{7,4},{8,9},{9,10},{10,1... | collective-permute-start | bytes 24584 | tf_op jit(solution)/shard_map/ppermute | solution.py:127
  45.5 2.6 %collective-permute-start.8 = (bf16[2,64,2,512]{3,1,0,2:T(8,128)(2,1)S(1)}, bf16[2,64,2,512]{3,1,0,2:T(8,128)(2,1)S(1)}, u32[]{:S(2)}, u32[]{:S(2)}) collective-permute-start(bf16[2,64,2,512]{3,1,0,2:T(8,128)(2,1)S(1)} %constant_dynamic-update-slice_fusion.4), channel_id=1, source_target_pairs={{0,128},{64,192},{128,0},{192,64},{1,129},{65,193},{129,1},{193,65... | collective-permute-start | bytes 786440 | tf_op jit(solution)/shard_map/ppermute | solution.py:102
  48.4 1.1 %collective-permute-start.9 = (bf16[2,64,2,512]{3,1,0,2:T(8,128)(2,1)S(1)}, bf16[2,64,2,512]{3,1,0,2:T(8,128)(2,1)S(1)}, u32[]{:S(2)}, u32[]{:S(2)}) collective-permute-start(bf16[2,64,2,512]{3,1,0,2:T(8,128)(2,1)S(1)} %constant_dynamic-update-slice_fusion.4), channel_id=1, source_target_pairs={{0,192},{64,0},{128,64},{192,128},{1,193},{65,1},{129,65},{193,129... | collective-permute-start | bytes 786440 | tf_op jit(solution)/shard_map/ppermute | solution.py:102
  49.6 0.1 broadcast_in_dim.53
  49.7 0.0 collective-permute-done.7
  49.7 0.7 collective-permute-start.12
  50.4 2.7 %collective-permute-done.8 = bf16[2,64,2,512]{3,1,0,2:T(8,128)(2,1)S(1)} collective-permute-done((bf16[2,64,2,512]{3,1,0,2:T(8,128)(2,1)S(1)}, bf16[2,64,2,512]{3,1,0,2:T(8,128)(2,1)S(1)}, u32[]{:S(2)}, u32[]{:S(2)}) %collective-permute-start.8) | collective-permute-done | bytes 262176 | tf_op jit(solution)/shard_map/ppermute | solution.py:102
  53.2 2.7 %collective-permute-done.9 = bf16[2,64,2,512]{3,1,0,2:T(8,128)(2,1)S(1)} collective-permute-done((bf16[2,64,2,512]{3,1,0,2:T(8,128)(2,1)S(1)}, bf16[2,64,2,512]{3,1,0,2:T(8,128)(2,1)S(1)}, u32[]{:S(2)}, u32[]{:S(2)}) %collective-permute-start.9) | collective-permute-done | bytes 262176 | tf_op jit(solution)/shard_map/ppermute | solution.py:102
  55.9 0.3 collective-permute-start.10
  56.2 0.0 collective-permute-done.11
  56.2 0.0 collective-permute-done.12
  56.3 0.0 collective-permute-done.13
  56.3 0.2 broadcast_in_dim.52
  56.5 0.1 bitcast_dynamic-update-slice_fusion.1
  56.6 2.2 %collective-permute-done.10 = bf16[2,256,2,512]{3,1,0,2:T(8,128)(2,1)S(1)} collective-permute-done((bf16[2,256,2,512]{3,1,0,2:T(8,128)(2,1)S(1)}, bf16[2,256,2,512]{3,1,0,2:T(8,128)(2,1)S(1)}, u32[]{:S(2)}, u32[]{:S(2)}) %collective-permute-start.10) | collective-permute-done | bytes 1048608 | tf_op jit(solution)/shard_map/ppermute | solution.py:102
  58.8 0.1 bitcast_dynamic-update-slice_fusion
  58.9 0.6 broadcast_in_dim.61
  59.5 0.4 slice_bitcast_fusion.1
  60.0 3.2 %add_reduce_fusion = (bf16[256,4,512]{2,0,1:T(8,128)(2,1)S(1)}, bf16[256,4,512]{2,0,1:T(8,128)(2,1)S(1)}) fusion(f32[4,4,512]{2,1,0:T(4,128)S(1)} %get-tuple-element.12, f32[4,256,512]{2,1,0:T(8,128)S(1)} %get-tuple-element.10, f32[4,4,512]{2,1,0:T(4,128)S(1)} %get-tuple-element.11, f32[4,256,512]{2,1,0:T(8,128)S(1)} %get-tuple-element.9), kind=kLoop, calls=%fused_computation.2 | loop fusion | flops 15728640 | bytes 6356992 | tf_op jit(solution)/shard_map/reduce_sum | solution.py:65
  63.1 0.3 pad_maximum_fusion
  63.4 1.6 %copy.9 = bf16[256,4,1024]{2,1,0:T(4,128)(2,1)S(1)} copy(bf16[256,4,1024]{2,0,1:T(8,128)(2,1)S(1)} %pad_maximum_fusion) | data formatting | bytes 4194304 | tf_op jit(solution)/shard_map/concatenate | solution.py:67
  65.1 2.0 %convert_element_type.13.lhs_ref = bf16[1024,1024]{1,0:T(8,128)(2,1)} reshape(bf16[256,4,1024]{2,1,0:T(4,128)(2,1)S(1)} %copy.9) | data formatting | bytes 4194304 | tf_op jit(solution)/shard_map/convert_element_type | solution.py:68
  67.1 9.0 %shard_map.46 = f32[256,4,2048]{2,1,0:T(4,128)} custom-call(bf16[1024,1024]{1,0:T(8,128)(2,1)} %convert_element_type.13.lhs_ref, bf16[1024,2048]{1,0:T(8,128)(2,1)} %constant.241.clone.w_ref), custom_call_target="tpu_custom_call" | custom-call | tf_op jit(solution)/shard_map/pallas_call | solution.py:82
  (28 shorter events, 0.4 us)
Async XLA Ops:
  0.0 1.5 %copy-start = (bf16[1,16,7680]{2,1,0:T(8,128)(2,1)S(1)}, bf16[1,16,7680]{2,1,0:T(8,128)(2,1)}, u32[]{:S(2)}) copy-start(bf16[1,16,7680]{2,1,0:T(8,128)(2,1)} %param.4) | copy-start | bytes 737284
  10.4 8.9 %collective-permute-start = (bf16[1,4,2,512]{3,2,1,0:T(2,128)(2,1)S(1)}, bf16[1,4,2,512]{3,2,1,0:T(2,128)(2,1)S(1)}, u32[]{:S(2)}, u32[]{:S(2)}) collective-permute-start(bf16[1,4,2,512]{3,2,1,0:T(2,128)(2,1)S(1)} %broadcast_select_fusion), channel_id=1, source_target_pairs={{0,2},{2,0},{1,3},{3,1},{4,6},{6,4},{5,7},{7,5},{8,10},{10,8},{9,1... | collective-permute-start | bytes 24584 | tf_op jit(solution)/shard_map/ppermute | solution.py:102
  19.2 6.9 %collective-permute-start.3 = (bf16[2,4,2,512]{3,1,0,2:T(4,128)(2,1)S(1)}, bf16[2,4,2,512]{3,1,0,2:T(4,128)(2,1)S(1)}, u32[]{:S(2)}, u32[]{:S(2)}) collective-permute-start(bf16[2,4,2,512]{3,1,0,2:T(4,128)(2,1)S(1)} %copy_dynamic-update-slice_fusion), channel_id=1, source_target_pairs={{0,12},{4,0},{8,4},{12,8},{1,13},{5,1},{9,5},{13,9},{2,14},{6,2},{... | collective-permute-start | bytes 49160 | tf_op jit(solution)/shard_map/ppermute | solution.py:102
  21.8 4.3 %collective-permute-start.2 = (bf16[2,4,2,512]{3,1,0,2:T(4,128)(2,1)S(1)}, bf16[2,4,2,512]{3,1,0,2:T(4,128)(2,1)S(1)}, u32[]{:S(2)}, u32[]{:S(2)}) collective-permute-start(bf16[2,4,2,512]{3,1,0,2:T(4,128)(2,1)S(1)} %copy_dynamic-update-slice_fusion), channel_id=1, source_target_pairs={{0,8},{4,12},{8,0},{12,4},{1,9},{5,13},{9,1},{13,5},{2,10},{6,14},... | collective-permute-start | bytes 49160 | tf_op jit(solution)/shard_map/ppermute | solution.py:102
  22.3 3.8 %collective-permute-start.1 = (bf16[2,4,2,512]{3,1,0,2:T(4,128)(2,1)S(1)}, bf16[2,4,2,512]{3,1,0,2:T(4,128)(2,1)S(1)}, u32[]{:S(2)}, u32[]{:S(2)}) collective-permute-start(bf16[2,4,2,512]{3,1,0,2:T(4,128)(2,1)S(1)} %copy_dynamic-update-slice_fusion), channel_id=1, source_target_pairs={{0,4},{4,8},{8,12},{12,0},{1,5},{5,9},{9,13},{13,1},{2,6},{6,10},{... | collective-permute-start | bytes 49160 | tf_op jit(solution)/shard_map/ppermute | solution.py:102
  26.2 8.1 %collective-permute-start.6 = (bf16[2,16,2,512]{3,1,0,2:T(8,128)(2,1)S(1)}, bf16[2,16,2,512]{3,1,0,2:T(8,128)(2,1)S(1)}, u32[]{:S(2)}, u32[]{:S(2)}) collective-permute-start(bf16[2,16,2,512]{3,1,0,2:T(8,128)(2,1)S(1)} %constant_dynamic-update-slice_fusion.8), channel_id=1, source_target_pairs={{0,48},{16,0},{32,16},{48,32},{1,49},{17,1},{33,17},{49,33},{2,50}... | collective-permute-start | bytes 196616 | tf_op jit(solution)/shard_map/ppermute | solution.py:102
  29.1 5.1 %collective-permute-start.5 = (bf16[2,16,2,512]{3,1,0,2:T(8,128)(2,1)S(1)}, bf16[2,16,2,512]{3,1,0,2:T(8,128)(2,1)S(1)}, u32[]{:S(2)}, u32[]{:S(2)}) collective-permute-start(bf16[2,16,2,512]{3,1,0,2:T(8,128)(2,1)S(1)} %constant_dynamic-update-slice_fusion.8), channel_id=1, source_target_pairs={{0,32},{16,48},{32,0},{48,16},{1,33},{17,49},{33,1},{49,17},{2,34}... | collective-permute-start | bytes 196616 | tf_op jit(solution)/shard_map/ppermute | solution.py:102
  29.1 5.1 %collective-permute-start.4 = (bf16[2,16,2,512]{3,1,0,2:T(8,128)(2,1)S(1)}, bf16[2,16,2,512]{3,1,0,2:T(8,128)(2,1)S(1)}, u32[]{:S(2)}, u32[]{:S(2)}) collective-permute-start(bf16[2,16,2,512]{3,1,0,2:T(8,128)(2,1)S(1)} %constant_dynamic-update-slice_fusion.8), channel_id=1, source_target_pairs={{0,16},{16,32},{32,48},{48,0},{1,17},{17,33},{33,49},{49,1},{2,18}... | collective-permute-start | bytes 196616 | tf_op jit(solution)/shard_map/ppermute | solution.py:102
  34.3 15.4 %collective-permute-start.7 = (bf16[2,64,2,512]{3,1,0,2:T(8,128)(2,1)S(1)}, bf16[2,64,2,512]{3,1,0,2:T(8,128)(2,1)S(1)}, u32[]{:S(2)}, u32[]{:S(2)}) collective-permute-start(bf16[2,64,2,512]{3,1,0,2:T(8,128)(2,1)S(1)} %constant_dynamic-update-slice_fusion.4), channel_id=1, source_target_pairs={{0,64},{64,128},{128,192},{192,0},{1,65},{65,129},{129,193},{193,1... | collective-permute-start | bytes 786440 | tf_op jit(solution)/shard_map/ppermute | solution.py:102
  35.7 20.6 %collective-permute-start.13 = (bf16[4,2,512]{2,0,1:T(4,128)(2,1)S(1)}, bf16[4,2,512]{2,0,1:T(4,128)(2,1)S(1)}, u32[]{:S(2)}, u32[]{:S(2)}) collective-permute-start(bf16[4,2,512]{2,0,1:T(4,128)(2,1)S(1)} %get-tuple-element.13), channel_id=1, source_target_pairs={{0,3},{1,0},{2,1},{3,2},{4,7},{5,4},{6,5},{7,6},{8,11},{9,8},{10,9... | collective-permute-start | bytes 24584 | tf_op jit(solution)/shard_map/ppermute | solution.py:127
  40.8 15.4 %collective-permute-start.11 = (bf16[4,2,512]{2,0,1:T(4,128)(2,1)S(1)}, bf16[4,2,512]{2,0,1:T(4,128)(2,1)S(1)}, u32[]{:S(2)}, u32[]{:S(2)}) collective-permute-start(bf16[4,2,512]{2,0,1:T(4,128)(2,1)S(1)} %get-tuple-element.14), channel_id=1, source_target_pairs={{0,1},{1,2},{2,3},{3,0},{4,5},{5,6},{6,7},{7,4},{8,9},{9,10},{10,1... | collective-permute-start | bytes 24584 | tf_op jit(solution)/shard_map/ppermute | solution.py:127
  45.5 7.6 %collective-permute-start.8 = (bf16[2,64,2,512]{3,1,0,2:T(8,128)(2,1)S(1)}, bf16[2,64,2,512]{3,1,0,2:T(8,128)(2,1)S(1)}, u32[]{:S(2)}, u32[]{:S(2)}) collective-permute-start(bf16[2,64,2,512]{3,1,0,2:T(8,128)(2,1)S(1)} %constant_dynamic-update-slice_fusion.4), channel_id=1, source_target_pairs={{0,128},{64,192},{128,0},{192,64},{1,129},{65,193},{129,1},{193,65... | collective-permute-start | bytes 786440 | tf_op jit(solution)/shard_map/ppermute | solution.py:102
  48.4 7.5 %collective-permute-start.9 = (bf16[2,64,2,512]{3,1,0,2:T(8,128)(2,1)S(1)}, bf16[2,64,2,512]{3,1,0,2:T(8,128)(2,1)S(1)}, u32[]{:S(2)}, u32[]{:S(2)}) collective-permute-start(bf16[2,64,2,512]{3,1,0,2:T(8,128)(2,1)S(1)} %constant_dynamic-update-slice_fusion.4), channel_id=1, source_target_pairs={{0,192},{64,0},{128,64},{192,128},{1,193},{65,1},{129,65},{193,129... | collective-permute-start | bytes 786440 | tf_op jit(solution)/shard_map/ppermute | solution.py:102
  49.7 6.5 %collective-permute-start.12 = (bf16[4,2,512]{2,0,1:T(4,128)(2,1)S(1)}, bf16[4,2,512]{2,0,1:T(4,128)(2,1)S(1)}, u32[]{:S(2)}, u32[]{:S(2)}) collective-permute-start(bf16[4,2,512]{2,0,1:T(4,128)(2,1)S(1)} %get-tuple-element.15), channel_id=1, source_target_pairs={{0,2},{1,3},{2,0},{3,1},{4,6},{5,7},{6,4},{7,5},{8,10},{9,11},{10,... | collective-permute-start | bytes 24584 | tf_op jit(solution)/shard_map/ppermute | solution.py:127
  55.9 2.9 %collective-permute-start.10 = (bf16[2,256,2,512]{3,1,0,2:T(8,128)(2,1)S(1)}, bf16[2,256,2,512]{3,1,0,2:T(8,128)(2,1)S(1)}, u32[]{:S(2)}, u32[]{:S(2)}) collective-permute-start(bf16[2,256,2,512]{3,1,0,2:T(8,128)(2,1)S(1)} %constant_dynamic-update-slice_fusion), channel_id=1, source_target_pairs={{0,1},{1,0},{2,3},{3,2},{4,5},{5,4},{6,7},{7,6},{8,9},{9,8},{10,11... | collective-permute-start | bytes 3145736 | tf_op jit(solution)/shard_map/ppermute | solution.py:102

commit v15 on v14

--- a/solution.py
+++ b/solution.py
@@ -68,7 +68,7 @@
     return lhs.astype(jnp.bfloat16)
 
 
-SOURCE_BLOCK = 64
+SOURCE_BLOCK = 128
 
 
 def lag_kernel(lhs_ref, w_ref, o_ref, *, scale):

time: 76.2 us -> 76.4 us (level)
  no operation moved by 1% of the time
where the time goes in v15:
time: 76.4 us; the launch traced here: 76.3 us
  starting transfers between devices  30.7 us (40%)
  waiting for transfers between devices  16.4 us (21%)
  Pallas kernels  9.22 us (12%)
  matrix products  7.3 us (10%)
  other arithmetic  6.45 us (8%)
  local copies, waits for them, and re-layouts  5.5 us (7%)
  between operations  0.79 us (1%)
    ppermute x11, starting transfers between devices, ring_gather(): lax.ppermute(value, axis_name, [(i, (i + shift) % size) for i in range(si...  20.2 us
    ppermute x11, waiting for transfers between devices, ring_gather(): lax.ppermute(value, axis_name, [(i, (i + shift) % size) for i in range(si...  16.3 us
    ppermute x3, starting transfers between devices, exchange_receivers(): lax.ppermute(block, WIN_AXES, [(i, (i + shift) % count) for i in range(co...  10.5 us
    pallas_call x1, Pallas kernels, transform(): pl.pallas_call(functools.partial(lag_kernel, scale=lag_scale), out_shape=...  9.22 us
    dot_general x1, matrix products, whiten(): jnp.dot(row_data, band_table(), preferred_element_type=jnp.float32)  7.3 us
    reduce_sum x1, other arithmetic, cross_lhs(): jnp.sum(src[..., 0, :] * rec[..., 0, :] + src[..., 1, :] * rec[..., 1, :]...  3.15 us
    convert_element_type x1, local copies, waits for them, and re-layouts, cross_lhs(): return lhs.astype(jnp.bfloat16)  2.05 us
    concatenate x1, local copies, waits for them, and re-layouts, cross_lhs(): lhs = jnp.concatenate([real_sum, imag_sum], axis=2).reshape(-1, 2 * NBINS)  1.63 us
  transfers between devices with their start and end apart: 14, of which 6 were waited for; matrix products, arithmetic and copies ran while one was open for 1% of the time, Pallas kernels for 0%

profile of v15, /device:TPU:1, one launch (start us, length us, event | category | flops | bytes accessed | tf_op | source)
XLA Modules:
  0.0 76.3 jit_solution(16198172363538878773)
XLA Ops:
  0.0 0.0 copy-start
  0.0 0.8 %fusion.13 = s32[4]{0:T(128)S(1)} fusion(s32[1,256]{1,0:T(1,128)} %param.5, s32[]{:T(128)S(6)} %select_n.229), kind=kLoop, calls=%fused_computation.124 | loop fusion | flops 12 | bytes 36 | tf_op jit(solution)/shard_map/jit(_take)/jit(_where)/select_n | solution.py:147
  0.8 0.7 compare_and_fusion
  1.5 0.0 copy-done
  1.5 7.3 %convolution_bitcast_fusion = f32[16,1152]{1,0:T(8,128)S(1)} fusion(bf16[7680,1152]{1,0:T(8,128)(2,1)} %constant.240.clone, bf16[1,16,7680]{2,1,0:T(8,128)(2,1)S(1)} %copy-done), kind=kOutput, calls=%fused_computation.3 | convolution fusion | flops 283115520 | bytes 18014208 | tf_op jit(solution)/shard_map/dot_general | solution.py:59
  8.8 0.1 fusion.2
  8.9 0.6 fusion.3
  9.6 0.1 fusion.6
  9.7 0.6 gather_fusion
  10.3 0.1 broadcast_select_fusion
  10.4 7.8 %collective-permute-start = (bf16[1,4,2,512]{3,2,1,0:T(2,128)(2,1)S(1)}, bf16[1,4,2,512]{3,2,1,0:T(2,128)(2,1)S(1)}, u32[]{:S(2)}, u32[]{:S(2)}) collective-permute-start(bf16[1,4,2,512]{3,2,1,0:T(2,128)(2,1)S(1)} %broadcast_select_fusion), channel_id=1, source_target_pairs={{0,2},{2,0},{1,3},{3,1},{4,6},{6,4},{5,7},{7,5},{8,10},{10,8},{9,1... | collective-permute-start | bytes 24584 | tf_op jit(solution)/shard_map/ppermute | solution.py:102
  18.4 0.8 %collective-permute-done = bf16[1,4,2,512]{3,2,1,0:T(2,128)(2,1)S(1)} collective-permute-done((bf16[1,4,2,512]{3,2,1,0:T(2,128)(2,1)S(1)}, bf16[1,4,2,512]{3,2,1,0:T(2,128)(2,1)S(1)}, u32[]{:S(2)}, u32[]{:S(2)}) %collective-permute-start) | collective-permute-done | bytes 8224 | tf_op jit(solution)/shard_map/ppermute | solution.py:102
  19.2 2.5 %collective-permute-start.3 = (bf16[2,4,2,512]{3,1,0,2:T(4,128)(2,1)S(1)}, bf16[2,4,2,512]{3,1,0,2:T(4,128)(2,1)S(1)}, u32[]{:S(2)}, u32[]{:S(2)}) collective-permute-start(bf16[2,4,2,512]{3,1,0,2:T(4,128)(2,1)S(1)} %copy_dynamic-update-slice_fusion), channel_id=1, source_target_pairs={{0,12},{4,0},{8,4},{12,8},{1,13},{5,1},{9,5},{13,9},{2,14},{6,2},{... | collective-permute-start | bytes 49160 | tf_op jit(solution)/shard_map/ppermute | solution.py:102
  21.8 0.5 collective-permute-start.2
  22.3 0.6 collective-permute-start.1
  22.9 3.2 %collective-permute-done.1 = bf16[2,4,2,512]{3,1,0,2:T(4,128)(2,1)S(1)} collective-permute-done((bf16[2,4,2,512]{3,1,0,2:T(4,128)(2,1)S(1)}, bf16[2,4,2,512]{3,1,0,2:T(4,128)(2,1)S(1)}, u32[]{:S(2)}, u32[]{:S(2)}) %collective-permute-start.1) | collective-permute-done | bytes 16416 | tf_op jit(solution)/shard_map/ppermute | solution.py:102
  26.1 0.0 collective-permute-done.2
  26.2 0.0 collective-permute-done.3
  26.2 2.9 %collective-permute-start.6 = (bf16[2,16,2,512]{3,1,0,2:T(8,128)(2,1)S(1)}, bf16[2,16,2,512]{3,1,0,2:T(8,128)(2,1)S(1)}, u32[]{:S(2)}, u32[]{:S(2)}) collective-permute-start(bf16[2,16,2,512]{3,1,0,2:T(8,128)(2,1)S(1)} %constant_dynamic-update-slice_fusion.8), channel_id=1, source_target_pairs={{0,48},{16,0},{32,16},{48,32},{1,49},{17,1},{33,17},{49,33},{2,50}... | collective-permute-start | bytes 196616 | tf_op jit(solution)/shard_map/ppermute | solution.py:102
  29.1 0.0 collective-permute-start.5
  29.1 0.4 collective-permute-start.4
  29.5 4.7 %collective-permute-done.4 = bf16[2,16,2,512]{3,1,0,2:T(8,128)(2,1)S(1)} collective-permute-done((bf16[2,16,2,512]{3,1,0,2:T(8,128)(2,1)S(1)}, bf16[2,16,2,512]{3,1,0,2:T(8,128)(2,1)S(1)}, u32[]{:S(2)}, u32[]{:S(2)}) %collective-permute-start.4) | collective-permute-done | bytes 65568 | tf_op jit(solution)/shard_map/ppermute | solution.py:102
  34.2 0.0 collective-permute-done.5
  34.2 0.0 collective-permute-done.6
  34.3 1.4 %collective-permute-start.7 = (bf16[2,64,2,512]{3,1,0,2:T(8,128)(2,1)S(1)}, bf16[2,64,2,512]{3,1,0,2:T(8,128)(2,1)S(1)}, u32[]{:S(2)}, u32[]{:S(2)}) collective-permute-start(bf16[2,64,2,512]{3,1,0,2:T(8,128)(2,1)S(1)} %constant_dynamic-update-slice_fusion.4), channel_id=1, source_target_pairs={{0,64},{64,128},{128,192},{192,0},{1,65},{65,129},{129,193},{193,1... | collective-permute-start | bytes 786440 | tf_op jit(solution)/shard_map/ppermute | solution.py:102
  35.7 5.1 %collective-permute-start.13 = (bf16[4,2,512]{2,0,1:T(4,128)(2,1)S(1)}, bf16[4,2,512]{2,0,1:T(4,128)(2,1)S(1)}, u32[]{:S(2)}, u32[]{:S(2)}) collective-permute-start(bf16[4,2,512]{2,0,1:T(4,128)(2,1)S(1)} %get-tuple-element.13), channel_id=1, source_target_pairs={{0,3},{1,0},{2,1},{3,2},{4,7},{5,4},{6,5},{7,6},{8,11},{9,8},{10,9... | collective-permute-start | bytes 24584 | tf_op jit(solution)/shard_map/ppermute | solution.py:127
  40.8 4.7 %collective-permute-start.11 = (bf16[4,2,512]{2,0,1:T(4,128)(2,1)S(1)}, bf16[4,2,512]{2,0,1:T(4,128)(2,1)S(1)}, u32[]{:S(2)}, u32[]{:S(2)}) collective-permute-start(bf16[4,2,512]{2,0,1:T(4,128)(2,1)S(1)} %get-tuple-element.14), channel_id=1, source_target_pairs={{0,1},{1,2},{2,3},{3,0},{4,5},{5,6},{6,7},{7,4},{8,9},{9,10},{10,1... | collective-permute-start | bytes 24584 | tf_op jit(solution)/shard_map/ppermute | solution.py:127
  45.5 2.6 %collective-permute-start.8 = (bf16[2,64,2,512]{3,1,0,2:T(8,128)(2,1)S(1)}, bf16[2,64,2,512]{3,1,0,2:T(8,128)(2,1)S(1)}, u32[]{:S(2)}, u32[]{:S(2)}) collective-permute-start(bf16[2,64,2,512]{3,1,0,2:T(8,128)(2,1)S(1)} %constant_dynamic-update-slice_fusion.4), channel_id=1, source_target_pairs={{0,128},{64,192},{128,0},{192,64},{1,129},{65,193},{129,1},{193,65... | collective-permute-start | bytes 786440 | tf_op jit(solution)/shard_map/ppermute | solution.py:102
  48.4 1.1 %collective-permute-start.9 = (bf16[2,64,2,512]{3,1,0,2:T(8,128)(2,1)S(1)}, bf16[2,64,2,512]{3,1,0,2:T(8,128)(2,1)S(1)}, u32[]{:S(2)}, u32[]{:S(2)}) collective-permute-start(bf16[2,64,2,512]{3,1,0,2:T(8,128)(2,1)S(1)} %constant_dynamic-update-slice_fusion.4), channel_id=1, source_target_pairs={{0,192},{64,0},{128,64},{192,128},{1,193},{65,1},{129,65},{193,129... | collective-permute-start | bytes 786440 | tf_op jit(solution)/shard_map/ppermute | solution.py:102
  49.6 0.1 broadcast_in_dim.53
  49.7 0.0 collective-permute-done.7
  49.7 0.7 collective-permute-start.12
  50.4 2.7 %collective-permute-done.8 = bf16[2,64,2,512]{3,1,0,2:T(8,128)(2,1)S(1)} collective-permute-done((bf16[2,64,2,512]{3,1,0,2:T(8,128)(2,1)S(1)}, bf16[2,64,2,512]{3,1,0,2:T(8,128)(2,1)S(1)}, u32[]{:S(2)}, u32[]{:S(2)}) %collective-permute-start.8) | collective-permute-done | bytes 262176 | tf_op jit(solution)/shard_map/ppermute | solution.py:102
  53.2 2.7 %collective-permute-done.9 = bf16[2,64,2,512]{3,1,0,2:T(8,128)(2,1)S(1)} collective-permute-done((bf16[2,64,2,512]{3,1,0,2:T(8,128)(2,1)S(1)}, bf16[2,64,2,512]{3,1,0,2:T(8,128)(2,1)S(1)}, u32[]{:S(2)}, u32[]{:S(2)}) %collective-permute-start.9) | collective-permute-done | bytes 262176 | tf_op jit(solution)/shard_map/ppermute | solution.py:102
  55.9 0.3 collective-permute-start.10
  56.2 0.0 collective-permute-done.11
  56.2 0.0 collective-permute-done.12
  56.3 0.0 collective-permute-done.13
  56.3 0.2 broadcast_in_dim.52
  56.5 0.1 bitcast_dynamic-update-slice_fusion.1
  56.6 2.2 %collective-permute-done.10 = bf16[2,256,2,512]{3,1,0,2:T(8,128)(2,1)S(1)} collective-permute-done((bf16[2,256,2,512]{3,1,0,2:T(8,128)(2,1)S(1)}, bf16[2,256,2,512]{3,1,0,2:T(8,128)(2,1)S(1)}, u32[]{:S(2)}, u32[]{:S(2)}) %collective-permute-start.10) | collective-permute-done | bytes 1048608 | tf_op jit(solution)/shard_map/ppermute | solution.py:102
  58.8 0.1 bitcast_dynamic-update-slice_fusion
  58.9 0.6 broadcast_in_dim.61
  59.5 0.4 slice_bitcast_fusion.1
  60.0 3.2 %add_reduce_fusion = (bf16[256,4,512]{2,0,1:T(8,128)(2,1)S(1)}, bf16[256,4,512]{2,0,1:T(8,128)(2,1)S(1)}) fusion(f32[4,4,512]{2,1,0:T(4,128)S(1)} %get-tuple-element.12, f32[4,256,512]{2,1,0:T(8,128)S(1)} %get-tuple-element.10, f32[4,4,512]{2,1,0:T(4,128)S(1)} %get-tuple-element.11, f32[4,256,512]{2,1,0:T(8,128)S(1)} %get-tuple-element.9), kind=kLoop, calls=%fused_computation.2 | loop fusion | flops 15728640 | bytes 6356992 | tf_op jit(solution)/shard_map/reduce_sum | solution.py:65
  63.1 0.3 pad_maximum_fusion
  63.4 1.6 %copy.9 = bf16[256,4,1024]{2,1,0:T(4,128)(2,1)S(1)} copy(bf16[256,4,1024]{2,0,1:T(8,128)(2,1)S(1)} %pad_maximum_fusion) | data formatting | bytes 4194304 | tf_op jit(solution)/shard_map/concatenate | solution.py:67
  65.1 2.0 %convert_element_type.13.lhs_ref = bf16[1024,1024]{1,0:T(8,128)(2,1)} reshape(bf16[256,4,1024]{2,1,0:T(4,128)(2,1)S(1)} %copy.9) | data formatting | bytes 4194304 | tf_op jit(solution)/shard_map/convert_element_type | solution.py:68
  67.1 9.2 %shard_map.46 = f32[256,4,2048]{2,1,0:T(4,128)} custom-call(bf16[1024,1024]{1,0:T(8,128)(2,1)} %convert_element_type.13.lhs_ref, bf16[1024,2048]{1,0:T(8,128)(2,1)} %constant.241.clone.w_ref), custom_call_target="tpu_custom_call" | custom-call | tf_op jit(solution)/shard_map/pallas_call | solution.py:82
  (28 shorter events, 0.4 us)
Async XLA Ops:
  0.0 1.5 %copy-start = (bf16[1,16,7680]{2,1,0:T(8,128)(2,1)S(1)}, bf16[1,16,7680]{2,1,0:T(8,128)(2,1)}, u32[]{:S(2)}) copy-start(bf16[1,16,7680]{2,1,0:T(8,128)(2,1)} %param.4) | copy-start | bytes 737284
  10.4 8.9 %collective-permute-start = (bf16[1,4,2,512]{3,2,1,0:T(2,128)(2,1)S(1)}, bf16[1,4,2,512]{3,2,1,0:T(2,128)(2,1)S(1)}, u32[]{:S(2)}, u32[]{:S(2)}) collective-permute-start(bf16[1,4,2,512]{3,2,1,0:T(2,128)(2,1)S(1)} %broadcast_select_fusion), channel_id=1, source_target_pairs={{0,2},{2,0},{1,3},{3,1},{4,6},{6,4},{5,7},{7,5},{8,10},{10,8},{9,1... | collective-permute-start | bytes 24584 | tf_op jit(solution)/shard_map/ppermute | solution.py:102
  19.2 6.9 %collective-permute-start.3 = (bf16[2,4,2,512]{3,1,0,2:T(4,128)(2,1)S(1)}, bf16[2,4,2,512]{3,1,0,2:T(4,128)(2,1)S(1)}, u32[]{:S(2)}, u32[]{:S(2)}) collective-permute-start(bf16[2,4,2,512]{3,1,0,2:T(4,128)(2,1)S(1)} %copy_dynamic-update-slice_fusion), channel_id=1, source_target_pairs={{0,12},{4,0},{8,4},{12,8},{1,13},{5,1},{9,5},{13,9},{2,14},{6,2},{... | collective-permute-start | bytes 49160 | tf_op jit(solution)/shard_map/ppermute | solution.py:102
  21.8 4.3 %collective-permute-start.2 = (bf16[2,4,2,512]{3,1,0,2:T(4,128)(2,1)S(1)}, bf16[2,4,2,512]{3,1,0,2:T(4,128)(2,1)S(1)}, u32[]{:S(2)}, u32[]{:S(2)}) collective-permute-start(bf16[2,4,2,512]{3,1,0,2:T(4,128)(2,1)S(1)} %copy_dynamic-update-slice_fusion), channel_id=1, source_target_pairs={{0,8},{4,12},{8,0},{12,4},{1,9},{5,13},{9,1},{13,5},{2,10},{6,14},... | collective-permute-start | bytes 49160 | tf_op jit(solution)/shard_map/ppermute | solution.py:102
  22.3 3.8 %collective-permute-start.1 = (bf16[2,4,2,512]{3,1,0,2:T(4,128)(2,1)S(1)}, bf16[2,4,2,512]{3,1,0,2:T(4,128)(2,1)S(1)}, u32[]{:S(2)}, u32[]{:S(2)}) collective-permute-start(bf16[2,4,2,512]{3,1,0,2:T(4,128)(2,1)S(1)} %copy_dynamic-update-slice_fusion), channel_id=1, source_target_pairs={{0,4},{4,8},{8,12},{12,0},{1,5},{5,9},{9,13},{13,1},{2,6},{6,10},{... | collective-permute-start | bytes 49160 | tf_op jit(solution)/shard_map/ppermute | solution.py:102
  26.2 8.1 %collective-permute-start.6 = (bf16[2,16,2,512]{3,1,0,2:T(8,128)(2,1)S(1)}, bf16[2,16,2,512]{3,1,0,2:T(8,128)(2,1)S(1)}, u32[]{:S(2)}, u32[]{:S(2)}) collective-permute-start(bf16[2,16,2,512]{3,1,0,2:T(8,128)(2,1)S(1)} %constant_dynamic-update-slice_fusion.8), channel_id=1, source_target_pairs={{0,48},{16,0},{32,16},{48,32},{1,49},{17,1},{33,17},{49,33},{2,50}... | collective-permute-start | bytes 196616 | tf_op jit(solution)/shard_map/ppermute | solution.py:102
  29.1 5.1 %collective-permute-start.5 = (bf16[2,16,2,512]{3,1,0,2:T(8,128)(2,1)S(1)}, bf16[2,16,2,512]{3,1,0,2:T(8,128)(2,1)S(1)}, u32[]{:S(2)}, u32[]{:S(2)}) collective-permute-start(bf16[2,16,2,512]{3,1,0,2:T(8,128)(2,1)S(1)} %constant_dynamic-update-slice_fusion.8), channel_id=1, source_target_pairs={{0,32},{16,48},{32,0},{48,16},{1,33},{17,49},{33,1},{49,17},{2,34}... | collective-permute-start | bytes 196616 | tf_op jit(solution)/shard_map/ppermute | solution.py:102
  29.1 5.1 %collective-permute-start.4 = (bf16[2,16,2,512]{3,1,0,2:T(8,128)(2,1)S(1)}, bf16[2,16,2,512]{3,1,0,2:T(8,128)(2,1)S(1)}, u32[]{:S(2)}, u32[]{:S(2)}) collective-permute-start(bf16[2,16,2,512]{3,1,0,2:T(8,128)(2,1)S(1)} %constant_dynamic-update-slice_fusion.8), channel_id=1, source_target_pairs={{0,16},{16,32},{32,48},{48,0},{1,17},{17,33},{33,49},{49,1},{2,18}... | collective-permute-start | bytes 196616 | tf_op jit(solution)/shard_map/ppermute | solution.py:102
  34.3 15.4 %collective-permute-start.7 = (bf16[2,64,2,512]{3,1,0,2:T(8,128)(2,1)S(1)}, bf16[2,64,2,512]{3,1,0,2:T(8,128)(2,1)S(1)}, u32[]{:S(2)}, u32[]{:S(2)}) collective-permute-start(bf16[2,64,2,512]{3,1,0,2:T(8,128)(2,1)S(1)} %constant_dynamic-update-slice_fusion.4), channel_id=1, source_target_pairs={{0,64},{64,128},{128,192},{192,0},{1,65},{65,129},{129,193},{193,1... | collective-permute-start | bytes 786440 | tf_op jit(solution)/shard_map/ppermute | solution.py:102
  35.7 20.6 %collective-permute-start.13 = (bf16[4,2,512]{2,0,1:T(4,128)(2,1)S(1)}, bf16[4,2,512]{2,0,1:T(4,128)(2,1)S(1)}, u32[]{:S(2)}, u32[]{:S(2)}) collective-permute-start(bf16[4,2,512]{2,0,1:T(4,128)(2,1)S(1)} %get-tuple-element.13), channel_id=1, source_target_pairs={{0,3},{1,0},{2,1},{3,2},{4,7},{5,4},{6,5},{7,6},{8,11},{9,8},{10,9... | collective-permute-start | bytes 24584 | tf_op jit(solution)/shard_map/ppermute | solution.py:127
  40.8 15.4 %collective-permute-start.11 = (bf16[4,2,512]{2,0,1:T(4,128)(2,1)S(1)}, bf16[4,2,512]{2,0,1:T(4,128)(2,1)S(1)}, u32[]{:S(2)}, u32[]{:S(2)}) collective-permute-start(bf16[4,2,512]{2,0,1:T(4,128)(2,1)S(1)} %get-tuple-element.14), channel_id=1, source_target_pairs={{0,1},{1,2},{2,3},{3,0},{4,5},{5,6},{6,7},{7,4},{8,9},{9,10},{10,1... | collective-permute-start | bytes 24584 | tf_op jit(solution)/shard_map/ppermute | solution.py:127
  45.5 7.6 %collective-permute-start.8 = (bf16[2,64,2,512]{3,1,0,2:T(8,128)(2,1)S(1)}, bf16[2,64,2,512]{3,1,0,2:T(8,128)(2,1)S(1)}, u32[]{:S(2)}, u32[]{:S(2)}) collective-permute-start(bf16[2,64,2,512]{3,1,0,2:T(8,128)(2,1)S(1)} %constant_dynamic-update-slice_fusion.4), channel_id=1, source_target_pairs={{0,128},{64,192},{128,0},{192,64},{1,129},{65,193},{129,1},{193,65... | collective-permute-start | bytes 786440 | tf_op jit(solution)/shard_map/ppermute | solution.py:102
  48.4 7.5 %collective-permute-start.9 = (bf16[2,64,2,512]{3,1,0,2:T(8,128)(2,1)S(1)}, bf16[2,64,2,512]{3,1,0,2:T(8,128)(2,1)S(1)}, u32[]{:S(2)}, u32[]{:S(2)}) collective-permute-start(bf16[2,64,2,512]{3,1,0,2:T(8,128)(2,1)S(1)} %constant_dynamic-update-slice_fusion.4), channel_id=1, source_target_pairs={{0,192},{64,0},{128,64},{192,128},{1,193},{65,1},{129,65},{193,129... | collective-permute-start | bytes 786440 | tf_op jit(solution)/shard_map/ppermute | solution.py:102
  49.7 6.5 %collective-permute-start.12 = (bf16[4,2,512]{2,0,1:T(4,128)(2,1)S(1)}, bf16[4,2,512]{2,0,1:T(4,128)(2,1)S(1)}, u32[]{:S(2)}, u32[]{:S(2)}) collective-permute-start(bf16[4,2,512]{2,0,1:T(4,128)(2,1)S(1)} %get-tuple-element.15), channel_id=1, source_target_pairs={{0,2},{1,3},{2,0},{3,1},{4,6},{5,7},{6,4},{7,5},{8,10},{9,11},{10,... | collective-permute-start | bytes 24584 | tf_op jit(solution)/shard_map/ppermute | solution.py:127
  55.9 2.9 %collective-permute-start.10 = (bf16[2,256,2,512]{3,1,0,2:T(8,128)(2,1)S(1)}, bf16[2,256,2,512]{3,1,0,2:T(8,128)(2,1)S(1)}, u32[]{:S(2)}, u32[]{:S(2)}) collective-permute-start(bf16[2,256,2,512]{3,1,0,2:T(8,128)(2,1)S(1)} %constant_dynamic-update-slice_fusion), channel_id=1, source_target_pairs={{0,1},{1,0},{2,3},{3,2},{4,5},{5,4},{6,7},{7,6},{8,9},{9,8},{10,11... | collective-permute-start | bytes 3145736 | tf_op jit(solution)/shard_map/ppermute | solution.py:102

commit v16 on v14

--- a/solution.py
+++ b/solution.py
@@ -59,36 +59,37 @@
     return normalize(jnp.dot(row_data, band_table(), preferred_element_type=jnp.float32))
 
 
-def cross_lhs(sources, receivers):
+def cross_parts(sources, receivers):
     src = sources.astype(jnp.float32)[:, :, None]
     rec = receivers.astype(jnp.float32)[:, None]
     real_sum = jnp.sum(src[..., 0, :] * rec[..., 0, :] + src[..., 1, :] * rec[..., 1, :], axis=0)
     imag_sum = jnp.sum(src[..., 1, :] * rec[..., 0, :] - src[..., 0, :] * rec[..., 1, :], axis=0)
-    lhs = jnp.concatenate([real_sum, imag_sum], axis=2).reshape(-1, 2 * NBINS)
-    return lhs.astype(jnp.bfloat16)
+    return real_sum.astype(jnp.bfloat16), imag_sum.astype(jnp.bfloat16)
 
 
 SOURCE_BLOCK = 64
 
 
-def lag_kernel(lhs_ref, w_ref, o_ref, *, scale):
-    result = jnp.dot(lhs_ref[...], w_ref[...], preferred_element_type=jnp.float32) * scale
-    o_ref[...] = result.reshape(o_ref.shape)
+def lag_kernel(re_ref, im_ref, w_ref, o_ref, *, scale):
+    def flat(ref):
+        return ref[...].astype(jnp.float32).reshape(-1, ref.shape[2]).astype(jnp.bfloat16)
+
+    bins = re_ref.shape[2]
+    result = jnp.dot(flat(re_ref), w_ref[:bins], preferred_element_type=jnp.float32)
+    result = result + jnp.dot(flat(im_ref), w_ref[bins:], preferred_element_type=jnp.float32)
+    o_ref[...] = (result * scale).reshape(o_ref.shape)
 
 
-def transform(lhs, weights, lag_scale, count_rec):
-    count_src = lhs.shape[0] // count_rec
-    rows = SOURCE_BLOCK * count_rec
+def transform(real_part, imag_part, weights, lag_scale):
+    count_src, count_rec, bins = real_part.shape
+    part_spec = pl.BlockSpec((SOURCE_BLOCK, count_rec, bins), lambda i: (i, 0, 0))
     return pl.pallas_call(
         functools.partial(lag_kernel, scale=lag_scale),
         out_shape=jax.ShapeDtypeStruct((count_src, count_rec, 2 * MAXLAG), jnp.float32),
         grid=(count_src // SOURCE_BLOCK,),
-        in_specs=[
-            pl.BlockSpec((rows, lhs.shape[1]), lambda i: (i, 0)),
-            pl.BlockSpec(weights.shape, lambda i: (0, 0)),
-        ],
+        in_specs=[part_spec, part_spec, pl.BlockSpec(weights.shape, lambda i: (0, 0))],
         out_specs=pl.BlockSpec((SOURCE_BLOCK, count_rec, 2 * MAXLAG), lambda i: (i, 0, 0)),
-    )(lhs, weights)
+    )(real_part, imag_part, weights)
 
 
 def ring_gather(value, axis_name, axis):
@@ -146,8 +147,8 @@
     own_rows = lax.dynamic_slice_in_dim(source_rows[0], shard * per_shard, per_shard)
     own_sources = jnp.take(whitened, own_rows, axis=1)
     sources = collect(own_sources)
-    lhs = cross_lhs(sources, receivers)
-    return transform(lhs, weights, lag_scale, receivers.shape[1])
+    real_part, imag_part = cross_parts(sources, receivers)
+    return transform(real_part, imag_part, weights, lag_scale)
 
 
 def split_mesh(mesh):

time: 76.2 us -> 75.8 us (level)
    reduce_sum x0 -> x2, local copies, waits for them, and re-layouts: none -> 3.6 us  [the longest x1 1.81 us: cross_parts(): jnp.sum(src[..., 1, :] * rec[..., 0, :] - src[..., 0, :] * rec[..., 1, :]...]
    convert_element_type x1 -> x0, local copies, waits for them, and re-layouts: 2.05 us -> none  [cross_lhs(): return lhs.astype(jnp.bfloat16)]
    concatenate x1 -> x0, local copies, waits for them, and re-layouts: 1.63 us -> none  [cross_lhs(): lhs = jnp.concatenate([real_sum, imag_sum], axis=2).reshape(-1, 2 * NBINS)]
where the time goes in v16:
time: 75.8 us; the launch traced here: 75.7 us
  starting transfers between devices  30.7 us (41%)
  waiting for transfers between devices  16.4 us (22%)
  Pallas kernels  8.94 us (12%)
  matrix products  7.3 us (10%)
  other arithmetic  6.16 us (8%)
  local copies, waits for them, and re-layouts  5.43 us (7%)
  between operations  0.78 us (1%)
    ppermute x11, starting transfers between devices, ring_gather(): lax.ppermute(value, axis_name, [(i, (i + shift) % size) for i in range(si...  20.2 us
    ppermute x11, waiting for transfers between devices, ring_gather(): lax.ppermute(value, axis_name, [(i, (i + shift) % size) for i in range(si...  16.3 us
    ppermute x3, starting transfers between devices, exchange_receivers(): lax.ppermute(block, WIN_AXES, [(i, (i + shift) % count) for i in range(co...  10.5 us
    pallas_call x1, Pallas kernels, transform(): pl.pallas_call(functools.partial(lag_kernel, scale=lag_scale), out_shape=...  8.94 us
    dot_general x1, matrix products, whiten(): jnp.dot(row_data, band_table(), preferred_element_type=jnp.float32)  7.3 us
    reduce_sum x1, other arithmetic, cross_parts(): jnp.sum(src[..., 1, :] * rec[..., 0, :] - src[..., 0, :] * rec[..., 1, :]...  3.15 us
    reduce_sum x1, local copies, waits for them, and re-layouts, cross_parts(): jnp.sum(src[..., 1, :] * rec[..., 0, :] - src[..., 0, :] * rec[..., 1, :]...  1.81 us
    reduce_sum x1, local copies, waits for them, and re-layouts, cross_parts(): jnp.sum(src[..., 0, :] * rec[..., 0, :] + src[..., 1, :] * rec[..., 1, :]...  1.79 us
  transfers between devices with their start and end apart: 14, of which 6 were waited for; matrix products, arithmetic and copies ran while one was open for 1% of the time, Pallas kernels for 0%

profile of v16, /device:TPU:1, one launch (start us, length us, event | category | flops | bytes accessed | tf_op | source)
XLA Modules:
  0.0 75.7 jit_solution(16551447262123706901)
XLA Ops:
  0.0 0.0 copy-start
  0.0 0.8 %fusion.13 = s32[4]{0:T(128)S(1)} fusion(s32[1,256]{1,0:T(1,128)} %param.5, s32[]{:T(128)S(6)} %select_n.229), kind=kLoop, calls=%fused_computation.125 | loop fusion | flops 12 | bytes 36 | tf_op jit(solution)/shard_map/jit(_take)/jit(_where)/select_n | solution.py:148
  0.8 0.7 compare_and_fusion
  1.5 0.0 copy-done
  1.5 7.3 %convolution_bitcast_fusion = f32[16,1152]{1,0:T(8,128)S(1)} fusion(bf16[7680,1152]{1,0:T(8,128)(2,1)} %constant.240.clone, bf16[1,16,7680]{2,1,0:T(8,128)(2,1)S(1)} %copy-done), kind=kOutput, calls=%fused_computation.3 | convolution fusion | flops 283115520 | bytes 18014208 | tf_op jit(solution)/shard_map/dot_general | solution.py:59
  8.8 0.1 fusion.2
  8.9 0.6 fusion.3
  9.6 0.1 fusion.6
  9.7 0.6 gather_fusion
  10.3 0.1 broadcast_select_fusion
  10.4 7.8 %collective-permute-start = (bf16[1,4,2,512]{3,2,1,0:T(2,128)(2,1)S(1)}, bf16[1,4,2,512]{3,2,1,0:T(2,128)(2,1)S(1)}, u32[]{:S(2)}, u32[]{:S(2)}) collective-permute-start(bf16[1,4,2,512]{3,2,1,0:T(2,128)(2,1)S(1)} %broadcast_select_fusion), channel_id=1, source_target_pairs={{0,2},{2,0},{1,3},{3,1},{4,6},{6,4},{5,7},{7,5},{8,10},{10,8},{9,1... | collective-permute-start | bytes 24584 | tf_op jit(solution)/shard_map/ppermute | solution.py:103
  18.4 0.8 %collective-permute-done = bf16[1,4,2,512]{3,2,1,0:T(2,128)(2,1)S(1)} collective-permute-done((bf16[1,4,2,512]{3,2,1,0:T(2,128)(2,1)S(1)}, bf16[1,4,2,512]{3,2,1,0:T(2,128)(2,1)S(1)}, u32[]{:S(2)}, u32[]{:S(2)}) %collective-permute-start) | collective-permute-done | bytes 8224 | tf_op jit(solution)/shard_map/ppermute | solution.py:103
  19.2 2.5 %collective-permute-start.3 = (bf16[2,4,2,512]{3,1,0,2:T(4,128)(2,1)S(1)}, bf16[2,4,2,512]{3,1,0,2:T(4,128)(2,1)S(1)}, u32[]{:S(2)}, u32[]{:S(2)}) collective-permute-start(bf16[2,4,2,512]{3,1,0,2:T(4,128)(2,1)S(1)} %copy_dynamic-update-slice_fusion), channel_id=1, source_target_pairs={{0,12},{4,0},{8,4},{12,8},{1,13},{5,1},{9,5},{13,9},{2,14},{6,2},{... | collective-permute-start | bytes 49160 | tf_op jit(solution)/shard_map/ppermute | solution.py:103
  21.8 0.5 collective-permute-start.2
  22.3 0.6 collective-permute-start.1
  22.9 3.2 %collective-permute-done.1 = bf16[2,4,2,512]{3,1,0,2:T(4,128)(2,1)S(1)} collective-permute-done((bf16[2,4,2,512]{3,1,0,2:T(4,128)(2,1)S(1)}, bf16[2,4,2,512]{3,1,0,2:T(4,128)(2,1)S(1)}, u32[]{:S(2)}, u32[]{:S(2)}) %collective-permute-start.1) | collective-permute-done | bytes 16416 | tf_op jit(solution)/shard_map/ppermute | solution.py:103
  26.1 0.0 collective-permute-done.2
  26.2 0.0 collective-permute-done.3
  26.2 2.9 %collective-permute-start.6 = (bf16[2,16,2,512]{3,1,0,2:T(8,128)(2,1)S(1)}, bf16[2,16,2,512]{3,1,0,2:T(8,128)(2,1)S(1)}, u32[]{:S(2)}, u32[]{:S(2)}) collective-permute-start(bf16[2,16,2,512]{3,1,0,2:T(8,128)(2,1)S(1)} %constant_dynamic-update-slice_fusion.8), channel_id=1, source_target_pairs={{0,48},{16,0},{32,16},{48,32},{1,49},{17,1},{33,17},{49,33},{2,50}... | collective-permute-start | bytes 196616 | tf_op jit(solution)/shard_map/ppermute | solution.py:103
  29.1 0.0 collective-permute-start.5
  29.1 0.4 collective-permute-start.4
  29.5 4.7 %collective-permute-done.4 = bf16[2,16,2,512]{3,1,0,2:T(8,128)(2,1)S(1)} collective-permute-done((bf16[2,16,2,512]{3,1,0,2:T(8,128)(2,1)S(1)}, bf16[2,16,2,512]{3,1,0,2:T(8,128)(2,1)S(1)}, u32[]{:S(2)}, u32[]{:S(2)}) %collective-permute-start.4) | collective-permute-done | bytes 65568 | tf_op jit(solution)/shard_map/ppermute | solution.py:103
  34.2 0.0 collective-permute-done.5
  34.2 0.0 collective-permute-done.6
  34.3 1.4 %collective-permute-start.7 = (bf16[2,64,2,512]{3,1,0,2:T(8,128)(2,1)S(1)}, bf16[2,64,2,512]{3,1,0,2:T(8,128)(2,1)S(1)}, u32[]{:S(2)}, u32[]{:S(2)}) collective-permute-start(bf16[2,64,2,512]{3,1,0,2:T(8,128)(2,1)S(1)} %constant_dynamic-update-slice_fusion.4), channel_id=1, source_target_pairs={{0,64},{64,128},{128,192},{192,0},{1,65},{65,129},{129,193},{193,1... | collective-permute-start | bytes 786440 | tf_op jit(solution)/shard_map/ppermute | solution.py:103
  35.7 5.1 %collective-permute-start.13 = (bf16[4,2,512]{2,0,1:T(4,128)(2,1)S(1)}, bf16[4,2,512]{2,0,1:T(4,128)(2,1)S(1)}, u32[]{:S(2)}, u32[]{:S(2)}) collective-permute-start(bf16[4,2,512]{2,0,1:T(4,128)(2,1)S(1)} %get-tuple-element.13), channel_id=1, source_target_pairs={{0,3},{1,0},{2,1},{3,2},{4,7},{5,4},{6,5},{7,6},{8,11},{9,8},{10,9... | collective-permute-start | bytes 24584 | tf_op jit(solution)/shard_map/ppermute | solution.py:128
  40.8 4.7 %collective-permute-start.11 = (bf16[4,2,512]{2,0,1:T(4,128)(2,1)S(1)}, bf16[4,2,512]{2,0,1:T(4,128)(2,1)S(1)}, u32[]{:S(2)}, u32[]{:S(2)}) collective-permute-start(bf16[4,2,512]{2,0,1:T(4,128)(2,1)S(1)} %get-tuple-element.14), channel_id=1, source_target_pairs={{0,1},{1,2},{2,3},{3,0},{4,5},{5,6},{6,7},{7,4},{8,9},{9,10},{10,1... | collective-permute-start | bytes 24584 | tf_op jit(solution)/shard_map/ppermute | solution.py:128
  45.5 2.6 %collective-permute-start.8 = (bf16[2,64,2,512]{3,1,0,2:T(8,128)(2,1)S(1)}, bf16[2,64,2,512]{3,1,0,2:T(8,128)(2,1)S(1)}, u32[]{:S(2)}, u32[]{:S(2)}) collective-permute-start(bf16[2,64,2,512]{3,1,0,2:T(8,128)(2,1)S(1)} %constant_dynamic-update-slice_fusion.4), channel_id=1, source_target_pairs={{0,128},{64,192},{128,0},{192,64},{1,129},{65,193},{129,1},{193,65... | collective-permute-start | bytes 786440 | tf_op jit(solution)/shard_map/ppermute | solution.py:103
  48.4 1.1 %collective-permute-start.9 = (bf16[2,64,2,512]{3,1,0,2:T(8,128)(2,1)S(1)}, bf16[2,64,2,512]{3,1,0,2:T(8,128)(2,1)S(1)}, u32[]{:S(2)}, u32[]{:S(2)}) collective-permute-start(bf16[2,64,2,512]{3,1,0,2:T(8,128)(2,1)S(1)} %constant_dynamic-update-slice_fusion.4), channel_id=1, source_target_pairs={{0,192},{64,0},{128,64},{192,128},{1,193},{65,1},{129,65},{193,129... | collective-permute-start | bytes 786440 | tf_op jit(solution)/shard_map/ppermute | solution.py:103
  49.6 0.1 broadcast_in_dim.53
  49.7 0.0 collective-permute-done.7
  49.7 0.7 collective-permute-start.12
  50.4 2.7 %collective-permute-done.8 = bf16[2,64,2,512]{3,1,0,2:T(8,128)(2,1)S(1)} collective-permute-done((bf16[2,64,2,512]{3,1,0,2:T(8,128)(2,1)S(1)}, bf16[2,64,2,512]{3,1,0,2:T(8,128)(2,1)S(1)}, u32[]{:S(2)}, u32[]{:S(2)}) %collective-permute-start.8) | collective-permute-done | bytes 262176 | tf_op jit(solution)/shard_map/ppermute | solution.py:103
  53.2 2.7 %collective-permute-done.9 = bf16[2,64,2,512]{3,1,0,2:T(8,128)(2,1)S(1)} collective-permute-done((bf16[2,64,2,512]{3,1,0,2:T(8,128)(2,1)S(1)}, bf16[2,64,2,512]{3,1,0,2:T(8,128)(2,1)S(1)}, u32[]{:S(2)}, u32[]{:S(2)}) %collective-permute-start.9) | collective-permute-done | bytes 262176 | tf_op jit(solution)/shard_map/ppermute | solution.py:103
  55.9 0.3 collective-permute-start.10
  56.2 0.0 collective-permute-done.11
  56.2 0.0 collective-permute-done.12
  56.3 0.0 collective-permute-done.13
  56.3 0.2 broadcast_in_dim.52
  56.5 0.1 bitcast_dynamic-update-slice_fusion.1
  56.6 2.2 %collective-permute-done.10 = bf16[2,256,2,512]{3,1,0,2:T(8,128)(2,1)S(1)} collective-permute-done((bf16[2,256,2,512]{3,1,0,2:T(8,128)(2,1)S(1)}, bf16[2,256,2,512]{3,1,0,2:T(8,128)(2,1)S(1)}, u32[]{:S(2)}, u32[]{:S(2)}) %collective-permute-start.10) | collective-permute-done | bytes 1048608 | tf_op jit(solution)/shard_map/ppermute | solution.py:103
  58.8 0.1 bitcast_dynamic-update-slice_fusion
  58.9 0.6 broadcast_in_dim.61
  59.5 0.4 slice_bitcast_fusion.1
  60.0 3.2 %subtract_reduce_fusion = (bf16[256,4,512]{2,0,1:T(8,128)(2,1)S(1)}, bf16[256,4,512]{2,0,1:T(8,128)(2,1)S(1)}) fusion(f32[4,4,512]{2,1,0:T(4,128)S(1)} %get-tuple-element.12, f32[4,256,512]{2,1,0:T(8,128)S(1)} %get-tuple-element.10, f32[4,4,512]{2,1,0:T(4,128)S(1)} %get-tuple-element.11, f32[4,256,512]{2,1,0:T(8,128)S(1)} %get-tuple-element.9), kind=kLoop, calls=%fused_computation.1 | loop fusion | flops 15728640 | bytes 6356992 | tf_op jit(solution)/shard_map/reduce_sum | solution.py:66
  63.1 1.8 %copy.15.im_ref = bf16[256,4,512]{2,1,0:T(4,128)(2,1)} copy(bf16[256,4,512]{2,0,1:T(8,128)(2,1)S(1)} %get-tuple-element.5) | data formatting | bytes 2097152 | tf_op jit(solution)/shard_map/reduce_sum | solution.py:66
  64.9 1.8 %copy.16.re_ref = bf16[256,4,512]{2,1,0:T(4,128)(2,1)} copy(bf16[256,4,512]{2,0,1:T(8,128)(2,1)S(1)} %get-tuple-element.6) | data formatting | bytes 2097152 | tf_op jit(solution)/shard_map/reduce_sum | solution.py:65
  66.7 8.9 %shard_map.46 = f32[256,4,2048]{2,1,0:T(4,128)} custom-call(bf16[256,4,512]{2,1,0:T(4,128)(2,1)} %copy.16.re_ref, bf16[256,4,512]{2,1,0:T(4,128)(2,1)} %copy.15.im_ref, bf16[1024,2048]{1,0:T(8,128)(2,1)} %constant.241.clone.w_ref), custom_call_target="tpu_custom_call" | custom-call | tf_op jit(solution)/shard_map/pallas_call | solution.py:86
  (28 shorter events, 0.4 us)
Async XLA Ops:
  0.0 1.5 %copy-start = (bf16[1,16,7680]{2,1,0:T(8,128)(2,1)S(1)}, bf16[1,16,7680]{2,1,0:T(8,128)(2,1)}, u32[]{:S(2)}) copy-start(bf16[1,16,7680]{2,1,0:T(8,128)(2,1)} %param.4) | copy-start | bytes 737284
  10.4 8.9 %collective-permute-start = (bf16[1,4,2,512]{3,2,1,0:T(2,128)(2,1)S(1)}, bf16[1,4,2,512]{3,2,1,0:T(2,128)(2,1)S(1)}, u32[]{:S(2)}, u32[]{:S(2)}) collective-permute-start(bf16[1,4,2,512]{3,2,1,0:T(2,128)(2,1)S(1)} %broadcast_select_fusion), channel_id=1, source_target_pairs={{0,2},{2,0},{1,3},{3,1},{4,6},{6,4},{5,7},{7,5},{8,10},{10,8},{9,1... | collective-permute-start | bytes 24584 | tf_op jit(solution)/shard_map/ppermute | solution.py:103
  19.2 6.9 %collective-permute-start.3 = (bf16[2,4,2,512]{3,1,0,2:T(4,128)(2,1)S(1)}, bf16[2,4,2,512]{3,1,0,2:T(4,128)(2,1)S(1)}, u32[]{:S(2)}, u32[]{:S(2)}) collective-permute-start(bf16[2,4,2,512]{3,1,0,2:T(4,128)(2,1)S(1)} %copy_dynamic-update-slice_fusion), channel_id=1, source_target_pairs={{0,12},{4,0},{8,4},{12,8},{1,13},{5,1},{9,5},{13,9},{2,14},{6,2},{... | collective-permute-start | bytes 49160 | tf_op jit(solution)/shard_map/ppermute | solution.py:103
  21.8 4.3 %collective-permute-start.2 = (bf16[2,4,2,512]{3,1,0,2:T(4,128)(2,1)S(1)}, bf16[2,4,2,512]{3,1,0,2:T(4,128)(2,1)S(1)}, u32[]{:S(2)}, u32[]{:S(2)}) collective-permute-start(bf16[2,4,2,512]{3,1,0,2:T(4,128)(2,1)S(1)} %copy_dynamic-update-slice_fusion), channel_id=1, source_target_pairs={{0,8},{4,12},{8,0},{12,4},{1,9},{5,13},{9,1},{13,5},{2,10},{6,14},... | collective-permute-start | bytes 49160 | tf_op jit(solution)/shard_map/ppermute | solution.py:103
  22.3 3.8 %collective-permute-start.1 = (bf16[2,4,2,512]{3,1,0,2:T(4,128)(2,1)S(1)}, bf16[2,4,2,512]{3,1,0,2:T(4,128)(2,1)S(1)}, u32[]{:S(2)}, u32[]{:S(2)}) collective-permute-start(bf16[2,4,2,512]{3,1,0,2:T(4,128)(2,1)S(1)} %copy_dynamic-update-slice_fusion), channel_id=1, source_target_pairs={{0,4},{4,8},{8,12},{12,0},{1,5},{5,9},{9,13},{13,1},{2,6},{6,10},{... | collective-permute-start | bytes 49160 | tf_op jit(solution)/shard_map/ppermute | solution.py:103
  26.2 8.1 %collective-permute-start.6 = (bf16[2,16,2,512]{3,1,0,2:T(8,128)(2,1)S(1)}, bf16[2,16,2,512]{3,1,0,2:T(8,128)(2,1)S(1)}, u32[]{:S(2)}, u32[]{:S(2)}) collective-permute-start(bf16[2,16,2,512]{3,1,0,2:T(8,128)(2,1)S(1)} %constant_dynamic-update-slice_fusion.8), channel_id=1, source_target_pairs={{0,48},{16,0},{32,16},{48,32},{1,49},{17,1},{33,17},{49,33},{2,50}... | collective-permute-start | bytes 196616 | tf_op jit(solution)/shard_map/ppermute | solution.py:103
  29.1 5.1 %collective-permute-start.5 = (bf16[2,16,2,512]{3,1,0,2:T(8,128)(2,1)S(1)}, bf16[2,16,2,512]{3,1,0,2:T(8,128)(2,1)S(1)}, u32[]{:S(2)}, u32[]{:S(2)}) collective-permute-start(bf16[2,16,2,512]{3,1,0,2:T(8,128)(2,1)S(1)} %constant_dynamic-update-slice_fusion.8), channel_id=1, source_target_pairs={{0,32},{16,48},{32,0},{48,16},{1,33},{17,49},{33,1},{49,17},{2,34}... | collective-permute-start | bytes 196616 | tf_op jit(solution)/shard_map/ppermute | solution.py:103
  29.1 5.1 %collective-permute-start.4 = (bf16[2,16,2,512]{3,1,0,2:T(8,128)(2,1)S(1)}, bf16[2,16,2,512]{3,1,0,2:T(8,128)(2,1)S(1)}, u32[]{:S(2)}, u32[]{:S(2)}) collective-permute-start(bf16[2,16,2,512]{3,1,0,2:T(8,128)(2,1)S(1)} %constant_dynamic-update-slice_fusion.8), channel_id=1, source_target_pairs={{0,16},{16,32},{32,48},{48,0},{1,17},{17,33},{33,49},{49,1},{2,18}... | collective-permute-start | bytes 196616 | tf_op jit(solution)/shard_map/ppermute | solution.py:103
  34.3 15.4 %collective-permute-start.7 = (bf16[2,64,2,512]{3,1,0,2:T(8,128)(2,1)S(1)}, bf16[2,64,2,512]{3,1,0,2:T(8,128)(2,1)S(1)}, u32[]{:S(2)}, u32[]{:S(2)}) collective-permute-start(bf16[2,64,2,512]{3,1,0,2:T(8,128)(2,1)S(1)} %constant_dynamic-update-slice_fusion.4), channel_id=1, source_target_pairs={{0,64},{64,128},{128,192},{192,0},{1,65},{65,129},{129,193},{193,1... | collective-permute-start | bytes 786440 | tf_op jit(solution)/shard_map/ppermute | solution.py:103
  35.7 20.6 %collective-permute-start.13 = (bf16[4,2,512]{2,0,1:T(4,128)(2,1)S(1)}, bf16[4,2,512]{2,0,1:T(4,128)(2,1)S(1)}, u32[]{:S(2)}, u32[]{:S(2)}) collective-permute-start(bf16[4,2,512]{2,0,1:T(4,128)(2,1)S(1)} %get-tuple-element.13), channel_id=1, source_target_pairs={{0,3},{1,0},{2,1},{3,2},{4,7},{5,4},{6,5},{7,6},{8,11},{9,8},{10,9... | collective-permute-start | bytes 24584 | tf_op jit(solution)/shard_map/ppermute | solution.py:128
  40.8 15.4 %collective-permute-start.11 = (bf16[4,2,512]{2,0,1:T(4,128)(2,1)S(1)}, bf16[4,2,512]{2,0,1:T(4,128)(2,1)S(1)}, u32[]{:S(2)}, u32[]{:S(2)}) collective-permute-start(bf16[4,2,512]{2,0,1:T(4,128)(2,1)S(1)} %get-tuple-element.14), channel_id=1, source_target_pairs={{0,1},{1,2},{2,3},{3,0},{4,5},{5,6},{6,7},{7,4},{8,9},{9,10},{10,1... | collective-permute-start | bytes 24584 | tf_op jit(solution)/shard_map/ppermute | solution.py:128
  45.5 7.6 %collective-permute-start.8 = (bf16[2,64,2,512]{3,1,0,2:T(8,128)(2,1)S(1)}, bf16[2,64,2,512]{3,1,0,2:T(8,128)(2,1)S(1)}, u32[]{:S(2)}, u32[]{:S(2)}) collective-permute-start(bf16[2,64,2,512]{3,1,0,2:T(8,128)(2,1)S(1)} %constant_dynamic-update-slice_fusion.4), channel_id=1, source_target_pairs={{0,128},{64,192},{128,0},{192,64},{1,129},{65,193},{129,1},{193,65... | collective-permute-start | bytes 786440 | tf_op jit(solution)/shard_map/ppermute | solution.py:103
  48.4 7.5 %collective-permute-start.9 = (bf16[2,64,2,512]{3,1,0,2:T(8,128)(2,1)S(1)}, bf16[2,64,2,512]{3,1,0,2:T(8,128)(2,1)S(1)}, u32[]{:S(2)}, u32[]{:S(2)}) collective-permute-start(bf16[2,64,2,512]{3,1,0,2:T(8,128)(2,1)S(1)} %constant_dynamic-update-slice_fusion.4), channel_id=1, source_target_pairs={{0,192},{64,0},{128,64},{192,128},{1,193},{65,1},{129,65},{193,129... | collective-permute-start | bytes 786440 | tf_op jit(solution)/shard_map/ppermute | solution.py:103
  49.7 6.5 %collective-permute-start.12 = (bf16[4,2,512]{2,0,1:T(4,128)(2,1)S(1)}, bf16[4,2,512]{2,0,1:T(4,128)(2,1)S(1)}, u32[]{:S(2)}, u32[]{:S(2)}) collective-permute-start(bf16[4,2,512]{2,0,1:T(4,128)(2,1)S(1)} %get-tuple-element.15), channel_id=1, source_target_pairs={{0,2},{1,3},{2,0},{3,1},{4,6},{5,7},{6,4},{7,5},{8,10},{9,11},{10,... | collective-permute-start | bytes 24584 | tf_op jit(solution)/shard_map/ppermute | solution.py:128
  55.9 2.9 %collective-permute-start.10 = (bf16[2,256,2,512]{3,1,0,2:T(8,128)(2,1)S(1)}, bf16[2,256,2,512]{3,1,0,2:T(8,128)(2,1)S(1)}, u32[]{:S(2)}, u32[]{:S(2)}) collective-permute-start(bf16[2,256,2,512]{3,1,0,2:T(8,128)(2,1)S(1)} %constant_dynamic-update-slice_fusion), channel_id=1, source_target_pairs={{0,1},{1,0},{2,3},{3,2},{4,5},{5,4},{6,7},{7,6},{8,9},{9,8},{10,11... | collective-permute-start | bytes 3145736 | tf_op jit(solution)/shard_map/ppermute | solution.py:103

commit v17 on v16

--- a/solution.py
+++ b/solution.py
@@ -71,25 +71,23 @@
 
 
 def lag_kernel(re_ref, im_ref, w_ref, o_ref, *, scale):
-    def flat(ref):
-        return ref[...].astype(jnp.float32).reshape(-1, ref.shape[2]).astype(jnp.bfloat16)
-
-    bins = re_ref.shape[2]
-    result = jnp.dot(flat(re_ref), w_ref[:bins], preferred_element_type=jnp.float32)
-    result = result + jnp.dot(flat(im_ref), w_ref[bins:], preferred_element_type=jnp.float32)
-    o_ref[...] = (result * scale).reshape(o_ref.shape)
+    count_rec, block, bins = re_ref.shape
+    result = jnp.dot(re_ref[...].reshape(-1, bins), w_ref[:bins], preferred_element_type=jnp.float32)
+    result = result + jnp.dot(im_ref[...].reshape(-1, bins), w_ref[bins:], preferred_element_type=jnp.float32)
+    result = (result * scale).reshape(count_rec, block, result.shape[1])
+    o_ref[...] = jnp.swapaxes(result, 0, 1)
 
 
 def transform(real_part, imag_part, weights, lag_scale):
     count_src, count_rec, bins = real_part.shape
-    part_spec = pl.BlockSpec((SOURCE_BLOCK, count_rec, bins), lambda i: (i, 0, 0))
+    part_spec = pl.BlockSpec((count_rec, SOURCE_BLOCK, bins), lambda i: (0, i, 0))
     return pl.pallas_call(
         functools.partial(lag_kernel, scale=lag_scale),
         out_shape=jax.ShapeDtypeStruct((count_src, count_rec, 2 * MAXLAG), jnp.float32),
         grid=(count_src // SOURCE_BLOCK,),
         in_specs=[part_spec, part_spec, pl.BlockSpec(weights.shape, lambda i: (0, 0))],
         out_specs=pl.BlockSpec((SOURCE_BLOCK, count_rec, 2 * MAXLAG), lambda i: (i, 0, 0)),
-    )(real_part, imag_part, weights)
+    )(jnp.swapaxes(real_part, 0, 1), jnp.swapaxes(imag_part, 0, 1), weights)
 
 
 def ring_gather(value, axis_name, axis):

time: 75.8 us -> 74.1 us (0.978)
  local copies, waits for them, and re-layouts: 5.43 us -> 1.82 us
  other arithmetic: 6.16 us -> 7.4 us
    reduce_sum x2 -> x0, local copies, waits for them, and re-layouts: 3.6 us -> none  [the longest x1 1.81 us: cross_parts(): jnp.sum(src[..., 1, :] * rec[..., 0, :] - src[..., 0, :] * rec[..., 1, :]...]
    reduce_sum x1, other arithmetic: 3.15 us -> 4.39 us  [cross_parts(): jnp.sum(src[..., 1, :] * rec[..., 0, :] - src[..., 0, :] * rec[..., 1, :]...]
where the time goes in v17:
time: 74.1 us; the launch traced here: 74 us
  starting transfers between devices  30.7 us (41%)
  waiting for transfers between devices  16.4 us (22%)
  Pallas kernels  9.65 us (13%)
  other arithmetic  7.4 us (10%)
  matrix products  7.3 us (10%)
  local copies, waits for them, and re-layouts  1.82 us (2%)
  between operations  0.77 us (1%)
    ppermute x11, starting transfers between devices, ring_gather(): lax.ppermute(value, axis_name, [(i, (i + shift) % size) for i in range(si...  20.2 us
    ppermute x11, waiting for transfers between devices, ring_gather(): lax.ppermute(value, axis_name, [(i, (i + shift) % size) for i in range(si...  16.3 us
    ppermute x3, starting transfers between devices, exchange_receivers(): lax.ppermute(block, WIN_AXES, [(i, (i + shift) % count) for i in range(co...  10.5 us
    pallas_call x1, Pallas kernels, transform(): pl.pallas_call(functools.partial(lag_kernel, scale=lag_scale), out_shape=...  9.65 us
    dot_general x1, matrix products, whiten(): jnp.dot(row_data, band_table(), preferred_element_type=jnp.float32)  7.3 us
    reduce_sum x1, other arithmetic, cross_parts(): jnp.sum(src[..., 1, :] * rec[..., 0, :] - src[..., 0, :] * rec[..., 1, :]...  4.39 us
  transfers between devices with their start and end apart: 14, of which 6 were waited for; matrix products, arithmetic and copies ran while one was open for 1% of the time, Pallas kernels for 0%

profile of v17, /device:TPU:1, one launch (start us, length us, event | category | flops | bytes accessed | tf_op | source)
XLA Modules:
  0.0 74.0 jit_solution(2037533363661375500)
XLA Ops:
  0.0 0.0 copy-start
  0.0 0.8 %fusion.13 = s32[4]{0:T(128)S(1)} fusion(s32[1,256]{1,0:T(1,128)} %param.5, s32[]{:T(128)S(6)} %select_n.229), kind=kLoop, calls=%fused_computation.125 | loop fusion | flops 12 | bytes 36 | tf_op jit(solution)/shard_map/jit(_take)/jit(_where)/select_n | solution.py:146
  0.8 0.7 compare_and_fusion
  1.5 0.0 copy-done
  1.5 7.3 %convolution_bitcast_fusion = f32[16,1152]{1,0:T(8,128)S(1)} fusion(bf16[7680,1152]{1,0:T(8,128)(2,1)} %constant.240.clone, bf16[1,16,7680]{2,1,0:T(8,128)(2,1)S(1)} %copy-done), kind=kOutput, calls=%fused_computation.3 | convolution fusion | flops 283115520 | bytes 18014208 | tf_op jit(solution)/shard_map/dot_general | solution.py:59
  8.8 0.1 fusion.2
  8.9 0.6 fusion.3
  9.6 0.1 fusion.6
  9.7 0.6 gather_fusion
  10.3 0.1 broadcast_select_fusion
  10.4 7.8 %collective-permute-start = (bf16[1,4,2,512]{3,2,1,0:T(2,128)(2,1)S(1)}, bf16[1,4,2,512]{3,2,1,0:T(2,128)(2,1)S(1)}, u32[]{:S(2)}, u32[]{:S(2)}) collective-permute-start(bf16[1,4,2,512]{3,2,1,0:T(2,128)(2,1)S(1)} %broadcast_select_fusion), channel_id=1, source_target_pairs={{0,2},{2,0},{1,3},{3,1},{4,6},{6,4},{5,7},{7,5},{8,10},{10,8},{9,1... | collective-permute-start | bytes 24584 | tf_op jit(solution)/shard_map/ppermute | solution.py:101
  18.4 0.8 %collective-permute-done = bf16[1,4,2,512]{3,2,1,0:T(2,128)(2,1)S(1)} collective-permute-done((bf16[1,4,2,512]{3,2,1,0:T(2,128)(2,1)S(1)}, bf16[1,4,2,512]{3,2,1,0:T(2,128)(2,1)S(1)}, u32[]{:S(2)}, u32[]{:S(2)}) %collective-permute-start) | collective-permute-done | bytes 8224 | tf_op jit(solution)/shard_map/ppermute | solution.py:101
  19.2 2.5 %collective-permute-start.3 = (bf16[2,4,2,512]{3,1,0,2:T(4,128)(2,1)S(1)}, bf16[2,4,2,512]{3,1,0,2:T(4,128)(2,1)S(1)}, u32[]{:S(2)}, u32[]{:S(2)}) collective-permute-start(bf16[2,4,2,512]{3,1,0,2:T(4,128)(2,1)S(1)} %copy_dynamic-update-slice_fusion), channel_id=1, source_target_pairs={{0,12},{4,0},{8,4},{12,8},{1,13},{5,1},{9,5},{13,9},{2,14},{6,2},{... | collective-permute-start | bytes 49160 | tf_op jit(solution)/shard_map/ppermute | solution.py:101
  21.8 0.5 collective-permute-start.2
  22.3 0.6 collective-permute-start.1
  22.9 3.2 %collective-permute-done.1 = bf16[2,4,2,512]{3,1,0,2:T(4,128)(2,1)S(1)} collective-permute-done((bf16[2,4,2,512]{3,1,0,2:T(4,128)(2,1)S(1)}, bf16[2,4,2,512]{3,1,0,2:T(4,128)(2,1)S(1)}, u32[]{:S(2)}, u32[]{:S(2)}) %collective-permute-start.1) | collective-permute-done | bytes 16416 | tf_op jit(solution)/shard_map/ppermute | solution.py:101
  26.1 0.0 collective-permute-done.2
  26.2 0.0 collective-permute-done.3
  26.2 2.9 %collective-permute-start.6 = (bf16[2,16,2,512]{3,1,0,2:T(8,128)(2,1)S(1)}, bf16[2,16,2,512]{3,1,0,2:T(8,128)(2,1)S(1)}, u32[]{:S(2)}, u32[]{:S(2)}) collective-permute-start(bf16[2,16,2,512]{3,1,0,2:T(8,128)(2,1)S(1)} %constant_dynamic-update-slice_fusion.8), channel_id=1, source_target_pairs={{0,48},{16,0},{32,16},{48,32},{1,49},{17,1},{33,17},{49,33},{2,50}... | collective-permute-start | bytes 196616 | tf_op jit(solution)/shard_map/ppermute | solution.py:101
  29.1 0.0 collective-permute-start.5
  29.1 0.4 collective-permute-start.4
  29.5 4.7 %collective-permute-done.4 = bf16[2,16,2,512]{3,1,0,2:T(8,128)(2,1)S(1)} collective-permute-done((bf16[2,16,2,512]{3,1,0,2:T(8,128)(2,1)S(1)}, bf16[2,16,2,512]{3,1,0,2:T(8,128)(2,1)S(1)}, u32[]{:S(2)}, u32[]{:S(2)}) %collective-permute-start.4) | collective-permute-done | bytes 65568 | tf_op jit(solution)/shard_map/ppermute | solution.py:101
  34.2 0.0 collective-permute-done.5
  34.2 0.0 collective-permute-done.6
  34.3 1.4 %collective-permute-start.7 = (bf16[2,64,2,512]{3,1,0,2:T(8,128)(2,1)S(1)}, bf16[2,64,2,512]{3,1,0,2:T(8,128)(2,1)S(1)}, u32[]{:S(2)}, u32[]{:S(2)}) collective-permute-start(bf16[2,64,2,512]{3,1,0,2:T(8,128)(2,1)S(1)} %constant_dynamic-update-slice_fusion.4), channel_id=1, source_target_pairs={{0,64},{64,128},{128,192},{192,0},{1,65},{65,129},{129,193},{193,1... | collective-permute-start | bytes 786440 | tf_op jit(solution)/shard_map/ppermute | solution.py:101
  35.7 5.1 %collective-permute-start.13 = (bf16[4,2,512]{2,0,1:T(4,128)(2,1)S(1)}, bf16[4,2,512]{2,0,1:T(4,128)(2,1)S(1)}, u32[]{:S(2)}, u32[]{:S(2)}) collective-permute-start(bf16[4,2,512]{2,0,1:T(4,128)(2,1)S(1)} %get-tuple-element.13), channel_id=1, source_target_pairs={{0,3},{1,0},{2,1},{3,2},{4,7},{5,4},{6,5},{7,6},{8,11},{9,8},{10,9... | collective-permute-start | bytes 24584 | tf_op jit(solution)/shard_map/ppermute | solution.py:126
  40.8 4.7 %collective-permute-start.11 = (bf16[4,2,512]{2,0,1:T(4,128)(2,1)S(1)}, bf16[4,2,512]{2,0,1:T(4,128)(2,1)S(1)}, u32[]{:S(2)}, u32[]{:S(2)}) collective-permute-start(bf16[4,2,512]{2,0,1:T(4,128)(2,1)S(1)} %get-tuple-element.14), channel_id=1, source_target_pairs={{0,1},{1,2},{2,3},{3,0},{4,5},{5,6},{6,7},{7,4},{8,9},{9,10},{10,1... | collective-permute-start | bytes 24584 | tf_op jit(solution)/shard_map/ppermute | solution.py:126
  45.5 2.6 %collective-permute-start.8 = (bf16[2,64,2,512]{3,1,0,2:T(8,128)(2,1)S(1)}, bf16[2,64,2,512]{3,1,0,2:T(8,128)(2,1)S(1)}, u32[]{:S(2)}, u32[]{:S(2)}) collective-permute-start(bf16[2,64,2,512]{3,1,0,2:T(8,128)(2,1)S(1)} %constant_dynamic-update-slice_fusion.4), channel_id=1, source_target_pairs={{0,128},{64,192},{128,0},{192,64},{1,129},{65,193},{129,1},{193,65... | collective-permute-start | bytes 786440 | tf_op jit(solution)/shard_map/ppermute | solution.py:101
  48.4 1.1 %collective-permute-start.9 = (bf16[2,64,2,512]{3,1,0,2:T(8,128)(2,1)S(1)}, bf16[2,64,2,512]{3,1,0,2:T(8,128)(2,1)S(1)}, u32[]{:S(2)}, u32[]{:S(2)}) collective-permute-start(bf16[2,64,2,512]{3,1,0,2:T(8,128)(2,1)S(1)} %constant_dynamic-update-slice_fusion.4), channel_id=1, source_target_pairs={{0,192},{64,0},{128,64},{192,128},{1,193},{65,1},{129,65},{193,129... | collective-permute-start | bytes 786440 | tf_op jit(solution)/shard_map/ppermute | solution.py:101
  49.6 0.1 broadcast_in_dim.53
  49.7 0.0 collective-permute-done.7
  49.7 0.7 collective-permute-start.12
  50.4 2.7 %collective-permute-done.8 = bf16[2,64,2,512]{3,1,0,2:T(8,128)(2,1)S(1)} collective-permute-done((bf16[2,64,2,512]{3,1,0,2:T(8,128)(2,1)S(1)}, bf16[2,64,2,512]{3,1,0,2:T(8,128)(2,1)S(1)}, u32[]{:S(2)}, u32[]{:S(2)}) %collective-permute-start.8) | collective-permute-done | bytes 262176 | tf_op jit(solution)/shard_map/ppermute | solution.py:101
  53.2 2.7 %collective-permute-done.9 = bf16[2,64,2,512]{3,1,0,2:T(8,128)(2,1)S(1)} collective-permute-done((bf16[2,64,2,512]{3,1,0,2:T(8,128)(2,1)S(1)}, bf16[2,64,2,512]{3,1,0,2:T(8,128)(2,1)S(1)}, u32[]{:S(2)}, u32[]{:S(2)}) %collective-permute-start.9) | collective-permute-done | bytes 262176 | tf_op jit(solution)/shard_map/ppermute | solution.py:101
  55.9 0.3 collective-permute-start.10
  56.2 0.0 collective-permute-done.11
  56.2 0.0 collective-permute-done.12
  56.3 0.0 collective-permute-done.13
  56.3 0.2 broadcast_in_dim.52
  56.5 0.1 bitcast_dynamic-update-slice_fusion.1
  56.6 2.2 %collective-permute-done.10 = bf16[2,256,2,512]{3,1,0,2:T(8,128)(2,1)S(1)} collective-permute-done((bf16[2,256,2,512]{3,1,0,2:T(8,128)(2,1)S(1)}, bf16[2,256,2,512]{3,1,0,2:T(8,128)(2,1)S(1)}, u32[]{:S(2)}, u32[]{:S(2)}) %collective-permute-start.10) | collective-permute-done | bytes 1048608 | tf_op jit(solution)/shard_map/ppermute | solution.py:101
  58.8 0.1 bitcast_dynamic-update-slice_fusion
  58.9 0.6 broadcast_in_dim.61
  59.5 0.4 slice_bitcast_fusion.1
  60.0 4.4 %subtract_reduce_fusion = (bf16[256,4,512]{2,0,1:T(8,128)(2,1)}, bf16[256,4,512]{2,0,1:T(8,128)(2,1)}) fusion(f32[4,4,512]{2,1,0:T(4,128)S(1)} %get-tuple-element.12, f32[4,256,512]{2,1,0:T(8,128)S(1)} %get-tuple-element.10, f32[4,4,512]{2,1,0:T(4,128)S(1)} %get-tuple-element.11, f32[4,256,512]{2,1,0:T(8,128)S(1)} %get-tuple-element.9), kind=kLoop, calls=%fused_computation.1 | loop fusion | flops 15728640 | bytes 6356992 | tf_op jit(solution)/shard_map/reduce_sum | solution.py:66
  64.4 9.7 %shard_map.46 = f32[256,4,2048]{2,1,0:T(4,128)} custom-call(bf16[4,256,512]{2,1,0:T(8,128)(2,1)} %bitcast.49, bf16[4,256,512]{2,1,0:T(8,128)(2,1)} %bitcast.48, bf16[1024,2048]{1,0:T(8,128)(2,1)} %constant.241.clone.w_ref), custom_call_target="tpu_custom_call" | custom-call | tf_op jit(solution)/shard_map/pallas_call | solution.py:84
  (28 shorter events, 0.4 us)
Async XLA Ops:
  0.0 1.5 %copy-start = (bf16[1,16,7680]{2,1,0:T(8,128)(2,1)S(1)}, bf16[1,16,7680]{2,1,0:T(8,128)(2,1)}, u32[]{:S(2)}) copy-start(bf16[1,16,7680]{2,1,0:T(8,128)(2,1)} %param.4) | copy-start | bytes 737284
  10.4 8.9 %collective-permute-start = (bf16[1,4,2,512]{3,2,1,0:T(2,128)(2,1)S(1)}, bf16[1,4,2,512]{3,2,1,0:T(2,128)(2,1)S(1)}, u32[]{:S(2)}, u32[]{:S(2)}) collective-permute-start(bf16[1,4,2,512]{3,2,1,0:T(2,128)(2,1)S(1)} %broadcast_select_fusion), channel_id=1, source_target_pairs={{0,2},{2,0},{1,3},{3,1},{4,6},{6,4},{5,7},{7,5},{8,10},{10,8},{9,1... | collective-permute-start | bytes 24584 | tf_op jit(solution)/shard_map/ppermute | solution.py:101
  19.2 6.9 %collective-permute-start.3 = (bf16[2,4,2,512]{3,1,0,2:T(4,128)(2,1)S(1)}, bf16[2,4,2,512]{3,1,0,2:T(4,128)(2,1)S(1)}, u32[]{:S(2)}, u32[]{:S(2)}) collective-permute-start(bf16[2,4,2,512]{3,1,0,2:T(4,128)(2,1)S(1)} %copy_dynamic-update-slice_fusion), channel_id=1, source_target_pairs={{0,12},{4,0},{8,4},{12,8},{1,13},{5,1},{9,5},{13,9},{2,14},{6,2},{... | collective-permute-start | bytes 49160 | tf_op jit(solution)/shard_map/ppermute | solution.py:101
  21.8 4.3 %collective-permute-start.2 = (bf16[2,4,2,512]{3,1,0,2:T(4,128)(2,1)S(1)}, bf16[2,4,2,512]{3,1,0,2:T(4,128)(2,1)S(1)}, u32[]{:S(2)}, u32[]{:S(2)}) collective-permute-start(bf16[2,4,2,512]{3,1,0,2:T(4,128)(2,1)S(1)} %copy_dynamic-update-slice_fusion), channel_id=1, source_target_pairs={{0,8},{4,12},{8,0},{12,4},{1,9},{5,13},{9,1},{13,5},{2,10},{6,14},... | collective-permute-start | bytes 49160 | tf_op jit(solution)/shard_map/ppermute | solution.py:101
  22.3 3.8 %collective-permute-start.1 = (bf16[2,4,2,512]{3,1,0,2:T(4,128)(2,1)S(1)}, bf16[2,4,2,512]{3,1,0,2:T(4,128)(2,1)S(1)}, u32[]{:S(2)}, u32[]{:S(2)}) collective-permute-start(bf16[2,4,2,512]{3,1,0,2:T(4,128)(2,1)S(1)} %copy_dynamic-update-slice_fusion), channel_id=1, source_target_pairs={{0,4},{4,8},{8,12},{12,0},{1,5},{5,9},{9,13},{13,1},{2,6},{6,10},{... | collective-permute-start | bytes 49160 | tf_op jit(solution)/shard_map/ppermute | solution.py:101
  26.2 8.1 %collective-permute-start.6 = (bf16[2,16,2,512]{3,1,0,2:T(8,128)(2,1)S(1)}, bf16[2,16,2,512]{3,1,0,2:T(8,128)(2,1)S(1)}, u32[]{:S(2)}, u32[]{:S(2)}) collective-permute-start(bf16[2,16,2,512]{3,1,0,2:T(8,128)(2,1)S(1)} %constant_dynamic-update-slice_fusion.8), channel_id=1, source_target_pairs={{0,48},{16,0},{32,16},{48,32},{1,49},{17,1},{33,17},{49,33},{2,50}... | collective-permute-start | bytes 196616 | tf_op jit(solution)/shard_map/ppermute | solution.py:101
  29.1 5.1 %collective-permute-start.5 = (bf16[2,16,2,512]{3,1,0,2:T(8,128)(2,1)S(1)}, bf16[2,16,2,512]{3,1,0,2:T(8,128)(2,1)S(1)}, u32[]{:S(2)}, u32[]{:S(2)}) collective-permute-start(bf16[2,16,2,512]{3,1,0,2:T(8,128)(2,1)S(1)} %constant_dynamic-update-slice_fusion.8), channel_id=1, source_target_pairs={{0,32},{16,48},{32,0},{48,16},{1,33},{17,49},{33,1},{49,17},{2,34}... | collective-permute-start | bytes 196616 | tf_op jit(solution)/shard_map/ppermute | solution.py:101
  29.1 5.1 %collective-permute-start.4 = (bf16[2,16,2,512]{3,1,0,2:T(8,128)(2,1)S(1)}, bf16[2,16,2,512]{3,1,0,2:T(8,128)(2,1)S(1)}, u32[]{:S(2)}, u32[]{:S(2)}) collective-permute-start(bf16[2,16,2,512]{3,1,0,2:T(8,128)(2,1)S(1)} %constant_dynamic-update-slice_fusion.8), channel_id=1, source_target_pairs={{0,16},{16,32},{32,48},{48,0},{1,17},{17,33},{33,49},{49,1},{2,18}... | collective-permute-start | bytes 196616 | tf_op jit(solution)/shard_map/ppermute | solution.py:101
  34.3 15.4 %collective-permute-start.7 = (bf16[2,64,2,512]{3,1,0,2:T(8,128)(2,1)S(1)}, bf16[2,64,2,512]{3,1,0,2:T(8,128)(2,1)S(1)}, u32[]{:S(2)}, u32[]{:S(2)}) collective-permute-start(bf16[2,64,2,512]{3,1,0,2:T(8,128)(2,1)S(1)} %constant_dynamic-update-slice_fusion.4), channel_id=1, source_target_pairs={{0,64},{64,128},{128,192},{192,0},{1,65},{65,129},{129,193},{193,1... | collective-permute-start | bytes 786440 | tf_op jit(solution)/shard_map/ppermute | solution.py:101
  35.7 20.6 %collective-permute-start.13 = (bf16[4,2,512]{2,0,1:T(4,128)(2,1)S(1)}, bf16[4,2,512]{2,0,1:T(4,128)(2,1)S(1)}, u32[]{:S(2)}, u32[]{:S(2)}) collective-permute-start(bf16[4,2,512]{2,0,1:T(4,128)(2,1)S(1)} %get-tuple-element.13), channel_id=1, source_target_pairs={{0,3},{1,0},{2,1},{3,2},{4,7},{5,4},{6,5},{7,6},{8,11},{9,8},{10,9... | collective-permute-start | bytes 24584 | tf_op jit(solution)/shard_map/ppermute | solution.py:126
  40.8 15.4 %collective-permute-start.11 = (bf16[4,2,512]{2,0,1:T(4,128)(2,1)S(1)}, bf16[4,2,512]{2,0,1:T(4,128)(2,1)S(1)}, u32[]{:S(2)}, u32[]{:S(2)}) collective-permute-start(bf16[4,2,512]{2,0,1:T(4,128)(2,1)S(1)} %get-tuple-element.14), channel_id=1, source_target_pairs={{0,1},{1,2},{2,3},{3,0},{4,5},{5,6},{6,7},{7,4},{8,9},{9,10},{10,1... | collective-permute-start | bytes 24584 | tf_op jit(solution)/shard_map/ppermute | solution.py:126
  45.5 7.6 %collective-permute-start.8 = (bf16[2,64,2,512]{3,1,0,2:T(8,128)(2,1)S(1)}, bf16[2,64,2,512]{3,1,0,2:T(8,128)(2,1)S(1)}, u32[]{:S(2)}, u32[]{:S(2)}) collective-permute-start(bf16[2,64,2,512]{3,1,0,2:T(8,128)(2,1)S(1)} %constant_dynamic-update-slice_fusion.4), channel_id=1, source_target_pairs={{0,128},{64,192},{128,0},{192,64},{1,129},{65,193},{129,1},{193,65... | collective-permute-start | bytes 786440 | tf_op jit(solution)/shard_map/ppermute | solution.py:101
  48.4 7.5 %collective-permute-start.9 = (bf16[2,64,2,512]{3,1,0,2:T(8,128)(2,1)S(1)}, bf16[2,64,2,512]{3,1,0,2:T(8,128)(2,1)S(1)}, u32[]{:S(2)}, u32[]{:S(2)}) collective-permute-start(bf16[2,64,2,512]{3,1,0,2:T(8,128)(2,1)S(1)} %constant_dynamic-update-slice_fusion.4), channel_id=1, source_target_pairs={{0,192},{64,0},{128,64},{192,128},{1,193},{65,1},{129,65},{193,129... | collective-permute-start | bytes 786440 | tf_op jit(solution)/shard_map/ppermute | solution.py:101
  49.7 6.5 %collective-permute-start.12 = (bf16[4,2,512]{2,0,1:T(4,128)(2,1)S(1)}, bf16[4,2,512]{2,0,1:T(4,128)(2,1)S(1)}, u32[]{:S(2)}, u32[]{:S(2)}) collective-permute-start(bf16[4,2,512]{2,0,1:T(4,128)(2,1)S(1)} %get-tuple-element.15), channel_id=1, source_target_pairs={{0,2},{1,3},{2,0},{3,1},{4,6},{5,7},{6,4},{7,5},{8,10},{9,11},{10,... | collective-permute-start | bytes 24584 | tf_op jit(solution)/shard_map/ppermute | solution.py:126
  55.9 2.9 %collective-permute-start.10 = (bf16[2,256,2,512]{3,1,0,2:T(8,128)(2,1)S(1)}, bf16[2,256,2,512]{3,1,0,2:T(8,128)(2,1)S(1)}, u32[]{:S(2)}, u32[]{:S(2)}) collective-permute-start(bf16[2,256,2,512]{3,1,0,2:T(8,128)(2,1)S(1)} %constant_dynamic-update-slice_fusion), channel_id=1, source_target_pairs={{0,1},{1,0},{2,3},{3,2},{4,5},{5,4},{6,7},{7,6},{8,9},{9,8},{10,11... | collective-permute-start | bytes 3145736 | tf_op jit(solution)/shard_map/ppermute | solution.py:101

commit v18 on v17

--- a/solution.py
+++ b/solution.py
@@ -143,7 +143,8 @@
     receivers = exchange_receivers(whitened[0])
     shard = lax.axis_index(CHAN_AXES)
     own_rows = lax.dynamic_slice_in_dim(source_rows[0], shard * per_shard, per_shard)
-    own_sources = jnp.take(whitened, own_rows, axis=1)
+    own_records = jnp.take(records[0], own_rows, axis=0)
+    own_sources = whiten(own_records).reshape(1, per_shard, 2, NBINS)
     sources = collect(own_sources)
     real_part, imag_part = cross_parts(sources, receivers)
     return transform(real_part, imag_part, weights, lag_scale)

time: 74.1 us -> 79.9 us (1.078)
  matrix products: 7.3 us -> 14.6 us
  waiting for transfers between devices: 16.4 us -> 15 us
  starting transfers between devices: 30.7 us -> 29.7 us
    dot_general x1 -> x2, matrix products: 7.3 us -> 14.6 us  [whiten(): jnp.dot(row_data, band_table(), preferred_element_type=jnp.float32)]
    ppermute x11, waiting for transfers between devices: 16.3 us -> 15 us  [ring_gather(): lax.ppermute(value, axis_name, [(i, (i + shift) % size) for i in range(si...]
    another operation x2 -> x6, other arithmetic: 0.03 us -> 1.16 us  [normalize(): return jnp.stack([centre_re, centre_im], axis=1).astype(jnp.bfloat16)]
  transfers between devices with their start and end apart: 14 -> 14, of which waited for: 6 -> 5; matrix products, arithmetic and copies ran while one was open for 1% -> 11% of each run, Pallas kernels for 0% -> 0%
where the time goes in v18:
time: 79.9 us; the launch traced here: 79.4 us
  starting transfers between devices  29.7 us (37%)
  waiting for transfers between devices  15 us (19%)
  matrix products  14.6 us (18%)
  Pallas kernels  9.65 us (12%)
  other arithmetic  7.85 us (10%)
  local copies, waits for them, and re-layouts  1.8 us (2%)
  between operations  0.8 us (1%)
    ppermute x11, starting transfers between devices, ring_gather(): lax.ppermute(value, axis_name, [(i, (i + shift) % size) for i in range(si...  19.9 us
    ppermute x11, waiting for transfers between devices, ring_gather(): lax.ppermute(value, axis_name, [(i, (i + shift) % size) for i in range(si...  15 us
    dot_general x2, matrix products, whiten(): jnp.dot(row_data, band_table(), preferred_element_type=jnp.float32)  14.6 us
    ppermute x3, starting transfers between devices, exchange_receivers(): lax.ppermute(block, WIN_AXES, [(i, (i + shift) % count) for i in range(co...  9.78 us
    pallas_call x1, Pallas kernels, transform(): pl.pallas_call(functools.partial(lag_kernel, scale=lag_scale), out_shape=...  9.65 us
    reduce_sum x1, other arithmetic, cross_parts(): jnp.sum(src[..., 1, :] * rec[..., 0, :] - src[..., 0, :] * rec[..., 1, :]...  4.39 us
  transfers between devices with their start and end apart: 14, of which 5 were waited for; matrix products, arithmetic and copies ran while one was open for 11% of the time, Pallas kernels for 0%

profile of v18, /device:TPU:1, one launch (start us, length us, event | category | flops | bytes accessed | tf_op | source)
XLA Modules:
  0.0 79.4 jit_solution(12689849950130778562)
XLA Ops:
  0.0 0.0 copy-start
  0.0 0.8 fusion.24
  0.8 0.7 compare_and_fusion
  1.5 0.0 copy-done
  1.5 0.6 gather_fusion
  2.1 7.3 %fusion = f32[4,1152]{1,0:T(4,128)S(1)} fusion(bf16[7680,1152]{1,0:T(8,128)(2,1)} %constant.243.clone, bf16[4,7680]{1,0:T(4,128)(2,1)S(1)} %gather_fusion, pred[4]{0:T(512)(128)(4,1)S(1)} %compare_and_fusion), kind=kOutput, calls=%fused_computation.11 | convolution fusion | flops 70809600 | bytes 17774596 | tf_op jit(solution)/shard_map/dot_general | solution.py:59
  9.5 0.1 fusion.11
  9.6 0.3 fusion.23
  9.9 0.1 fusion.22
  10.0 7.8 %collective-permute-start = (bf16[1,4,2,512]{3,1,2,0:T(4,128)(2,1)S(1)}, bf16[1,4,2,512]{3,1,2,0:T(4,128)(2,1)S(1)}, u32[]{:S(2)}, u32[]{:S(2)}) collective-permute-start(bf16[1,4,2,512]{3,1,2,0:T(4,128)(2,1)S(1)} %pad_maximum_fusion), channel_id=1, source_target_pairs={{0,2},{2,0},{1,3},{3,1},{4,6},{6,4},{5,7},{7,5},{8,10},{10,8},{9,1... | collective-permute-start | bytes 24584 | tf_op jit(solution)/shard_map/ppermute | solution.py:101
  17.8 7.3 %convolution_bitcast_fusion = f32[16,1152]{1,0:T(8,128)S(1)} fusion(bf16[7680,1152]{1,0:T(8,128)(2,1)} %constant.243.clone, bf16[1,16,7680]{2,1,0:T(8,128)(2,1)S(1)} %copy-done), kind=kOutput, calls=%fused_computation.3 | convolution fusion | flops 283115520 | bytes 18014208 | tf_op jit(solution)/shard_map/dot_general | solution.py:59
  25.1 0.1 fusion.2
  25.2 0.6 fusion.9
  25.9 0.1 fusion.8
  26.2 0.0 collective-permute-done
  26.2 2.6 %collective-permute-start.3 = (bf16[2,4,2,512]{3,1,0,2:T(4,128)(2,1)S(1)}, bf16[2,4,2,512]{3,1,0,2:T(4,128)(2,1)S(1)}, u32[]{:S(2)}, u32[]{:S(2)}) collective-permute-start(bf16[2,4,2,512]{3,1,0,2:T(4,128)(2,1)S(1)} %bitcast_dynamic-update-slice_fusion.5), channel_id=1, source_target_pairs={{0,12},{4,0},{8,4},{12,8},{1,13},{5,1},{9,5},{13,9},{2,14},{6,2},{... | collective-permute-start | bytes 49160 | tf_op jit(solution)/shard_map/ppermute | solution.py:101
  28.8 0.5 collective-permute-start.2
  29.3 0.6 collective-permute-start.1
  30.0 3.2 %collective-permute-done.1 = bf16[2,4,2,512]{3,1,0,2:T(4,128)(2,1)S(1)} collective-permute-done((bf16[2,4,2,512]{3,1,0,2:T(4,128)(2,1)S(1)}, bf16[2,4,2,512]{3,1,0,2:T(4,128)(2,1)S(1)}, u32[]{:S(2)}, u32[]{:S(2)}) %collective-permute-start.1) | collective-permute-done | bytes 16416 | tf_op jit(solution)/shard_map/ppermute | solution.py:101
  33.1 0.0 collective-permute-done.2
  33.2 0.0 collective-permute-done.3
  33.2 1.7 %collective-permute-start.6 = (bf16[2,16,2,512]{3,1,0,2:T(8,128)(2,1)S(1)}, bf16[2,16,2,512]{3,1,0,2:T(8,128)(2,1)S(1)}, u32[]{:S(2)}, u32[]{:S(2)}) collective-permute-start(bf16[2,16,2,512]{3,1,0,2:T(8,128)(2,1)S(1)} %constant_dynamic-update-slice_fusion.8), channel_id=1, source_target_pairs={{0,48},{16,0},{32,16},{48,32},{1,49},{17,1},{33,17},{49,33},{2,50}... | collective-permute-start | bytes 196616 | tf_op jit(solution)/shard_map/ppermute | solution.py:101
  34.9 0.3 collective-permute-start.5
  35.2 0.7 collective-permute-start.4
  36.0 4.5 %collective-permute-done.4 = bf16[2,16,2,512]{3,1,0,2:T(8,128)(2,1)S(1)} collective-permute-done((bf16[2,16,2,512]{3,1,0,2:T(8,128)(2,1)S(1)}, bf16[2,16,2,512]{3,1,0,2:T(8,128)(2,1)S(1)}, u32[]{:S(2)}, u32[]{:S(2)}) %collective-permute-start.4) | collective-permute-done | bytes 65568 | tf_op jit(solution)/shard_map/ppermute | solution.py:101
  40.5 0.0 collective-permute-done.5
  40.6 0.0 collective-permute-done.6
  40.6 1.4 %collective-permute-start.7 = (bf16[2,64,2,512]{3,1,0,2:T(8,128)(2,1)S(1)}, bf16[2,64,2,512]{3,1,0,2:T(8,128)(2,1)S(1)}, u32[]{:S(2)}, u32[]{:S(2)}) collective-permute-start(bf16[2,64,2,512]{3,1,0,2:T(8,128)(2,1)S(1)} %constant_dynamic-update-slice_fusion.4), channel_id=1, source_target_pairs={{0,64},{64,128},{128,192},{192,0},{1,65},{65,129},{129,193},{193,1... | collective-permute-start | bytes 786440 | tf_op jit(solution)/shard_map/ppermute | solution.py:101
  42.0 4.3 %collective-permute-start.13 = (bf16[4,2,512]{2,0,1:T(4,128)(2,1)S(1)}, bf16[4,2,512]{2,0,1:T(4,128)(2,1)S(1)}, u32[]{:S(2)}, u32[]{:S(2)}) collective-permute-start(bf16[4,2,512]{2,0,1:T(4,128)(2,1)S(1)} %get-tuple-element.15), channel_id=1, source_target_pairs={{0,3},{1,0},{2,1},{3,2},{4,7},{5,4},{6,5},{7,6},{8,11},{9,8},{10,9... | collective-permute-start | bytes 24584 | tf_op jit(solution)/shard_map/ppermute | solution.py:126
  46.3 1.4 %collective-permute-start.11 = (bf16[4,2,512]{2,0,1:T(4,128)(2,1)S(1)}, bf16[4,2,512]{2,0,1:T(4,128)(2,1)S(1)}, u32[]{:S(2)}, u32[]{:S(2)}) collective-permute-start(bf16[4,2,512]{2,0,1:T(4,128)(2,1)S(1)} %get-tuple-element.16), channel_id=1, source_target_pairs={{0,1},{1,2},{2,3},{3,0},{4,5},{5,6},{6,7},{7,4},{8,9},{9,10},{10,1... | collective-permute-start | bytes 24584 | tf_op jit(solution)/shard_map/ppermute | solution.py:126
  47.7 2.6 %collective-permute-start.8 = (bf16[2,64,2,512]{3,1,0,2:T(8,128)(2,1)S(1)}, bf16[2,64,2,512]{3,1,0,2:T(8,128)(2,1)S(1)}, u32[]{:S(2)}, u32[]{:S(2)}) collective-permute-start(bf16[2,64,2,512]{3,1,0,2:T(8,128)(2,1)S(1)} %constant_dynamic-update-slice_fusion.4), channel_id=1, source_target_pairs={{0,128},{64,192},{128,0},{192,64},{1,129},{65,193},{129,1},{193,65... | collective-permute-start | bytes 786440 | tf_op jit(solution)/shard_map/ppermute | solution.py:101
  50.6 1.3 %collective-permute-start.9 = (bf16[2,64,2,512]{3,1,0,2:T(8,128)(2,1)S(1)}, bf16[2,64,2,512]{3,1,0,2:T(8,128)(2,1)S(1)}, u32[]{:S(2)}, u32[]{:S(2)}) collective-permute-start(bf16[2,64,2,512]{3,1,0,2:T(8,128)(2,1)S(1)} %constant_dynamic-update-slice_fusion.4), channel_id=1, source_target_pairs={{0,192},{64,0},{128,64},{192,128},{1,193},{65,1},{129,65},{193,129... | collective-permute-start | bytes 786440 | tf_op jit(solution)/shard_map/ppermute | solution.py:101
  52.0 0.1 broadcast_in_dim.53
  52.1 0.0 collective-permute-done.7
  52.1 4.0 %collective-permute-start.12 = (bf16[4,2,512]{2,0,1:T(4,128)(2,1)S(1)}, bf16[4,2,512]{2,0,1:T(4,128)(2,1)S(1)}, u32[]{:S(2)}, u32[]{:S(2)}) collective-permute-start(bf16[4,2,512]{2,0,1:T(4,128)(2,1)S(1)} %get-tuple-element.17), channel_id=1, source_target_pairs={{0,2},{1,3},{2,0},{3,1},{4,6},{5,7},{6,4},{7,5},{8,10},{9,11},{10,... | collective-permute-start | bytes 24584 | tf_op jit(solution)/shard_map/ppermute | solution.py:126
  56.2 1.4 %collective-permute-done.8 = bf16[2,64,2,512]{3,1,0,2:T(8,128)(2,1)S(1)} collective-permute-done((bf16[2,64,2,512]{3,1,0,2:T(8,128)(2,1)S(1)}, bf16[2,64,2,512]{3,1,0,2:T(8,128)(2,1)S(1)}, u32[]{:S(2)}, u32[]{:S(2)}) %collective-permute-start.8) | collective-permute-done | bytes 262176 | tf_op jit(solution)/shard_map/ppermute | solution.py:101
  57.6 3.8 %collective-permute-done.9 = bf16[2,64,2,512]{3,1,0,2:T(8,128)(2,1)S(1)} collective-permute-done((bf16[2,64,2,512]{3,1,0,2:T(8,128)(2,1)S(1)}, bf16[2,64,2,512]{3,1,0,2:T(8,128)(2,1)S(1)}, u32[]{:S(2)}, u32[]{:S(2)}) %collective-permute-start.9) | collective-permute-done | bytes 262176 | tf_op jit(solution)/shard_map/ppermute | solution.py:101
  61.5 0.3 collective-permute-start.10
  61.9 0.0 collective-permute-done.11
  61.9 0.0 collective-permute-done.12
  61.9 0.0 collective-permute-done.13
  62.0 0.2 broadcast_in_dim.52
  62.1 0.1 bitcast_dynamic-update-slice_fusion.1
  62.2 2.0 %collective-permute-done.10 = bf16[2,256,2,512]{3,1,0,2:T(8,128)(2,1)S(1)} collective-permute-done((bf16[2,256,2,512]{3,1,0,2:T(8,128)(2,1)S(1)}, bf16[2,256,2,512]{3,1,0,2:T(8,128)(2,1)S(1)}, u32[]{:S(2)}, u32[]{:S(2)}) %collective-permute-start.10) | collective-permute-done | bytes 1048608 | tf_op jit(solution)/shard_map/ppermute | solution.py:101
  64.3 0.1 bitcast_dynamic-update-slice_fusion
  64.4 0.6 broadcast_in_dim.61
  64.9 0.4 slice_bitcast_fusion.1
  65.4 4.4 %subtract_reduce_fusion = (bf16[256,4,512]{2,0,1:T(8,128)(2,1)}, bf16[256,4,512]{2,0,1:T(8,128)(2,1)}) fusion(f32[4,4,512]{2,1,0:T(4,128)S(1)} %get-tuple-element.14, f32[4,256,512]{2,1,0:T(8,128)S(1)} %get-tuple-element.12, f32[4,4,512]{2,1,0:T(4,128)S(1)} %get-tuple-element.13, f32[4,256,512]{2,1,0:T(8,128)S(1)} %get-tuple-element.11), kind=kLoop, calls=%fused_computation.1 | loop fusion | flops 15728640 | bytes 6356992 | tf_op jit(solution)/shard_map/reduce_sum | solution.py:66
  69.8 9.7 %shard_map.55 = f32[256,4,2048]{2,1,0:T(4,128)} custom-call(bf16[4,256,512]{2,1,0:T(8,128)(2,1)} %bitcast.55, bf16[4,256,512]{2,1,0:T(8,128)(2,1)} %bitcast.54, bf16[1024,2048]{1,0:T(8,128)(2,1)} %constant.244.clone.w_ref), custom_call_target="tpu_custom_call" | custom-call | tf_op jit(solution)/shard_map/pallas_call | solution.py:84
  (27 shorter events, 0.4 us)
Async XLA Ops:
  0.0 1.5 %copy-start = (bf16[1,16,7680]{2,1,0:T(8,128)(2,1)S(1)}, bf16[1,16,7680]{2,1,0:T(8,128)(2,1)}, u32[]{:S(2)}) copy-start(bf16[1,16,7680]{2,1,0:T(8,128)(2,1)} %param.5) | copy-start | bytes 737284
  10.0 16.2 %collective-permute-start = (bf16[1,4,2,512]{3,1,2,0:T(4,128)(2,1)S(1)}, bf16[1,4,2,512]{3,1,2,0:T(4,128)(2,1)S(1)}, u32[]{:S(2)}, u32[]{:S(2)}) collective-permute-start(bf16[1,4,2,512]{3,1,2,0:T(4,128)(2,1)S(1)} %pad_maximum_fusion), channel_id=1, source_target_pairs={{0,2},{2,0},{1,3},{3,1},{4,6},{6,4},{5,7},{7,5},{8,10},{10,8},{9,1... | collective-permute-start | bytes 24584 | tf_op jit(solution)/shard_map/ppermute | solution.py:101
  26.2 6.9 %collective-permute-start.3 = (bf16[2,4,2,512]{3,1,0,2:T(4,128)(2,1)S(1)}, bf16[2,4,2,512]{3,1,0,2:T(4,128)(2,1)S(1)}, u32[]{:S(2)}, u32[]{:S(2)}) collective-permute-start(bf16[2,4,2,512]{3,1,0,2:T(4,128)(2,1)S(1)} %bitcast_dynamic-update-slice_fusion.5), channel_id=1, source_target_pairs={{0,12},{4,0},{8,4},{12,8},{1,13},{5,1},{9,5},{13,9},{2,14},{6,2},{... | collective-permute-start | bytes 49160 | tf_op jit(solution)/shard_map/ppermute | solution.py:101
  28.8 4.3 %collective-permute-start.2 = (bf16[2,4,2,512]{3,1,0,2:T(4,128)(2,1)S(1)}, bf16[2,4,2,512]{3,1,0,2:T(4,128)(2,1)S(1)}, u32[]{:S(2)}, u32[]{:S(2)}) collective-permute-start(bf16[2,4,2,512]{3,1,0,2:T(4,128)(2,1)S(1)} %bitcast_dynamic-update-slice_fusion.5), channel_id=1, source_target_pairs={{0,8},{4,12},{8,0},{12,4},{1,9},{5,13},{9,1},{13,5},{2,10},{6,14},... | collective-permute-start | bytes 49160 | tf_op jit(solution)/shard_map/ppermute | solution.py:101
  29.3 3.8 %collective-permute-start.1 = (bf16[2,4,2,512]{3,1,0,2:T(4,128)(2,1)S(1)}, bf16[2,4,2,512]{3,1,0,2:T(4,128)(2,1)S(1)}, u32[]{:S(2)}, u32[]{:S(2)}) collective-permute-start(bf16[2,4,2,512]{3,1,0,2:T(4,128)(2,1)S(1)} %bitcast_dynamic-update-slice_fusion.5), channel_id=1, source_target_pairs={{0,4},{4,8},{8,12},{12,0},{1,5},{5,9},{9,13},{13,1},{2,6},{6,10},{... | collective-permute-start | bytes 49160 | tf_op jit(solution)/shard_map/ppermute | solution.py:101
  33.2 7.3 %collective-permute-start.6 = (bf16[2,16,2,512]{3,1,0,2:T(8,128)(2,1)S(1)}, bf16[2,16,2,512]{3,1,0,2:T(8,128)(2,1)S(1)}, u32[]{:S(2)}, u32[]{:S(2)}) collective-permute-start(bf16[2,16,2,512]{3,1,0,2:T(8,128)(2,1)S(1)} %constant_dynamic-update-slice_fusion.8), channel_id=1, source_target_pairs={{0,48},{16,0},{32,16},{48,32},{1,49},{17,1},{33,17},{49,33},{2,50}... | collective-permute-start | bytes 196616 | tf_op jit(solution)/shard_map/ppermute | solution.py:101
  34.9 5.6 %collective-permute-start.5 = (bf16[2,16,2,512]{3,1,0,2:T(8,128)(2,1)S(1)}, bf16[2,16,2,512]{3,1,0,2:T(8,128)(2,1)S(1)}, u32[]{:S(2)}, u32[]{:S(2)}) collective-permute-start(bf16[2,16,2,512]{3,1,0,2:T(8,128)(2,1)S(1)} %constant_dynamic-update-slice_fusion.8), channel_id=1, source_target_pairs={{0,32},{16,48},{32,0},{48,16},{1,33},{17,49},{33,1},{49,17},{2,34}... | collective-permute-start | bytes 196616 | tf_op jit(solution)/shard_map/ppermute | solution.py:101
  35.2 5.3 %collective-permute-start.4 = (bf16[2,16,2,512]{3,1,0,2:T(8,128)(2,1)S(1)}, bf16[2,16,2,512]{3,1,0,2:T(8,128)(2,1)S(1)}, u32[]{:S(2)}, u32[]{:S(2)}) collective-permute-start(bf16[2,16,2,512]{3,1,0,2:T(8,128)(2,1)S(1)} %constant_dynamic-update-slice_fusion.8), channel_id=1, source_target_pairs={{0,16},{16,32},{32,48},{48,0},{1,17},{17,33},{33,49},{49,1},{2,18}... | collective-permute-start | bytes 196616 | tf_op jit(solution)/shard_map/ppermute | solution.py:101
  40.6 11.5 %collective-permute-start.7 = (bf16[2,64,2,512]{3,1,0,2:T(8,128)(2,1)S(1)}, bf16[2,64,2,512]{3,1,0,2:T(8,128)(2,1)S(1)}, u32[]{:S(2)}, u32[]{:S(2)}) collective-permute-start(bf16[2,64,2,512]{3,1,0,2:T(8,128)(2,1)S(1)} %constant_dynamic-update-slice_fusion.4), channel_id=1, source_target_pairs={{0,64},{64,128},{128,192},{192,0},{1,65},{65,129},{129,193},{193,1... | collective-permute-start | bytes 786440 | tf_op jit(solution)/shard_map/ppermute | solution.py:101
  42.0 19.9 %collective-permute-start.13 = (bf16[4,2,512]{2,0,1:T(4,128)(2,1)S(1)}, bf16[4,2,512]{2,0,1:T(4,128)(2,1)S(1)}, u32[]{:S(2)}, u32[]{:S(2)}) collective-permute-start(bf16[4,2,512]{2,0,1:T(4,128)(2,1)S(1)} %get-tuple-element.15), channel_id=1, source_target_pairs={{0,3},{1,0},{2,1},{3,2},{4,7},{5,4},{6,5},{7,6},{8,11},{9,8},{10,9... | collective-permute-start | bytes 24584 | tf_op jit(solution)/shard_map/ppermute | solution.py:126
  46.3 15.5 %collective-permute-start.11 = (bf16[4,2,512]{2,0,1:T(4,128)(2,1)S(1)}, bf16[4,2,512]{2,0,1:T(4,128)(2,1)S(1)}, u32[]{:S(2)}, u32[]{:S(2)}) collective-permute-start(bf16[4,2,512]{2,0,1:T(4,128)(2,1)S(1)} %get-tuple-element.16), channel_id=1, source_target_pairs={{0,1},{1,2},{2,3},{3,0},{4,5},{5,6},{6,7},{7,4},{8,9},{9,10},{10,1... | collective-permute-start | bytes 24584 | tf_op jit(solution)/shard_map/ppermute | solution.py:126
  47.7 9.9 %collective-permute-start.8 = (bf16[2,64,2,512]{3,1,0,2:T(8,128)(2,1)S(1)}, bf16[2,64,2,512]{3,1,0,2:T(8,128)(2,1)S(1)}, u32[]{:S(2)}, u32[]{:S(2)}) collective-permute-start(bf16[2,64,2,512]{3,1,0,2:T(8,128)(2,1)S(1)} %constant_dynamic-update-slice_fusion.4), channel_id=1, source_target_pairs={{0,128},{64,192},{128,0},{192,64},{1,129},{65,193},{129,1},{193,65... | collective-permute-start | bytes 786440 | tf_op jit(solution)/shard_map/ppermute | solution.py:101
  50.6 10.8 %collective-permute-start.9 = (bf16[2,64,2,512]{3,1,0,2:T(8,128)(2,1)S(1)}, bf16[2,64,2,512]{3,1,0,2:T(8,128)(2,1)S(1)}, u32[]{:S(2)}, u32[]{:S(2)}) collective-permute-start(bf16[2,64,2,512]{3,1,0,2:T(8,128)(2,1)S(1)} %constant_dynamic-update-slice_fusion.4), channel_id=1, source_target_pairs={{0,192},{64,0},{128,64},{192,128},{1,193},{65,1},{129,65},{193,129... | collective-permute-start | bytes 786440 | tf_op jit(solution)/shard_map/ppermute | solution.py:101
  52.1 9.8 %collective-permute-start.12 = (bf16[4,2,512]{2,0,1:T(4,128)(2,1)S(1)}, bf16[4,2,512]{2,0,1:T(4,128)(2,1)S(1)}, u32[]{:S(2)}, u32[]{:S(2)}) collective-permute-start(bf16[4,2,512]{2,0,1:T(4,128)(2,1)S(1)} %get-tuple-element.17), channel_id=1, source_target_pairs={{0,2},{1,3},{2,0},{3,1},{4,6},{5,7},{6,4},{7,5},{8,10},{9,11},{10,... | collective-permute-start | bytes 24584 | tf_op jit(solution)/shard_map/ppermute | solution.py:126
  61.5 2.7 %collective-permute-start.10 = (bf16[2,256,2,512]{3,1,0,2:T(8,128)(2,1)S(1)}, bf16[2,256,2,512]{3,1,0,2:T(8,128)(2,1)S(1)}, u32[]{:S(2)}, u32[]{:S(2)}) collective-permute-start(bf16[2,256,2,512]{3,1,0,2:T(8,128)(2,1)S(1)} %constant_dynamic-update-slice_fusion), channel_id=1, source_target_pairs={{0,1},{1,0},{2,3},{3,2},{4,5},{5,4},{6,7},{7,6},{8,9},{9,8},{10,11... | collective-permute-start | bytes 3145736 | tf_op jit(solution)/shard_map/ppermute | solution.py:101

commit v19 on v17

--- a/solution.py
+++ b/solution.py
@@ -67,7 +67,7 @@
     return real_sum.astype(jnp.bfloat16), imag_sum.astype(jnp.bfloat16)
 
 
-SOURCE_BLOCK = 64
+SOURCE_BLOCK = 128
 
 
 def lag_kernel(re_ref, im_ref, w_ref, o_ref, *, scale):

time: 74.1 us -> 75.2 us (1.015)
  Pallas kernels: 9.65 us -> 10.7 us
    pallas_call x1, Pallas kernels: 9.65 us -> 10.7 us  [transform(): pl.pallas_call(functools.partial(lag_kernel, scale=lag_scale), out_shape=...]
where the time goes in v19:
time: 75.2 us; the launch traced here: 75.1 us
  starting transfers between devices  30.7 us (41%)
  waiting for transfers between devices  16.4 us (22%)
  Pallas kernels  10.7 us (14%)
  other arithmetic  7.4 us (10%)
  matrix products  7.3 us (10%)
  local copies, waits for them, and re-layouts  1.82 us (2%)
  between operations  0.77 us (1%)
    ppermute x11, starting transfers between devices, ring_gather(): lax.ppermute(value, axis_name, [(i, (i + shift) % size) for i in range(si...  20.2 us
    ppermute x11, waiting for transfers between devices, ring_gather(): lax.ppermute(value, axis_name, [(i, (i + shift) % size) for i in range(si...  16.3 us
    pallas_call x1, Pallas kernels, transform(): pl.pallas_call(functools.partial(lag_kernel, scale=lag_scale), out_shape=...  10.7 us
    ppermute x3, starting transfers between devices, exchange_receivers(): lax.ppermute(block, WIN_AXES, [(i, (i + shift) % count) for i in range(co...  10.5 us
    dot_general x1, matrix products, whiten(): jnp.dot(row_data, band_table(), preferred_element_type=jnp.float32)  7.3 us
    reduce_sum x1, other arithmetic, cross_parts(): jnp.sum(src[..., 1, :] * rec[..., 0, :] - src[..., 0, :] * rec[..., 1, :]...  4.39 us
  transfers between devices with their start and end apart: 14, of which 6 were waited for; matrix products, arithmetic and copies ran while one was open for 1% of the time, Pallas kernels for 0%

profile of v19, /device:TPU:1, one launch (start us, length us, event | category | flops | bytes accessed | tf_op | source)
XLA Modules:
  0.0 75.1 jit_solution(1260763245822952)
XLA Ops:
  0.0 0.0 copy-start
  0.0 0.8 %fusion.13 = s32[4]{0:T(128)S(1)} fusion(s32[1,256]{1,0:T(1,128)} %param.5, s32[]{:T(128)S(6)} %select_n.229), kind=kLoop, calls=%fused_computation.125 | loop fusion | flops 12 | bytes 36 | tf_op jit(solution)/shard_map/jit(_take)/jit(_where)/select_n | solution.py:146
  0.8 0.7 compare_and_fusion
  1.5 0.0 copy-done
  1.5 7.3 %convolution_bitcast_fusion = f32[16,1152]{1,0:T(8,128)S(1)} fusion(bf16[7680,1152]{1,0:T(8,128)(2,1)} %constant.240.clone, bf16[1,16,7680]{2,1,0:T(8,128)(2,1)S(1)} %copy-done), kind=kOutput, calls=%fused_computation.3 | convolution fusion | flops 283115520 | bytes 18014208 | tf_op jit(solution)/shard_map/dot_general | solution.py:59
  8.8 0.1 fusion.2
  8.9 0.6 fusion.3
  9.6 0.1 fusion.6
  9.7 0.6 gather_fusion
  10.3 0.1 broadcast_select_fusion
  10.4 7.8 %collective-permute-start = (bf16[1,4,2,512]{3,2,1,0:T(2,128)(2,1)S(1)}, bf16[1,4,2,512]{3,2,1,0:T(2,128)(2,1)S(1)}, u32[]{:S(2)}, u32[]{:S(2)}) collective-permute-start(bf16[1,4,2,512]{3,2,1,0:T(2,128)(2,1)S(1)} %broadcast_select_fusion), channel_id=1, source_target_pairs={{0,2},{2,0},{1,3},{3,1},{4,6},{6,4},{5,7},{7,5},{8,10},{10,8},{9,1... | collective-permute-start | bytes 24584 | tf_op jit(solution)/shard_map/ppermute | solution.py:101
  18.4 0.8 %collective-permute-done = bf16[1,4,2,512]{3,2,1,0:T(2,128)(2,1)S(1)} collective-permute-done((bf16[1,4,2,512]{3,2,1,0:T(2,128)(2,1)S(1)}, bf16[1,4,2,512]{3,2,1,0:T(2,128)(2,1)S(1)}, u32[]{:S(2)}, u32[]{:S(2)}) %collective-permute-start) | collective-permute-done | bytes 8224 | tf_op jit(solution)/shard_map/ppermute | solution.py:101
  19.2 2.5 %collective-permute-start.3 = (bf16[2,4,2,512]{3,1,0,2:T(4,128)(2,1)S(1)}, bf16[2,4,2,512]{3,1,0,2:T(4,128)(2,1)S(1)}, u32[]{:S(2)}, u32[]{:S(2)}) collective-permute-start(bf16[2,4,2,512]{3,1,0,2:T(4,128)(2,1)S(1)} %copy_dynamic-update-slice_fusion), channel_id=1, source_target_pairs={{0,12},{4,0},{8,4},{12,8},{1,13},{5,1},{9,5},{13,9},{2,14},{6,2},{... | collective-permute-start | bytes 49160 | tf_op jit(solution)/shard_map/ppermute | solution.py:101
  21.8 0.5 collective-permute-start.2
  22.3 0.6 collective-permute-start.1
  22.9 3.2 %collective-permute-done.1 = bf16[2,4,2,512]{3,1,0,2:T(4,128)(2,1)S(1)} collective-permute-done((bf16[2,4,2,512]{3,1,0,2:T(4,128)(2,1)S(1)}, bf16[2,4,2,512]{3,1,0,2:T(4,128)(2,1)S(1)}, u32[]{:S(2)}, u32[]{:S(2)}) %collective-permute-start.1) | collective-permute-done | bytes 16416 | tf_op jit(solution)/shard_map/ppermute | solution.py:101
  26.1 0.0 collective-permute-done.2
  26.2 0.0 collective-permute-done.3
  26.2 2.9 %collective-permute-start.6 = (bf16[2,16,2,512]{3,1,0,2:T(8,128)(2,1)S(1)}, bf16[2,16,2,512]{3,1,0,2:T(8,128)(2,1)S(1)}, u32[]{:S(2)}, u32[]{:S(2)}) collective-permute-start(bf16[2,16,2,512]{3,1,0,2:T(8,128)(2,1)S(1)} %constant_dynamic-update-slice_fusion.8), channel_id=1, source_target_pairs={{0,48},{16,0},{32,16},{48,32},{1,49},{17,1},{33,17},{49,33},{2,50}... | collective-permute-start | bytes 196616 | tf_op jit(solution)/shard_map/ppermute | solution.py:101
  29.1 0.0 collective-permute-start.5
  29.1 0.4 collective-permute-start.4
  29.5 4.7 %collective-permute-done.4 = bf16[2,16,2,512]{3,1,0,2:T(8,128)(2,1)S(1)} collective-permute-done((bf16[2,16,2,512]{3,1,0,2:T(8,128)(2,1)S(1)}, bf16[2,16,2,512]{3,1,0,2:T(8,128)(2,1)S(1)}, u32[]{:S(2)}, u32[]{:S(2)}) %collective-permute-start.4) | collective-permute-done | bytes 65568 | tf_op jit(solution)/shard_map/ppermute | solution.py:101
  34.2 0.0 collective-permute-done.5
  34.2 0.0 collective-permute-done.6
  34.3 1.4 %collective-permute-start.7 = (bf16[2,64,2,512]{3,1,0,2:T(8,128)(2,1)S(1)}, bf16[2,64,2,512]{3,1,0,2:T(8,128)(2,1)S(1)}, u32[]{:S(2)}, u32[]{:S(2)}) collective-permute-start(bf16[2,64,2,512]{3,1,0,2:T(8,128)(2,1)S(1)} %constant_dynamic-update-slice_fusion.4), channel_id=1, source_target_pairs={{0,64},{64,128},{128,192},{192,0},{1,65},{65,129},{129,193},{193,1... | collective-permute-start | bytes 786440 | tf_op jit(solution)/shard_map/ppermute | solution.py:101
  35.7 5.1 %collective-permute-start.13 = (bf16[4,2,512]{2,0,1:T(4,128)(2,1)S(1)}, bf16[4,2,512]{2,0,1:T(4,128)(2,1)S(1)}, u32[]{:S(2)}, u32[]{:S(2)}) collective-permute-start(bf16[4,2,512]{2,0,1:T(4,128)(2,1)S(1)} %get-tuple-element.13), channel_id=1, source_target_pairs={{0,3},{1,0},{2,1},{3,2},{4,7},{5,4},{6,5},{7,6},{8,11},{9,8},{10,9... | collective-permute-start | bytes 24584 | tf_op jit(solution)/shard_map/ppermute | solution.py:126
  40.8 4.7 %collective-permute-start.11 = (bf16[4,2,512]{2,0,1:T(4,128)(2,1)S(1)}, bf16[4,2,512]{2,0,1:T(4,128)(2,1)S(1)}, u32[]{:S(2)}, u32[]{:S(2)}) collective-permute-start(bf16[4,2,512]{2,0,1:T(4,128)(2,1)S(1)} %get-tuple-element.14), channel_id=1, source_target_pairs={{0,1},{1,2},{2,3},{3,0},{4,5},{5,6},{6,7},{7,4},{8,9},{9,10},{10,1... | collective-permute-start | bytes 24584 | tf_op jit(solution)/shard_map/ppermute | solution.py:126
  45.5 2.6 %collective-permute-start.8 = (bf16[2,64,2,512]{3,1,0,2:T(8,128)(2,1)S(1)}, bf16[2,64,2,512]{3,1,0,2:T(8,128)(2,1)S(1)}, u32[]{:S(2)}, u32[]{:S(2)}) collective-permute-start(bf16[2,64,2,512]{3,1,0,2:T(8,128)(2,1)S(1)} %constant_dynamic-update-slice_fusion.4), channel_id=1, source_target_pairs={{0,128},{64,192},{128,0},{192,64},{1,129},{65,193},{129,1},{193,65... | collective-permute-start | bytes 786440 | tf_op jit(solution)/shard_map/ppermute | solution.py:101
  48.4 1.1 %collective-permute-start.9 = (bf16[2,64,2,512]{3,1,0,2:T(8,128)(2,1)S(1)}, bf16[2,64,2,512]{3,1,0,2:T(8,128)(2,1)S(1)}, u32[]{:S(2)}, u32[]{:S(2)}) collective-permute-start(bf16[2,64,2,512]{3,1,0,2:T(8,128)(2,1)S(1)} %constant_dynamic-update-slice_fusion.4), channel_id=1, source_target_pairs={{0,192},{64,0},{128,64},{192,128},{1,193},{65,1},{129,65},{193,129... | collective-permute-start | bytes 786440 | tf_op jit(solution)/shard_map/ppermute | solution.py:101
  49.6 0.1 broadcast_in_dim.53
  49.7 0.0 collective-permute-done.7
  49.7 0.7 collective-permute-start.12
  50.4 2.7 %collective-permute-done.8 = bf16[2,64,2,512]{3,1,0,2:T(8,128)(2,1)S(1)} collective-permute-done((bf16[2,64,2,512]{3,1,0,2:T(8,128)(2,1)S(1)}, bf16[2,64,2,512]{3,1,0,2:T(8,128)(2,1)S(1)}, u32[]{:S(2)}, u32[]{:S(2)}) %collective-permute-start.8) | collective-permute-done | bytes 262176 | tf_op jit(solution)/shard_map/ppermute | solution.py:101
  53.2 2.7 %collective-permute-done.9 = bf16[2,64,2,512]{3,1,0,2:T(8,128)(2,1)S(1)} collective-permute-done((bf16[2,64,2,512]{3,1,0,2:T(8,128)(2,1)S(1)}, bf16[2,64,2,512]{3,1,0,2:T(8,128)(2,1)S(1)}, u32[]{:S(2)}, u32[]{:S(2)}) %collective-permute-start.9) | collective-permute-done | bytes 262176 | tf_op jit(solution)/shard_map/ppermute | solution.py:101
  55.9 0.3 collective-permute-start.10
  56.2 0.0 collective-permute-done.11
  56.2 0.0 collective-permute-done.12
  56.3 0.0 collective-permute-done.13
  56.3 0.2 broadcast_in_dim.52
  56.5 0.1 bitcast_dynamic-update-slice_fusion.1
  56.6 2.2 %collective-permute-done.10 = bf16[2,256,2,512]{3,1,0,2:T(8,128)(2,1)S(1)} collective-permute-done((bf16[2,256,2,512]{3,1,0,2:T(8,128)(2,1)S(1)}, bf16[2,256,2,512]{3,1,0,2:T(8,128)(2,1)S(1)}, u32[]{:S(2)}, u32[]{:S(2)}) %collective-permute-start.10) | collective-permute-done | bytes 1048608 | tf_op jit(solution)/shard_map/ppermute | solution.py:101
  58.8 0.1 bitcast_dynamic-update-slice_fusion
  58.9 0.6 broadcast_in_dim.61
  59.5 0.4 slice_bitcast_fusion.1
  60.0 4.4 %subtract_reduce_fusion = (bf16[256,4,512]{2,0,1:T(8,128)(2,1)}, bf16[256,4,512]{2,0,1:T(8,128)(2,1)}) fusion(f32[4,4,512]{2,1,0:T(4,128)S(1)} %get-tuple-element.12, f32[4,256,512]{2,1,0:T(8,128)S(1)} %get-tuple-element.10, f32[4,4,512]{2,1,0:T(4,128)S(1)} %get-tuple-element.11, f32[4,256,512]{2,1,0:T(8,128)S(1)} %get-tuple-element.9), kind=kLoop, calls=%fused_computation.1 | loop fusion | flops 15728640 | bytes 6356992 | tf_op jit(solution)/shard_map/reduce_sum | solution.py:66
  64.4 10.7 %shard_map.46 = f32[256,4,2048]{2,1,0:T(4,128)} custom-call(bf16[4,256,512]{2,1,0:T(8,128)(2,1)} %bitcast.49, bf16[4,256,512]{2,1,0:T(8,128)(2,1)} %bitcast.48, bf16[1024,2048]{1,0:T(8,128)(2,1)} %constant.241.clone.w_ref), custom_call_target="tpu_custom_call" | custom-call | tf_op jit(solution)/shard_map/pallas_call | solution.py:84
  (28 shorter events, 0.4 us)
Async XLA Ops:
  0.0 1.5 %copy-start = (bf16[1,16,7680]{2,1,0:T(8,128)(2,1)S(1)}, bf16[1,16,7680]{2,1,0:T(8,128)(2,1)}, u32[]{:S(2)}) copy-start(bf16[1,16,7680]{2,1,0:T(8,128)(2,1)} %param.4) | copy-start | bytes 737284
  10.4 8.9 %collective-permute-start = (bf16[1,4,2,512]{3,2,1,0:T(2,128)(2,1)S(1)}, bf16[1,4,2,512]{3,2,1,0:T(2,128)(2,1)S(1)}, u32[]{:S(2)}, u32[]{:S(2)}) collective-permute-start(bf16[1,4,2,512]{3,2,1,0:T(2,128)(2,1)S(1)} %broadcast_select_fusion), channel_id=1, source_target_pairs={{0,2},{2,0},{1,3},{3,1},{4,6},{6,4},{5,7},{7,5},{8,10},{10,8},{9,1... | collective-permute-start | bytes 24584 | tf_op jit(solution)/shard_map/ppermute | solution.py:101
  19.2 6.9 %collective-permute-start.3 = (bf16[2,4,2,512]{3,1,0,2:T(4,128)(2,1)S(1)}, bf16[2,4,2,512]{3,1,0,2:T(4,128)(2,1)S(1)}, u32[]{:S(2)}, u32[]{:S(2)}) collective-permute-start(bf16[2,4,2,512]{3,1,0,2:T(4,128)(2,1)S(1)} %copy_dynamic-update-slice_fusion), channel_id=1, source_target_pairs={{0,12},{4,0},{8,4},{12,8},{1,13},{5,1},{9,5},{13,9},{2,14},{6,2},{... | collective-permute-start | bytes 49160 | tf_op jit(solution)/shard_map/ppermute | solution.py:101
  21.8 4.3 %collective-permute-start.2 = (bf16[2,4,2,512]{3,1,0,2:T(4,128)(2,1)S(1)}, bf16[2,4,2,512]{3,1,0,2:T(4,128)(2,1)S(1)}, u32[]{:S(2)}, u32[]{:S(2)}) collective-permute-start(bf16[2,4,2,512]{3,1,0,2:T(4,128)(2,1)S(1)} %copy_dynamic-update-slice_fusion), channel_id=1, source_target_pairs={{0,8},{4,12},{8,0},{12,4},{1,9},{5,13},{9,1},{13,5},{2,10},{6,14},... | collective-permute-start | bytes 49160 | tf_op jit(solution)/shard_map/ppermute | solution.py:101
  22.3 3.8 %collective-permute-start.1 = (bf16[2,4,2,512]{3,1,0,2:T(4,128)(2,1)S(1)}, bf16[2,4,2,512]{3,1,0,2:T(4,128)(2,1)S(1)}, u32[]{:S(2)}, u32[]{:S(2)}) collective-permute-start(bf16[2,4,2,512]{3,1,0,2:T(4,128)(2,1)S(1)} %copy_dynamic-update-slice_fusion), channel_id=1, source_target_pairs={{0,4},{4,8},{8,12},{12,0},{1,5},{5,9},{9,13},{13,1},{2,6},{6,10},{... | collective-permute-start | bytes 49160 | tf_op jit(solution)/shard_map/ppermute | solution.py:101
  26.2 8.1 %collective-permute-start.6 = (bf16[2,16,2,512]{3,1,0,2:T(8,128)(2,1)S(1)}, bf16[2,16,2,512]{3,1,0,2:T(8,128)(2,1)S(1)}, u32[]{:S(2)}, u32[]{:S(2)}) collective-permute-start(bf16[2,16,2,512]{3,1,0,2:T(8,128)(2,1)S(1)} %constant_dynamic-update-slice_fusion.8), channel_id=1, source_target_pairs={{0,48},{16,0},{32,16},{48,32},{1,49},{17,1},{33,17},{49,33},{2,50}... | collective-permute-start | bytes 196616 | tf_op jit(solution)/shard_map/ppermute | solution.py:101
  29.1 5.1 %collective-permute-start.5 = (bf16[2,16,2,512]{3,1,0,2:T(8,128)(2,1)S(1)}, bf16[2,16,2,512]{3,1,0,2:T(8,128)(2,1)S(1)}, u32[]{:S(2)}, u32[]{:S(2)}) collective-permute-start(bf16[2,16,2,512]{3,1,0,2:T(8,128)(2,1)S(1)} %constant_dynamic-update-slice_fusion.8), channel_id=1, source_target_pairs={{0,32},{16,48},{32,0},{48,16},{1,33},{17,49},{33,1},{49,17},{2,34}... | collective-permute-start | bytes 196616 | tf_op jit(solution)/shard_map/ppermute | solution.py:101
  29.1 5.1 %collective-permute-start.4 = (bf16[2,16,2,512]{3,1,0,2:T(8,128)(2,1)S(1)}, bf16[2,16,2,512]{3,1,0,2:T(8,128)(2,1)S(1)}, u32[]{:S(2)}, u32[]{:S(2)}) collective-permute-start(bf16[2,16,2,512]{3,1,0,2:T(8,128)(2,1)S(1)} %constant_dynamic-update-slice_fusion.8), channel_id=1, source_target_pairs={{0,16},{16,32},{32,48},{48,0},{1,17},{17,33},{33,49},{49,1},{2,18}... | collective-permute-start | bytes 196616 | tf_op jit(solution)/shard_map/ppermute | solution.py:101
  34.3 15.4 %collective-permute-start.7 = (bf16[2,64,2,512]{3,1,0,2:T(8,128)(2,1)S(1)}, bf16[2,64,2,512]{3,1,0,2:T(8,128)(2,1)S(1)}, u32[]{:S(2)}, u32[]{:S(2)}) collective-permute-start(bf16[2,64,2,512]{3,1,0,2:T(8,128)(2,1)S(1)} %constant_dynamic-update-slice_fusion.4), channel_id=1, source_target_pairs={{0,64},{64,128},{128,192},{192,0},{1,65},{65,129},{129,193},{193,1... | collective-permute-start | bytes 786440 | tf_op jit(solution)/shard_map/ppermute | solution.py:101
  35.7 20.6 %collective-permute-start.13 = (bf16[4,2,512]{2,0,1:T(4,128)(2,1)S(1)}, bf16[4,2,512]{2,0,1:T(4,128)(2,1)S(1)}, u32[]{:S(2)}, u32[]{:S(2)}) collective-permute-start(bf16[4,2,512]{2,0,1:T(4,128)(2,1)S(1)} %get-tuple-element.13), channel_id=1, source_target_pairs={{0,3},{1,0},{2,1},{3,2},{4,7},{5,4},{6,5},{7,6},{8,11},{9,8},{10,9... | collective-permute-start | bytes 24584 | tf_op jit(solution)/shard_map/ppermute | solution.py:126
  40.8 15.4 %collective-permute-start.11 = (bf16[4,2,512]{2,0,1:T(4,128)(2,1)S(1)}, bf16[4,2,512]{2,0,1:T(4,128)(2,1)S(1)}, u32[]{:S(2)}, u32[]{:S(2)}) collective-permute-start(bf16[4,2,512]{2,0,1:T(4,128)(2,1)S(1)} %get-tuple-element.14), channel_id=1, source_target_pairs={{0,1},{1,2},{2,3},{3,0},{4,5},{5,6},{6,7},{7,4},{8,9},{9,10},{10,1... | collective-permute-start | bytes 24584 | tf_op jit(solution)/shard_map/ppermute | solution.py:126
  45.5 7.6 %collective-permute-start.8 = (bf16[2,64,2,512]{3,1,0,2:T(8,128)(2,1)S(1)}, bf16[2,64,2,512]{3,1,0,2:T(8,128)(2,1)S(1)}, u32[]{:S(2)}, u32[]{:S(2)}) collective-permute-start(bf16[2,64,2,512]{3,1,0,2:T(8,128)(2,1)S(1)} %constant_dynamic-update-slice_fusion.4), channel_id=1, source_target_pairs={{0,128},{64,192},{128,0},{192,64},{1,129},{65,193},{129,1},{193,65... | collective-permute-start | bytes 786440 | tf_op jit(solution)/shard_map/ppermute | solution.py:101
  48.4 7.5 %collective-permute-start.9 = (bf16[2,64,2,512]{3,1,0,2:T(8,128)(2,1)S(1)}, bf16[2,64,2,512]{3,1,0,2:T(8,128)(2,1)S(1)}, u32[]{:S(2)}, u32[]{:S(2)}) collective-permute-start(bf16[2,64,2,512]{3,1,0,2:T(8,128)(2,1)S(1)} %constant_dynamic-update-slice_fusion.4), channel_id=1, source_target_pairs={{0,192},{64,0},{128,64},{192,128},{1,193},{65,1},{129,65},{193,129... | collective-permute-start | bytes 786440 | tf_op jit(solution)/shard_map/ppermute | solution.py:101
  49.7 6.5 %collective-permute-start.12 = (bf16[4,2,512]{2,0,1:T(4,128)(2,1)S(1)}, bf16[4,2,512]{2,0,1:T(4,128)(2,1)S(1)}, u32[]{:S(2)}, u32[]{:S(2)}) collective-permute-start(bf16[4,2,512]{2,0,1:T(4,128)(2,1)S(1)} %get-tuple-element.15), channel_id=1, source_target_pairs={{0,2},{1,3},{2,0},{3,1},{4,6},{5,7},{6,4},{7,5},{8,10},{9,11},{10,... | collective-permute-start | bytes 24584 | tf_op jit(solution)/shard_map/ppermute | solution.py:126
  55.9 2.9 %collective-permute-start.10 = (bf16[2,256,2,512]{3,1,0,2:T(8,128)(2,1)S(1)}, bf16[2,256,2,512]{3,1,0,2:T(8,128)(2,1)S(1)}, u32[]{:S(2)}, u32[]{:S(2)}) collective-permute-start(bf16[2,256,2,512]{3,1,0,2:T(8,128)(2,1)S(1)} %constant_dynamic-update-slice_fusion), channel_id=1, source_target_pairs={{0,1},{1,0},{2,3},{3,2},{4,5},{5,4},{6,7},{7,6},{8,9},{9,8},{10,11... | collective-permute-start | bytes 3145736 | tf_op jit(solution)/shard_map/ppermute | solution.py:101

commit v20 on v19

--- a/solution.py
+++ b/solution.py
@@ -67,7 +67,7 @@
     return real_sum.astype(jnp.bfloat16), imag_sum.astype(jnp.bfloat16)
 
 
-SOURCE_BLOCK = 128
+SOURCE_BLOCK = 32
 
 
 def lag_kernel(re_ref, im_ref, w_ref, o_ref, *, scale):

time: 75.2 us -> 76.2 us (1.013)
  Pallas kernels: 10.7 us -> 11.5 us
    pallas_call x1, Pallas kernels: 10.7 us -> 11.5 us  [transform(): pl.pallas_call(functools.partial(lag_kernel, scale=lag_scale), out_shape=...]
where the time goes in v20:
time: 76.2 us; the launch traced here: 75.9 us
  starting transfers between devices  30.7 us (40%)
  waiting for transfers between devices  16.4 us (22%)
  Pallas kernels  11.5 us (15%)
  other arithmetic  7.4 us (10%)
  matrix products  7.3 us (10%)
  local copies, waits for them, and re-layouts  1.82 us (2%)
  between operations  0.77 us (1%)
    ppermute x11, starting transfers between devices, ring_gather(): lax.ppermute(value, axis_name, [(i, (i + shift) % size) for i in range(si...  20.2 us
    ppermute x11, waiting for transfers between devices, ring_gather(): lax.ppermute(value, axis_name, [(i, (i + shift) % size) for i in range(si...  16.3 us
    pallas_call x1, Pallas kernels, transform(): pl.pallas_call(functools.partial(lag_kernel, scale=lag_scale), out_shape=...  11.5 us
    ppermute x3, starting transfers between devices, exchange_receivers(): lax.ppermute(block, WIN_AXES, [(i, (i + shift) % count) for i in range(co...  10.5 us
    dot_general x1, matrix products, whiten(): jnp.dot(row_data, band_table(), preferred_element_type=jnp.float32)  7.3 us
    reduce_sum x1, other arithmetic, cross_parts(): jnp.sum(src[..., 1, :] * rec[..., 0, :] - src[..., 0, :] * rec[..., 1, :]...  4.39 us
  transfers between devices with their start and end apart: 14, of which 6 were waited for; matrix products, arithmetic and copies ran while one was open for 1% of the time, Pallas kernels for 0%

profile of v20, /device:TPU:1, one launch (start us, length us, event | category | flops | bytes accessed | tf_op | source)
XLA Modules:
  0.0 75.9 jit_solution(10104328075182674194)
XLA Ops:
  0.0 0.0 copy-start
  0.0 0.8 %fusion.13 = s32[4]{0:T(128)S(1)} fusion(s32[1,256]{1,0:T(1,128)} %param.5, s32[]{:T(128)S(6)} %select_n.229), kind=kLoop, calls=%fused_computation.125 | loop fusion | flops 12 | bytes 36 | tf_op jit(solution)/shard_map/jit(_take)/jit(_where)/select_n | solution.py:146
  0.8 0.7 compare_and_fusion
  1.5 0.0 copy-done
  1.5 7.3 %convolution_bitcast_fusion = f32[16,1152]{1,0:T(8,128)S(1)} fusion(bf16[7680,1152]{1,0:T(8,128)(2,1)} %constant.240.clone, bf16[1,16,7680]{2,1,0:T(8,128)(2,1)S(1)} %copy-done), kind=kOutput, calls=%fused_computation.3 | convolution fusion | flops 283115520 | bytes 18014208 | tf_op jit(solution)/shard_map/dot_general | solution.py:59
  8.8 0.1 fusion.2
  8.9 0.6 fusion.3
  9.6 0.1 fusion.6
  9.7 0.6 gather_fusion
  10.3 0.1 broadcast_select_fusion
  10.4 7.8 %collective-permute-start = (bf16[1,4,2,512]{3,2,1,0:T(2,128)(2,1)S(1)}, bf16[1,4,2,512]{3,2,1,0:T(2,128)(2,1)S(1)}, u32[]{:S(2)}, u32[]{:S(2)}) collective-permute-start(bf16[1,4,2,512]{3,2,1,0:T(2,128)(2,1)S(1)} %broadcast_select_fusion), channel_id=1, source_target_pairs={{0,2},{2,0},{1,3},{3,1},{4,6},{6,4},{5,7},{7,5},{8,10},{10,8},{9,1... | collective-permute-start | bytes 24584 | tf_op jit(solution)/shard_map/ppermute | solution.py:101
  18.4 0.8 %collective-permute-done = bf16[1,4,2,512]{3,2,1,0:T(2,128)(2,1)S(1)} collective-permute-done((bf16[1,4,2,512]{3,2,1,0:T(2,128)(2,1)S(1)}, bf16[1,4,2,512]{3,2,1,0:T(2,128)(2,1)S(1)}, u32[]{:S(2)}, u32[]{:S(2)}) %collective-permute-start) | collective-permute-done | bytes 8224 | tf_op jit(solution)/shard_map/ppermute | solution.py:101
  19.2 2.5 %collective-permute-start.3 = (bf16[2,4,2,512]{3,1,0,2:T(4,128)(2,1)S(1)}, bf16[2,4,2,512]{3,1,0,2:T(4,128)(2,1)S(1)}, u32[]{:S(2)}, u32[]{:S(2)}) collective-permute-start(bf16[2,4,2,512]{3,1,0,2:T(4,128)(2,1)S(1)} %copy_dynamic-update-slice_fusion), channel_id=1, source_target_pairs={{0,12},{4,0},{8,4},{12,8},{1,13},{5,1},{9,5},{13,9},{2,14},{6,2},{... | collective-permute-start | bytes 49160 | tf_op jit(solution)/shard_map/ppermute | solution.py:101
  21.8 0.5 collective-permute-start.2
  22.3 0.6 collective-permute-start.1
  22.9 3.2 %collective-permute-done.1 = bf16[2,4,2,512]{3,1,0,2:T(4,128)(2,1)S(1)} collective-permute-done((bf16[2,4,2,512]{3,1,0,2:T(4,128)(2,1)S(1)}, bf16[2,4,2,512]{3,1,0,2:T(4,128)(2,1)S(1)}, u32[]{:S(2)}, u32[]{:S(2)}) %collective-permute-start.1) | collective-permute-done | bytes 16416 | tf_op jit(solution)/shard_map/ppermute | solution.py:101
  26.1 0.0 collective-permute-done.2
  26.2 0.0 collective-permute-done.3
  26.2 2.9 %collective-permute-start.6 = (bf16[2,16,2,512]{3,1,0,2:T(8,128)(2,1)S(1)}, bf16[2,16,2,512]{3,1,0,2:T(8,128)(2,1)S(1)}, u32[]{:S(2)}, u32[]{:S(2)}) collective-permute-start(bf16[2,16,2,512]{3,1,0,2:T(8,128)(2,1)S(1)} %constant_dynamic-update-slice_fusion.8), channel_id=1, source_target_pairs={{0,48},{16,0},{32,16},{48,32},{1,49},{17,1},{33,17},{49,33},{2,50}... | collective-permute-start | bytes 196616 | tf_op jit(solution)/shard_map/ppermute | solution.py:101
  29.1 0.0 collective-permute-start.5
  29.1 0.4 collective-permute-start.4
  29.5 4.7 %collective-permute-done.4 = bf16[2,16,2,512]{3,1,0,2:T(8,128)(2,1)S(1)} collective-permute-done((bf16[2,16,2,512]{3,1,0,2:T(8,128)(2,1)S(1)}, bf16[2,16,2,512]{3,1,0,2:T(8,128)(2,1)S(1)}, u32[]{:S(2)}, u32[]{:S(2)}) %collective-permute-start.4) | collective-permute-done | bytes 65568 | tf_op jit(solution)/shard_map/ppermute | solution.py:101
  34.2 0.0 collective-permute-done.5
  34.2 0.0 collective-permute-done.6
  34.3 1.4 %collective-permute-start.7 = (bf16[2,64,2,512]{3,1,0,2:T(8,128)(2,1)S(1)}, bf16[2,64,2,512]{3,1,0,2:T(8,128)(2,1)S(1)}, u32[]{:S(2)}, u32[]{:S(2)}) collective-permute-start(bf16[2,64,2,512]{3,1,0,2:T(8,128)(2,1)S(1)} %constant_dynamic-update-slice_fusion.4), channel_id=1, source_target_pairs={{0,64},{64,128},{128,192},{192,0},{1,65},{65,129},{129,193},{193,1... | collective-permute-start | bytes 786440 | tf_op jit(solution)/shard_map/ppermute | solution.py:101
  35.7 5.1 %collective-permute-start.13 = (bf16[4,2,512]{2,0,1:T(4,128)(2,1)S(1)}, bf16[4,2,512]{2,0,1:T(4,128)(2,1)S(1)}, u32[]{:S(2)}, u32[]{:S(2)}) collective-permute-start(bf16[4,2,512]{2,0,1:T(4,128)(2,1)S(1)} %get-tuple-element.13), channel_id=1, source_target_pairs={{0,3},{1,0},{2,1},{3,2},{4,7},{5,4},{6,5},{7,6},{8,11},{9,8},{10,9... | collective-permute-start | bytes 24584 | tf_op jit(solution)/shard_map/ppermute | solution.py:126
  40.8 4.7 %collective-permute-start.11 = (bf16[4,2,512]{2,0,1:T(4,128)(2,1)S(1)}, bf16[4,2,512]{2,0,1:T(4,128)(2,1)S(1)}, u32[]{:S(2)}, u32[]{:S(2)}) collective-permute-start(bf16[4,2,512]{2,0,1:T(4,128)(2,1)S(1)} %get-tuple-element.14), channel_id=1, source_target_pairs={{0,1},{1,2},{2,3},{3,0},{4,5},{5,6},{6,7},{7,4},{8,9},{9,10},{10,1... | collective-permute-start | bytes 24584 | tf_op jit(solution)/shard_map/ppermute | solution.py:126
  45.5 2.6 %collective-permute-start.8 = (bf16[2,64,2,512]{3,1,0,2:T(8,128)(2,1)S(1)}, bf16[2,64,2,512]{3,1,0,2:T(8,128)(2,1)S(1)}, u32[]{:S(2)}, u32[]{:S(2)}) collective-permute-start(bf16[2,64,2,512]{3,1,0,2:T(8,128)(2,1)S(1)} %constant_dynamic-update-slice_fusion.4), channel_id=1, source_target_pairs={{0,128},{64,192},{128,0},{192,64},{1,129},{65,193},{129,1},{193,65... | collective-permute-start | bytes 786440 | tf_op jit(solution)/shard_map/ppermute | solution.py:101
  48.4 1.1 %collective-permute-start.9 = (bf16[2,64,2,512]{3,1,0,2:T(8,128)(2,1)S(1)}, bf16[2,64,2,512]{3,1,0,2:T(8,128)(2,1)S(1)}, u32[]{:S(2)}, u32[]{:S(2)}) collective-permute-start(bf16[2,64,2,512]{3,1,0,2:T(8,128)(2,1)S(1)} %constant_dynamic-update-slice_fusion.4), channel_id=1, source_target_pairs={{0,192},{64,0},{128,64},{192,128},{1,193},{65,1},{129,65},{193,129... | collective-permute-start | bytes 786440 | tf_op jit(solution)/shard_map/ppermute | solution.py:101
  49.6 0.1 broadcast_in_dim.53
  49.7 0.0 collective-permute-done.7
  49.7 0.7 collective-permute-start.12
  50.4 2.7 %collective-permute-done.8 = bf16[2,64,2,512]{3,1,0,2:T(8,128)(2,1)S(1)} collective-permute-done((bf16[2,64,2,512]{3,1,0,2:T(8,128)(2,1)S(1)}, bf16[2,64,2,512]{3,1,0,2:T(8,128)(2,1)S(1)}, u32[]{:S(2)}, u32[]{:S(2)}) %collective-permute-start.8) | collective-permute-done | bytes 262176 | tf_op jit(solution)/shard_map/ppermute | solution.py:101
  53.2 2.7 %collective-permute-done.9 = bf16[2,64,2,512]{3,1,0,2:T(8,128)(2,1)S(1)} collective-permute-done((bf16[2,64,2,512]{3,1,0,2:T(8,128)(2,1)S(1)}, bf16[2,64,2,512]{3,1,0,2:T(8,128)(2,1)S(1)}, u32[]{:S(2)}, u32[]{:S(2)}) %collective-permute-start.9) | collective-permute-done | bytes 262176 | tf_op jit(solution)/shard_map/ppermute | solution.py:101
  55.9 0.3 collective-permute-start.10
  56.2 0.0 collective-permute-done.11
  56.2 0.0 collective-permute-done.12
  56.3 0.0 collective-permute-done.13
  56.3 0.2 broadcast_in_dim.52
  56.5 0.1 bitcast_dynamic-update-slice_fusion.1
  56.6 2.2 %collective-permute-done.10 = bf16[2,256,2,512]{3,1,0,2:T(8,128)(2,1)S(1)} collective-permute-done((bf16[2,256,2,512]{3,1,0,2:T(8,128)(2,1)S(1)}, bf16[2,256,2,512]{3,1,0,2:T(8,128)(2,1)S(1)}, u32[]{:S(2)}, u32[]{:S(2)}) %collective-permute-start.10) | collective-permute-done | bytes 1048608 | tf_op jit(solution)/shard_map/ppermute | solution.py:101
  58.8 0.1 bitcast_dynamic-update-slice_fusion
  58.9 0.6 broadcast_in_dim.61
  59.5 0.4 slice_bitcast_fusion.1
  60.0 4.4 %subtract_reduce_fusion = (bf16[256,4,512]{2,0,1:T(8,128)(2,1)}, bf16[256,4,512]{2,0,1:T(8,128)(2,1)}) fusion(f32[4,4,512]{2,1,0:T(4,128)S(1)} %get-tuple-element.12, f32[4,256,512]{2,1,0:T(8,128)S(1)} %get-tuple-element.10, f32[4,4,512]{2,1,0:T(4,128)S(1)} %get-tuple-element.11, f32[4,256,512]{2,1,0:T(8,128)S(1)} %get-tuple-element.9), kind=kLoop, calls=%fused_computation.1 | loop fusion | flops 15728640 | bytes 6356992 | tf_op jit(solution)/shard_map/reduce_sum | solution.py:66
  64.4 11.5 %shard_map.46 = f32[256,4,2048]{2,1,0:T(4,128)} custom-call(bf16[4,256,512]{2,1,0:T(8,128)(2,1)} %bitcast.49, bf16[4,256,512]{2,1,0:T(8,128)(2,1)} %bitcast.48, bf16[1024,2048]{1,0:T(8,128)(2,1)} %constant.241.clone.w_ref), custom_call_target="tpu_custom_call" | custom-call | tf_op jit(solution)/shard_map/pallas_call | solution.py:84
  (28 shorter events, 0.4 us)
Async XLA Ops:
  0.0 1.5 %copy-start = (bf16[1,16,7680]{2,1,0:T(8,128)(2,1)S(1)}, bf16[1,16,7680]{2,1,0:T(8,128)(2,1)}, u32[]{:S(2)}) copy-start(bf16[1,16,7680]{2,1,0:T(8,128)(2,1)} %param.4) | copy-start | bytes 737284
  10.4 8.9 %collective-permute-start = (bf16[1,4,2,512]{3,2,1,0:T(2,128)(2,1)S(1)}, bf16[1,4,2,512]{3,2,1,0:T(2,128)(2,1)S(1)}, u32[]{:S(2)}, u32[]{:S(2)}) collective-permute-start(bf16[1,4,2,512]{3,2,1,0:T(2,128)(2,1)S(1)} %broadcast_select_fusion), channel_id=1, source_target_pairs={{0,2},{2,0},{1,3},{3,1},{4,6},{6,4},{5,7},{7,5},{8,10},{10,8},{9,1... | collective-permute-start | bytes 24584 | tf_op jit(solution)/shard_map/ppermute | solution.py:101
  19.2 6.9 %collective-permute-start.3 = (bf16[2,4,2,512]{3,1,0,2:T(4,128)(2,1)S(1)}, bf16[2,4,2,512]{3,1,0,2:T(4,128)(2,1)S(1)}, u32[]{:S(2)}, u32[]{:S(2)}) collective-permute-start(bf16[2,4,2,512]{3,1,0,2:T(4,128)(2,1)S(1)} %copy_dynamic-update-slice_fusion), channel_id=1, source_target_pairs={{0,12},{4,0},{8,4},{12,8},{1,13},{5,1},{9,5},{13,9},{2,14},{6,2},{... | collective-permute-start | bytes 49160 | tf_op jit(solution)/shard_map/ppermute | solution.py:101
  21.8 4.3 %collective-permute-start.2 = (bf16[2,4,2,512]{3,1,0,2:T(4,128)(2,1)S(1)}, bf16[2,4,2,512]{3,1,0,2:T(4,128)(2,1)S(1)}, u32[]{:S(2)}, u32[]{:S(2)}) collective-permute-start(bf16[2,4,2,512]{3,1,0,2:T(4,128)(2,1)S(1)} %copy_dynamic-update-slice_fusion), channel_id=1, source_target_pairs={{0,8},{4,12},{8,0},{12,4},{1,9},{5,13},{9,1},{13,5},{2,10},{6,14},... | collective-permute-start | bytes 49160 | tf_op jit(solution)/shard_map/ppermute | solution.py:101
  22.3 3.8 %collective-permute-start.1 = (bf16[2,4,2,512]{3,1,0,2:T(4,128)(2,1)S(1)}, bf16[2,4,2,512]{3,1,0,2:T(4,128)(2,1)S(1)}, u32[]{:S(2)}, u32[]{:S(2)}) collective-permute-start(bf16[2,4,2,512]{3,1,0,2:T(4,128)(2,1)S(1)} %copy_dynamic-update-slice_fusion), channel_id=1, source_target_pairs={{0,4},{4,8},{8,12},{12,0},{1,5},{5,9},{9,13},{13,1},{2,6},{6,10},{... | collective-permute-start | bytes 49160 | tf_op jit(solution)/shard_map/ppermute | solution.py:101
  26.2 8.1 %collective-permute-start.6 = (bf16[2,16,2,512]{3,1,0,2:T(8,128)(2,1)S(1)}, bf16[2,16,2,512]{3,1,0,2:T(8,128)(2,1)S(1)}, u32[]{:S(2)}, u32[]{:S(2)}) collective-permute-start(bf16[2,16,2,512]{3,1,0,2:T(8,128)(2,1)S(1)} %constant_dynamic-update-slice_fusion.8), channel_id=1, source_target_pairs={{0,48},{16,0},{32,16},{48,32},{1,49},{17,1},{33,17},{49,33},{2,50}... | collective-permute-start | bytes 196616 | tf_op jit(solution)/shard_map/ppermute | solution.py:101
  29.1 5.1 %collective-permute-start.5 = (bf16[2,16,2,512]{3,1,0,2:T(8,128)(2,1)S(1)}, bf16[2,16,2,512]{3,1,0,2:T(8,128)(2,1)S(1)}, u32[]{:S(2)}, u32[]{:S(2)}) collective-permute-start(bf16[2,16,2,512]{3,1,0,2:T(8,128)(2,1)S(1)} %constant_dynamic-update-slice_fusion.8), channel_id=1, source_target_pairs={{0,32},{16,48},{32,0},{48,16},{1,33},{17,49},{33,1},{49,17},{2,34}... | collective-permute-start | bytes 196616 | tf_op jit(solution)/shard_map/ppermute | solution.py:101
  29.1 5.1 %collective-permute-start.4 = (bf16[2,16,2,512]{3,1,0,2:T(8,128)(2,1)S(1)}, bf16[2,16,2,512]{3,1,0,2:T(8,128)(2,1)S(1)}, u32[]{:S(2)}, u32[]{:S(2)}) collective-permute-start(bf16[2,16,2,512]{3,1,0,2:T(8,128)(2,1)S(1)} %constant_dynamic-update-slice_fusion.8), channel_id=1, source_target_pairs={{0,16},{16,32},{32,48},{48,0},{1,17},{17,33},{33,49},{49,1},{2,18}... | collective-permute-start | bytes 196616 | tf_op jit(solution)/shard_map/ppermute | solution.py:101
  34.3 15.4 %collective-permute-start.7 = (bf16[2,64,2,512]{3,1,0,2:T(8,128)(2,1)S(1)}, bf16[2,64,2,512]{3,1,0,2:T(8,128)(2,1)S(1)}, u32[]{:S(2)}, u32[]{:S(2)}) collective-permute-start(bf16[2,64,2,512]{3,1,0,2:T(8,128)(2,1)S(1)} %constant_dynamic-update-slice_fusion.4), channel_id=1, source_target_pairs={{0,64},{64,128},{128,192},{192,0},{1,65},{65,129},{129,193},{193,1... | collective-permute-start | bytes 786440 | tf_op jit(solution)/shard_map/ppermute | solution.py:101
  35.7 20.6 %collective-permute-start.13 = (bf16[4,2,512]{2,0,1:T(4,128)(2,1)S(1)}, bf16[4,2,512]{2,0,1:T(4,128)(2,1)S(1)}, u32[]{:S(2)}, u32[]{:S(2)}) collective-permute-start(bf16[4,2,512]{2,0,1:T(4,128)(2,1)S(1)} %get-tuple-element.13), channel_id=1, source_target_pairs={{0,3},{1,0},{2,1},{3,2},{4,7},{5,4},{6,5},{7,6},{8,11},{9,8},{10,9... | collective-permute-start | bytes 24584 | tf_op jit(solution)/shard_map/ppermute | solution.py:126
  40.8 15.4 %collective-permute-start.11 = (bf16[4,2,512]{2,0,1:T(4,128)(2,1)S(1)}, bf16[4,2,512]{2,0,1:T(4,128)(2,1)S(1)}, u32[]{:S(2)}, u32[]{:S(2)}) collective-permute-start(bf16[4,2,512]{2,0,1:T(4,128)(2,1)S(1)} %get-tuple-element.14), channel_id=1, source_target_pairs={{0,1},{1,2},{2,3},{3,0},{4,5},{5,6},{6,7},{7,4},{8,9},{9,10},{10,1... | collective-permute-start | bytes 24584 | tf_op jit(solution)/shard_map/ppermute | solution.py:126
  45.5 7.6 %collective-permute-start.8 = (bf16[2,64,2,512]{3,1,0,2:T(8,128)(2,1)S(1)}, bf16[2,64,2,512]{3,1,0,2:T(8,128)(2,1)S(1)}, u32[]{:S(2)}, u32[]{:S(2)}) collective-permute-start(bf16[2,64,2,512]{3,1,0,2:T(8,128)(2,1)S(1)} %constant_dynamic-update-slice_fusion.4), channel_id=1, source_target_pairs={{0,128},{64,192},{128,0},{192,64},{1,129},{65,193},{129,1},{193,65... | collective-permute-start | bytes 786440 | tf_op jit(solution)/shard_map/ppermute | solution.py:101
  48.4 7.5 %collective-permute-start.9 = (bf16[2,64,2,512]{3,1,0,2:T(8,128)(2,1)S(1)}, bf16[2,64,2,512]{3,1,0,2:T(8,128)(2,1)S(1)}, u32[]{:S(2)}, u32[]{:S(2)}) collective-permute-start(bf16[2,64,2,512]{3,1,0,2:T(8,128)(2,1)S(1)} %constant_dynamic-update-slice_fusion.4), channel_id=1, source_target_pairs={{0,192},{64,0},{128,64},{192,128},{1,193},{65,1},{129,65},{193,129... | collective-permute-start | bytes 786440 | tf_op jit(solution)/shard_map/ppermute | solution.py:101
  49.7 6.5 %collective-permute-start.12 = (bf16[4,2,512]{2,0,1:T(4,128)(2,1)S(1)}, bf16[4,2,512]{2,0,1:T(4,128)(2,1)S(1)}, u32[]{:S(2)}, u32[]{:S(2)}) collective-permute-start(bf16[4,2,512]{2,0,1:T(4,128)(2,1)S(1)} %get-tuple-element.15), channel_id=1, source_target_pairs={{0,2},{1,3},{2,0},{3,1},{4,6},{5,7},{6,4},{7,5},{8,10},{9,11},{10,... | collective-permute-start | bytes 24584 | tf_op jit(solution)/shard_map/ppermute | solution.py:126
  55.9 2.9 %collective-permute-start.10 = (bf16[2,256,2,512]{3,1,0,2:T(8,128)(2,1)S(1)}, bf16[2,256,2,512]{3,1,0,2:T(8,128)(2,1)S(1)}, u32[]{:S(2)}, u32[]{:S(2)}) collective-permute-start(bf16[2,256,2,512]{3,1,0,2:T(8,128)(2,1)S(1)} %constant_dynamic-update-slice_fusion), channel_id=1, source_target_pairs={{0,1},{1,0},{2,3},{3,2},{4,5},{5,4},{6,7},{7,6},{8,9},{9,8},{10,11... | collective-permute-start | bytes 3145736 | tf_op jit(solution)/shard_map/ppermute | solution.py:101
